TPU v7x, 32 devices: a whole 2x2x4 slice. The times are simulated.
32 devices in a mesh: atoms: 8 (over z, x), samples: 4 (over y, core).
Axes of the slice: x: 2, y: 2, z: 4, core: 2. Of those that a mesh axis runs over, the one named last changes fastest.
Arguments:
- token_feats: bfloat16 [2048, 768], P('atoms', 'samples'), may hold values from -6 to 6
- proj_w: bfloat16 [768, 128], P('samples'), may hold values from -0.21875 to 0.21875
- atom_single: bfloat16 [16384, 128], P('atoms'), may hold values from -6 to 6
- atom_token: int32 [16384], P('atoms'), may hold values from 0 to 2047, as said below
- true_coords: float32 [3, 16384], P(None, 'atoms'), may hold values from -12 to 12
- noise: float32 [4, 3, 16384], P('samples', None, 'atoms'), may hold values from -6 to 6
- sigma: float32 [4], P('samples'), may hold values from 0.5 to 4
- coord_in: float32 [3, 128], replicated, may hold values from -3.5 to 3.5
- w_qkv: bfloat16 [3, 128, 384], replicated, as said below
- w_o: bfloat16 [3, 128, 128], replicated, may hold values from -0.5 to 0.5
- w_gu: bfloat16 [3, 128, 512], replicated, may hold values from -0.5 to 0.5
- w_down: bfloat16 [3, 256, 128], replicated, may hold values from -0.375 to 0.375
- gains: float32 [3, 2, 128], replicated, may hold values from 0.1 to 1.9
- w_out: float32 [128, 3], replicated, may hold values from -0.5 to 0.5
- pair_blocks: int32 [128, 13], P('atoms'), may hold values from 0 to 127, as said below
- pair_count: int32 [128], P('atoms'), may hold values from 1 to 13, as said below
Outputs:
- coord_grad: float32 [4, 3, 16384], P('samples', None, 'atoms')
- lddt_grad: float32 [4, 3, 16384], P('samples', None, 'atoms')
Inputs may be any that keep to these rules, and one draw needn't show every extreme that they name: `atom_token`: atom a belongs to a token that differs from a // 8 by at most 16 before clipping to the token range; in each aligned run of 2048 atoms the first atom is -16 and the last +16 from that value before clipping. `pair_blocks`: the first pair_count[b] entries of row b are distinct blocks, the first being b itself; entries past pair_count[b] are b. Listing is symmetric: c is among the live entries of row b exactly when b is among the live entries of row c. `pair_count`: some block has 13 live entries. `w_qkv`: Queries, keys and values stand side by side along the last dimension.
All inputs are finite; a program needn't handle non-finite values.
Results may differ from a plain program's by a relative error of at most 0.018.
Values may be sent and summed in bfloat16 or wider, within the bound.
No kernel may reach another device: no remote copies, remote signals or barrier semaphores. Data moves between devices by JAX's collectives and lax.ppermute only.
A program may use at most 64 MiB of HBM per device.

v0:
```python
import math

import jax
import jax.numpy as jnp
from jax import lax
from jax.experimental import pallas as pl
from jax.experimental.pallas import tpu as pltpu
from jax.sharding import PartitionSpec as P

HEADS = 4
FF_ATOM = 256
LAYERS = 3
QBLK = 32
KWIN = 128
HALO_TOK = 16
PAIR_BLK = 128


sigma_data = 2.0
norm_epsilon = 1e-05
thresholds = (0.5, 1.0, 2.0, 4.0)


def extended(value, sides, width):
    for axis, dim in sides:
        peers, length = (lax.axis_size(axis), value.shape[dim])
        up = [(i, (i + 1) % peers) for i in range(peers - 1)]
        down = [(j, i) for i, j in up]
        last = lax.slice_in_dim(value, length - width, length, axis=dim)
        first = lax.slice_in_dim(value, 0, width, axis=dim)
        before = lax.ppermute(last, axis, up)
        after = lax.ppermute(first, axis, down)
        value = jnp.concatenate([before, value, after], axis=dim)
    return value


def ring_parts(value, axis):
    peers = lax.axis_size(axis)
    parts = [value]
    for shift in range(1, peers):
        pairs = [(i, (i + shift) % peers) for i in range(peers)]
        parts.append(lax.ppermute(value, axis, pairs))
    return jnp.stack(parts)


def rms_norm(tensor):
    return tensor * lax.rsqrt(jnp.mean(tensor * tensor, axis=-1, keepdims=True) + norm_epsilon)


WIN_GROUP = 8


def attend_kernel(q_ref, kv_ref, mask_ref, out_ref):
    tile = pl.program_id(0)
    head_dim = q_ref.shape[1] // HEADS
    channels = q_ref.shape[1]
    scale = head_dim ** (-0.5)
    pieces = []
    for local in range(WIN_GROUP):
        start = pl.multiple_of(tile * (WIN_GROUP * QBLK) + local * QBLK, QBLK)
        keys_vals = kv_ref[pl.ds(start, KWIN), :]
        live = mask_ref[local : local + 1, :] > 0.0
        query_rows = q_ref[local * QBLK : (local + 1) * QBLK, :]
        heads = []
        for head in range(HEADS):
            cols = slice(head * head_dim, (head + 1) * head_dim)
            vcols = slice(channels + head * head_dim, channels + (head + 1) * head_dim)
            scores = lax.dot_general(
                query_rows[:, cols], keys_vals[:, cols], (((1,), (1,)), ((), ())),
                preferred_element_type=jnp.float32,
            ) * scale
            scores = jnp.where(live, scores, -1e30)
            row_max = jnp.max(scores, axis=-1, keepdims=True)
            exp_scores = jnp.exp(scores - row_max)
            weights = (exp_scores / jnp.sum(exp_scores, axis=-1, keepdims=True)).astype(jnp.bfloat16)
            heads.append(
                jnp.dot(weights, keys_vals[:, vcols], preferred_element_type=jnp.float32).astype(
                    jnp.bfloat16
                )
            )
        pieces.append(jnp.concatenate(heads, axis=1))
    out_ref[...] = jnp.concatenate(pieces, axis=0)


def window_attend(queries, padded_kv, mask_tab):
    atoms, channels = queries.shape
    rows = WIN_GROUP * QBLK
    return pl.pallas_call(
        attend_kernel,
        grid=(atoms // rows,),
        in_specs=[
            pl.BlockSpec((rows, channels), lambda t: (t, 0)),
            pl.BlockSpec(padded_kv.shape, lambda t: (0, 0)),
            pl.BlockSpec((WIN_GROUP, KWIN), lambda t: (t, 0)),
        ],
        out_specs=pl.BlockSpec((rows, channels), lambda t: (t, 0)),
        out_shape=jax.ShapeDtypeStruct((atoms, channels), jnp.bfloat16),
    )(queries, padded_kv, mask_tab)


ROW_CHUNK = 16


def lddt_kernel(slots_ref, count_ref, own_ref, part_ref, out_ref):
    block = pl.program_id(0)
    live = count_ref[block]
    max_slots = slots_ref.shape[0] // count_ref.shape[0]
    lane = lax.broadcasted_iota(jnp.int32, (ROW_CHUNK, PAIR_BLK), 1)
    shape = (ROW_CHUNK, PAIR_BLK)

    def row_body(row_index, carry):
        row = pl.multiple_of(row_index * ROW_CHUNK, ROW_CHUNK)
        own = own_ref[pl.ds(row, ROW_CHUNK), :]
        own_cols = [jnp.broadcast_to(own[:, d : d + 1], shape) for d in range(6)]

        def slot_body(slot_index, accs):
            part = part_ref[slots_ref[block * max_slots + slot_index]]
            gaps = [own_cols[d] - part[d : d + 1, :] for d in range(3)]
            true_gaps = [own_cols[3 + d] - part[3 + d : 4 + d, :] for d in range(3)]
            square_pred = gaps[0] * gaps[0] + gaps[1] * gaps[1] + gaps[2] * gaps[2]
            square_true = (
                true_gaps[0] * true_gaps[0] + true_gaps[1] * true_gaps[1] + true_gaps[2] * true_gaps[2]
            )
            dist_pred = jnp.sqrt(square_pred + 1.0)
            dist_true = jnp.sqrt(square_true + 1.0)
            gap_dist = dist_pred - dist_true
            error_soft = jnp.sqrt(gap_dist * gap_dist + 0.01)
            decay = jnp.exp(-error_soft)
            ys = [decay * math.exp(t) for t in thresholds]
            dens = [(1.0 + y) * (1.0 + y) for y in ys]
            low = dens[0] * dens[1]
            high = dens[2] * dens[3]
            numer = (ys[0] * dens[1] + ys[1] * dens[0]) * high + (ys[2] * dens[3] + ys[3] * dens[2]) * low
            coef = (-0.25 * numer * gap_dist) / (low * high * error_soft * dist_pred)
            return tuple(acc + coef * gap for acc, gap in zip(accs, gaps))

        zero = jnp.zeros(shape, jnp.float32)
        accs = lax.fori_loop(0, live, slot_body, (zero, zero, zero))
        sums = [jnp.sum(acc, axis=1, keepdims=True) for acc in accs]
        tile = jnp.where(lane == 0, sums[0], jnp.where(lane == 1, sums[1], jnp.where(lane == 2, sums[2], 0.0)))
        out_ref[pl.ds(row, ROW_CHUNK), :] = tile
        return carry

    lax.fori_loop(0, PAIR_BLK // ROW_CHUNK, row_body, 0)


def lddt_sums(slots, counts, own_tab, part_tab):
    blocks = counts.shape[0]
    table_rows = part_tab.shape[0]
    out = pl.pallas_call(
        lddt_kernel,
        grid_spec=pltpu.PrefetchScalarGridSpec(
            num_scalar_prefetch=2,
            grid=(blocks,),
            in_specs=[
                pl.BlockSpec((PAIR_BLK, PAIR_BLK), lambda b, *_: (b, 0)),
                pl.BlockSpec((table_rows, 8, PAIR_BLK), lambda b, *_: (0, 0, 0)),
            ],
            out_specs=pl.BlockSpec((PAIR_BLK, PAIR_BLK), lambda b, *_: (b, 0)),
        ),
        out_shape=jax.ShapeDtypeStruct((blocks * PAIR_BLK, PAIR_BLK), jnp.float32),
    )(slots, counts, own_tab, part_tab)
    return out[:, :3].T


def dense(left, right):
    return jnp.einsum("sac,cf->saf", left, right, preferred_element_type=jnp.float32)


def on_device(
    token_feats,
    proj_w,
    atom_single,
    atom_token,
    true_coords,
    noise,
    sigma,
    coord_in,
    w_qkv,
    w_o,
    w_gu,
    w_down,
    gains,
    w_out,
    pair_blocks,
    pair_count,
):
    atom_rank = lax.axis_index("atoms")
    tok_rows = token_feats.shape[0]
    atom_rows = atom_single.shape[0]
    total_atoms = atom_rows * lax.axis_size("atoms")
    samples = noise.shape[0]
    feat_parts = ring_parts(token_feats, "samples")
    proj_parts = ring_parts(proj_w, "samples")
    token_sum = jnp.einsum(
        "kti,kio->to", feat_parts, proj_parts, preferred_element_type=jnp.float32
    )
    token_proj = token_sum.astype(jnp.bfloat16)
    padded_tok = extended(token_proj, (("atoms", 0),), HALO_TOK)
    first_token = atom_rank * tok_rows - HALO_TOK
    relative = atom_token - first_token
    onehot = (
        relative[:, None] == jnp.arange(tok_rows + 2 * HALO_TOK, dtype=jnp.int32)[None, :]
    ).astype(jnp.bfloat16)
    atom_base = atom_single.astype(jnp.float32) + jnp.dot(
        onehot, padded_tok, preferred_element_type=jnp.float32
    )
    sigma_col = sigma[:, None, None]
    noisy = true_coords[None] + sigma_col * noise
    noise_total = sigma_col * sigma_col + sigma_data * sigma_data
    scaled = noisy / jnp.sqrt(noise_total)
    hidden = atom_base[None] + jnp.einsum(
        "sda,dc->sac", scaled, coord_in, precision=lax.Precision.HIGHEST
    )
    key_halo = (KWIN - QBLK) // 2
    position = (
        atom_rank * atom_rows - key_halo + jnp.arange(atom_rows + 2 * key_halo, dtype=jnp.int32)
    )
    valid = ((position >= 0) & (position < total_atoms)).astype(jnp.float32)
    window_start = QBLK * jnp.arange(atom_rows // QBLK, dtype=jnp.int32)
    mask_tab = jnp.take(valid, window_start[:, None] + jnp.arange(KWIN, dtype=jnp.int32)[None, :])
    channels = hidden.shape[2]
    for layer_index in range(LAYERS):
        normed = (rms_norm(hidden) * gains[layer_index, 0]).astype(jnp.bfloat16)
        qkv_all = dense(normed, w_qkv[layer_index]).astype(jnp.bfloat16)
        queries = qkv_all[:, :, :channels]
        padded = extended(qkv_all[:, :, channels:], (("atoms", 1),), key_halo)
        attended = jnp.stack(
            [window_attend(queries[s], padded[s], mask_tab) for s in range(samples)]
        )
        hidden = hidden + dense(attended, w_o[layer_index])
        normed = (rms_norm(hidden) * gains[layer_index, 1]).astype(jnp.bfloat16)
        gate_up = dense(normed, w_gu[layer_index])
        inner_act = (jax.nn.silu(gate_up[..., :FF_ATOM]) * gate_up[..., FF_ATOM:]).astype(
            jnp.bfloat16
        )
        hidden = hidden + dense(inner_act, w_down[layer_index])
    update = jnp.einsum("sac,cd->sda", rms_norm(hidden), w_out, precision=lax.Precision.HIGHEST)
    predicted = (
        sigma_data * sigma_data / noise_total * noisy
        + sigma_col * sigma_data / jnp.sqrt(noise_total) * update
    )
    mse_part = (
        2.0 / 3.0 * (noise_total / (sigma_col * sigma_data) ** 2) * (predicted - true_coords[None])
    )
    block_count = atom_rows // PAIR_BLK
    atom_peers = lax.axis_size("atoms")
    count_row = jnp.zeros((1, atom_rows), jnp.float32).at[0, 0].set(
        jnp.sum(pair_count.astype(jnp.float32) * (PAIR_BLK * PAIR_BLK) - PAIR_BLK)
    )
    true_parts = ring_parts(jnp.concatenate([true_coords, count_row], axis=0), "atoms")
    pred_parts = ring_parts(predicted[0], "atoms")
    pair_total = jnp.sum(true_parts[:, 3, 0])
    coord_parts = jnp.concatenate(
        [pred_parts, true_parts[:, :3], jnp.zeros((atom_peers, 2, atom_rows), jnp.float32)], axis=1
    )
    part_tab = jnp.moveaxis(
        coord_parts.reshape(atom_peers, 8, block_count, PAIR_BLK), 2, 1
    ).reshape(atom_peers * block_count, 8, PAIR_BLK)
    own_tab = jnp.pad(
        jnp.concatenate([predicted[0], true_coords], axis=0).T, ((0, 0), (0, PAIR_BLK - 6))
    )
    source = (atom_rank - pair_blocks // block_count) % atom_peers
    slots = (source * block_count + pair_blocks % block_count).reshape(-1)
    pair_grad = 2.0 * lddt_sums(slots, pair_count, own_tab, part_tab)[None]
    lddt_grad = total_atoms * PAIR_BLK / pair_total * pair_grad.reshape(samples, 3, atom_rows)
    coord_grad = mse_part - lddt_grad / PAIR_BLK
    return (coord_grad, lddt_grad)


def solution(mesh):
    in_specs = (
        P("atoms", "samples"),
        P("samples", None),
        P("atoms", None),
        P("atoms"),
        P(None, "atoms"),
        P("samples", None, "atoms"),
        P("samples"),
        P(),
        P(),
        P(),
        P(),
        P(),
        P(),
        P(),
        P("atoms", None),
        P("atoms"),
    )
    out_specs = (P("samples", None, "atoms"), P("samples", None, "atoms"))
    return jax.shard_map(
        on_device, mesh=mesh, in_specs=in_specs, out_specs=out_specs, check_vma=False
    )
```

profile of v0, /device:TPU:26, one launch (start us, length us, event | category | flops | bytes accessed | tf_op | source)
XLA Modules:
  0.0 522.8 jit_solution(12930875409596792033)
XLA Ops:
  4.7 1.8 collective-permute-start.22
  6.4 1.6 collective-permute-start.23
  9.3 1.8 collective-permute-start.25
  14.9 45.5 %gather_fusion = f32[8192]{0:T(1024)S(1)} fusion(f32[2144]{0:T(1024)S(1)} %fusion.90, s32[8192]{0:T(1024)S(1)} %fusion.77), kind=kCustom, calls=%fused_computation | custom fusion | bytes 98304 | tf_op jit(solution)/shard_map/jit(_take)/gather | solution.py:221
  61.2 2.2 fusion.16
  65.4 1.7 collective-permute-start
  67.6 1.7 collective-permute-done.26
  69.2 2.2 collective-permute-done.27
  78.8 4.5 collective-permute-start.7
  84.9 2.3 multiply_reduce_fusion.6
  90.1 4.6 collective-permute-start.9
  97.3 85.8 %shard_map.167 = bf16[2048,128]{1,0:T(8,128)(2,1)} custom-call(bf16[2048,128]{1,0:T(8,128)(2,1)} %slice_bitcast_fusion.2.q_ref, bf16[2144,256]{1,0:T(8,128)(2,1)} %maximum_bitcast_fusion.kv_ref, f32[64,128]{1,0:T(8,128)} %bitcast_select_fusion.mask_ref), custom_call_target="tpu_custom_call" | custom-call | tf_op jit(solution)/shard_map/pallas_call | solution.py:88
  184.5 1.7 convolution_bitcast_fusion.2
  186.2 1.7 multiply_reduce_fusion.4
  190.8 5.6 %collective-permute-start.11 = (bf16[1,48,256]{2,1,0:T(8,128)(2,1)S(1)}, bf16[1,48,256]{2,1,0:T(8,128)(2,1)S(1)}, u32[]{:S(2)}, u32[]{:S(2)}) collective-permute-start(bf16[1,48,256]{2,1,0:T(8,128)(2,1)S(1)} %get-tuple-element.27), channel_id=1, source_target_pairs={{4,0},{8,4},{12,8},{16,12},{20,16},{24,20},{28,24},{5,1},{9,5},{13... | collective-permute-start | bytes 73736 | tf_op jit(solution)/shard_map/ppermute | solution.py:32
  198.8 85.8 %shard_map.168 = bf16[2048,128]{1,0:T(8,128)(2,1)} custom-call(bf16[2048,128]{1,0:T(8,128)(2,1)} %slice_bitcast_fusion.1.q_ref, bf16[2144,256]{1,0:T(8,128)(2,1)} %maximum_bitcast_fusion.1.kv_ref, f32[64,128]{1,0:T(8,128)} %bitcast_select_fusion.mask_ref), custom_call_target="tpu_custom_call" | custom-call | tf_op jit(solution)/shard_map/pallas_call | solution.py:88
  286.1 1.7 convolution_bitcast_fusion.1
  287.8 1.7 multiply_reduce_fusion.2
  292.4 5.7 %collective-permute-start.13 = (bf16[1,48,256]{2,1,0:T(8,128)(2,1)S(1)}, bf16[1,48,256]{2,1,0:T(8,128)(2,1)S(1)}, u32[]{:S(2)}, u32[]{:S(2)}) collective-permute-start(bf16[1,48,256]{2,1,0:T(8,128)(2,1)S(1)} %get-tuple-element.25), channel_id=1, source_target_pairs={{4,0},{8,4},{12,8},{16,12},{20,16},{24,20},{28,24},{5,1},{9,5},{13... | collective-permute-start | bytes 73736 | tf_op jit(solution)/shard_map/ppermute | solution.py:32
  300.7 85.8 %shard_map.169 = bf16[2048,128]{1,0:T(8,128)(2,1)} custom-call(bf16[2048,128]{1,0:T(8,128)(2,1)} %slice_bitcast_fusion.q_ref, bf16[2144,256]{1,0:T(8,128)(2,1)} %maximum_bitcast_fusion.2.kv_ref, f32[64,128]{1,0:T(8,128)} %bitcast_select_fusion.mask_ref), custom_call_target="tpu_custom_call" | custom-call | tf_op jit(solution)/shard_map/pallas_call | solution.py:88
  387.9 1.7 convolution_bitcast_fusion
  389.6 1.7 multiply_reduce_fusion
  391.3 2.8 constant_dynamic-update-slice_fusion
  394.5 6.4 %collective-permute-start.14 = (f32[3,2048]{1,0:T(4,128)S(1)}, f32[3,2048]{1,0:T(4,128)}, u32[]{:S(2)}, u32[]{:S(2)}) collective-permute-start(f32[3,2048]{1,0:T(4,128)S(1)} %copy.110), channel_id=1, source_target_pairs={{0,4},{4,8},{8,12},{12,16},{16,20},{20,24},{24,28},{28,0},{1,5},{5... | collective-permute-start | bytes 73736 | tf_op jit(solution)/shard_map/ppermute | solution.py:42
  402.9 1.8 collective-permute-start.17
  406.4 2.4 collective-permute-start.19
  411.0 2.0 collective-permute-start.20
  423.9 5.2 copy.132
  430.0 84.9 %shard_map.170 = f32[2048,128]{1,0:T(8,128)} custom-call(s32[208]{0:T(256)} %reshape.331.slots_ref, s32[16]{0:T(128)} %count_ref.1, f32[2048,128]{1,0:T(8,128)} %pad.10.own_ref, f32[128,8,128]{2,1,0:T(8,128)} %bitcast.192), custom_call_target="tpu_custom_call" | custom-call | tf_op jit(solution)/shard_map/pallas_call | solution.py:150
  515.0 2.4 fusion.24
  517.3 2.2 copy.135
  520.7 2.2 copy.134
  (140 shorter events, 57.5 us)
Async XLA Ops:
  0.6 60.6 %copy-start = (f32[3,128]{1,0:T(4,128)S(1)}, f32[3,128]{1,0:T(4,128)}, u32[]{:S(2)}) copy-start(f32[3,128]{1,0:T(4,128)} %param.25) | copy-start | bytes 4612
  4.6 58.8 %collective-permute-start.21 = (f32[4,2048]{1,0:T(4,128)S(1)}, f32[4,2048]{1,0:T(4,128)S(1)}, u32[]{:S(2)}, u32[]{:S(2)}) collective-permute-start(f32[4,2048]{1,0:T(4,128)S(1)} %select_maximum_fusion), channel_id=1, source_target_pairs={{0,4},{4,8},{8,12},{12,16},{16,20},{20,24},{24,28},{28,0},{1,5},{5... | collective-permute-start | bytes 98312 | tf_op jit(solution)/shard_map/ppermute | solution.py:42
  4.7 60.2 %collective-permute-start.22 = (f32[4,2048]{1,0:T(4,128)S(1)}, f32[4,2048]{1,0:T(4,128)S(1)}, u32[]{:S(2)}, u32[]{:S(2)}) collective-permute-start(f32[4,2048]{1,0:T(4,128)S(1)} %select_maximum_fusion), channel_id=1, source_target_pairs={{0,8},{4,12},{8,16},{12,20},{16,24},{20,28},{24,0},{28,4},{1,9},{5... | collective-permute-start | bytes 98312 | tf_op jit(solution)/shard_map/ppermute | solution.py:42
  6.4 58.9 %collective-permute-start.23 = (f32[4,2048]{1,0:T(4,128)S(1)}, f32[4,2048]{1,0:T(4,128)S(1)}, u32[]{:S(2)}, u32[]{:S(2)}) collective-permute-start(f32[4,2048]{1,0:T(4,128)S(1)} %select_maximum_fusion), channel_id=1, source_target_pairs={{0,12},{4,16},{8,20},{12,24},{16,28},{20,0},{24,4},{28,8},{1,13},{... | collective-permute-start | bytes 98312 | tf_op jit(solution)/shard_map/ppermute | solution.py:42
  8.0 57.3 %collective-permute-start.24 = (f32[4,2048]{1,0:T(4,128)S(1)}, f32[4,2048]{1,0:T(4,128)S(1)}, u32[]{:S(2)}, u32[]{:S(2)}) collective-permute-start(f32[4,2048]{1,0:T(4,128)S(1)} %select_maximum_fusion), channel_id=1, source_target_pairs={{0,16},{4,20},{8,24},{12,28},{16,0},{20,4},{24,8},{28,12},{1,17},{... | collective-permute-start | bytes 98312 | tf_op jit(solution)/shard_map/ppermute | solution.py:42
  9.3 57.8 %collective-permute-start.25 = (f32[4,2048]{1,0:T(4,128)S(1)}, f32[4,2048]{1,0:T(4,128)S(1)}, u32[]{:S(2)}, u32[]{:S(2)}) collective-permute-start(f32[4,2048]{1,0:T(4,128)S(1)} %select_maximum_fusion), channel_id=1, source_target_pairs={{0,20},{4,24},{8,28},{12,0},{16,4},{20,8},{24,12},{28,16},{1,21},{... | collective-permute-start | bytes 98312 | tf_op jit(solution)/shard_map/ppermute | solution.py:42
  60.5 12.5 %copy-start.6 = (f32[3,2,128]{2,1,0:T(2,128)S(1)}, f32[3,2,128]{2,1,0:T(2,128)}, u32[]{:S(2)}) copy-start(f32[3,2,128]{2,1,0:T(2,128)} %param.30) | copy-start | bytes 9220
  60.5 13.2 %copy-start.2 = (bf16[2048,128]{1,0:T(8,128)(2,1)S(1)}, bf16[2048,128]{1,0:T(8,128)(2,1)}, u32[]{:S(2)}) copy-start(bf16[2048,128]{1,0:T(8,128)(2,1)} %param.20) | copy-start | bytes 1572868
  63.5 5.8 %collective-permute-start.26 = (f32[4,2048]{1,0:T(4,128)S(1)}, f32[4,2048]{1,0:T(4,128)S(1)}, u32[]{:S(2)}, u32[]{:S(2)}) collective-permute-start(f32[4,2048]{1,0:T(4,128)S(1)} %select_maximum_fusion), channel_id=1, source_target_pairs={{0,24},{4,28},{8,0},{12,4},{16,8},{20,12},{24,16},{28,20},{1,25},{... | collective-permute-start | bytes 98312 | tf_op jit(solution)/shard_map/ppermute | solution.py:42
  64.9 6.6 %collective-permute-start.27 = (f32[4,2048]{1,0:T(4,128)S(1)}, f32[4,2048]{1,0:T(4,128)S(1)}, u32[]{:S(2)}, u32[]{:S(2)}) collective-permute-start(f32[4,2048]{1,0:T(4,128)S(1)} %select_maximum_fusion), channel_id=1, source_target_pairs={{0,28},{4,0},{8,4},{12,8},{16,12},{20,16},{24,20},{28,24},{1,29},{... | collective-permute-start | bytes 98312 | tf_op jit(solution)/shard_map/ppermute | solution.py:42
  65.3 7.7 %collective-permute-start.3 = (bf16[192,128]{1,0:T(8,128)(2,1)S(1)}, bf16[192,128]{1,0:T(8,128)(2,1)S(1)}, u32[]{:S(2)}, u32[]{:S(2)}) collective-permute-start(bf16[192,128]{1,0:T(8,128)(2,1)S(1)} %copy-done.9), channel_id=1, source_target_pairs={{0,1},{1,2},{2,3},{3,0},{4,5},{5,6},{6,7},{7,4},{8,9},{9,10},{10,1... | collective-permute-start | bytes 147464 | tf_op jit(solution)/shard_map/ppermute | solution.py:42
  65.4 10.9 %collective-permute-start = (bf16[256,192]{0,1:T(8,128)(2,1)S(1)}, bf16[256,192]{0,1:T(8,128)(2,1)S(1)}, u32[]{:S(2)}, u32[]{:S(2)}) collective-permute-start(bf16[256,192]{0,1:T(8,128)(2,1)S(1)} %copy-done.8), channel_id=1, source_target_pairs={{0,1},{1,2},{2,3},{3,0},{4,5},{5,6},{6,7},{7,4},{8,9},{9,10},{10,1... | collective-permute-start | bytes 294920 | tf_op jit(solution)/shard_map/ppermute | solution.py:42
  67.1 9.2 %collective-permute-start.1 = (bf16[256,192]{0,1:T(8,128)(2,1)S(1)}, bf16[256,192]{0,1:T(8,128)(2,1)S(1)}, u32[]{:S(2)}, u32[]{:S(2)}) collective-permute-start(bf16[256,192]{0,1:T(8,128)(2,1)S(1)} %copy-done.8), channel_id=1, source_target_pairs={{0,2},{1,3},{2,0},{3,1},{4,6},{5,7},{6,4},{7,5},{8,10},{9,11},{10,... | collective-permute-start | bytes 294920 | tf_op jit(solution)/shard_map/ppermute | solution.py:42
  69.2 7.1 %collective-permute-start.2 = (bf16[256,192]{0,1:T(8,128)(2,1)S(1)}, bf16[256,192]{0,1:T(8,128)(2,1)S(1)}, u32[]{:S(2)}, u32[]{:S(2)}) collective-permute-start(bf16[256,192]{0,1:T(8,128)(2,1)S(1)} %copy-done.8), channel_id=1, source_target_pairs={{0,3},{1,0},{2,1},{3,2},{4,7},{5,4},{6,5},{7,6},{8,11},{9,8},{10,9... | collective-permute-start | bytes 294920 | tf_op jit(solution)/shard_map/ppermute | solution.py:42
  71.5 4.8 collective-permute-start.4
  73.0 3.3 collective-permute-start.5
  77.5 7.4 %collective-permute-start.6 = (bf16[16,128]{1,0:T(8,128)(2,1)S(1)}, bf16[16,128]{1,0:T(8,128)(2,1)S(1)}, u32[]{:S(2)}, u32[]{:S(2)}) collective-permute-start(bf16[16,128]{1,0:T(8,128)(2,1)S(1)} %get-tuple-element.30), channel_id=1, source_target_pairs={{0,4},{4,8},{8,12},{12,16},{16,20},{20,24},{24,28},{1,5},{5,9},{9,... | collective-permute-start | bytes 12296 | tf_op jit(solution)/shard_map/ppermute | solution.py:31
  78.8 6.1 %collective-permute-start.7 = (bf16[16,128]{1,0:T(8,128)(2,1)S(1)}, bf16[16,128]{1,0:T(8,128)(2,1)S(1)}, u32[]{:S(2)}, u32[]{:S(2)}) collective-permute-start(bf16[16,128]{1,0:T(8,128)(2,1)S(1)} %get-tuple-element.31), channel_id=1, source_target_pairs={{4,0},{8,4},{12,8},{16,12},{20,16},{24,20},{28,24},{5,1},{9,5},{13... | collective-permute-start | bytes 12296 | tf_op jit(solution)/shard_map/ppermute | solution.py:32
  88.8 6.8 %collective-permute-start.8 = (bf16[1,48,256]{2,1,0:T(8,128)(2,1)S(1)}, bf16[1,48,256]{2,1,0:T(8,128)(2,1)S(1)}, u32[]{:S(2)}, u32[]{:S(2)}) collective-permute-start(bf16[1,48,256]{2,1,0:T(8,128)(2,1)S(1)} %get-tuple-element.28), channel_id=1, source_target_pairs={{0,4},{4,8},{8,12},{12,16},{16,20},{20,24},{24,28},{1,5},{5,9},{9,... | collective-permute-start | bytes 73736 | tf_op jit(solution)/shard_map/ppermute | solution.py:31
  90.1 6.1 %collective-permute-start.9 = (bf16[1,48,256]{2,1,0:T(8,128)(2,1)S(1)}, bf16[1,48,256]{2,1,0:T(8,128)(2,1)S(1)}, u32[]{:S(2)}, u32[]{:S(2)}) collective-permute-start(bf16[1,48,256]{2,1,0:T(8,128)(2,1)S(1)} %get-tuple-element.29), channel_id=1, source_target_pairs={{4,0},{8,4},{12,8},{16,12},{20,16},{24,20},{28,24},{5,1},{9,5},{13... | collective-permute-start | bytes 73736 | tf_op jit(solution)/shard_map/ppermute | solution.py:32
  95.6 87.5 %copy-start.3 = (bf16[3,128,128]{2,1,0:T(8,128)(2,1)S(1)}, bf16[3,128,128]{2,1,0:T(8,128)(2,1)}, u32[]{:S(2)}) copy-start(bf16[3,128,128]{2,1,0:T(8,128)(2,1)} %param.27) | copy-start | bytes 294916
  189.5 7.8 %collective-permute-start.10 = (bf16[1,48,256]{2,1,0:T(8,128)(2,1)S(1)}, bf16[1,48,256]{2,1,0:T(8,128)(2,1)S(1)}, u32[]{:S(2)}, u32[]{:S(2)}) collective-permute-start(bf16[1,48,256]{2,1,0:T(8,128)(2,1)S(1)} %get-tuple-element.26), channel_id=1, source_target_pairs={{0,4},{4,8},{8,12},{12,16},{16,20},{20,24},{24,28},{1,5},{5,9},{9,... | collective-permute-start | bytes 73736 | tf_op jit(solution)/shard_map/ppermute | solution.py:31
  190.8 7.0 %collective-permute-start.11 = (bf16[1,48,256]{2,1,0:T(8,128)(2,1)S(1)}, bf16[1,48,256]{2,1,0:T(8,128)(2,1)S(1)}, u32[]{:S(2)}, u32[]{:S(2)}) collective-permute-start(bf16[1,48,256]{2,1,0:T(8,128)(2,1)S(1)} %get-tuple-element.27), channel_id=1, source_target_pairs={{4,0},{8,4},{12,8},{16,12},{20,16},{24,20},{28,24},{5,1},{9,5},{13... | collective-permute-start | bytes 73736 | tf_op jit(solution)/shard_map/ppermute | solution.py:32
  291.1 8.0 %collective-permute-start.12 = (bf16[1,48,256]{2,1,0:T(8,128)(2,1)S(1)}, bf16[1,48,256]{2,1,0:T(8,128)(2,1)S(1)}, u32[]{:S(2)}, u32[]{:S(2)}) collective-permute-start(bf16[1,48,256]{2,1,0:T(8,128)(2,1)S(1)} %get-tuple-element.24), channel_id=1, source_target_pairs={{0,4},{4,8},{8,12},{12,16},{16,20},{20,24},{24,28},{1,5},{5,9},{9,... | collective-permute-start | bytes 73736 | tf_op jit(solution)/shard_map/ppermute | solution.py:31
  292.4 7.2 %collective-permute-start.13 = (bf16[1,48,256]{2,1,0:T(8,128)(2,1)S(1)}, bf16[1,48,256]{2,1,0:T(8,128)(2,1)S(1)}, u32[]{:S(2)}, u32[]{:S(2)}) collective-permute-start(bf16[1,48,256]{2,1,0:T(8,128)(2,1)S(1)} %get-tuple-element.25), channel_id=1, source_target_pairs={{4,0},{8,4},{12,8},{16,12},{20,16},{24,20},{28,24},{5,1},{9,5},{13... | collective-permute-start | bytes 73736 | tf_op jit(solution)/shard_map/ppermute | solution.py:32
  394.5 11.9 %collective-permute-start.14 = (f32[3,2048]{1,0:T(4,128)S(1)}, f32[3,2048]{1,0:T(4,128)}, u32[]{:S(2)}, u32[]{:S(2)}) collective-permute-start(f32[3,2048]{1,0:T(4,128)S(1)} %copy.110), channel_id=1, source_target_pairs={{0,4},{4,8},{8,12},{12,16},{16,20},{20,24},{24,28},{28,0},{1,5},{5... | collective-permute-start | bytes 73736 | tf_op jit(solution)/shard_map/ppermute | solution.py:42
  400.9 10.1 %collective-permute-start.15 = (f32[3,2048]{1,0:T(4,128)S(1)}, f32[3,2048]{1,0:T(4,128)}, u32[]{:S(2)}, u32[]{:S(2)}) collective-permute-start(f32[3,2048]{1,0:T(4,128)S(1)} %copy.110), channel_id=1, source_target_pairs={{0,8},{4,12},{8,16},{12,20},{16,24},{20,28},{24,0},{28,4},{1,9},{5... | collective-permute-start | bytes 73736 | tf_op jit(solution)/shard_map/ppermute | solution.py:42
  402.0 13.2 %collective-permute-start.16 = (f32[3,2048]{1,0:T(4,128)S(1)}, f32[3,2048]{1,0:T(4,128)}, u32[]{:S(2)}, u32[]{:S(2)}) collective-permute-start(f32[3,2048]{1,0:T(4,128)S(1)} %copy.110), channel_id=1, source_target_pairs={{0,12},{4,16},{8,20},{12,24},{16,28},{20,0},{24,4},{28,8},{1,13},{... | collective-permute-start | bytes 73736 | tf_op jit(solution)/shard_map/ppermute | solution.py:42
  402.9 14.4 %collective-permute-start.17 = (f32[3,2048]{1,0:T(4,128)S(1)}, f32[3,2048]{1,0:T(4,128)S(1)}, u32[]{:S(2)}, u32[]{:S(2)}) collective-permute-start(f32[3,2048]{1,0:T(4,128)S(1)} %copy.110), channel_id=1, source_target_pairs={{0,16},{4,20},{8,24},{12,28},{16,0},{20,4},{24,8},{28,12},{1,17},{... | collective-permute-start | bytes 73736 | tf_op jit(solution)/shard_map/ppermute | solution.py:42
  404.8 14.0 %collective-permute-start.18 = (f32[3,2048]{1,0:T(4,128)S(1)}, f32[3,2048]{1,0:T(4,128)S(1)}, u32[]{:S(2)}, u32[]{:S(2)}) collective-permute-start(f32[3,2048]{1,0:T(4,128)S(1)} %copy.110), channel_id=1, source_target_pairs={{0,20},{4,24},{8,28},{12,0},{16,4},{20,8},{24,12},{28,16},{1,21},{... | collective-permute-start | bytes 73736 | tf_op jit(solution)/shard_map/ppermute | solution.py:42
  406.4 13.8 %collective-permute-start.19 = (f32[3,2048]{1,0:T(4,128)S(1)}, f32[3,2048]{1,0:T(4,128)S(1)}, u32[]{:S(2)}, u32[]{:S(2)}) collective-permute-start(f32[3,2048]{1,0:T(4,128)S(1)} %copy.110), channel_id=1, source_target_pairs={{0,24},{4,28},{8,0},{12,4},{16,8},{20,12},{24,16},{28,20},{1,25},{... | collective-permute-start | bytes 73736 | tf_op jit(solution)/shard_map/ppermute | solution.py:42
  411.0 10.6 %collective-permute-start.20 = (f32[3,2048]{1,0:T(4,128)S(1)}, f32[3,2048]{1,0:T(4,128)}, u32[]{:S(2)}, u32[]{:S(2)}) collective-permute-start(f32[3,2048]{1,0:T(4,128)S(1)} %copy.110), channel_id=1, source_target_pairs={{0,28},{4,0},{8,4},{12,8},{16,12},{20,16},{24,20},{28,24},{1,29},{... | collective-permute-start | bytes 73736 | tf_op jit(solution)/shard_map/ppermute | solution.py:42
  (7 other events, 24.5 us)
where the time goes:
time: 529 us; the launch traced here: 523 us
  Pallas kernels  342 us (65%)
  local copies, waits for them, and re-layouts  77 us (15%)
  starting transfers between devices  52.5 us (10%)
  matrix products  27.5 us (5%)
  other arithmetic  13.8 us (3%)
  waiting for transfers between devices  5.51 us (1%)
    pallas_call x3, Pallas kernels, window_attend(): pl.pallas_call(attend_kernel, grid=(atoms // rows,), in_specs=[pl.BlockSp...  257 us
    pallas_call x1, Pallas kernels, lddt_sums(): pl.pallas_call(lddt_kernel, grid_spec=pltpu.PrefetchScalarGridSpec(num_sc...  84.9 us
    gather x1, local copies, waits for them, and re-layouts, on_device(): jnp.take(valid, window_start[:, None] + jnp.arange(KWIN, dtype=jnp.int32)...  45.5 us
    ppermute x20, starting transfers between devices, ring_parts(): parts.append(lax.ppermute(value, axis, pairs))  26.9 us
    ppermute x4, starting transfers between devices, extended(): after = lax.ppermute(first, axis, down)  20.5 us
    dot_general x12, matrix products, dense(): jnp.einsum('sac,cf->saf', left, right, preferred_element_type=jnp.float32)  19 us
    unnamed x32, local copies, waits for them, and re-layouts  13.4 us
  transfers between devices with their start and end apart: 28, of which 5 were waited for; matrix products, arithmetic and copies ran while one was open for 13% of the time, Pallas kernels for 0%

commit v1 on v0

--- a/solution.py
+++ b/solution.py
@@ -47,56 +47,56 @@
     return tensor * lax.rsqrt(jnp.mean(tensor * tensor, axis=-1, keepdims=True) + norm_epsilon)
 
 
-WIN_GROUP = 8
-
-
-def attend_kernel(q_ref, kv_ref, mask_ref, out_ref):
+Q_TILE = 128
+K_SPAN = 256
+
+
+def attend_kernel(q_ref, kv_ref, band_ref, valid_ref, out_ref):
     tile = pl.program_id(0)
     head_dim = q_ref.shape[1] // HEADS
     channels = q_ref.shape[1]
     scale = head_dim ** (-0.5)
-    pieces = []
-    for local in range(WIN_GROUP):
-        start = pl.multiple_of(tile * (WIN_GROUP * QBLK) + local * QBLK, QBLK)
-        keys_vals = kv_ref[pl.ds(start, KWIN), :]
-        live = mask_ref[local : local + 1, :] > 0.0
-        query_rows = q_ref[local * QBLK : (local + 1) * QBLK, :]
-        heads = []
-        for head in range(HEADS):
-            cols = slice(head * head_dim, (head + 1) * head_dim)
-            vcols = slice(channels + head * head_dim, channels + (head + 1) * head_dim)
-            scores = lax.dot_general(
-                query_rows[:, cols], keys_vals[:, cols], (((1,), (1,)), ((), ())),
-                preferred_element_type=jnp.float32,
-            ) * scale
-            scores = jnp.where(live, scores, -1e30)
-            row_max = jnp.max(scores, axis=-1, keepdims=True)
-            exp_scores = jnp.exp(scores - row_max)
-            weights = (exp_scores / jnp.sum(exp_scores, axis=-1, keepdims=True)).astype(jnp.bfloat16)
-            heads.append(
-                jnp.dot(weights, keys_vals[:, vcols], preferred_element_type=jnp.float32).astype(
-                    jnp.bfloat16
-                )
+    start = pl.multiple_of(tile * Q_TILE, Q_TILE)
+    keys_vals = kv_ref[pl.ds(start, K_SPAN), :]
+    live = (band_ref[...] * valid_ref[pl.ds(tile, 1), :]) > 0.0
+    query_rows = q_ref[...]
+    heads = []
+    for head in range(HEADS):
+        cols = slice(head * head_dim, (head + 1) * head_dim)
+        vcols = slice(channels + head * head_dim, channels + (head + 1) * head_dim)
+        scores = lax.dot_general(
+            query_rows[:, cols], keys_vals[:, cols], (((1,), (1,)), ((), ())),
+            preferred_element_type=jnp.float32,
+        ) * scale
+        scores = jnp.where(live, scores, -1e30)
+        row_max = jnp.max(scores, axis=-1, keepdims=True)
+        exp_scores = jnp.exp(scores - row_max)
+        inverse = 1.0 / jnp.sum(exp_scores, axis=-1, keepdims=True)
+        weights = (exp_scores * inverse).astype(jnp.bfloat16)
+        heads.append(
+            jnp.dot(weights, keys_vals[:, vcols], preferred_element_type=jnp.float32).astype(
+                jnp.bfloat16
             )
-        pieces.append(jnp.concatenate(heads, axis=1))
-    out_ref[...] = jnp.concatenate(pieces, axis=0)
-
-
-def window_attend(queries, padded_kv, mask_tab):
+        )
+    out_ref[...] = jnp.concatenate(heads, axis=1)
+
+
+def window_attend(queries, padded_kv, band, valid_tab):
     atoms, channels = queries.shape
-    rows = WIN_GROUP * QBLK
+    extra = atoms + K_SPAN - Q_TILE - padded_kv.shape[0]
+    padded_kv = jnp.pad(padded_kv, ((0, extra), (0, 0)))
     return pl.pallas_call(
         attend_kernel,
-        grid=(atoms // rows,),
+        grid=(atoms // Q_TILE,),
         in_specs=[
-            pl.BlockSpec((rows, channels), lambda t: (t, 0)),
+            pl.BlockSpec((Q_TILE, channels), lambda t: (t, 0)),
             pl.BlockSpec(padded_kv.shape, lambda t: (0, 0)),
-            pl.BlockSpec((WIN_GROUP, KWIN), lambda t: (t, 0)),
+            pl.BlockSpec(band.shape, lambda t: (0, 0)),
+            pl.BlockSpec(valid_tab.shape, lambda t: (0, 0)),
         ],
-        out_specs=pl.BlockSpec((rows, channels), lambda t: (t, 0)),
+        out_specs=pl.BlockSpec((Q_TILE, channels), lambda t: (t, 0)),
         out_shape=jax.ShapeDtypeStruct((atoms, channels), jnp.bfloat16),
-    )(queries, padded_kv, mask_tab)
-
+    )(queries, padded_kv, band, valid_tab)
 
 ROW_CHUNK = 16
 
@@ -213,12 +213,14 @@
         "sda,dc->sac", scaled, coord_in, precision=lax.Precision.HIGHEST
     )
     key_halo = (KWIN - QBLK) // 2
-    position = (
-        atom_rank * atom_rows - key_halo + jnp.arange(atom_rows + 2 * key_halo, dtype=jnp.int32)
-    )
-    valid = ((position >= 0) & (position < total_atoms)).astype(jnp.float32)
-    window_start = QBLK * jnp.arange(atom_rows // QBLK, dtype=jnp.int32)
-    mask_tab = jnp.take(valid, window_start[:, None] + jnp.arange(KWIN, dtype=jnp.int32)[None, :])
+    tile_start = atom_rank * atom_rows - key_halo + Q_TILE * jnp.arange(
+        atom_rows // Q_TILE, dtype=jnp.int32
+    )
+    position = tile_start[:, None] + jnp.arange(K_SPAN, dtype=jnp.int32)[None, :]
+    valid_tab = ((position >= 0) & (position < total_atoms)).astype(jnp.float32)
+    query_win = jnp.arange(Q_TILE, dtype=jnp.int32)[:, None] // QBLK * QBLK
+    key_index = jnp.arange(K_SPAN, dtype=jnp.int32)[None, :]
+    band = ((key_index >= query_win) & (key_index < query_win + KWIN)).astype(jnp.float32)
     channels = hidden.shape[2]
     for layer_index in range(LAYERS):
         normed = (rms_norm(hidden) * gains[layer_index, 0]).astype(jnp.bfloat16)
@@ -226,7 +228,7 @@
         queries = qkv_all[:, :, :channels]
         padded = extended(qkv_all[:, :, channels:], (("atoms", 1),), key_halo)
         attended = jnp.stack(
-            [window_attend(queries[s], padded[s], mask_tab) for s in range(samples)]
+            [window_attend(queries[s], padded[s], band, valid_tab) for s in range(samples)]
         )
         hidden = hidden + dense(attended, w_o[layer_index])
         normed = (rms_norm(hidden) * gains[layer_index, 1]).astype(jnp.bfloat16)

time: 529 us -> 279 us (0.53)
  Pallas kernels: 342 us -> 140 us
  local copies, waits for them, and re-layouts: 77 us -> 34.1 us
    pallas_call x3, Pallas kernels: 257 us -> 55 us  [window_attend(): pl.pallas_call(attend_kernel, grid=(atoms // Q_TILE,), in_specs=[pl.Block...]
    gather x1 -> x0, local copies, waits for them, and re-layouts: 45.5 us -> none  [on_device(): jnp.take(valid, window_start[:, None] + jnp.arange(KWIN, dtype=jnp.int32)...]
  transfers between devices with their start and end apart: 28 -> 28, of which waited for: 5 -> 5; matrix products, arithmetic and copies ran while one was open for 13% -> 9% of each run, Pallas kernels for 0% -> 0%
where the time goes in v1:
time: 279 us; the launch traced here: 276 us
  Pallas kernels  140 us (50%)
  starting transfers between devices  52.5 us (19%)
  local copies, waits for them, and re-layouts  34.1 us (12%)
  matrix products  27.5 us (10%)
  other arithmetic  11.3 us (4%)
  waiting for transfers between devices  5.53 us (2%)
  between operations  4.16 us (1%)
    pallas_call x1, Pallas kernels, lddt_sums(): pl.pallas_call(lddt_kernel, grid_spec=pltpu.PrefetchScalarGridSpec(num_sc...  85.3 us
    pallas_call x3, Pallas kernels, window_attend(): pl.pallas_call(attend_kernel, grid=(atoms // Q_TILE,), in_specs=[pl.Block...  55 us
    ppermute x20, starting transfers between devices, ring_parts(): parts.append(lax.ppermute(value, axis, pairs))  26.9 us
    ppermute x4, starting transfers between devices, extended(): after = lax.ppermute(first, axis, down)  20.5 us
    dot_general x12, matrix products, dense(): jnp.einsum('sac,cf->saf', left, right, preferred_element_type=jnp.float32)  19 us
    unnamed x32, local copies, waits for them, and re-layouts  12.8 us
    another operation x11, local copies, waits for them, and re-layouts, ring_parts(): return jnp.stack(parts)  7.02 us
  transfers between devices with their start and end apart: 28, of which 5 were waited for; matrix products, arithmetic and copies ran while one was open for 9% of the time, Pallas kernels for 0%

profile of v1, /device:TPU:26, one launch (start us, length us, event | category | flops | bytes accessed | tf_op | source)
XLA Modules:
  0.0 275.6 jit_solution(15307245214699547375)
XLA Ops:
  4.7 1.8 collective-permute-start.22
  6.4 1.6 collective-permute-start.23
  9.3 1.8 collective-permute-start.25
  16.3 2.2 fusion.16
  20.5 1.7 collective-permute-start
  22.7 1.7 collective-permute-done.26
  24.3 2.2 collective-permute-done.27
  33.3 4.5 %collective-permute-start.7 = (bf16[16,128]{1,0:T(8,128)(2,1)S(1)}, bf16[16,128]{1,0:T(8,128)(2,1)S(1)}, u32[]{:S(2)}, u32[]{:S(2)}) collective-permute-start(bf16[16,128]{1,0:T(8,128)(2,1)S(1)} %get-tuple-element.29), channel_id=1, source_target_pairs={{4,0},{8,4},{12,8},{16,12},{20,16},{24,20},{28,24},{5,1},{9,5},{13... | collective-permute-start | bytes 12296 | tf_op jit(solution)/shard_map/ppermute | solution.py:32
  39.3 2.3 multiply_reduce_fusion.6
  44.5 4.6 %collective-permute-start.9 = (bf16[1,48,256]{2,1,0:T(8,128)(2,1)S(1)}, bf16[1,48,256]{2,1,0:T(8,128)(2,1)S(1)}, u32[]{:S(2)}, u32[]{:S(2)}) collective-permute-start(bf16[1,48,256]{2,1,0:T(8,128)(2,1)S(1)} %get-tuple-element.27), channel_id=1, source_target_pairs={{4,0},{8,4},{12,8},{16,12},{20,16},{24,20},{28,24},{5,1},{9,5},{13... | collective-permute-start | bytes 73736 | tf_op jit(solution)/shard_map/ppermute | solution.py:32
  51.8 18.3 %shard_map.167 = bf16[2048,128]{1,0:T(8,128)(2,1)} custom-call(bf16[2048,128]{1,0:T(8,128)(2,1)} %slice_bitcast_fusion.2.q_ref, bf16[2176,256]{1,0:T(8,128)(2,1)} %pad.20.kv_ref, f32[128,256]{1,0:T(8,128)} %fusion.60.band_ref, f32[16,256]{1,0:T(8,128)} %fusion.87.valid_ref), custom_call_target="tpu_custom_call" | custom-call | tf_op jit(solution)/shard_map/pallas_call | solution.py:88
  71.6 1.7 convolution_bitcast_fusion.2
  73.3 1.7 multiply_reduce_fusion.4
  75.0 1.6 fusion.2
  77.9 5.6 %collective-permute-start.11 = (bf16[1,48,256]{2,1,0:T(8,128)(2,1)S(1)}, bf16[1,48,256]{2,1,0:T(8,128)(2,1)S(1)}, u32[]{:S(2)}, u32[]{:S(2)}) collective-permute-start(bf16[1,48,256]{2,1,0:T(8,128)(2,1)S(1)} %get-tuple-element.25), channel_id=1, source_target_pairs={{4,0},{8,4},{12,8},{16,12},{20,16},{24,20},{28,24},{5,1},{9,5},{13... | collective-permute-start | bytes 73736 | tf_op jit(solution)/shard_map/ppermute | solution.py:32
  86.1 18.3 %shard_map.168 = bf16[2048,128]{1,0:T(8,128)(2,1)} custom-call(bf16[2048,128]{1,0:T(8,128)(2,1)} %slice_bitcast_fusion.1.q_ref, bf16[2176,256]{1,0:T(8,128)(2,1)} %pad.21.kv_ref, f32[128,256]{1,0:T(8,128)} %fusion.60.band_ref, f32[16,256]{1,0:T(8,128)} %fusion.87.valid_ref), custom_call_target="tpu_custom_call" | custom-call | tf_op jit(solution)/shard_map/pallas_call | solution.py:88
  105.8 1.7 convolution_bitcast_fusion.1
  107.5 1.7 multiply_reduce_fusion.2
  112.1 5.7 %collective-permute-start.13 = (bf16[1,48,256]{2,1,0:T(8,128)(2,1)S(1)}, bf16[1,48,256]{2,1,0:T(8,128)(2,1)S(1)}, u32[]{:S(2)}, u32[]{:S(2)}) collective-permute-start(bf16[1,48,256]{2,1,0:T(8,128)(2,1)S(1)} %get-tuple-element.23), channel_id=1, source_target_pairs={{4,0},{8,4},{12,8},{16,12},{20,16},{24,20},{28,24},{5,1},{9,5},{13... | collective-permute-start | bytes 73736 | tf_op jit(solution)/shard_map/ppermute | solution.py:32
  120.5 18.3 %shard_map.169 = bf16[2048,128]{1,0:T(8,128)(2,1)} custom-call(bf16[2048,128]{1,0:T(8,128)(2,1)} %slice_bitcast_fusion.q_ref, bf16[2176,256]{1,0:T(8,128)(2,1)} %pad.22.kv_ref, f32[128,256]{1,0:T(8,128)} %fusion.60.band_ref, f32[16,256]{1,0:T(8,128)} %fusion.87.valid_ref), custom_call_target="tpu_custom_call" | custom-call | tf_op jit(solution)/shard_map/pallas_call | solution.py:88
  140.3 1.7 convolution_bitcast_fusion
  142.0 1.7 multiply_reduce_fusion
  143.7 2.8 %constant_dynamic-update-slice_fusion = (f32[8,3,2048]{1,2,0:T(8,128)}, f32[1,3,2048]{1,2,0:T(8,128)S(1)}) fusion(f32[128,3]{0,1:T(4,128)S(1)} %copy-done.8, f32[2048,128]{0,1:T(8,128)S(1)} %get-tuple-element.49, f32[2048]{0:T(1024)S(1)} %add_rsqrt_fusion, f32[]{:T(128)} %bitcast.4, f32[1,3,2048]{1,2,0:T(8,128)S(1)} %copy.95, f32[3,2048]{0,1:T(8,128)S(1)} %copy.94, ...), kind=kOutput, calls=%fused_computation.136 | convolution fusion | flops 9723903 | bytes 2180616 | tf_op jit(solution)/shard_map/sac,cd->sda/dot_general | solution.py:240
  146.9 7.0 %collective-permute-start.14 = (f32[3,2048]{1,0:T(4,128)S(1)}, f32[3,2048]{1,0:T(4,128)}, u32[]{:S(2)}, u32[]{:S(2)}) collective-permute-start(f32[3,2048]{1,0:T(4,128)S(1)} %copy.100), channel_id=1, source_target_pairs={{0,4},{4,8},{8,12},{12,16},{16,20},{20,24},{24,28},{28,0},{1,5},{5... | collective-permute-start | bytes 73736 | tf_op jit(solution)/shard_map/ppermute | solution.py:42
  155.3 2.4 collective-permute-start.17
  159.3 1.9 collective-permute-start.19
  163.4 2.0 collective-permute-start.20
  176.2 5.2 %copy.122 = f32[8,3,2048]{2,1,0:T(4,128)S(1)} copy(f32[8,3,2048]{1,2,0:T(8,128)} %bitcast_dynamic-update-slice_fusion) | data formatting | bytes 393216 | tf_op jit(solution)/shard_map/stack | solution.py:43
  182.4 85.3 %shard_map.170 = f32[2048,128]{1,0:T(8,128)} custom-call(s32[208]{0:T(256)} %reshape.317.slots_ref, s32[16]{0:T(128)} %count_ref.1, f32[2048,128]{1,0:T(8,128)} %pad.23.own_ref, f32[128,8,128]{2,1,0:T(8,128)} %bitcast.186), custom_call_target="tpu_custom_call" | custom-call | tf_op jit(solution)/shard_map/pallas_call | solution.py:150
  267.7 2.3 fusion.24
  270.1 2.2 copy.125
  273.4 2.2 copy.124
  (142 shorter events, 55.5 us)
Async XLA Ops:
  0.6 15.7 %copy-start = (f32[3,128]{1,0:T(4,128)S(1)}, f32[3,128]{1,0:T(4,128)}, u32[]{:S(2)}) copy-start(f32[3,128]{1,0:T(4,128)} %param.25) | copy-start | bytes 4612
  4.6 13.9 %collective-permute-start.21 = (f32[4,2048]{1,0:T(4,128)S(1)}, f32[4,2048]{1,0:T(4,128)S(1)}, u32[]{:S(2)}, u32[]{:S(2)}) collective-permute-start(f32[4,2048]{1,0:T(4,128)S(1)} %select_maximum_fusion), channel_id=1, source_target_pairs={{0,4},{4,8},{8,12},{12,16},{16,20},{20,24},{24,28},{28,0},{1,5},{5... | collective-permute-start | bytes 98312 | tf_op jit(solution)/shard_map/ppermute | solution.py:42
  4.7 15.3 %collective-permute-start.22 = (f32[4,2048]{1,0:T(4,128)S(1)}, f32[4,2048]{1,0:T(4,128)S(1)}, u32[]{:S(2)}, u32[]{:S(2)}) collective-permute-start(f32[4,2048]{1,0:T(4,128)S(1)} %select_maximum_fusion), channel_id=1, source_target_pairs={{0,8},{4,12},{8,16},{12,20},{16,24},{20,28},{24,0},{28,4},{1,9},{5... | collective-permute-start | bytes 98312 | tf_op jit(solution)/shard_map/ppermute | solution.py:42
  6.4 14.0 %collective-permute-start.23 = (f32[4,2048]{1,0:T(4,128)S(1)}, f32[4,2048]{1,0:T(4,128)S(1)}, u32[]{:S(2)}, u32[]{:S(2)}) collective-permute-start(f32[4,2048]{1,0:T(4,128)S(1)} %select_maximum_fusion), channel_id=1, source_target_pairs={{0,12},{4,16},{8,20},{12,24},{16,28},{20,0},{24,4},{28,8},{1,13},{... | collective-permute-start | bytes 98312 | tf_op jit(solution)/shard_map/ppermute | solution.py:42
  8.0 12.4 %collective-permute-start.24 = (f32[4,2048]{1,0:T(4,128)S(1)}, f32[4,2048]{1,0:T(4,128)S(1)}, u32[]{:S(2)}, u32[]{:S(2)}) collective-permute-start(f32[4,2048]{1,0:T(4,128)S(1)} %select_maximum_fusion), channel_id=1, source_target_pairs={{0,16},{4,20},{8,24},{12,28},{16,0},{20,4},{24,8},{28,12},{1,17},{... | collective-permute-start | bytes 98312 | tf_op jit(solution)/shard_map/ppermute | solution.py:42
  9.3 12.9 %collective-permute-start.25 = (f32[4,2048]{1,0:T(4,128)S(1)}, f32[4,2048]{1,0:T(4,128)S(1)}, u32[]{:S(2)}, u32[]{:S(2)}) collective-permute-start(f32[4,2048]{1,0:T(4,128)S(1)} %select_maximum_fusion), channel_id=1, source_target_pairs={{0,20},{4,24},{8,28},{12,0},{16,4},{20,8},{24,12},{28,16},{1,21},{... | collective-permute-start | bytes 98312 | tf_op jit(solution)/shard_map/ppermute | solution.py:42
  14.8 13.2 %copy-start.7 = (f32[3,2,128]{2,1,0:T(2,128)S(1)}, f32[3,2,128]{2,1,0:T(2,128)}, u32[]{:S(2)}) copy-start(f32[3,2,128]{2,1,0:T(2,128)} %param.30) | copy-start | bytes 9220
  14.9 13.3 %copy-start.3 = (bf16[2048,128]{1,0:T(8,128)(2,1)S(1)}, bf16[2048,128]{1,0:T(8,128)(2,1)}, u32[]{:S(2)}) copy-start(bf16[2048,128]{1,0:T(8,128)(2,1)} %param.20) | copy-start | bytes 1572868
  18.5 5.8 %collective-permute-start.26 = (f32[4,2048]{1,0:T(4,128)S(1)}, f32[4,2048]{1,0:T(4,128)S(1)}, u32[]{:S(2)}, u32[]{:S(2)}) collective-permute-start(f32[4,2048]{1,0:T(4,128)S(1)} %select_maximum_fusion), channel_id=1, source_target_pairs={{0,24},{4,28},{8,0},{12,4},{16,8},{20,12},{24,16},{28,20},{1,25},{... | collective-permute-start | bytes 98312 | tf_op jit(solution)/shard_map/ppermute | solution.py:42
  20.0 6.6 %collective-permute-start.27 = (f32[4,2048]{1,0:T(4,128)S(1)}, f32[4,2048]{1,0:T(4,128)S(1)}, u32[]{:S(2)}, u32[]{:S(2)}) collective-permute-start(f32[4,2048]{1,0:T(4,128)S(1)} %select_maximum_fusion), channel_id=1, source_target_pairs={{0,28},{4,0},{8,4},{12,8},{16,12},{20,16},{24,20},{28,24},{1,29},{... | collective-permute-start | bytes 98312 | tf_op jit(solution)/shard_map/ppermute | solution.py:42
  20.4 7.7 %collective-permute-start.3 = (bf16[192,128]{1,0:T(8,128)(2,1)S(1)}, bf16[192,128]{1,0:T(8,128)(2,1)S(1)}, u32[]{:S(2)}, u32[]{:S(2)}) collective-permute-start(bf16[192,128]{1,0:T(8,128)(2,1)S(1)} %copy-done.10), channel_id=1, source_target_pairs={{0,1},{1,2},{2,3},{3,0},{4,5},{5,6},{6,7},{7,4},{8,9},{9,10},{10,1... | collective-permute-start | bytes 147464 | tf_op jit(solution)/shard_map/ppermute | solution.py:42
  20.5 10.3 %collective-permute-start = (bf16[256,192]{0,1:T(8,128)(2,1)S(1)}, bf16[256,192]{0,1:T(8,128)(2,1)S(1)}, u32[]{:S(2)}, u32[]{:S(2)}) collective-permute-start(bf16[256,192]{0,1:T(8,128)(2,1)S(1)} %copy-done.9), channel_id=1, source_target_pairs={{0,1},{1,2},{2,3},{3,0},{4,5},{5,6},{6,7},{7,4},{8,9},{9,10},{10,1... | collective-permute-start | bytes 294920 | tf_op jit(solution)/shard_map/ppermute | solution.py:42
  22.2 8.6 %collective-permute-start.1 = (bf16[256,192]{0,1:T(8,128)(2,1)S(1)}, bf16[256,192]{0,1:T(8,128)(2,1)S(1)}, u32[]{:S(2)}, u32[]{:S(2)}) collective-permute-start(bf16[256,192]{0,1:T(8,128)(2,1)S(1)} %copy-done.9), channel_id=1, source_target_pairs={{0,2},{1,3},{2,0},{3,1},{4,6},{5,7},{6,4},{7,5},{8,10},{9,11},{10,... | collective-permute-start | bytes 294920 | tf_op jit(solution)/shard_map/ppermute | solution.py:42
  24.3 6.5 %collective-permute-start.2 = (bf16[256,192]{0,1:T(8,128)(2,1)S(1)}, bf16[256,192]{0,1:T(8,128)(2,1)S(1)}, u32[]{:S(2)}, u32[]{:S(2)}) collective-permute-start(bf16[256,192]{0,1:T(8,128)(2,1)S(1)} %copy-done.9), channel_id=1, source_target_pairs={{0,3},{1,0},{2,1},{3,2},{4,7},{5,4},{6,5},{7,6},{8,11},{9,8},{10,9... | collective-permute-start | bytes 294920 | tf_op jit(solution)/shard_map/ppermute | solution.py:42
  26.6 4.2 %collective-permute-start.4 = (bf16[192,128]{1,0:T(8,128)(2,1)S(1)}, bf16[192,128]{1,0:T(8,128)(2,1)}, u32[]{:S(2)}, u32[]{:S(2)}) collective-permute-start(bf16[192,128]{1,0:T(8,128)(2,1)S(1)} %copy-done.10), channel_id=1, source_target_pairs={{0,2},{1,3},{2,0},{3,1},{4,6},{5,7},{6,4},{7,5},{8,10},{9,11},{10,... | collective-permute-start | bytes 147464 | tf_op jit(solution)/shard_map/ppermute | solution.py:42
  28.1 2.7 collective-permute-start.5
  32.0 7.3 %collective-permute-start.6 = (bf16[16,128]{1,0:T(8,128)(2,1)S(1)}, bf16[16,128]{1,0:T(8,128)(2,1)S(1)}, u32[]{:S(2)}, u32[]{:S(2)}) collective-permute-start(bf16[16,128]{1,0:T(8,128)(2,1)S(1)} %get-tuple-element.28), channel_id=1, source_target_pairs={{0,4},{4,8},{8,12},{12,16},{16,20},{20,24},{24,28},{1,5},{5,9},{9,... | collective-permute-start | bytes 12296 | tf_op jit(solution)/shard_map/ppermute | solution.py:31
  33.3 6.0 %collective-permute-start.7 = (bf16[16,128]{1,0:T(8,128)(2,1)S(1)}, bf16[16,128]{1,0:T(8,128)(2,1)S(1)}, u32[]{:S(2)}, u32[]{:S(2)}) collective-permute-start(bf16[16,128]{1,0:T(8,128)(2,1)S(1)} %get-tuple-element.29), channel_id=1, source_target_pairs={{4,0},{8,4},{12,8},{16,12},{20,16},{24,20},{28,24},{5,1},{9,5},{13... | collective-permute-start | bytes 12296 | tf_op jit(solution)/shard_map/ppermute | solution.py:32
  43.2 6.9 %collective-permute-start.8 = (bf16[1,48,256]{2,1,0:T(8,128)(2,1)S(1)}, bf16[1,48,256]{2,1,0:T(8,128)(2,1)S(1)}, u32[]{:S(2)}, u32[]{:S(2)}) collective-permute-start(bf16[1,48,256]{2,1,0:T(8,128)(2,1)S(1)} %get-tuple-element.26), channel_id=1, source_target_pairs={{0,4},{4,8},{8,12},{12,16},{16,20},{20,24},{24,28},{1,5},{5,9},{9,... | collective-permute-start | bytes 73736 | tf_op jit(solution)/shard_map/ppermute | solution.py:31
  44.5 6.1 %collective-permute-start.9 = (bf16[1,48,256]{2,1,0:T(8,128)(2,1)S(1)}, bf16[1,48,256]{2,1,0:T(8,128)(2,1)S(1)}, u32[]{:S(2)}, u32[]{:S(2)}) collective-permute-start(bf16[1,48,256]{2,1,0:T(8,128)(2,1)S(1)} %get-tuple-element.27), channel_id=1, source_target_pairs={{4,0},{8,4},{12,8},{16,12},{20,16},{24,20},{28,24},{5,1},{9,5},{13... | collective-permute-start | bytes 73736 | tf_op jit(solution)/shard_map/ppermute | solution.py:32
  50.7 19.5 %copy-start.4 = (bf16[3,128,128]{2,1,0:T(8,128)(2,1)S(1)}, bf16[3,128,128]{2,1,0:T(8,128)(2,1)}, u32[]{:S(2)}) copy-start(bf16[3,128,128]{2,1,0:T(8,128)(2,1)} %param.27) | copy-start | bytes 294916
  76.6 7.8 %collective-permute-start.10 = (bf16[1,48,256]{2,1,0:T(8,128)(2,1)S(1)}, bf16[1,48,256]{2,1,0:T(8,128)(2,1)S(1)}, u32[]{:S(2)}, u32[]{:S(2)}) collective-permute-start(bf16[1,48,256]{2,1,0:T(8,128)(2,1)S(1)} %get-tuple-element.24), channel_id=1, source_target_pairs={{0,4},{4,8},{8,12},{12,16},{16,20},{20,24},{24,28},{1,5},{5,9},{9,... | collective-permute-start | bytes 73736 | tf_op jit(solution)/shard_map/ppermute | solution.py:31
  77.9 7.0 %collective-permute-start.11 = (bf16[1,48,256]{2,1,0:T(8,128)(2,1)S(1)}, bf16[1,48,256]{2,1,0:T(8,128)(2,1)S(1)}, u32[]{:S(2)}, u32[]{:S(2)}) collective-permute-start(bf16[1,48,256]{2,1,0:T(8,128)(2,1)S(1)} %get-tuple-element.25), channel_id=1, source_target_pairs={{4,0},{8,4},{12,8},{16,12},{20,16},{24,20},{28,24},{5,1},{9,5},{13... | collective-permute-start | bytes 73736 | tf_op jit(solution)/shard_map/ppermute | solution.py:32
  110.8 7.9 %collective-permute-start.12 = (bf16[1,48,256]{2,1,0:T(8,128)(2,1)S(1)}, bf16[1,48,256]{2,1,0:T(8,128)(2,1)S(1)}, u32[]{:S(2)}, u32[]{:S(2)}) collective-permute-start(bf16[1,48,256]{2,1,0:T(8,128)(2,1)S(1)} %get-tuple-element.22), channel_id=1, source_target_pairs={{0,4},{4,8},{8,12},{12,16},{16,20},{20,24},{24,28},{1,5},{5,9},{9,... | collective-permute-start | bytes 73736 | tf_op jit(solution)/shard_map/ppermute | solution.py:31
  112.1 7.2 %collective-permute-start.13 = (bf16[1,48,256]{2,1,0:T(8,128)(2,1)S(1)}, bf16[1,48,256]{2,1,0:T(8,128)(2,1)S(1)}, u32[]{:S(2)}, u32[]{:S(2)}) collective-permute-start(bf16[1,48,256]{2,1,0:T(8,128)(2,1)S(1)} %get-tuple-element.23), channel_id=1, source_target_pairs={{4,0},{8,4},{12,8},{16,12},{20,16},{24,20},{28,24},{5,1},{9,5},{13... | collective-permute-start | bytes 73736 | tf_op jit(solution)/shard_map/ppermute | solution.py:32
  146.9 12.5 %collective-permute-start.14 = (f32[3,2048]{1,0:T(4,128)S(1)}, f32[3,2048]{1,0:T(4,128)}, u32[]{:S(2)}, u32[]{:S(2)}) collective-permute-start(f32[3,2048]{1,0:T(4,128)S(1)} %copy.100), channel_id=1, source_target_pairs={{0,4},{4,8},{8,12},{12,16},{16,20},{20,24},{24,28},{28,0},{1,5},{5... | collective-permute-start | bytes 73736 | tf_op jit(solution)/shard_map/ppermute | solution.py:42
  153.9 9.5 %collective-permute-start.15 = (f32[3,2048]{1,0:T(4,128)S(1)}, f32[3,2048]{1,0:T(4,128)}, u32[]{:S(2)}, u32[]{:S(2)}) collective-permute-start(f32[3,2048]{1,0:T(4,128)S(1)} %copy.100), channel_id=1, source_target_pairs={{0,8},{4,12},{8,16},{12,20},{16,24},{20,28},{24,0},{28,4},{1,9},{5... | collective-permute-start | bytes 73736 | tf_op jit(solution)/shard_map/ppermute | solution.py:42
  154.9 12.6 %collective-permute-start.16 = (f32[3,2048]{1,0:T(4,128)S(1)}, f32[3,2048]{1,0:T(4,128)}, u32[]{:S(2)}, u32[]{:S(2)}) collective-permute-start(f32[3,2048]{1,0:T(4,128)S(1)} %copy.100), channel_id=1, source_target_pairs={{0,12},{4,16},{8,20},{12,24},{16,28},{20,0},{24,4},{28,8},{1,13},{... | collective-permute-start | bytes 73736 | tf_op jit(solution)/shard_map/ppermute | solution.py:42
  155.3 14.4 %collective-permute-start.17 = (f32[3,2048]{1,0:T(4,128)S(1)}, f32[3,2048]{1,0:T(4,128)S(1)}, u32[]{:S(2)}, u32[]{:S(2)}) collective-permute-start(f32[3,2048]{1,0:T(4,128)S(1)} %copy.100), channel_id=1, source_target_pairs={{0,16},{4,20},{8,24},{12,28},{16,0},{20,4},{24,8},{28,12},{1,17},{... | collective-permute-start | bytes 73736 | tf_op jit(solution)/shard_map/ppermute | solution.py:42
  157.8 13.4 %collective-permute-start.18 = (f32[3,2048]{1,0:T(4,128)S(1)}, f32[3,2048]{1,0:T(4,128)S(1)}, u32[]{:S(2)}, u32[]{:S(2)}) collective-permute-start(f32[3,2048]{1,0:T(4,128)S(1)} %copy.100), channel_id=1, source_target_pairs={{0,20},{4,24},{8,28},{12,0},{16,4},{20,8},{24,12},{28,16},{1,21},{... | collective-permute-start | bytes 73736 | tf_op jit(solution)/shard_map/ppermute | solution.py:42
  159.3 13.2 %collective-permute-start.19 = (f32[3,2048]{1,0:T(4,128)S(1)}, f32[3,2048]{1,0:T(4,128)S(1)}, u32[]{:S(2)}, u32[]{:S(2)}) collective-permute-start(f32[3,2048]{1,0:T(4,128)S(1)} %copy.100), channel_id=1, source_target_pairs={{0,24},{4,28},{8,0},{12,4},{16,8},{20,12},{24,16},{28,20},{1,25},{... | collective-permute-start | bytes 73736 | tf_op jit(solution)/shard_map/ppermute | solution.py:42
  163.4 10.6 %collective-permute-start.20 = (f32[3,2048]{1,0:T(4,128)S(1)}, f32[3,2048]{1,0:T(4,128)}, u32[]{:S(2)}, u32[]{:S(2)}) collective-permute-start(f32[3,2048]{1,0:T(4,128)S(1)} %copy.100), channel_id=1, source_target_pairs={{0,28},{4,0},{8,4},{12,8},{16,12},{20,16},{24,20},{28,24},{1,29},{... | collective-permute-start | bytes 73736 | tf_op jit(solution)/shard_map/ppermute | solution.py:42
  (7 other events, 30.2 us)

commit v2 on v1

--- a/solution.py
+++ b/solution.py
@@ -98,40 +98,45 @@
         out_shape=jax.ShapeDtypeStruct((atoms, channels), jnp.bfloat16),
     )(queries, padded_kv, band, valid_tab)
 
-ROW_CHUNK = 16
-
-
-def lddt_kernel(slots_ref, count_ref, own_ref, part_ref, out_ref):
+ROW_CHUNK = 32
+
+
+def lddt_kernel(slots_ref, count_ref, own_ref, part_ref, out_ref, cols_ref):
     block = pl.program_id(0)
     live = count_ref[block]
     max_slots = slots_ref.shape[0] // count_ref.shape[0]
-    lane = lax.broadcasted_iota(jnp.int32, (ROW_CHUNK, PAIR_BLK), 1)
     shape = (ROW_CHUNK, PAIR_BLK)
+    lane = lax.broadcasted_iota(jnp.int32, shape, 1)
+    for chunk in range(PAIR_BLK // ROW_CHUNK):
+        rows = slice(chunk * ROW_CHUNK, (chunk + 1) * ROW_CHUNK)
+        own = own_ref[rows, :]
+        for d in range(6):
+            cols_ref[d, rows, :] = jnp.broadcast_to(own[:, d : d + 1], shape)
 
     def row_body(row_index, carry):
         row = pl.multiple_of(row_index * ROW_CHUNK, ROW_CHUNK)
-        own = own_ref[pl.ds(row, ROW_CHUNK), :]
-        own_cols = [jnp.broadcast_to(own[:, d : d + 1], shape) for d in range(6)]
 
         def slot_body(slot_index, accs):
             part = part_ref[slots_ref[block * max_slots + slot_index]]
-            gaps = [own_cols[d] - part[d : d + 1, :] for d in range(3)]
-            true_gaps = [own_cols[3 + d] - part[3 + d : 4 + d, :] for d in range(3)]
-            square_pred = gaps[0] * gaps[0] + gaps[1] * gaps[1] + gaps[2] * gaps[2]
+            gaps = [cols_ref[d, pl.ds(row, ROW_CHUNK), :] - part[d : d + 1, :] for d in range(3)]
+            true_gaps = [
+                cols_ref[3 + d, pl.ds(row, ROW_CHUNK), :] - part[3 + d : 4 + d, :] for d in range(3)
+            ]
+            square_pred = gaps[0] * gaps[0] + gaps[1] * gaps[1] + gaps[2] * gaps[2] + 1.0
             square_true = (
                 true_gaps[0] * true_gaps[0] + true_gaps[1] * true_gaps[1] + true_gaps[2] * true_gaps[2]
-            )
-            dist_pred = jnp.sqrt(square_pred + 1.0)
-            dist_true = jnp.sqrt(square_true + 1.0)
-            gap_dist = dist_pred - dist_true
-            error_soft = jnp.sqrt(gap_dist * gap_dist + 0.01)
-            decay = jnp.exp(-error_soft)
+            ) + 1.0
+            inv_pred = lax.rsqrt(square_pred)
+            gap_dist = square_pred * inv_pred - square_true * lax.rsqrt(square_true)
+            square_err = gap_dist * gap_dist + 0.01
+            inv_err = lax.rsqrt(square_err)
+            decay = jnp.exp(-(square_err * inv_err))
             ys = [decay * math.exp(t) for t in thresholds]
             dens = [(1.0 + y) * (1.0 + y) for y in ys]
             low = dens[0] * dens[1]
             high = dens[2] * dens[3]
             numer = (ys[0] * dens[1] + ys[1] * dens[0]) * high + (ys[2] * dens[3] + ys[3] * dens[2]) * low
-            coef = (-0.25 * numer * gap_dist) / (low * high * error_soft * dist_pred)
+            coef = (-0.25 * numer * gap_dist * (inv_err * inv_pred)) / (low * high)
             return tuple(acc + coef * gap for acc, gap in zip(accs, gaps))
 
         zero = jnp.zeros(shape, jnp.float32)
@@ -157,6 +162,7 @@
                 pl.BlockSpec((table_rows, 8, PAIR_BLK), lambda b, *_: (0, 0, 0)),
             ],
             out_specs=pl.BlockSpec((PAIR_BLK, PAIR_BLK), lambda b, *_: (b, 0)),
+            scratch_shapes=[pltpu.VMEM((6, PAIR_BLK, PAIR_BLK), jnp.float32)],
         ),
         out_shape=jax.ShapeDtypeStruct((blocks * PAIR_BLK, PAIR_BLK), jnp.float32),
     )(slots, counts, own_tab, part_tab)

time: 279 us -> 242 us (0.87)
  Pallas kernels: 140 us -> 104 us
    pallas_call x1, Pallas kernels: 85.3 us -> 49.3 us  [lddt_sums(): pl.pallas_call(lddt_kernel, grid_spec=pltpu.PrefetchScalarGridSpec(num_sc...]
  transfers between devices with their start and end apart: 28 -> 28, of which waited for: 5 -> 5; matrix products, arithmetic and copies ran while one was open for 9% -> 10% of each run, Pallas kernels for 0% -> 0%
where the time goes in v2:
time: 242 us; the launch traced here: 239 us
  Pallas kernels  104 us (43%)
  starting transfers between devices  52.5 us (22%)
  local copies, waits for them, and re-layouts  34.1 us (14%)
  matrix products  27.5 us (11%)
  other arithmetic  11.3 us (5%)
  waiting for transfers between devices  5.53 us (2%)
  between operations  4.16 us (2%)
    pallas_call x3, Pallas kernels, window_attend(): pl.pallas_call(attend_kernel, grid=(atoms // Q_TILE,), in_specs=[pl.Block...  55 us
    pallas_call x1, Pallas kernels, lddt_sums(): pl.pallas_call(lddt_kernel, grid_spec=pltpu.PrefetchScalarGridSpec(num_sc...  49.3 us
    ppermute x20, starting transfers between devices, ring_parts(): parts.append(lax.ppermute(value, axis, pairs))  26.9 us
    ppermute x4, starting transfers between devices, extended(): after = lax.ppermute(first, axis, down)  20.5 us
    dot_general x12, matrix products, dense(): jnp.einsum('sac,cf->saf', left, right, preferred_element_type=jnp.float32)  19 us
    unnamed x32, local copies, waits for them, and re-layouts  12.8 us
    another operation x11, local copies, waits for them, and re-layouts, ring_parts(): return jnp.stack(parts)  7.02 us
    ppermute x7, local copies, waits for them, and re-layouts, ring_parts(): parts.append(lax.ppermute(value, axis, pairs))  5.53 us
  transfers between devices with their start and end apart: 28, of which 5 were waited for; matrix products, arithmetic and copies ran while one was open for 10% of the time, Pallas kernels for 0%

profile of v2, /device:TPU:26, one launch (start us, length us, event | category | flops | bytes accessed | tf_op | source)
XLA Modules:
  0.0 239.5 jit_solution(9050274671086256717)
XLA Ops:
  4.7 1.8 collective-permute-start.22
  6.4 1.6 collective-permute-start.23
  9.3 1.8 collective-permute-start.25
  16.3 2.2 fusion.16
  20.5 1.7 collective-permute-start
  22.7 1.7 collective-permute-done.26
  24.3 2.2 collective-permute-done.27
  33.3 4.5 %collective-permute-start.7 = (bf16[16,128]{1,0:T(8,128)(2,1)S(1)}, bf16[16,128]{1,0:T(8,128)(2,1)S(1)}, u32[]{:S(2)}, u32[]{:S(2)}) collective-permute-start(bf16[16,128]{1,0:T(8,128)(2,1)S(1)} %get-tuple-element.29), channel_id=1, source_target_pairs={{4,0},{8,4},{12,8},{16,12},{20,16},{24,20},{28,24},{5,1},{9,5},{13... | collective-permute-start | bytes 12296 | tf_op jit(solution)/shard_map/ppermute | solution.py:32
  39.3 2.3 multiply_reduce_fusion.6
  44.5 4.6 %collective-permute-start.9 = (bf16[1,48,256]{2,1,0:T(8,128)(2,1)S(1)}, bf16[1,48,256]{2,1,0:T(8,128)(2,1)S(1)}, u32[]{:S(2)}, u32[]{:S(2)}) collective-permute-start(bf16[1,48,256]{2,1,0:T(8,128)(2,1)S(1)} %get-tuple-element.27), channel_id=1, source_target_pairs={{4,0},{8,4},{12,8},{16,12},{20,16},{24,20},{28,24},{5,1},{9,5},{13... | collective-permute-start | bytes 73736 | tf_op jit(solution)/shard_map/ppermute | solution.py:32
  51.8 18.3 %shard_map.167 = bf16[2048,128]{1,0:T(8,128)(2,1)} custom-call(bf16[2048,128]{1,0:T(8,128)(2,1)} %slice_bitcast_fusion.2.q_ref, bf16[2176,256]{1,0:T(8,128)(2,1)} %pad.20.kv_ref, f32[128,256]{1,0:T(8,128)} %fusion.60.band_ref, f32[16,256]{1,0:T(8,128)} %fusion.87.valid_ref), custom_call_target="tpu_custom_call" | custom-call | tf_op jit(solution)/shard_map/pallas_call | solution.py:88
  71.6 1.7 convolution_bitcast_fusion.2
  73.3 1.7 multiply_reduce_fusion.4
  75.0 1.6 fusion.2
  77.9 5.6 %collective-permute-start.11 = (bf16[1,48,256]{2,1,0:T(8,128)(2,1)S(1)}, bf16[1,48,256]{2,1,0:T(8,128)(2,1)S(1)}, u32[]{:S(2)}, u32[]{:S(2)}) collective-permute-start(bf16[1,48,256]{2,1,0:T(8,128)(2,1)S(1)} %get-tuple-element.25), channel_id=1, source_target_pairs={{4,0},{8,4},{12,8},{16,12},{20,16},{24,20},{28,24},{5,1},{9,5},{13... | collective-permute-start | bytes 73736 | tf_op jit(solution)/shard_map/ppermute | solution.py:32
  86.1 18.3 %shard_map.168 = bf16[2048,128]{1,0:T(8,128)(2,1)} custom-call(bf16[2048,128]{1,0:T(8,128)(2,1)} %slice_bitcast_fusion.1.q_ref, bf16[2176,256]{1,0:T(8,128)(2,1)} %pad.21.kv_ref, f32[128,256]{1,0:T(8,128)} %fusion.60.band_ref, f32[16,256]{1,0:T(8,128)} %fusion.87.valid_ref), custom_call_target="tpu_custom_call" | custom-call | tf_op jit(solution)/shard_map/pallas_call | solution.py:88
  105.8 1.7 convolution_bitcast_fusion.1
  107.5 1.7 multiply_reduce_fusion.2
  112.1 5.7 %collective-permute-start.13 = (bf16[1,48,256]{2,1,0:T(8,128)(2,1)S(1)}, bf16[1,48,256]{2,1,0:T(8,128)(2,1)S(1)}, u32[]{:S(2)}, u32[]{:S(2)}) collective-permute-start(bf16[1,48,256]{2,1,0:T(8,128)(2,1)S(1)} %get-tuple-element.23), channel_id=1, source_target_pairs={{4,0},{8,4},{12,8},{16,12},{20,16},{24,20},{28,24},{5,1},{9,5},{13... | collective-permute-start | bytes 73736 | tf_op jit(solution)/shard_map/ppermute | solution.py:32
  120.5 18.3 %shard_map.169 = bf16[2048,128]{1,0:T(8,128)(2,1)} custom-call(bf16[2048,128]{1,0:T(8,128)(2,1)} %slice_bitcast_fusion.q_ref, bf16[2176,256]{1,0:T(8,128)(2,1)} %pad.22.kv_ref, f32[128,256]{1,0:T(8,128)} %fusion.60.band_ref, f32[16,256]{1,0:T(8,128)} %fusion.87.valid_ref), custom_call_target="tpu_custom_call" | custom-call | tf_op jit(solution)/shard_map/pallas_call | solution.py:88
  140.3 1.7 convolution_bitcast_fusion
  142.0 1.7 multiply_reduce_fusion
  143.7 2.8 %constant_dynamic-update-slice_fusion = (f32[8,3,2048]{1,2,0:T(8,128)}, f32[1,3,2048]{1,2,0:T(8,128)S(1)}) fusion(f32[128,3]{0,1:T(4,128)S(1)} %copy-done.8, f32[2048,128]{0,1:T(8,128)S(1)} %get-tuple-element.49, f32[2048]{0:T(1024)S(1)} %add_rsqrt_fusion, f32[]{:T(128)} %bitcast.4, f32[1,3,2048]{1,2,0:T(8,128)S(1)} %copy.95, f32[3,2048]{0,1:T(8,128)S(1)} %copy.94, ...), kind=kOutput, calls=%fused_computation.136 | convolution fusion | flops 9723903 | bytes 2180616 | tf_op jit(solution)/shard_map/sac,cd->sda/dot_general | solution.py:246
  146.9 7.0 %collective-permute-start.14 = (f32[3,2048]{1,0:T(4,128)S(1)}, f32[3,2048]{1,0:T(4,128)}, u32[]{:S(2)}, u32[]{:S(2)}) collective-permute-start(f32[3,2048]{1,0:T(4,128)S(1)} %copy.100), channel_id=1, source_target_pairs={{0,4},{4,8},{8,12},{12,16},{16,20},{20,24},{24,28},{28,0},{1,5},{5... | collective-permute-start | bytes 73736 | tf_op jit(solution)/shard_map/ppermute | solution.py:42
  155.3 2.4 %collective-permute-start.17 = (f32[3,2048]{1,0:T(4,128)S(1)}, f32[3,2048]{1,0:T(4,128)S(1)}, u32[]{:S(2)}, u32[]{:S(2)}) collective-permute-start(f32[3,2048]{1,0:T(4,128)S(1)} %copy.100), channel_id=1, source_target_pairs={{0,16},{4,20},{8,24},{12,28},{16,0},{20,4},{24,8},{28,12},{1,17},{... | collective-permute-start | bytes 73736 | tf_op jit(solution)/shard_map/ppermute | solution.py:42
  159.3 1.9 collective-permute-start.19
  163.4 2.0 collective-permute-start.20
  176.2 5.2 %copy.122 = f32[8,3,2048]{2,1,0:T(4,128)S(1)} copy(f32[8,3,2048]{1,2,0:T(8,128)} %bitcast_dynamic-update-slice_fusion) | data formatting | bytes 393216 | tf_op jit(solution)/shard_map/stack | solution.py:43
  182.4 49.3 %shard_map.170 = f32[2048,128]{1,0:T(8,128)} custom-call(s32[208]{0:T(256)} %reshape.317.slots_ref, s32[16]{0:T(128)} %count_ref.1, f32[2048,128]{1,0:T(8,128)} %pad.23.own_ref, f32[128,8,128]{2,1,0:T(8,128)} %bitcast.186), custom_call_target="tpu_custom_call" | custom-call | tf_op jit(solution)/shard_map/pallas_call | solution.py:155
  231.7 2.3 fusion.24
  234.0 2.2 copy.125
  237.3 2.2 copy.124
  (142 shorter events, 55.5 us)
Async XLA Ops:
  0.6 15.7 %copy-start = (f32[3,128]{1,0:T(4,128)S(1)}, f32[3,128]{1,0:T(4,128)}, u32[]{:S(2)}) copy-start(f32[3,128]{1,0:T(4,128)} %param.25) | copy-start | bytes 4612
  4.6 13.9 %collective-permute-start.21 = (f32[4,2048]{1,0:T(4,128)S(1)}, f32[4,2048]{1,0:T(4,128)S(1)}, u32[]{:S(2)}, u32[]{:S(2)}) collective-permute-start(f32[4,2048]{1,0:T(4,128)S(1)} %select_maximum_fusion), channel_id=1, source_target_pairs={{0,4},{4,8},{8,12},{12,16},{16,20},{20,24},{24,28},{28,0},{1,5},{5... | collective-permute-start | bytes 98312 | tf_op jit(solution)/shard_map/ppermute | solution.py:42
  4.7 15.3 %collective-permute-start.22 = (f32[4,2048]{1,0:T(4,128)S(1)}, f32[4,2048]{1,0:T(4,128)S(1)}, u32[]{:S(2)}, u32[]{:S(2)}) collective-permute-start(f32[4,2048]{1,0:T(4,128)S(1)} %select_maximum_fusion), channel_id=1, source_target_pairs={{0,8},{4,12},{8,16},{12,20},{16,24},{20,28},{24,0},{28,4},{1,9},{5... | collective-permute-start | bytes 98312 | tf_op jit(solution)/shard_map/ppermute | solution.py:42
  6.4 14.0 %collective-permute-start.23 = (f32[4,2048]{1,0:T(4,128)S(1)}, f32[4,2048]{1,0:T(4,128)S(1)}, u32[]{:S(2)}, u32[]{:S(2)}) collective-permute-start(f32[4,2048]{1,0:T(4,128)S(1)} %select_maximum_fusion), channel_id=1, source_target_pairs={{0,12},{4,16},{8,20},{12,24},{16,28},{20,0},{24,4},{28,8},{1,13},{... | collective-permute-start | bytes 98312 | tf_op jit(solution)/shard_map/ppermute | solution.py:42
  8.0 12.4 %collective-permute-start.24 = (f32[4,2048]{1,0:T(4,128)S(1)}, f32[4,2048]{1,0:T(4,128)S(1)}, u32[]{:S(2)}, u32[]{:S(2)}) collective-permute-start(f32[4,2048]{1,0:T(4,128)S(1)} %select_maximum_fusion), channel_id=1, source_target_pairs={{0,16},{4,20},{8,24},{12,28},{16,0},{20,4},{24,8},{28,12},{1,17},{... | collective-permute-start | bytes 98312 | tf_op jit(solution)/shard_map/ppermute | solution.py:42
  9.3 12.9 %collective-permute-start.25 = (f32[4,2048]{1,0:T(4,128)S(1)}, f32[4,2048]{1,0:T(4,128)S(1)}, u32[]{:S(2)}, u32[]{:S(2)}) collective-permute-start(f32[4,2048]{1,0:T(4,128)S(1)} %select_maximum_fusion), channel_id=1, source_target_pairs={{0,20},{4,24},{8,28},{12,0},{16,4},{20,8},{24,12},{28,16},{1,21},{... | collective-permute-start | bytes 98312 | tf_op jit(solution)/shard_map/ppermute | solution.py:42
  14.8 13.2 %copy-start.7 = (f32[3,2,128]{2,1,0:T(2,128)S(1)}, f32[3,2,128]{2,1,0:T(2,128)}, u32[]{:S(2)}) copy-start(f32[3,2,128]{2,1,0:T(2,128)} %param.30) | copy-start | bytes 9220
  14.9 13.3 %copy-start.3 = (bf16[2048,128]{1,0:T(8,128)(2,1)S(1)}, bf16[2048,128]{1,0:T(8,128)(2,1)}, u32[]{:S(2)}) copy-start(bf16[2048,128]{1,0:T(8,128)(2,1)} %param.20) | copy-start | bytes 1572868
  18.5 5.8 %collective-permute-start.26 = (f32[4,2048]{1,0:T(4,128)S(1)}, f32[4,2048]{1,0:T(4,128)S(1)}, u32[]{:S(2)}, u32[]{:S(2)}) collective-permute-start(f32[4,2048]{1,0:T(4,128)S(1)} %select_maximum_fusion), channel_id=1, source_target_pairs={{0,24},{4,28},{8,0},{12,4},{16,8},{20,12},{24,16},{28,20},{1,25},{... | collective-permute-start | bytes 98312 | tf_op jit(solution)/shard_map/ppermute | solution.py:42
  20.0 6.6 %collective-permute-start.27 = (f32[4,2048]{1,0:T(4,128)S(1)}, f32[4,2048]{1,0:T(4,128)S(1)}, u32[]{:S(2)}, u32[]{:S(2)}) collective-permute-start(f32[4,2048]{1,0:T(4,128)S(1)} %select_maximum_fusion), channel_id=1, source_target_pairs={{0,28},{4,0},{8,4},{12,8},{16,12},{20,16},{24,20},{28,24},{1,29},{... | collective-permute-start | bytes 98312 | tf_op jit(solution)/shard_map/ppermute | solution.py:42
  20.4 7.7 %collective-permute-start.3 = (bf16[192,128]{1,0:T(8,128)(2,1)S(1)}, bf16[192,128]{1,0:T(8,128)(2,1)S(1)}, u32[]{:S(2)}, u32[]{:S(2)}) collective-permute-start(bf16[192,128]{1,0:T(8,128)(2,1)S(1)} %copy-done.10), channel_id=1, source_target_pairs={{0,1},{1,2},{2,3},{3,0},{4,5},{5,6},{6,7},{7,4},{8,9},{9,10},{10,1... | collective-permute-start | bytes 147464 | tf_op jit(solution)/shard_map/ppermute | solution.py:42
  20.5 10.3 %collective-permute-start = (bf16[256,192]{0,1:T(8,128)(2,1)S(1)}, bf16[256,192]{0,1:T(8,128)(2,1)S(1)}, u32[]{:S(2)}, u32[]{:S(2)}) collective-permute-start(bf16[256,192]{0,1:T(8,128)(2,1)S(1)} %copy-done.9), channel_id=1, source_target_pairs={{0,1},{1,2},{2,3},{3,0},{4,5},{5,6},{6,7},{7,4},{8,9},{9,10},{10,1... | collective-permute-start | bytes 294920 | tf_op jit(solution)/shard_map/ppermute | solution.py:42
  22.2 8.6 %collective-permute-start.1 = (bf16[256,192]{0,1:T(8,128)(2,1)S(1)}, bf16[256,192]{0,1:T(8,128)(2,1)S(1)}, u32[]{:S(2)}, u32[]{:S(2)}) collective-permute-start(bf16[256,192]{0,1:T(8,128)(2,1)S(1)} %copy-done.9), channel_id=1, source_target_pairs={{0,2},{1,3},{2,0},{3,1},{4,6},{5,7},{6,4},{7,5},{8,10},{9,11},{10,... | collective-permute-start | bytes 294920 | tf_op jit(solution)/shard_map/ppermute | solution.py:42
  24.3 6.5 %collective-permute-start.2 = (bf16[256,192]{0,1:T(8,128)(2,1)S(1)}, bf16[256,192]{0,1:T(8,128)(2,1)S(1)}, u32[]{:S(2)}, u32[]{:S(2)}) collective-permute-start(bf16[256,192]{0,1:T(8,128)(2,1)S(1)} %copy-done.9), channel_id=1, source_target_pairs={{0,3},{1,0},{2,1},{3,2},{4,7},{5,4},{6,5},{7,6},{8,11},{9,8},{10,9... | collective-permute-start | bytes 294920 | tf_op jit(solution)/shard_map/ppermute | solution.py:42
  26.6 4.2 %collective-permute-start.4 = (bf16[192,128]{1,0:T(8,128)(2,1)S(1)}, bf16[192,128]{1,0:T(8,128)(2,1)}, u32[]{:S(2)}, u32[]{:S(2)}) collective-permute-start(bf16[192,128]{1,0:T(8,128)(2,1)S(1)} %copy-done.10), channel_id=1, source_target_pairs={{0,2},{1,3},{2,0},{3,1},{4,6},{5,7},{6,4},{7,5},{8,10},{9,11},{10,... | collective-permute-start | bytes 147464 | tf_op jit(solution)/shard_map/ppermute | solution.py:42
  28.1 2.7 %collective-permute-start.5 = (bf16[192,128]{1,0:T(8,128)(2,1)S(1)}, bf16[192,128]{1,0:T(8,128)(2,1)}, u32[]{:S(2)}, u32[]{:S(2)}) collective-permute-start(bf16[192,128]{1,0:T(8,128)(2,1)S(1)} %copy-done.10), channel_id=1, source_target_pairs={{0,3},{1,0},{2,1},{3,2},{4,7},{5,4},{6,5},{7,6},{8,11},{9,8},{10,9... | collective-permute-start | bytes 147464 | tf_op jit(solution)/shard_map/ppermute | solution.py:42
  32.0 7.3 %collective-permute-start.6 = (bf16[16,128]{1,0:T(8,128)(2,1)S(1)}, bf16[16,128]{1,0:T(8,128)(2,1)S(1)}, u32[]{:S(2)}, u32[]{:S(2)}) collective-permute-start(bf16[16,128]{1,0:T(8,128)(2,1)S(1)} %get-tuple-element.28), channel_id=1, source_target_pairs={{0,4},{4,8},{8,12},{12,16},{16,20},{20,24},{24,28},{1,5},{5,9},{9,... | collective-permute-start | bytes 12296 | tf_op jit(solution)/shard_map/ppermute | solution.py:31
  33.3 6.0 %collective-permute-start.7 = (bf16[16,128]{1,0:T(8,128)(2,1)S(1)}, bf16[16,128]{1,0:T(8,128)(2,1)S(1)}, u32[]{:S(2)}, u32[]{:S(2)}) collective-permute-start(bf16[16,128]{1,0:T(8,128)(2,1)S(1)} %get-tuple-element.29), channel_id=1, source_target_pairs={{4,0},{8,4},{12,8},{16,12},{20,16},{24,20},{28,24},{5,1},{9,5},{13... | collective-permute-start | bytes 12296 | tf_op jit(solution)/shard_map/ppermute | solution.py:32
  43.2 6.9 %collective-permute-start.8 = (bf16[1,48,256]{2,1,0:T(8,128)(2,1)S(1)}, bf16[1,48,256]{2,1,0:T(8,128)(2,1)S(1)}, u32[]{:S(2)}, u32[]{:S(2)}) collective-permute-start(bf16[1,48,256]{2,1,0:T(8,128)(2,1)S(1)} %get-tuple-element.26), channel_id=1, source_target_pairs={{0,4},{4,8},{8,12},{12,16},{16,20},{20,24},{24,28},{1,5},{5,9},{9,... | collective-permute-start | bytes 73736 | tf_op jit(solution)/shard_map/ppermute | solution.py:31
  44.5 6.1 %collective-permute-start.9 = (bf16[1,48,256]{2,1,0:T(8,128)(2,1)S(1)}, bf16[1,48,256]{2,1,0:T(8,128)(2,1)S(1)}, u32[]{:S(2)}, u32[]{:S(2)}) collective-permute-start(bf16[1,48,256]{2,1,0:T(8,128)(2,1)S(1)} %get-tuple-element.27), channel_id=1, source_target_pairs={{4,0},{8,4},{12,8},{16,12},{20,16},{24,20},{28,24},{5,1},{9,5},{13... | collective-permute-start | bytes 73736 | tf_op jit(solution)/shard_map/ppermute | solution.py:32
  50.7 19.5 %copy-start.4 = (bf16[3,128,128]{2,1,0:T(8,128)(2,1)S(1)}, bf16[3,128,128]{2,1,0:T(8,128)(2,1)}, u32[]{:S(2)}) copy-start(bf16[3,128,128]{2,1,0:T(8,128)(2,1)} %param.27) | copy-start | bytes 294916
  76.6 7.8 %collective-permute-start.10 = (bf16[1,48,256]{2,1,0:T(8,128)(2,1)S(1)}, bf16[1,48,256]{2,1,0:T(8,128)(2,1)S(1)}, u32[]{:S(2)}, u32[]{:S(2)}) collective-permute-start(bf16[1,48,256]{2,1,0:T(8,128)(2,1)S(1)} %get-tuple-element.24), channel_id=1, source_target_pairs={{0,4},{4,8},{8,12},{12,16},{16,20},{20,24},{24,28},{1,5},{5,9},{9,... | collective-permute-start | bytes 73736 | tf_op jit(solution)/shard_map/ppermute | solution.py:31
  77.9 7.0 %collective-permute-start.11 = (bf16[1,48,256]{2,1,0:T(8,128)(2,1)S(1)}, bf16[1,48,256]{2,1,0:T(8,128)(2,1)S(1)}, u32[]{:S(2)}, u32[]{:S(2)}) collective-permute-start(bf16[1,48,256]{2,1,0:T(8,128)(2,1)S(1)} %get-tuple-element.25), channel_id=1, source_target_pairs={{4,0},{8,4},{12,8},{16,12},{20,16},{24,20},{28,24},{5,1},{9,5},{13... | collective-permute-start | bytes 73736 | tf_op jit(solution)/shard_map/ppermute | solution.py:32
  110.8 7.9 %collective-permute-start.12 = (bf16[1,48,256]{2,1,0:T(8,128)(2,1)S(1)}, bf16[1,48,256]{2,1,0:T(8,128)(2,1)S(1)}, u32[]{:S(2)}, u32[]{:S(2)}) collective-permute-start(bf16[1,48,256]{2,1,0:T(8,128)(2,1)S(1)} %get-tuple-element.22), channel_id=1, source_target_pairs={{0,4},{4,8},{8,12},{12,16},{16,20},{20,24},{24,28},{1,5},{5,9},{9,... | collective-permute-start | bytes 73736 | tf_op jit(solution)/shard_map/ppermute | solution.py:31
  112.1 7.2 %collective-permute-start.13 = (bf16[1,48,256]{2,1,0:T(8,128)(2,1)S(1)}, bf16[1,48,256]{2,1,0:T(8,128)(2,1)S(1)}, u32[]{:S(2)}, u32[]{:S(2)}) collective-permute-start(bf16[1,48,256]{2,1,0:T(8,128)(2,1)S(1)} %get-tuple-element.23), channel_id=1, source_target_pairs={{4,0},{8,4},{12,8},{16,12},{20,16},{24,20},{28,24},{5,1},{9,5},{13... | collective-permute-start | bytes 73736 | tf_op jit(solution)/shard_map/ppermute | solution.py:32
  146.9 12.5 %collective-permute-start.14 = (f32[3,2048]{1,0:T(4,128)S(1)}, f32[3,2048]{1,0:T(4,128)}, u32[]{:S(2)}, u32[]{:S(2)}) collective-permute-start(f32[3,2048]{1,0:T(4,128)S(1)} %copy.100), channel_id=1, source_target_pairs={{0,4},{4,8},{8,12},{12,16},{16,20},{20,24},{24,28},{28,0},{1,5},{5... | collective-permute-start | bytes 73736 | tf_op jit(solution)/shard_map/ppermute | solution.py:42
  153.9 9.5 %collective-permute-start.15 = (f32[3,2048]{1,0:T(4,128)S(1)}, f32[3,2048]{1,0:T(4,128)}, u32[]{:S(2)}, u32[]{:S(2)}) collective-permute-start(f32[3,2048]{1,0:T(4,128)S(1)} %copy.100), channel_id=1, source_target_pairs={{0,8},{4,12},{8,16},{12,20},{16,24},{20,28},{24,0},{28,4},{1,9},{5... | collective-permute-start | bytes 73736 | tf_op jit(solution)/shard_map/ppermute | solution.py:42
  154.9 12.6 %collective-permute-start.16 = (f32[3,2048]{1,0:T(4,128)S(1)}, f32[3,2048]{1,0:T(4,128)}, u32[]{:S(2)}, u32[]{:S(2)}) collective-permute-start(f32[3,2048]{1,0:T(4,128)S(1)} %copy.100), channel_id=1, source_target_pairs={{0,12},{4,16},{8,20},{12,24},{16,28},{20,0},{24,4},{28,8},{1,13},{... | collective-permute-start | bytes 73736 | tf_op jit(solution)/shard_map/ppermute | solution.py:42
  155.3 14.4 %collective-permute-start.17 = (f32[3,2048]{1,0:T(4,128)S(1)}, f32[3,2048]{1,0:T(4,128)S(1)}, u32[]{:S(2)}, u32[]{:S(2)}) collective-permute-start(f32[3,2048]{1,0:T(4,128)S(1)} %copy.100), channel_id=1, source_target_pairs={{0,16},{4,20},{8,24},{12,28},{16,0},{20,4},{24,8},{28,12},{1,17},{... | collective-permute-start | bytes 73736 | tf_op jit(solution)/shard_map/ppermute | solution.py:42
  157.8 13.4 %collective-permute-start.18 = (f32[3,2048]{1,0:T(4,128)S(1)}, f32[3,2048]{1,0:T(4,128)S(1)}, u32[]{:S(2)}, u32[]{:S(2)}) collective-permute-start(f32[3,2048]{1,0:T(4,128)S(1)} %copy.100), channel_id=1, source_target_pairs={{0,20},{4,24},{8,28},{12,0},{16,4},{20,8},{24,12},{28,16},{1,21},{... | collective-permute-start | bytes 73736 | tf_op jit(solution)/shard_map/ppermute | solution.py:42
  159.3 13.2 %collective-permute-start.19 = (f32[3,2048]{1,0:T(4,128)S(1)}, f32[3,2048]{1,0:T(4,128)S(1)}, u32[]{:S(2)}, u32[]{:S(2)}) collective-permute-start(f32[3,2048]{1,0:T(4,128)S(1)} %copy.100), channel_id=1, source_target_pairs={{0,24},{4,28},{8,0},{12,4},{16,8},{20,12},{24,16},{28,20},{1,25},{... | collective-permute-start | bytes 73736 | tf_op jit(solution)/shard_map/ppermute | solution.py:42
  163.4 10.6 %collective-permute-start.20 = (f32[3,2048]{1,0:T(4,128)S(1)}, f32[3,2048]{1,0:T(4,128)}, u32[]{:S(2)}, u32[]{:S(2)}) collective-permute-start(f32[3,2048]{1,0:T(4,128)S(1)} %copy.100), channel_id=1, source_target_pairs={{0,28},{4,0},{8,4},{12,8},{16,12},{20,16},{24,20},{28,24},{1,29},{... | collective-permute-start | bytes 73736 | tf_op jit(solution)/shard_map/ppermute | solution.py:42
  (7 other events, 30.2 us)

commit v3 on v2

--- a/solution.py
+++ b/solution.py
@@ -36,12 +36,19 @@
 
 def ring_parts(value, axis):
     peers = lax.axis_size(axis)
-    parts = [value]
-    for shift in range(1, peers):
-        pairs = [(i, (i + shift) % peers) for i in range(peers)]
-        parts.append(lax.ppermute(value, axis, pairs))
-    return jnp.stack(parts)
-
+    parts = value[None]
+    span = 1
+    while span < peers and peers % (2 * span) == 0:
+        pairs = [(i, (i + span) % peers) for i in range(peers)]
+        parts = jnp.concatenate([parts, lax.ppermute(parts, axis, pairs)])
+        span *= 2
+    if span < peers:
+        extra = [value[None]]
+        for shift in range(span, peers):
+            pairs = [(i, (i + shift) % peers) for i in range(peers)]
+            extra.append(lax.ppermute(value, axis, pairs)[None])
+        parts = jnp.concatenate([parts] + extra[1:])
+    return parts
 
 def rms_norm(tensor):
     return tensor * lax.rsqrt(jnp.mean(tensor * tensor, axis=-1, keepdims=True) + norm_epsilon)
@@ -101,10 +108,11 @@
 ROW_CHUNK = 32
 
 
-def lddt_kernel(slots_ref, count_ref, own_ref, part_ref, out_ref, cols_ref):
+def lddt_kernel(slots_ref, count_ref, own_ref, pred_ref, true_ref, out_ref, cols_ref):
     block = pl.program_id(0)
     live = count_ref[block]
-    max_slots = slots_ref.shape[0] // count_ref.shape[0]
+    blocks = count_ref.shape[0]
+    max_slots = slots_ref.shape[0] // blocks
     shape = (ROW_CHUNK, PAIR_BLK)
     lane = lax.broadcasted_iota(jnp.int32, shape, 1)
     for chunk in range(PAIR_BLK // ROW_CHUNK):
@@ -117,10 +125,14 @@
         row = pl.multiple_of(row_index * ROW_CHUNK, ROW_CHUNK)
 
         def slot_body(slot_index, accs):
-            part = part_ref[slots_ref[block * max_slots + slot_index]]
-            gaps = [cols_ref[d, pl.ds(row, ROW_CHUNK), :] - part[d : d + 1, :] for d in range(3)]
+            slot = slots_ref[block * max_slots + slot_index]
+            peer = slot // blocks
+            start = pl.multiple_of((slot % blocks) * PAIR_BLK, PAIR_BLK)
+            part_pred = pred_ref[peer, :, pl.ds(start, PAIR_BLK)]
+            part_true = true_ref[peer, :, pl.ds(start, PAIR_BLK)]
+            gaps = [cols_ref[d, pl.ds(row, ROW_CHUNK), :] - part_pred[d : d + 1, :] for d in range(3)]
             true_gaps = [
-                cols_ref[3 + d, pl.ds(row, ROW_CHUNK), :] - part[3 + d : 4 + d, :] for d in range(3)
+                cols_ref[3 + d, pl.ds(row, ROW_CHUNK), :] - part_true[d : d + 1, :] for d in range(3)
             ]
             square_pred = gaps[0] * gaps[0] + gaps[1] * gaps[1] + gaps[2] * gaps[2] + 1.0
             square_true = (
@@ -149,25 +161,24 @@
     lax.fori_loop(0, PAIR_BLK // ROW_CHUNK, row_body, 0)
 
 
-def lddt_sums(slots, counts, own_tab, part_tab):
+def lddt_sums(slots, counts, own_tab, pred_parts, true_parts):
     blocks = counts.shape[0]
-    table_rows = part_tab.shape[0]
     out = pl.pallas_call(
         lddt_kernel,
         grid_spec=pltpu.PrefetchScalarGridSpec(
             num_scalar_prefetch=2,
             grid=(blocks,),
             in_specs=[
-                pl.BlockSpec((PAIR_BLK, PAIR_BLK), lambda b, *_: (b, 0)),
-                pl.BlockSpec((table_rows, 8, PAIR_BLK), lambda b, *_: (0, 0, 0)),
+                pl.BlockSpec((PAIR_BLK, own_tab.shape[1]), lambda b, *_: (b, 0)),
+                pl.BlockSpec(pred_parts.shape, lambda b, *_: (0, 0, 0)),
+                pl.BlockSpec(true_parts.shape, lambda b, *_: (0, 0, 0)),
             ],
             out_specs=pl.BlockSpec((PAIR_BLK, PAIR_BLK), lambda b, *_: (b, 0)),
             scratch_shapes=[pltpu.VMEM((6, PAIR_BLK, PAIR_BLK), jnp.float32)],
         ),
         out_shape=jax.ShapeDtypeStruct((blocks * PAIR_BLK, PAIR_BLK), jnp.float32),
-    )(slots, counts, own_tab, part_tab)
+    )(slots, counts, own_tab, pred_parts, true_parts)
     return out[:, :3].T
-
 
 def dense(left, right):
     return jnp.einsum("sac,cf->saf", left, right, preferred_element_type=jnp.float32)
@@ -259,18 +270,12 @@
     true_parts = ring_parts(jnp.concatenate([true_coords, count_row], axis=0), "atoms")
     pred_parts = ring_parts(predicted[0], "atoms")
     pair_total = jnp.sum(true_parts[:, 3, 0])
-    coord_parts = jnp.concatenate(
-        [pred_parts, true_parts[:, :3], jnp.zeros((atom_peers, 2, atom_rows), jnp.float32)], axis=1
-    )
-    part_tab = jnp.moveaxis(
-        coord_parts.reshape(atom_peers, 8, block_count, PAIR_BLK), 2, 1
-    ).reshape(atom_peers * block_count, 8, PAIR_BLK)
-    own_tab = jnp.pad(
-        jnp.concatenate([predicted[0], true_coords], axis=0).T, ((0, 0), (0, PAIR_BLK - 6))
-    )
+    own_tab = jnp.concatenate(
+        [predicted[0], true_coords, jnp.zeros((2, atom_rows), jnp.float32)], axis=0
+    ).T
     source = (atom_rank - pair_blocks // block_count) % atom_peers
     slots = (source * block_count + pair_blocks % block_count).reshape(-1)
-    pair_grad = 2.0 * lddt_sums(slots, pair_count, own_tab, part_tab)[None]
+    pair_grad = 2.0 * lddt_sums(slots, pair_count, own_tab, pred_parts, true_parts)[None]
     lddt_grad = total_atoms * PAIR_BLK / pair_total * pair_grad.reshape(samples, 3, atom_rows)
     coord_grad = mse_part - lddt_grad / PAIR_BLK
     return (coord_grad, lddt_grad)

time: 242 us -> 205 us (0.85)
  local copies, waits for them, and re-layouts: 34.1 us -> 11.8 us
  matrix products: 27.5 us -> 14.8 us
  waiting for transfers between devices: 5.53 us -> 13.6 us
  starting transfers between devices: 52.5 us -> 44.8 us
  Pallas kernels: 104 us -> 107 us
  other arithmetic: 11.3 us -> 8.73 us
    unnamed x32 -> x26, local copies, waits for them, and re-layouts: 12.8 us -> 3.01 us
    ppermute x20 -> x10, starting transfers between devices: 26.9 us -> 18.7 us  [ring_parts(): parts = jnp.concatenate([parts, lax.ppermute(parts, axis, pairs)])]
    ppermute x20 -> x10, waiting for transfers between devices: 3.95 us -> 12.1 us  [ring_parts(): parts = jnp.concatenate([parts, lax.ppermute(parts, axis, pairs)])]
    dot_general x12, matrix products: 19 us -> 11.1 us  [dense(): jnp.einsum('sac,cf->saf', left, right, preferred_element_type=jnp.float32)]
    another operation x11 -> x0, local copies, waits for them, and re-layouts: 7.02 us -> none  [ring_parts(): return jnp.stack(parts)]
    ppermute x7 -> x0, local copies, waits for them, and re-layouts: 5.53 us -> none  [ring_parts(): parts.append(lax.ppermute(value, axis, pairs))]
  transfers between devices with their start and end apart: 28 -> 18, of which waited for: 5 -> 8; matrix products, arithmetic and copies ran while one was open for 10% -> 15% of each run, Pallas kernels for 0% -> 27%
where the time goes in v3:
time: 205 us; the launch traced here: 204 us
  Pallas kernels  107 us (52%)
  starting transfers between devices  44.8 us (22%)
  matrix products  14.8 us (7%)
  waiting for transfers between devices  13.6 us (7%)
  local copies, waits for them, and re-layouts  11.8 us (6%)
  other arithmetic  8.73 us (4%)
  between operations  3.99 us (2%)
    pallas_call x3, Pallas kernels, window_attend(): pl.pallas_call(attend_kernel, grid=(atoms // Q_TILE,), in_specs=[pl.Block...  55.1 us
    pallas_call x1, Pallas kernels, lddt_sums(): pl.pallas_call(lddt_kernel, grid_spec=pltpu.PrefetchScalarGridSpec(num_sc...  51.6 us
    ppermute x4, starting transfers between devices, extended(): after = lax.ppermute(first, axis, down)  20.9 us
    ppermute x10, starting transfers between devices, ring_parts(): parts = jnp.concatenate([parts, lax.ppermute(parts, axis, pairs)])  18.7 us
    ppermute x10, waiting for transfers between devices, ring_parts(): parts = jnp.concatenate([parts, lax.ppermute(parts, axis, pairs)])  12.1 us
    dot_general x12, matrix products, dense(): jnp.einsum('sac,cf->saf', left, right, preferred_element_type=jnp.float32)  11.1 us
    ppermute x4, starting transfers between devices, extended(): before = lax.ppermute(last, axis, up)  5.17 us
  transfers between devices with their start and end apart: 18, of which 8 were waited for; matrix products, arithmetic and copies ran while one was open for 15% of the time, Pallas kernels for 27%

profile of v3, /device:TPU:26, one launch (start us, length us, event | category | flops | bytes accessed | tf_op | source)
XLA Modules:
  0.0 204.5 jit_solution(13204233406364143223)
XLA Ops:
  0.7 1.6 collective-permute-start.2
  3.0 1.3 add_reduce_fusion
  10.2 1.8 fusion.72
  12.8 1.2 copy.19
  15.3 1.8 collective-permute-start.1
  17.1 1.6 collective-permute-start.16
  18.7 1.9 collective-permute-done.3
  20.6 3.1 %collective-permute-done.1 = bf16[2,256,192]{1,2,0:T(8,128)(2,1)S(1)} collective-permute-done((bf16[2,256,192]{1,2,0:T(8,128)(2,1)S(1)}, bf16[2,256,192]{1,2,0:T(8,128)(2,1)S(1)}, u32[]{:S(2)}, u32[]{:S(2)}) %collective-permute-start.1) | collective-permute-done | bytes 196640 | tf_op jit(solution)/shard_map/ppermute | solution.py:43
  24.1 1.3 collective-permute-start.4
  25.4 4.5 %collective-permute-start.5 = (bf16[16,128]{1,0:T(8,128)(2,1)S(1)}, bf16[16,128]{1,0:T(8,128)(2,1)S(1)}, u32[]{:S(2)}, u32[]{:S(2)}) collective-permute-start(bf16[16,128]{1,0:T(8,128)(2,1)S(1)} %get-tuple-element.23), channel_id=1, source_target_pairs={{4,0},{8,4},{12,8},{16,12},{20,16},{24,20},{28,24},{5,1},{9,5},{13... | collective-permute-start | bytes 12296 | tf_op jit(solution)/shard_map/ppermute | solution.py:32
  30.0 1.7 collective-permute-start.17
  33.3 1.3 collective-permute-start.6
  34.6 4.8 %collective-permute-start.7 = (bf16[1,48,256]{2,1,0:T(8,128)(2,1)S(1)}, bf16[1,48,256]{2,1,0:T(8,128)(2,1)S(1)}, u32[]{:S(2)}, u32[]{:S(2)}) collective-permute-start(bf16[1,48,256]{2,1,0:T(8,128)(2,1)S(1)} %get-tuple-element.21), channel_id=1, source_target_pairs={{4,0},{8,4},{12,8},{16,12},{20,16},{24,20},{28,24},{5,1},{9,5},{13... | collective-permute-start | bytes 73736 | tf_op jit(solution)/shard_map/ppermute | solution.py:32
  40.9 1.1 pad.16.kv_ref
  42.0 18.4 %shard_map.167 = bf16[2048,128]{1,0:T(8,128)(2,1)} custom-call(bf16[2048,128]{1,0:T(8,128)(2,1)} %slice_bitcast_fusion.2.q_ref, bf16[2176,256]{1,0:T(8,128)(2,1)} %pad.16.kv_ref, f32[128,256]{1,0:T(8,128)} %fusion.50.band_ref, f32[16,256]{1,0:T(8,128)} %fusion.83.valid_ref), custom_call_target="tpu_custom_call" | custom-call | tf_op jit(solution)/shard_map/pallas_call | solution.py:95
  60.4 1.4 multiply_reduce_fusion.5
  64.3 1.3 collective-permute-start.8
  65.6 5.7 %collective-permute-start.9 = (bf16[1,48,256]{2,1,0:T(8,128)(2,1)S(1)}, bf16[1,48,256]{2,1,0:T(8,128)(2,1)S(1)}, u32[]{:S(2)}, u32[]{:S(2)}) collective-permute-start(bf16[1,48,256]{2,1,0:T(8,128)(2,1)S(1)} %get-tuple-element.19), channel_id=1, source_target_pairs={{4,0},{8,4},{12,8},{16,12},{20,16},{24,20},{28,24},{5,1},{9,5},{13... | collective-permute-start | bytes 73736 | tf_op jit(solution)/shard_map/ppermute | solution.py:32
  74.0 18.4 %shard_map.168 = bf16[2048,128]{1,0:T(8,128)(2,1)} custom-call(bf16[2048,128]{1,0:T(8,128)(2,1)} %slice_bitcast_fusion.1.q_ref, bf16[2176,256]{1,0:T(8,128)(2,1)} %pad.17.kv_ref, f32[128,256]{1,0:T(8,128)} %fusion.50.band_ref, f32[16,256]{1,0:T(8,128)} %fusion.83.valid_ref), custom_call_target="tpu_custom_call" | custom-call | tf_op jit(solution)/shard_map/pallas_call | solution.py:95
  92.3 1.4 multiply_reduce_fusion.3
  96.1 1.3 collective-permute-start.10
  97.4 5.9 %collective-permute-start.11 = (bf16[1,48,256]{2,1,0:T(8,128)(2,1)S(1)}, bf16[1,48,256]{2,1,0:T(8,128)(2,1)S(1)}, u32[]{:S(2)}, u32[]{:S(2)}) collective-permute-start(bf16[1,48,256]{2,1,0:T(8,128)(2,1)S(1)} %get-tuple-element.17), channel_id=1, source_target_pairs={{4,0},{8,4},{12,8},{16,12},{20,16},{24,20},{28,24},{5,1},{9,5},{13... | collective-permute-start | bytes 73736 | tf_op jit(solution)/shard_map/ppermute | solution.py:32
  105.8 18.4 %shard_map.169 = bf16[2048,128]{1,0:T(8,128)(2,1)} custom-call(bf16[2048,128]{1,0:T(8,128)(2,1)} %slice_bitcast_fusion.q_ref, bf16[2176,256]{1,0:T(8,128)(2,1)} %pad.18.kv_ref, f32[128,256]{1,0:T(8,128)} %fusion.50.band_ref, f32[16,256]{1,0:T(8,128)} %fusion.83.valid_ref), custom_call_target="tpu_custom_call" | custom-call | tf_op jit(solution)/shard_map/pallas_call | solution.py:95
  124.1 1.4 multiply_reduce_fusion.1
  128.0 7.9 %collective-permute-start.12 = (f32[1,3,2048]{2,1,0:T(4,128)S(1)}, f32[1,3,2048]{2,1,0:T(4,128)S(1)}, u32[]{:S(2)}, u32[]{:S(2)}) collective-permute-start(f32[1,3,2048]{2,1,0:T(4,128)S(1)} %fusion.7), channel_id=1, source_target_pairs={{0,4},{4,8},{8,12},{12,16},{16,20},{20,24},{24,28},{28,0},{1,5},{5... | collective-permute-start | bytes 73736 | tf_op jit(solution)/shard_map/ppermute | solution.py:43
  136.0 1.5 collective-permute-done.12
  137.5 2.0 collective-permute-start.13
  141.9 1.5 collective-permute-start.14
  143.4 1.3 copy.20.own_ref
  144.7 4.5 %collective-permute-done.14 = f32[4,3,2048]{2,1,0:T(4,128)S(1)} collective-permute-done((f32[4,3,2048]{2,1,0:T(4,128)S(1)}, f32[4,3,2048]{2,1,0:T(4,128)S(1)}, u32[]{:S(2)}, u32[]{:S(2)}) %collective-permute-start.14) | collective-permute-done | bytes 98336 | tf_op jit(solution)/shard_map/ppermute | solution.py:43
  150.0 51.6 %shard_map.170 = f32[2048,128]{1,0:T(8,128)} custom-call(s32[208]{0:T(256)} %reshape.311.slots_ref, s32[16]{0:T(128)} %count_ref.1, f32[2048,8]{1,0:T(8,128)} %copy.20.own_ref, f32[8,3,2048]{2,1,0:T(4,128)} %pad_maximum_fusion.pred_ref, f32[8,4,2048]{2,1,0:T(4,128)} %copy-done.1), custom_call_target="tpu_custom_call" | custom-call | tf_op jit(solution)/shard_map/pallas_call | solution.py:166
  201.5 1.3 slice_multiply_fusion.3
  (99 shorter events, 26.5 us)
Async XLA Ops:
  0.6 9.5 %copy-start = (f32[3,128]{1,0:T(4,128)S(1)}, f32[3,128]{1,0:T(4,128)}, u32[]{:S(2)}) copy-start(f32[3,128]{1,0:T(4,128)} %param.25) | copy-start | bytes 4612
  0.6 14.6 %copy-start.6 = (bf16[256,192]{0,1:T(8,128)(2,1)S(1)}, bf16[256,192]{0,1:T(8,128)(2,1)}, u32[]{:S(2)}) copy-start(bf16[256,192]{0,1:T(8,128)(2,1)} %param.18) | copy-start | bytes 294916
  0.7 14.2 %copy-start.8 = (bf16[192,128]{1,0:T(8,128)(2,1)S(1)}, bf16[192,128]{1,0:T(8,128)(2,1)}, u32[]{:S(2)}) copy-start(bf16[192,128]{1,0:T(8,128)(2,1)} %param.19) | copy-start | bytes 147460
  0.7 14.6 %collective-permute-start = (bf16[1,256,192]{1,2,0:T(8,128)(2,1)}, bf16[1,256,192]{1,2,0:T(8,128)(2,1)S(1)}, u32[]{:S(2)}, u32[]{:S(2)}) collective-permute-start(bf16[1,256,192]{1,2,0:T(8,128)(2,1)} %bitcast.154), channel_id=1, source_target_pairs={{0,1},{1,2},{2,3},{3,0},{4,5},{5,6},{6,7},{7,4},{8,9},{9,10},{10,1... | collective-permute-start | bytes 294920 | tf_op jit(solution)/shard_map/ppermute | solution.py:43
  0.7 14.1 %collective-permute-start.2 = (bf16[1,192,128]{2,1,0:T(8,128)(2,1)}, bf16[1,192,128]{2,1,0:T(8,128)(2,1)S(1)}, u32[]{:S(2)}, u32[]{:S(2)}) collective-permute-start(bf16[1,192,128]{2,1,0:T(8,128)(2,1)} %bitcast.157), channel_id=1, source_target_pairs={{0,1},{1,2},{2,3},{3,0},{4,5},{5,6},{6,7},{7,4},{8,9},{9,10},{10,1... | collective-permute-start | bytes 147464 | tf_op jit(solution)/shard_map/ppermute | solution.py:43
  6.3 10.7 %collective-permute-start.15 = (f32[1,4,2048]{2,1,0:T(4,128)S(1)}, f32[1,4,2048]{2,1,0:T(4,128)S(1)}, u32[]{:S(2)}, u32[]{:S(2)}) collective-permute-start(f32[1,4,2048]{2,1,0:T(4,128)S(1)} %fusion.68), channel_id=1, source_target_pairs={{0,4},{4,8},{8,12},{12,16},{16,20},{20,24},{24,28},{28,0},{1,5},{5... | collective-permute-start | bytes 98312 | tf_op jit(solution)/shard_map/ppermute | solution.py:43
  14.9 5.7 %collective-permute-start.3 = (bf16[2,192,128]{2,1,0:T(8,128)(2,1)S(1)}, bf16[2,192,128]{2,1,0:T(8,128)(2,1)S(1)}, u32[]{:S(2)}, u32[]{:S(2)}) collective-permute-start(bf16[2,192,128]{2,1,0:T(8,128)(2,1)S(1)} %pad_maximum_fusion.5), channel_id=1, source_target_pairs={{0,2},{1,3},{2,0},{3,1},{4,6},{5,7},{6,4},{7,5},{8,10},{9,11},{10,... | collective-permute-start | bytes 294920 | tf_op jit(solution)/shard_map/ppermute | solution.py:43
  15.3 8.4 %collective-permute-start.1 = (bf16[2,256,192]{1,2,0:T(8,128)(2,1)S(1)}, bf16[2,256,192]{1,2,0:T(8,128)(2,1)S(1)}, u32[]{:S(2)}, u32[]{:S(2)}) collective-permute-start(bf16[2,256,192]{1,2,0:T(8,128)(2,1)S(1)} %pad_maximum_fusion.2), channel_id=1, source_target_pairs={{0,2},{1,3},{2,0},{3,1},{4,6},{5,7},{6,4},{7,5},{8,10},{9,11},{10,... | collective-permute-start | bytes 589832 | tf_op jit(solution)/shard_map/ppermute | solution.py:43
  17.1 15.5 %copy-start.4 = (bf16[3,128,384]{2,1,0:T(8,128)(2,1)S(1)}, bf16[3,128,384]{2,1,0:T(8,128)(2,1)}, u32[]{:S(2)}) copy-start(bf16[3,128,384]{2,1,0:T(8,128)(2,1)} %param.26) | copy-start | bytes 884740
  17.1 12.8 %collective-permute-start.16 = (f32[2,4,2048]{2,1,0:T(4,128)S(1)}, f32[2,4,2048]{2,1,0:T(4,128)S(1)}, u32[]{:S(2)}, u32[]{:S(2)}) collective-permute-start(f32[2,4,2048]{2,1,0:T(4,128)S(1)} %pad_maximum_fusion.7), channel_id=1, source_target_pairs={{0,8},{4,12},{8,16},{12,20},{16,24},{20,28},{24,0},{28,4},{1,9},{5... | collective-permute-start | bytes 196616 | tf_op jit(solution)/shard_map/ppermute | solution.py:43
  24.1 7.6 %collective-permute-start.4 = (bf16[16,128]{1,0:T(8,128)(2,1)S(1)}, bf16[16,128]{1,0:T(8,128)(2,1)S(1)}, u32[]{:S(2)}, u32[]{:S(2)}) collective-permute-start(bf16[16,128]{1,0:T(8,128)(2,1)S(1)} %get-tuple-element.22), channel_id=1, source_target_pairs={{0,4},{4,8},{8,12},{12,16},{16,20},{20,24},{24,28},{1,5},{5,9},{9,... | collective-permute-start | bytes 12296 | tf_op jit(solution)/shard_map/ppermute | solution.py:31
  25.4 6.3 %collective-permute-start.5 = (bf16[16,128]{1,0:T(8,128)(2,1)S(1)}, bf16[16,128]{1,0:T(8,128)(2,1)S(1)}, u32[]{:S(2)}, u32[]{:S(2)}) collective-permute-start(bf16[16,128]{1,0:T(8,128)(2,1)S(1)} %get-tuple-element.23), channel_id=1, source_target_pairs={{4,0},{8,4},{12,8},{16,12},{20,16},{24,20},{28,24},{5,1},{9,5},{13... | collective-permute-start | bytes 12296 | tf_op jit(solution)/shard_map/ppermute | solution.py:32
  30.0 105.9 %collective-permute-start.17 = (f32[4,4,2048]{2,1,0:T(4,128)S(1)}, f32[4,4,2048]{2,1,0:T(4,128)S(1)}, u32[]{:S(2)}, u32[]{:S(2)}) collective-permute-start(f32[4,4,2048]{2,1,0:T(4,128)S(1)} %pad_maximum_fusion.4), channel_id=1, source_target_pairs={{0,16},{4,20},{8,24},{12,28},{16,0},{20,4},{24,8},{28,12},{1,17},{... | collective-permute-start | bytes 393224 | tf_op jit(solution)/shard_map/ppermute | solution.py:43
  33.3 7.0 %collective-permute-start.6 = (bf16[1,48,256]{2,1,0:T(8,128)(2,1)S(1)}, bf16[1,48,256]{2,1,0:T(8,128)(2,1)S(1)}, u32[]{:S(2)}, u32[]{:S(2)}) collective-permute-start(bf16[1,48,256]{2,1,0:T(8,128)(2,1)S(1)} %get-tuple-element.20), channel_id=1, source_target_pairs={{0,4},{4,8},{8,12},{12,16},{16,20},{20,24},{24,28},{1,5},{5,9},{9,... | collective-permute-start | bytes 73736 | tf_op jit(solution)/shard_map/ppermute | solution.py:31
  34.6 6.3 %collective-permute-start.7 = (bf16[1,48,256]{2,1,0:T(8,128)(2,1)S(1)}, bf16[1,48,256]{2,1,0:T(8,128)(2,1)S(1)}, u32[]{:S(2)}, u32[]{:S(2)}) collective-permute-start(bf16[1,48,256]{2,1,0:T(8,128)(2,1)S(1)} %get-tuple-element.21), channel_id=1, source_target_pairs={{4,0},{8,4},{12,8},{16,12},{20,16},{24,20},{28,24},{5,1},{9,5},{13... | collective-permute-start | bytes 73736 | tf_op jit(solution)/shard_map/ppermute | solution.py:32
  40.9 19.5 %copy-start.7 = (bf16[3,128,128]{2,1,0:T(8,128)(2,1)S(1)}, bf16[3,128,128]{2,1,0:T(8,128)(2,1)}, u32[]{:S(2)}) copy-start(bf16[3,128,128]{2,1,0:T(8,128)(2,1)} %param.27) | copy-start | bytes 294916
  42.0 19.8 %copy-start.3 = (bf16[3,128,512]{2,1,0:T(8,128)(2,1)S(1)}, bf16[3,128,512]{2,1,0:T(8,128)(2,1)}, u32[]{:S(2)}) copy-start(bf16[3,128,512]{2,1,0:T(8,128)(2,1)} %param.28) | copy-start | bytes 1179652
  61.8 0.9 copy-start.10
  64.3 8.0 %collective-permute-start.8 = (bf16[1,48,256]{2,1,0:T(8,128)(2,1)S(1)}, bf16[1,48,256]{2,1,0:T(8,128)(2,1)S(1)}, u32[]{:S(2)}, u32[]{:S(2)}) collective-permute-start(bf16[1,48,256]{2,1,0:T(8,128)(2,1)S(1)} %get-tuple-element.18), channel_id=1, source_target_pairs={{0,4},{4,8},{8,12},{12,16},{16,20},{20,24},{24,28},{1,5},{5,9},{9,... | collective-permute-start | bytes 73736 | tf_op jit(solution)/shard_map/ppermute | solution.py:31
  65.6 7.2 %collective-permute-start.9 = (bf16[1,48,256]{2,1,0:T(8,128)(2,1)S(1)}, bf16[1,48,256]{2,1,0:T(8,128)(2,1)S(1)}, u32[]{:S(2)}, u32[]{:S(2)}) collective-permute-start(bf16[1,48,256]{2,1,0:T(8,128)(2,1)S(1)} %get-tuple-element.19), channel_id=1, source_target_pairs={{4,0},{8,4},{12,8},{16,12},{20,16},{24,20},{28,24},{5,1},{9,5},{13... | collective-permute-start | bytes 73736 | tf_op jit(solution)/shard_map/ppermute | solution.py:32
  96.1 8.2 %collective-permute-start.10 = (bf16[1,48,256]{2,1,0:T(8,128)(2,1)S(1)}, bf16[1,48,256]{2,1,0:T(8,128)(2,1)S(1)}, u32[]{:S(2)}, u32[]{:S(2)}) collective-permute-start(bf16[1,48,256]{2,1,0:T(8,128)(2,1)S(1)} %get-tuple-element.16), channel_id=1, source_target_pairs={{0,4},{4,8},{8,12},{12,16},{16,20},{20,24},{24,28},{1,5},{5,9},{9,... | collective-permute-start | bytes 73736 | tf_op jit(solution)/shard_map/ppermute | solution.py:31
  97.4 7.2 %collective-permute-start.11 = (bf16[1,48,256]{2,1,0:T(8,128)(2,1)S(1)}, bf16[1,48,256]{2,1,0:T(8,128)(2,1)S(1)}, u32[]{:S(2)}, u32[]{:S(2)}) collective-permute-start(bf16[1,48,256]{2,1,0:T(8,128)(2,1)S(1)} %get-tuple-element.17), channel_id=1, source_target_pairs={{4,0},{8,4},{12,8},{16,12},{20,16},{24,20},{28,24},{5,1},{9,5},{13... | collective-permute-start | bytes 73736 | tf_op jit(solution)/shard_map/ppermute | solution.py:32
  126.4 0.9 copy-start.2
  126.4 0.9 copy-start.5
  126.4 0.9 copy-start.9
  128.0 9.5 %collective-permute-start.12 = (f32[1,3,2048]{2,1,0:T(4,128)S(1)}, f32[1,3,2048]{2,1,0:T(4,128)S(1)}, u32[]{:S(2)}, u32[]{:S(2)}) collective-permute-start(f32[1,3,2048]{2,1,0:T(4,128)S(1)} %fusion.7), channel_id=1, source_target_pairs={{0,4},{4,8},{8,12},{12,16},{16,20},{20,24},{24,28},{28,0},{1,5},{5... | collective-permute-start | bytes 73736 | tf_op jit(solution)/shard_map/ppermute | solution.py:43
  136.0 14.0 %copy-start.1 = (f32[8,4,2048]{2,1,0:T(4,128)}, f32[8,4,2048]{2,1,0:T(4,128)S(1)}, u32[]{:S(2)}) copy-start(f32[8,4,2048]{2,1,0:T(4,128)S(1)} %pad_maximum_fusion.1.true_ref) | copy-start | bytes 786436
  137.5 4.3 %collective-permute-start.13 = (f32[2,3,2048]{2,1,0:T(4,128)S(1)}, f32[2,3,2048]{2,1,0:T(4,128)S(1)}, u32[]{:S(2)}, u32[]{:S(2)}) collective-permute-start(f32[2,3,2048]{2,1,0:T(4,128)S(1)} %pad_maximum_fusion.6), channel_id=1, source_target_pairs={{0,8},{4,12},{8,16},{12,20},{16,24},{20,28},{24,0},{28,4},{1,9},{5... | collective-permute-start | bytes 147464 | tf_op jit(solution)/shard_map/ppermute | solution.py:43
  141.9 7.3 %collective-permute-start.14 = (f32[4,3,2048]{2,1,0:T(4,128)S(1)}, f32[4,3,2048]{2,1,0:T(4,128)S(1)}, u32[]{:S(2)}, u32[]{:S(2)}) collective-permute-start(f32[4,3,2048]{2,1,0:T(4,128)S(1)} %pad_maximum_fusion.3), channel_id=1, source_target_pairs={{0,16},{4,20},{8,24},{12,28},{16,0},{20,4},{24,8},{28,12},{1,17},{... | collective-permute-start | bytes 294920 | tf_op jit(solution)/shard_map/ppermute | solution.py:43

commit v4 on v3

--- a/solution.py
+++ b/solution.py
@@ -74,10 +74,10 @@
         scores = lax.dot_general(
             query_rows[:, cols], keys_vals[:, cols], (((1,), (1,)), ((), ())),
             preferred_element_type=jnp.float32,
-        ) * scale
+        )
         scores = jnp.where(live, scores, -1e30)
         row_max = jnp.max(scores, axis=-1, keepdims=True)
-        exp_scores = jnp.exp(scores - row_max)
+        exp_scores = jnp.exp2((scores - row_max) * (scale * math.log2(math.e)))
         inverse = 1.0 / jnp.sum(exp_scores, axis=-1, keepdims=True)
         weights = (exp_scores * inverse).astype(jnp.bfloat16)
         heads.append(
@@ -105,7 +105,7 @@
         out_shape=jax.ShapeDtypeStruct((atoms, channels), jnp.bfloat16),
     )(queries, padded_kv, band, valid_tab)
 
-ROW_CHUNK = 32
+ROW_CHUNK = 64
 
 
 def lddt_kernel(slots_ref, count_ref, own_ref, pred_ref, true_ref, out_ref, cols_ref):
@@ -148,12 +148,12 @@
             low = dens[0] * dens[1]
             high = dens[2] * dens[3]
             numer = (ys[0] * dens[1] + ys[1] * dens[0]) * high + (ys[2] * dens[3] + ys[3] * dens[2]) * low
-            coef = (-0.25 * numer * gap_dist * (inv_err * inv_pred)) / (low * high)
+            coef = (numer * gap_dist * (inv_err * inv_pred)) / (low * high)
             return tuple(acc + coef * gap for acc, gap in zip(accs, gaps))
 
         zero = jnp.zeros(shape, jnp.float32)
         accs = lax.fori_loop(0, live, slot_body, (zero, zero, zero))
-        sums = [jnp.sum(acc, axis=1, keepdims=True) for acc in accs]
+        sums = [-0.25 * jnp.sum(acc, axis=1, keepdims=True) for acc in accs]
         tile = jnp.where(lane == 0, sums[0], jnp.where(lane == 1, sums[1], jnp.where(lane == 2, sums[2], 0.0)))
         out_ref[pl.ds(row, ROW_CHUNK), :] = tile
         return carry

time: 205 us -> 195 us (0.951)
  Pallas kernels: 107 us -> 97.1 us
    pallas_call x1, Pallas kernels: 51.6 us -> 42.1 us  [lddt_sums(): pl.pallas_call(lddt_kernel, grid_spec=pltpu.PrefetchScalarGridSpec(num_sc...]
  transfers between devices with their start and end apart: 18 -> 18, of which waited for: 8 -> 8; matrix products, arithmetic and copies ran while one was open for 15% -> 16% of each run, Pallas kernels for 27% -> 28%
where the time goes in v4:
time: 195 us
  Pallas kernels  97.1 us (50%)
  starting transfers between devices  44.8 us (23%)
  matrix products  14.8 us (8%)
  waiting for transfers between devices  13.6 us (7%)
  local copies, waits for them, and re-layouts  11.8 us (6%)
  other arithmetic  8.73 us (4%)
  between operations  3.99 us (2%)
    pallas_call x3, Pallas kernels, window_attend(): pl.pallas_call(attend_kernel, grid=(atoms // Q_TILE,), in_specs=[pl.Block...  54.9 us
    pallas_call x1, Pallas kernels, lddt_sums(): pl.pallas_call(lddt_kernel, grid_spec=pltpu.PrefetchScalarGridSpec(num_sc...  42.1 us
    ppermute x4, starting transfers between devices, extended(): after = lax.ppermute(first, axis, down)  20.9 us
    ppermute x10, starting transfers between devices, ring_parts(): parts = jnp.concatenate([parts, lax.ppermute(parts, axis, pairs)])  18.7 us
    ppermute x10, waiting for transfers between devices, ring_parts(): parts = jnp.concatenate([parts, lax.ppermute(parts, axis, pairs)])  12.1 us
    dot_general x12, matrix products, dense(): jnp.einsum('sac,cf->saf', left, right, preferred_element_type=jnp.float32)  11.1 us
    ppermute x4, starting transfers between devices, extended(): before = lax.ppermute(last, axis, up)  5.17 us
  transfers between devices with their start and end apart: 18, of which 8 were waited for; matrix products, arithmetic and copies ran while one was open for 16% of the time, Pallas kernels for 28%

profile of v4, /device:TPU:26, one launch (start us, length us, event | category | flops | bytes accessed | tf_op | source)
XLA Modules:
  0.0 194.9 jit_solution(5330369978337548832)
XLA Ops:
  0.7 1.6 collective-permute-start.2
  3.0 1.3 add_reduce_fusion
  10.2 1.8 fusion.72
  12.8 1.2 copy.19
  15.3 1.8 collective-permute-start.1
  17.1 1.6 collective-permute-start.16
  18.7 1.9 collective-permute-done.3
  20.6 3.1 %collective-permute-done.1 = bf16[2,256,192]{1,2,0:T(8,128)(2,1)S(1)} collective-permute-done((bf16[2,256,192]{1,2,0:T(8,128)(2,1)S(1)}, bf16[2,256,192]{1,2,0:T(8,128)(2,1)S(1)}, u32[]{:S(2)}, u32[]{:S(2)}) %collective-permute-start.1) | collective-permute-done | bytes 196640 | tf_op jit(solution)/shard_map/ppermute | solution.py:43
  24.1 1.3 collective-permute-start.4
  25.4 4.5 %collective-permute-start.5 = (bf16[16,128]{1,0:T(8,128)(2,1)S(1)}, bf16[16,128]{1,0:T(8,128)(2,1)S(1)}, u32[]{:S(2)}, u32[]{:S(2)}) collective-permute-start(bf16[16,128]{1,0:T(8,128)(2,1)S(1)} %get-tuple-element.23), channel_id=1, source_target_pairs={{4,0},{8,4},{12,8},{16,12},{20,16},{24,20},{28,24},{5,1},{9,5},{13... | collective-permute-start | bytes 12296 | tf_op jit(solution)/shard_map/ppermute | solution.py:32
  30.0 1.7 collective-permute-start.17
  33.3 1.3 collective-permute-start.6
  34.6 4.8 %collective-permute-start.7 = (bf16[1,48,256]{2,1,0:T(8,128)(2,1)S(1)}, bf16[1,48,256]{2,1,0:T(8,128)(2,1)S(1)}, u32[]{:S(2)}, u32[]{:S(2)}) collective-permute-start(bf16[1,48,256]{2,1,0:T(8,128)(2,1)S(1)} %get-tuple-element.21), channel_id=1, source_target_pairs={{4,0},{8,4},{12,8},{16,12},{20,16},{24,20},{28,24},{5,1},{9,5},{13... | collective-permute-start | bytes 73736 | tf_op jit(solution)/shard_map/ppermute | solution.py:32
  40.9 1.1 pad.16.kv_ref
  42.0 18.3 %shard_map.167 = bf16[2048,128]{1,0:T(8,128)(2,1)} custom-call(bf16[2048,128]{1,0:T(8,128)(2,1)} %slice_bitcast_fusion.2.q_ref, bf16[2176,256]{1,0:T(8,128)(2,1)} %pad.16.kv_ref, f32[128,256]{1,0:T(8,128)} %fusion.50.band_ref, f32[16,256]{1,0:T(8,128)} %fusion.83.valid_ref), custom_call_target="tpu_custom_call" | custom-call | tf_op jit(solution)/shard_map/pallas_call | solution.py:95
  60.4 1.4 multiply_reduce_fusion.5
  64.3 1.3 collective-permute-start.8
  65.6 5.7 %collective-permute-start.9 = (bf16[1,48,256]{2,1,0:T(8,128)(2,1)S(1)}, bf16[1,48,256]{2,1,0:T(8,128)(2,1)S(1)}, u32[]{:S(2)}, u32[]{:S(2)}) collective-permute-start(bf16[1,48,256]{2,1,0:T(8,128)(2,1)S(1)} %get-tuple-element.19), channel_id=1, source_target_pairs={{4,0},{8,4},{12,8},{16,12},{20,16},{24,20},{28,24},{5,1},{9,5},{13... | collective-permute-start | bytes 73736 | tf_op jit(solution)/shard_map/ppermute | solution.py:32
  73.9 18.3 %shard_map.168 = bf16[2048,128]{1,0:T(8,128)(2,1)} custom-call(bf16[2048,128]{1,0:T(8,128)(2,1)} %slice_bitcast_fusion.1.q_ref, bf16[2176,256]{1,0:T(8,128)(2,1)} %pad.17.kv_ref, f32[128,256]{1,0:T(8,128)} %fusion.50.band_ref, f32[16,256]{1,0:T(8,128)} %fusion.83.valid_ref), custom_call_target="tpu_custom_call" | custom-call | tf_op jit(solution)/shard_map/pallas_call | solution.py:95
  92.2 1.4 multiply_reduce_fusion.3
  96.0 1.3 collective-permute-start.10
  97.3 5.9 %collective-permute-start.11 = (bf16[1,48,256]{2,1,0:T(8,128)(2,1)S(1)}, bf16[1,48,256]{2,1,0:T(8,128)(2,1)S(1)}, u32[]{:S(2)}, u32[]{:S(2)}) collective-permute-start(bf16[1,48,256]{2,1,0:T(8,128)(2,1)S(1)} %get-tuple-element.17), channel_id=1, source_target_pairs={{4,0},{8,4},{12,8},{16,12},{20,16},{24,20},{28,24},{5,1},{9,5},{13... | collective-permute-start | bytes 73736 | tf_op jit(solution)/shard_map/ppermute | solution.py:32
  105.7 18.3 %shard_map.169 = bf16[2048,128]{1,0:T(8,128)(2,1)} custom-call(bf16[2048,128]{1,0:T(8,128)(2,1)} %slice_bitcast_fusion.q_ref, bf16[2176,256]{1,0:T(8,128)(2,1)} %pad.18.kv_ref, f32[128,256]{1,0:T(8,128)} %fusion.50.band_ref, f32[16,256]{1,0:T(8,128)} %fusion.83.valid_ref), custom_call_target="tpu_custom_call" | custom-call | tf_op jit(solution)/shard_map/pallas_call | solution.py:95
  124.0 1.4 multiply_reduce_fusion.1
  127.8 7.9 %collective-permute-start.12 = (f32[1,3,2048]{2,1,0:T(4,128)S(1)}, f32[1,3,2048]{2,1,0:T(4,128)S(1)}, u32[]{:S(2)}, u32[]{:S(2)}) collective-permute-start(f32[1,3,2048]{2,1,0:T(4,128)S(1)} %fusion.7), channel_id=1, source_target_pairs={{0,4},{4,8},{8,12},{12,16},{16,20},{20,24},{24,28},{28,0},{1,5},{5... | collective-permute-start | bytes 73736 | tf_op jit(solution)/shard_map/ppermute | solution.py:43
  135.8 1.5 collective-permute-done.12
  137.4 2.0 %collective-permute-start.13 = (f32[2,3,2048]{2,1,0:T(4,128)S(1)}, f32[2,3,2048]{2,1,0:T(4,128)S(1)}, u32[]{:S(2)}, u32[]{:S(2)}) collective-permute-start(f32[2,3,2048]{2,1,0:T(4,128)S(1)} %pad_maximum_fusion.6), channel_id=1, source_target_pairs={{0,8},{4,12},{8,16},{12,20},{16,24},{20,28},{24,0},{28,4},{1,9},{5... | collective-permute-start | bytes 147464 | tf_op jit(solution)/shard_map/ppermute | solution.py:43
  141.7 1.5 collective-permute-start.14
  143.3 1.3 copy.20.own_ref
  144.6 4.5 %collective-permute-done.14 = f32[4,3,2048]{2,1,0:T(4,128)S(1)} collective-permute-done((f32[4,3,2048]{2,1,0:T(4,128)S(1)}, f32[4,3,2048]{2,1,0:T(4,128)S(1)}, u32[]{:S(2)}, u32[]{:S(2)}) %collective-permute-start.14) | collective-permute-done | bytes 98336 | tf_op jit(solution)/shard_map/ppermute | solution.py:43
  149.8 42.1 %shard_map.170 = f32[2048,128]{1,0:T(8,128)} custom-call(s32[208]{0:T(256)} %reshape.311.slots_ref, s32[16]{0:T(128)} %count_ref.1, f32[2048,8]{1,0:T(8,128)} %copy.20.own_ref, f32[8,3,2048]{2,1,0:T(4,128)} %pad_maximum_fusion.pred_ref, f32[8,4,2048]{2,1,0:T(4,128)} %copy-done.1), custom_call_target="tpu_custom_call" | custom-call | tf_op jit(solution)/shard_map/pallas_call | solution.py:166
  191.9 1.3 slice_multiply_fusion.3
  (99 shorter events, 26.5 us)
Async XLA Ops:
  0.6 9.5 %copy-start = (f32[3,128]{1,0:T(4,128)S(1)}, f32[3,128]{1,0:T(4,128)}, u32[]{:S(2)}) copy-start(f32[3,128]{1,0:T(4,128)} %param.25) | copy-start | bytes 4612
  0.6 14.6 %copy-start.6 = (bf16[256,192]{0,1:T(8,128)(2,1)S(1)}, bf16[256,192]{0,1:T(8,128)(2,1)}, u32[]{:S(2)}) copy-start(bf16[256,192]{0,1:T(8,128)(2,1)} %param.18) | copy-start | bytes 294916
  0.7 14.2 %copy-start.8 = (bf16[192,128]{1,0:T(8,128)(2,1)S(1)}, bf16[192,128]{1,0:T(8,128)(2,1)}, u32[]{:S(2)}) copy-start(bf16[192,128]{1,0:T(8,128)(2,1)} %param.19) | copy-start | bytes 147460
  0.7 14.6 %collective-permute-start = (bf16[1,256,192]{1,2,0:T(8,128)(2,1)}, bf16[1,256,192]{1,2,0:T(8,128)(2,1)S(1)}, u32[]{:S(2)}, u32[]{:S(2)}) collective-permute-start(bf16[1,256,192]{1,2,0:T(8,128)(2,1)} %bitcast.154), channel_id=1, source_target_pairs={{0,1},{1,2},{2,3},{3,0},{4,5},{5,6},{6,7},{7,4},{8,9},{9,10},{10,1... | collective-permute-start | bytes 294920 | tf_op jit(solution)/shard_map/ppermute | solution.py:43
  0.7 14.1 %collective-permute-start.2 = (bf16[1,192,128]{2,1,0:T(8,128)(2,1)}, bf16[1,192,128]{2,1,0:T(8,128)(2,1)S(1)}, u32[]{:S(2)}, u32[]{:S(2)}) collective-permute-start(bf16[1,192,128]{2,1,0:T(8,128)(2,1)} %bitcast.157), channel_id=1, source_target_pairs={{0,1},{1,2},{2,3},{3,0},{4,5},{5,6},{6,7},{7,4},{8,9},{9,10},{10,1... | collective-permute-start | bytes 147464 | tf_op jit(solution)/shard_map/ppermute | solution.py:43
  6.3 10.7 %collective-permute-start.15 = (f32[1,4,2048]{2,1,0:T(4,128)S(1)}, f32[1,4,2048]{2,1,0:T(4,128)S(1)}, u32[]{:S(2)}, u32[]{:S(2)}) collective-permute-start(f32[1,4,2048]{2,1,0:T(4,128)S(1)} %fusion.68), channel_id=1, source_target_pairs={{0,4},{4,8},{8,12},{12,16},{16,20},{20,24},{24,28},{28,0},{1,5},{5... | collective-permute-start | bytes 98312 | tf_op jit(solution)/shard_map/ppermute | solution.py:43
  14.9 5.7 %collective-permute-start.3 = (bf16[2,192,128]{2,1,0:T(8,128)(2,1)S(1)}, bf16[2,192,128]{2,1,0:T(8,128)(2,1)S(1)}, u32[]{:S(2)}, u32[]{:S(2)}) collective-permute-start(bf16[2,192,128]{2,1,0:T(8,128)(2,1)S(1)} %pad_maximum_fusion.5), channel_id=1, source_target_pairs={{0,2},{1,3},{2,0},{3,1},{4,6},{5,7},{6,4},{7,5},{8,10},{9,11},{10,... | collective-permute-start | bytes 294920 | tf_op jit(solution)/shard_map/ppermute | solution.py:43
  15.3 8.4 %collective-permute-start.1 = (bf16[2,256,192]{1,2,0:T(8,128)(2,1)S(1)}, bf16[2,256,192]{1,2,0:T(8,128)(2,1)S(1)}, u32[]{:S(2)}, u32[]{:S(2)}) collective-permute-start(bf16[2,256,192]{1,2,0:T(8,128)(2,1)S(1)} %pad_maximum_fusion.2), channel_id=1, source_target_pairs={{0,2},{1,3},{2,0},{3,1},{4,6},{5,7},{6,4},{7,5},{8,10},{9,11},{10,... | collective-permute-start | bytes 589832 | tf_op jit(solution)/shard_map/ppermute | solution.py:43
  17.1 15.5 %copy-start.4 = (bf16[3,128,384]{2,1,0:T(8,128)(2,1)S(1)}, bf16[3,128,384]{2,1,0:T(8,128)(2,1)}, u32[]{:S(2)}) copy-start(bf16[3,128,384]{2,1,0:T(8,128)(2,1)} %param.26) | copy-start | bytes 884740
  17.1 12.8 %collective-permute-start.16 = (f32[2,4,2048]{2,1,0:T(4,128)S(1)}, f32[2,4,2048]{2,1,0:T(4,128)S(1)}, u32[]{:S(2)}, u32[]{:S(2)}) collective-permute-start(f32[2,4,2048]{2,1,0:T(4,128)S(1)} %pad_maximum_fusion.7), channel_id=1, source_target_pairs={{0,8},{4,12},{8,16},{12,20},{16,24},{20,28},{24,0},{28,4},{1,9},{5... | collective-permute-start | bytes 196616 | tf_op jit(solution)/shard_map/ppermute | solution.py:43
  24.1 7.6 %collective-permute-start.4 = (bf16[16,128]{1,0:T(8,128)(2,1)S(1)}, bf16[16,128]{1,0:T(8,128)(2,1)S(1)}, u32[]{:S(2)}, u32[]{:S(2)}) collective-permute-start(bf16[16,128]{1,0:T(8,128)(2,1)S(1)} %get-tuple-element.22), channel_id=1, source_target_pairs={{0,4},{4,8},{8,12},{12,16},{16,20},{20,24},{24,28},{1,5},{5,9},{9,... | collective-permute-start | bytes 12296 | tf_op jit(solution)/shard_map/ppermute | solution.py:31
  25.4 6.3 %collective-permute-start.5 = (bf16[16,128]{1,0:T(8,128)(2,1)S(1)}, bf16[16,128]{1,0:T(8,128)(2,1)S(1)}, u32[]{:S(2)}, u32[]{:S(2)}) collective-permute-start(bf16[16,128]{1,0:T(8,128)(2,1)S(1)} %get-tuple-element.23), channel_id=1, source_target_pairs={{4,0},{8,4},{12,8},{16,12},{20,16},{24,20},{28,24},{5,1},{9,5},{13... | collective-permute-start | bytes 12296 | tf_op jit(solution)/shard_map/ppermute | solution.py:32
  30.0 105.8 %collective-permute-start.17 = (f32[4,4,2048]{2,1,0:T(4,128)S(1)}, f32[4,4,2048]{2,1,0:T(4,128)S(1)}, u32[]{:S(2)}, u32[]{:S(2)}) collective-permute-start(f32[4,4,2048]{2,1,0:T(4,128)S(1)} %pad_maximum_fusion.4), channel_id=1, source_target_pairs={{0,16},{4,20},{8,24},{12,28},{16,0},{20,4},{24,8},{28,12},{1,17},{... | collective-permute-start | bytes 393224 | tf_op jit(solution)/shard_map/ppermute | solution.py:43
  33.3 7.0 %collective-permute-start.6 = (bf16[1,48,256]{2,1,0:T(8,128)(2,1)S(1)}, bf16[1,48,256]{2,1,0:T(8,128)(2,1)S(1)}, u32[]{:S(2)}, u32[]{:S(2)}) collective-permute-start(bf16[1,48,256]{2,1,0:T(8,128)(2,1)S(1)} %get-tuple-element.20), channel_id=1, source_target_pairs={{0,4},{4,8},{8,12},{12,16},{16,20},{20,24},{24,28},{1,5},{5,9},{9,... | collective-permute-start | bytes 73736 | tf_op jit(solution)/shard_map/ppermute | solution.py:31
  34.6 6.3 %collective-permute-start.7 = (bf16[1,48,256]{2,1,0:T(8,128)(2,1)S(1)}, bf16[1,48,256]{2,1,0:T(8,128)(2,1)S(1)}, u32[]{:S(2)}, u32[]{:S(2)}) collective-permute-start(bf16[1,48,256]{2,1,0:T(8,128)(2,1)S(1)} %get-tuple-element.21), channel_id=1, source_target_pairs={{4,0},{8,4},{12,8},{16,12},{20,16},{24,20},{28,24},{5,1},{9,5},{13... | collective-permute-start | bytes 73736 | tf_op jit(solution)/shard_map/ppermute | solution.py:32
  40.9 19.4 %copy-start.7 = (bf16[3,128,128]{2,1,0:T(8,128)(2,1)S(1)}, bf16[3,128,128]{2,1,0:T(8,128)(2,1)}, u32[]{:S(2)}) copy-start(bf16[3,128,128]{2,1,0:T(8,128)(2,1)} %param.27) | copy-start | bytes 294916
  42.0 19.8 %copy-start.3 = (bf16[3,128,512]{2,1,0:T(8,128)(2,1)S(1)}, bf16[3,128,512]{2,1,0:T(8,128)(2,1)}, u32[]{:S(2)}) copy-start(bf16[3,128,512]{2,1,0:T(8,128)(2,1)} %param.28) | copy-start | bytes 1179652
  61.8 0.9 copy-start.10
  64.3 8.0 %collective-permute-start.8 = (bf16[1,48,256]{2,1,0:T(8,128)(2,1)S(1)}, bf16[1,48,256]{2,1,0:T(8,128)(2,1)S(1)}, u32[]{:S(2)}, u32[]{:S(2)}) collective-permute-start(bf16[1,48,256]{2,1,0:T(8,128)(2,1)S(1)} %get-tuple-element.18), channel_id=1, source_target_pairs={{0,4},{4,8},{8,12},{12,16},{16,20},{20,24},{24,28},{1,5},{5,9},{9,... | collective-permute-start | bytes 73736 | tf_op jit(solution)/shard_map/ppermute | solution.py:31
  65.6 7.2 %collective-permute-start.9 = (bf16[1,48,256]{2,1,0:T(8,128)(2,1)S(1)}, bf16[1,48,256]{2,1,0:T(8,128)(2,1)S(1)}, u32[]{:S(2)}, u32[]{:S(2)}) collective-permute-start(bf16[1,48,256]{2,1,0:T(8,128)(2,1)S(1)} %get-tuple-element.19), channel_id=1, source_target_pairs={{4,0},{8,4},{12,8},{16,12},{20,16},{24,20},{28,24},{5,1},{9,5},{13... | collective-permute-start | bytes 73736 | tf_op jit(solution)/shard_map/ppermute | solution.py:32
  96.0 8.2 %collective-permute-start.10 = (bf16[1,48,256]{2,1,0:T(8,128)(2,1)S(1)}, bf16[1,48,256]{2,1,0:T(8,128)(2,1)S(1)}, u32[]{:S(2)}, u32[]{:S(2)}) collective-permute-start(bf16[1,48,256]{2,1,0:T(8,128)(2,1)S(1)} %get-tuple-element.16), channel_id=1, source_target_pairs={{0,4},{4,8},{8,12},{12,16},{16,20},{20,24},{24,28},{1,5},{5,9},{9,... | collective-permute-start | bytes 73736 | tf_op jit(solution)/shard_map/ppermute | solution.py:31
  97.3 7.2 %collective-permute-start.11 = (bf16[1,48,256]{2,1,0:T(8,128)(2,1)S(1)}, bf16[1,48,256]{2,1,0:T(8,128)(2,1)S(1)}, u32[]{:S(2)}, u32[]{:S(2)}) collective-permute-start(bf16[1,48,256]{2,1,0:T(8,128)(2,1)S(1)} %get-tuple-element.17), channel_id=1, source_target_pairs={{4,0},{8,4},{12,8},{16,12},{20,16},{24,20},{28,24},{5,1},{9,5},{13... | collective-permute-start | bytes 73736 | tf_op jit(solution)/shard_map/ppermute | solution.py:32
  126.2 0.9 copy-start.2
  126.2 0.9 copy-start.5
  126.2 0.9 copy-start.9
  127.8 9.5 %collective-permute-start.12 = (f32[1,3,2048]{2,1,0:T(4,128)S(1)}, f32[1,3,2048]{2,1,0:T(4,128)S(1)}, u32[]{:S(2)}, u32[]{:S(2)}) collective-permute-start(f32[1,3,2048]{2,1,0:T(4,128)S(1)} %fusion.7), channel_id=1, source_target_pairs={{0,4},{4,8},{8,12},{12,16},{16,20},{20,24},{24,28},{28,0},{1,5},{5... | collective-permute-start | bytes 73736 | tf_op jit(solution)/shard_map/ppermute | solution.py:43
  135.8 14.0 %copy-start.1 = (f32[8,4,2048]{2,1,0:T(4,128)}, f32[8,4,2048]{2,1,0:T(4,128)S(1)}, u32[]{:S(2)}) copy-start(f32[8,4,2048]{2,1,0:T(4,128)S(1)} %pad_maximum_fusion.1.true_ref) | copy-start | bytes 786436
  137.4 4.3 %collective-permute-start.13 = (f32[2,3,2048]{2,1,0:T(4,128)S(1)}, f32[2,3,2048]{2,1,0:T(4,128)S(1)}, u32[]{:S(2)}, u32[]{:S(2)}) collective-permute-start(f32[2,3,2048]{2,1,0:T(4,128)S(1)} %pad_maximum_fusion.6), channel_id=1, source_target_pairs={{0,8},{4,12},{8,16},{12,20},{16,24},{20,28},{24,0},{28,4},{1,9},{5... | collective-permute-start | bytes 147464 | tf_op jit(solution)/shard_map/ppermute | solution.py:43
  141.7 7.3 %collective-permute-start.14 = (f32[4,3,2048]{2,1,0:T(4,128)S(1)}, f32[4,3,2048]{2,1,0:T(4,128)S(1)}, u32[]{:S(2)}, u32[]{:S(2)}) collective-permute-start(f32[4,3,2048]{2,1,0:T(4,128)S(1)} %pad_maximum_fusion.3), channel_id=1, source_target_pairs={{0,16},{4,20},{8,24},{12,28},{16,0},{20,4},{24,8},{28,12},{1,17},{... | collective-permute-start | bytes 294920 | tf_op jit(solution)/shard_map/ppermute | solution.py:43

commit v5 on v4

--- a/solution.py
+++ b/solution.py
@@ -230,30 +230,44 @@
         "sda,dc->sac", scaled, coord_in, precision=lax.Precision.HIGHEST
     )
     key_halo = (KWIN - QBLK) // 2
-    tile_start = atom_rank * atom_rows - key_halo + Q_TILE * jnp.arange(
-        atom_rows // Q_TILE, dtype=jnp.int32
-    )
-    position = tile_start[:, None] + jnp.arange(K_SPAN, dtype=jnp.int32)[None, :]
-    valid_tab = ((position >= 0) & (position < total_atoms)).astype(jnp.float32)
+    reaches = [0]
+    for _ in range(LAYERS - 1):
+        reaches.insert(0, -(-(reaches[0] + key_halo) // QBLK) * QBLK)
+    buffer_start = -(reaches[0] + key_halo)
+    hidden = extended(hidden, (("atoms", 1),), -buffer_start)
     query_win = jnp.arange(Q_TILE, dtype=jnp.int32)[:, None] // QBLK * QBLK
     key_index = jnp.arange(K_SPAN, dtype=jnp.int32)[None, :]
     band = ((key_index >= query_win) & (key_index < query_win + KWIN)).astype(jnp.float32)
     channels = hidden.shape[2]
     for layer_index in range(LAYERS):
+        reach = reaches[layer_index]
+        kv_off = -(reach + key_halo) - buffer_start
+        q_off = kv_off + key_halo
+        tiles = -(-(atom_rows + 2 * reach) // Q_TILE)
+        tile_start = atom_rank * atom_rows - reach - key_halo + Q_TILE * jnp.arange(
+            tiles, dtype=jnp.int32
+        )
+        position = tile_start[:, None] + key_index
+        valid_tab = ((position >= 0) & (position < total_atoms)).astype(jnp.float32)
         normed = (rms_norm(hidden) * gains[layer_index, 0]).astype(jnp.bfloat16)
         qkv_all = dense(normed, w_qkv[layer_index]).astype(jnp.bfloat16)
-        queries = qkv_all[:, :, :channels]
-        padded = extended(qkv_all[:, :, channels:], (("atoms", 1),), key_halo)
+        span_rows = kv_off + tiles * Q_TILE + K_SPAN - Q_TILE
+        qkv_all = jnp.pad(qkv_all, ((0, 0), (0, max(0, span_rows - qkv_all.shape[1])), (0, 0)))
+        queries = qkv_all[:, q_off : q_off + tiles * Q_TILE, :channels]
+        key_vals = qkv_all[:, kv_off:span_rows, channels:]
         attended = jnp.stack(
-            [window_attend(queries[s], padded[s], band, valid_tab) for s in range(samples)]
-        )
-        hidden = hidden + dense(attended, w_o[layer_index])
+            [window_attend(queries[s], key_vals[s], band, valid_tab) for s in range(samples)]
+        )
+        hidden = jnp.pad(hidden, ((0, 0), (0, max(0, span_rows - hidden.shape[1])), (0, 0)))
+        hidden = hidden[:, q_off : q_off + tiles * Q_TILE] + dense(attended, w_o[layer_index])
+        buffer_start = -reach
         normed = (rms_norm(hidden) * gains[layer_index, 1]).astype(jnp.bfloat16)
         gate_up = dense(normed, w_gu[layer_index])
         inner_act = (jax.nn.silu(gate_up[..., :FF_ATOM]) * gate_up[..., FF_ATOM:]).astype(
             jnp.bfloat16
         )
         hidden = hidden + dense(inner_act, w_down[layer_index])
+    hidden = hidden[:, -buffer_start : -buffer_start + atom_rows]
     update = jnp.einsum("sac,cd->sda", rms_norm(hidden), w_out, precision=lax.Precision.HIGHEST)
     predicted = (
         sigma_data * sigma_data / noise_total * noisy

time: 195 us -> 181 us (0.928)
  starting transfers between devices: 44.8 us -> 30.1 us
  local copies, waits for them, and re-layouts: 11.8 us -> 9.74 us
    ppermute x4 -> x2, starting transfers between devices: 20.9 us -> 9.64 us  [extended(): after = lax.ppermute(first, axis, down)]
    squeeze x0 -> x3, local copies, waits for them, and re-layouts: none -> 3.29 us  [on_device(): key_vals[s]]
    pad x3 -> x0, local copies, waits for them, and re-layouts: 3.21 us -> none  [window_attend(): padded_kv = jnp.pad(padded_kv, ((0, extra), (0, 0)))]
    pallas_call x3, Pallas kernels: 54.9 us -> 58 us  [window_attend(): pl.pallas_call(attend_kernel, grid=(atoms // Q_TILE,), in_specs=[pl.Block...]
    ppermute x4 -> x2, starting transfers between devices: 5.17 us -> 2.58 us  [extended(): before = lax.ppermute(last, axis, up)]
  transfers between devices with their start and end apart: 18 -> 14, of which waited for: 8 -> 5; matrix products, arithmetic and copies ran while one was open for 16% -> 18% of each run, Pallas kernels for 28% -> 32%
where the time goes in v5:
time: 181 us; the launch traced here: 180 us
  Pallas kernels  98.3 us (54%)
  starting transfers between devices  30.1 us (17%)
  matrix products  16.7 us (9%)
  waiting for transfers between devices  12 us (7%)
  local copies, waits for them, and re-layouts  9.74 us (5%)
  other arithmetic  9.63 us (5%)
  between operations  3.91 us (2%)
    pallas_call x3, Pallas kernels, window_attend(): pl.pallas_call(attend_kernel, grid=(atoms // Q_TILE,), in_specs=[pl.Block...  58 us
    pallas_call x1, Pallas kernels, lddt_sums(): pl.pallas_call(lddt_kernel, grid_spec=pltpu.PrefetchScalarGridSpec(num_sc...  40.3 us
    ppermute x10, starting transfers between devices, ring_parts(): parts = jnp.concatenate([parts, lax.ppermute(parts, axis, pairs)])  17.9 us
    ppermute x10, waiting for transfers between devices, ring_parts(): parts = jnp.concatenate([parts, lax.ppermute(parts, axis, pairs)])  12 us
    dot_general x12, matrix products, dense(): jnp.einsum('sac,cf->saf', left, right, preferred_element_type=jnp.float32)  11.8 us
    ppermute x2, starting transfers between devices, extended(): after = lax.ppermute(first, axis, down)  9.64 us
  transfers between devices with their start and end apart: 14, of which 5 were waited for; matrix products, arithmetic and copies ran while one was open for 18% of the time, Pallas kernels for 32%

profile of v5, /device:TPU:26, one launch (start us, length us, event | category | flops | bytes accessed | tf_op | source)
XLA Modules:
  0.0 180.3 jit_solution(12446788792845131723)
XLA Ops:
  0.8 1.6 collective-permute-start.2
  3.0 1.3 add_reduce_fusion
  10.8 2.6 %fusion.96 = f32[2048,128]{1,0:T(8,128)S(1)} fusion(f32[3,128]{1,0:T(4,128)S(1)} %copy-done, f32[]{:T(128)} %bitcast.8, f32[3,2048]{1,0:T(4,128)} %param.22, f32[1,3,2048]{2,0,1:T(1,128)} %param.23, f32[]{:T(128)} %bitcast.198), kind=kOutput, calls=%fused_computation.140 | convolution fusion | flops 9455616 | bytes 1099272 | tf_op jit(solution)/shard_map/sda,dc->sac/dot_general | solution.py:229
  13.9 1.8 collective-permute-start.1
  16.6 2.6 %collective-permute-done.3 = bf16[2,192,128]{2,1,0:T(8,128)(2,1)S(1)} collective-permute-done((bf16[2,192,128]{2,1,0:T(8,128)(2,1)S(1)}, bf16[2,192,128]{2,1,0:T(8,128)(2,1)S(1)}, u32[]{:S(2)}, u32[]{:S(2)}) %collective-permute-start.3) | collective-permute-done | bytes 98336 | tf_op jit(solution)/shard_map/ppermute | solution.py:43
  19.3 3.1 %collective-permute-done.1 = bf16[2,256,192]{1,2,0:T(8,128)(2,1)S(1)} collective-permute-done((bf16[2,256,192]{1,2,0:T(8,128)(2,1)S(1)}, bf16[2,256,192]{1,2,0:T(8,128)(2,1)S(1)}, u32[]{:S(2)}, u32[]{:S(2)}) %collective-permute-start.1) | collective-permute-done | bytes 196640 | tf_op jit(solution)/shard_map/ppermute | solution.py:43
  22.7 1.3 collective-permute-start.4
  24.0 4.5 %collective-permute-start.5 = (bf16[16,128]{1,0:T(8,128)(2,1)S(1)}, bf16[16,128]{1,0:T(8,128)(2,1)S(1)}, u32[]{:S(2)}, u32[]{:S(2)}) collective-permute-start(bf16[16,128]{1,0:T(8,128)(2,1)S(1)} %get-tuple-element.21), channel_id=1, source_target_pairs={{4,0},{8,4},{12,8},{16,12},{20,16},{24,20},{28,24},{5,1},{9,5},{13... | collective-permute-start | bytes 12296 | tf_op jit(solution)/shard_map/ppermute | solution.py:32
  28.6 1.5 collective-permute-start.12
  31.0 1.3 collective-permute-start.6
  32.3 5.1 %collective-permute-start.7 = (f32[1,176,128]{2,1,0:T(8,128)S(1)}, f32[1,176,128]{2,1,0:T(8,128)S(1)}, u32[]{:S(2)}, u32[]{:S(2)}) collective-permute-start(f32[1,176,128]{2,1,0:T(8,128)S(1)} %get-tuple-element.19), channel_id=1, source_target_pairs={{4,0},{8,4},{12,8},{16,12},{20,16},{24,20},{28,24},{5,1},{9,5},{13... | collective-permute-start | bytes 270344 | tf_op jit(solution)/shard_map/ppermute | solution.py:32
  37.4 3.7 %collective-permute-start.13 = (f32[4,4,2048]{2,1,0:T(4,128)S(1)}, f32[4,4,2048]{2,1,0:T(4,128)S(1)}, u32[]{:S(2)}, u32[]{:S(2)}) collective-permute-start(f32[4,4,2048]{2,1,0:T(4,128)S(1)} %pad_maximum_fusion.5), channel_id=1, source_target_pairs={{0,16},{4,20},{8,24},{12,28},{16,0},{20,4},{24,8},{28,12},{1,17},{... | collective-permute-start | bytes 393224 | tf_op jit(solution)/shard_map/ppermute | solution.py:43
  42.3 1.1 fusion.17.kv_ref
  43.4 0.9 slice_bitcast_fusion.q_ref
  44.3 20.4 %shard_map.167 = bf16[2304,128]{1,0:T(8,128)(2,1)} custom-call(bf16[2304,128]{1,0:T(8,128)(2,1)} %slice_bitcast_fusion.q_ref, bf16[2432,256]{1,0:T(8,128)(2,1)} %fusion.17.kv_ref, f32[128,256]{1,0:T(8,128)} %fusion.72.band_ref, f32[18,256]{1,0:T(8,128)} %fusion.108.valid_ref), custom_call_target="tpu_custom_call" | custom-call | tf_op jit(solution)/shard_map/pallas_call | solution.py:95
  64.7 1.7 multiply_reduce_fusion.2
  67.3 0.9 multiply_reduce_fusion.1
  69.0 1.1 fusion.20.kv_ref
  70.9 19.3 %shard_map.168 = bf16[2176,128]{1,0:T(8,128)(2,1)} custom-call(bf16[2176,128]{1,0:T(8,128)(2,1)} %slice_bitcast_fusion.1.q_ref, bf16[2304,256]{1,0:T(8,128)(2,1)} %fusion.20.kv_ref, f32[128,256]{1,0:T(8,128)} %fusion.72.band_ref, f32[17,256]{1,0:T(8,128)} %fusion.110.valid_ref), custom_call_target="tpu_custom_call" | custom-call | tf_op jit(solution)/shard_map/pallas_call | solution.py:95
  90.3 1.6 multiply_reduce_fusion.4
  94.2 1.1 fusion.24.kv_ref
  96.1 18.3 %shard_map.169 = bf16[2048,128]{1,0:T(8,128)(2,1)} custom-call(bf16[2048,128]{1,0:T(8,128)(2,1)} %slice_bitcast_fusion.2.q_ref, bf16[2176,256]{1,0:T(8,128)(2,1)} %fusion.24.kv_ref, f32[128,256]{1,0:T(8,128)} %fusion.72.band_ref, f32[16,256]{1,0:T(8,128)} %fusion.115.valid_ref), custom_call_target="tpu_custom_call" | custom-call | tf_op jit(solution)/shard_map/pallas_call | solution.py:95
  114.4 1.5 multiply_reduce_fusion.6
  117.6 1.2 fusion.14
  118.8 4.0 %collective-permute-start.8 = (f32[1,3,2048]{2,1,0:T(4,128)S(1)}, f32[1,3,2048]{2,1,0:T(4,128)S(1)}, u32[]{:S(2)}, u32[]{:S(2)}) collective-permute-start(f32[1,3,2048]{2,1,0:T(4,128)S(1)} %fusion.14), channel_id=1, source_target_pairs={{0,4},{4,8},{8,12},{12,16},{16,20},{20,24},{24,28},{28,0},{1,5},{5... | collective-permute-start | bytes 73736 | tf_op jit(solution)/shard_map/ppermute | solution.py:43
  122.8 1.5 collective-permute-done.8
  124.4 2.8 %collective-permute-start.9 = (f32[2,3,2048]{2,1,0:T(4,128)S(1)}, f32[2,3,2048]{2,1,0:T(4,128)S(1)}, u32[]{:S(2)}, u32[]{:S(2)}) collective-permute-start(f32[2,3,2048]{2,1,0:T(4,128)S(1)} %pad_maximum_fusion.7), channel_id=1, source_target_pairs={{0,8},{4,12},{8,16},{12,20},{16,24},{20,28},{24,0},{28,4},{1,9},{5... | collective-permute-start | bytes 147464 | tf_op jit(solution)/shard_map/ppermute | solution.py:43
  129.1 1.9 %collective-permute-start.10 = (f32[4,3,2048]{2,1,0:T(4,128)S(1)}, f32[4,3,2048]{2,1,0:T(4,128)S(1)}, u32[]{:S(2)}, u32[]{:S(2)}) collective-permute-start(f32[4,3,2048]{2,1,0:T(4,128)S(1)} %pad_maximum_fusion.4), channel_id=1, source_target_pairs={{0,16},{4,20},{8,24},{12,28},{16,0},{20,4},{24,8},{28,12},{1,17},{... | collective-permute-start | bytes 294920 | tf_op jit(solution)/shard_map/ppermute | solution.py:43
  131.0 1.3 copy.25.own_ref
  132.3 4.1 %collective-permute-done.10 = f32[4,3,2048]{2,1,0:T(4,128)S(1)} collective-permute-done((f32[4,3,2048]{2,1,0:T(4,128)S(1)}, f32[4,3,2048]{2,1,0:T(4,128)S(1)}, u32[]{:S(2)}, u32[]{:S(2)}) %collective-permute-start.10) | collective-permute-done | bytes 98336 | tf_op jit(solution)/shard_map/ppermute | solution.py:43
  137.2 40.3 %shard_map.170 = f32[2048,128]{1,0:T(8,128)} custom-call(s32[208]{0:T(256)} %reshape.383.slots_ref, s32[16]{0:T(128)} %count_ref.1, f32[2048,8]{1,0:T(8,128)} %copy.25.own_ref, f32[8,3,2048]{2,1,0:T(4,128)} %pad_maximum_fusion.1.pred_ref, f32[8,4,2048]{2,1,0:T(4,128)} %copy-done.1), custom_call_target="tpu_custom_call" | custom-call | tf_op jit(solution)/shard_map/pallas_call | solution.py:166
  177.4 1.3 slice_multiply_fusion.3
  (93 shorter events, 19.9 us)
Async XLA Ops:
  0.6 10.2 %copy-start = (f32[3,128]{1,0:T(4,128)S(1)}, f32[3,128]{1,0:T(4,128)}, u32[]{:S(2)}) copy-start(f32[3,128]{1,0:T(4,128)} %param.25) | copy-start | bytes 4612
  0.6 13.3 %copy-start.8 = (bf16[256,192]{0,1:T(8,128)(2,1)S(1)}, bf16[256,192]{0,1:T(8,128)(2,1)}, u32[]{:S(2)}) copy-start(bf16[256,192]{0,1:T(8,128)(2,1)} %param.18) | copy-start | bytes 294916
  0.7 12.8 %copy-start.9 = (bf16[192,128]{1,0:T(8,128)(2,1)S(1)}, bf16[192,128]{1,0:T(8,128)(2,1)}, u32[]{:S(2)}) copy-start(bf16[192,128]{1,0:T(8,128)(2,1)} %param.19) | copy-start | bytes 147460
  0.7 12.8 %copy-start.10 = (s32[2048]{0:T(1024)S(1)}, s32[2048]{0:T(1024)}, u32[]{:S(2)}) copy-start(s32[2048]{0:T(1024)} %param.21) | copy-start | bytes 24580
  0.7 15.0 %copy-start.11 = (f32[3,2,128]{2,1,0:T(2,128)S(1)}, f32[3,2,128]{2,1,0:T(2,128)}, u32[]{:S(2)}) copy-start(f32[3,2,128]{2,1,0:T(2,128)} %param.30) | copy-start | bytes 9220
  0.7 13.2 %collective-permute-start = (bf16[1,256,192]{1,2,0:T(8,128)(2,1)}, bf16[1,256,192]{1,2,0:T(8,128)(2,1)S(1)}, u32[]{:S(2)}, u32[]{:S(2)}) collective-permute-start(bf16[1,256,192]{1,2,0:T(8,128)(2,1)} %bitcast.205), channel_id=1, source_target_pairs={{0,1},{1,2},{2,3},{3,0},{4,5},{5,6},{6,7},{7,4},{8,9},{9,10},{10,1... | collective-permute-start | bytes 294920 | tf_op jit(solution)/shard_map/ppermute | solution.py:43
  0.8 12.7 %collective-permute-start.2 = (bf16[1,192,128]{2,1,0:T(8,128)(2,1)}, bf16[1,192,128]{2,1,0:T(8,128)(2,1)S(1)}, u32[]{:S(2)}, u32[]{:S(2)}) collective-permute-start(bf16[1,192,128]{2,1,0:T(8,128)(2,1)} %bitcast.208), channel_id=1, source_target_pairs={{0,1},{1,2},{2,3},{3,0},{4,5},{5,6},{6,7},{7,4},{8,9},{9,10},{10,1... | collective-permute-start | bytes 147464 | tf_op jit(solution)/shard_map/ppermute | solution.py:43
  6.3 22.2 %collective-permute-start.11 = (f32[1,4,2048]{2,1,0:T(4,128)S(1)}, f32[1,4,2048]{2,1,0:T(4,128)S(1)}, u32[]{:S(2)}, u32[]{:S(2)}) collective-permute-start(f32[1,4,2048]{2,1,0:T(4,128)S(1)} %fusion.90), channel_id=1, source_target_pairs={{0,4},{4,8},{8,12},{12,16},{16,20},{20,24},{24,28},{28,0},{1,5},{5... | collective-permute-start | bytes 98312 | tf_op jit(solution)/shard_map/ppermute | solution.py:43
  13.5 16.7 %copy-start.3 = (bf16[2048,128]{1,0:T(8,128)(2,1)S(1)}, bf16[2048,128]{1,0:T(8,128)(2,1)}, u32[]{:S(2)}) copy-start(bf16[2048,128]{1,0:T(8,128)(2,1)} %param.20) | copy-start | bytes 1572868
  13.5 5.7 %collective-permute-start.3 = (bf16[2,192,128]{2,1,0:T(8,128)(2,1)S(1)}, bf16[2,192,128]{2,1,0:T(8,128)(2,1)S(1)}, u32[]{:S(2)}, u32[]{:S(2)}) collective-permute-start(bf16[2,192,128]{2,1,0:T(8,128)(2,1)S(1)} %pad_maximum_fusion.6), channel_id=1, source_target_pairs={{0,2},{1,3},{2,0},{3,1},{4,6},{5,7},{6,4},{7,5},{8,10},{9,11},{10,... | collective-permute-start | bytes 294920 | tf_op jit(solution)/shard_map/ppermute | solution.py:43
  13.9 8.4 %collective-permute-start.1 = (bf16[2,256,192]{1,2,0:T(8,128)(2,1)S(1)}, bf16[2,256,192]{1,2,0:T(8,128)(2,1)S(1)}, u32[]{:S(2)}, u32[]{:S(2)}) collective-permute-start(bf16[2,256,192]{1,2,0:T(8,128)(2,1)S(1)} %pad_maximum_fusion.3), channel_id=1, source_target_pairs={{0,2},{1,3},{2,0},{3,1},{4,6},{5,7},{6,4},{7,5},{8,10},{9,11},{10,... | collective-permute-start | bytes 589832 | tf_op jit(solution)/shard_map/ppermute | solution.py:43
  22.7 7.4 %collective-permute-start.4 = (bf16[16,128]{1,0:T(8,128)(2,1)S(1)}, bf16[16,128]{1,0:T(8,128)(2,1)S(1)}, u32[]{:S(2)}, u32[]{:S(2)}) collective-permute-start(bf16[16,128]{1,0:T(8,128)(2,1)S(1)} %get-tuple-element.20), channel_id=1, source_target_pairs={{0,4},{4,8},{8,12},{12,16},{16,20},{20,24},{24,28},{1,5},{5,9},{9,... | collective-permute-start | bytes 12296 | tf_op jit(solution)/shard_map/ppermute | solution.py:31
  24.0 6.1 %collective-permute-start.5 = (bf16[16,128]{1,0:T(8,128)(2,1)S(1)}, bf16[16,128]{1,0:T(8,128)(2,1)S(1)}, u32[]{:S(2)}, u32[]{:S(2)}) collective-permute-start(bf16[16,128]{1,0:T(8,128)(2,1)S(1)} %get-tuple-element.21), channel_id=1, source_target_pairs={{4,0},{8,4},{12,8},{16,12},{20,16},{24,20},{28,24},{5,1},{9,5},{13... | collective-permute-start | bytes 12296 | tf_op jit(solution)/shard_map/ppermute | solution.py:32
  28.6 8.8 %collective-permute-start.12 = (f32[2,4,2048]{2,1,0:T(4,128)S(1)}, f32[2,4,2048]{2,1,0:T(4,128)S(1)}, u32[]{:S(2)}, u32[]{:S(2)}) collective-permute-start(f32[2,4,2048]{2,1,0:T(4,128)S(1)} %pad_maximum_fusion.8), channel_id=1, source_target_pairs={{0,8},{4,12},{8,16},{12,20},{16,24},{20,28},{24,0},{28,4},{1,9},{5... | collective-permute-start | bytes 196616 | tf_op jit(solution)/shard_map/ppermute | solution.py:43
  31.0 10.1 %collective-permute-start.6 = (f32[1,176,128]{2,1,0:T(8,128)S(1)}, f32[1,176,128]{2,1,0:T(8,128)S(1)}, u32[]{:S(2)}, u32[]{:S(2)}) collective-permute-start(f32[1,176,128]{2,1,0:T(8,128)S(1)} %get-tuple-element.18), channel_id=1, source_target_pairs={{0,4},{4,8},{8,12},{12,16},{16,20},{20,24},{24,28},{1,5},{5,9},{9,... | collective-permute-start | bytes 270344 | tf_op jit(solution)/shard_map/ppermute | solution.py:31
  32.3 8.8 %collective-permute-start.7 = (f32[1,176,128]{2,1,0:T(8,128)S(1)}, f32[1,176,128]{2,1,0:T(8,128)S(1)}, u32[]{:S(2)}, u32[]{:S(2)}) collective-permute-start(f32[1,176,128]{2,1,0:T(8,128)S(1)} %get-tuple-element.19), channel_id=1, source_target_pairs={{4,0},{8,4},{12,8},{16,12},{20,16},{24,20},{28,24},{5,1},{9,5},{13... | collective-permute-start | bytes 270344 | tf_op jit(solution)/shard_map/ppermute | solution.py:32
  37.4 4.1 %copy-start.5 = (bf16[3,128,384]{2,1,0:T(8,128)(2,1)S(1)}, bf16[3,128,384]{2,1,0:T(8,128)(2,1)}, u32[]{:S(2)}) copy-start(bf16[3,128,384]{2,1,0:T(8,128)(2,1)} %param.26) | copy-start | bytes 884740
  37.4 85.3 %collective-permute-start.13 = (f32[4,4,2048]{2,1,0:T(4,128)S(1)}, f32[4,4,2048]{2,1,0:T(4,128)S(1)}, u32[]{:S(2)}, u32[]{:S(2)}) collective-permute-start(f32[4,4,2048]{2,1,0:T(4,128)S(1)} %pad_maximum_fusion.5), channel_id=1, source_target_pairs={{0,16},{4,20},{8,24},{12,28},{16,0},{20,4},{24,8},{28,12},{1,17},{... | collective-permute-start | bytes 393224 | tf_op jit(solution)/shard_map/ppermute | solution.py:43
  44.3 20.4 %copy-start.7 = (bf16[3,128,128]{2,1,0:T(8,128)(2,1)S(1)}, bf16[3,128,128]{2,1,0:T(8,128)(2,1)}, u32[]{:S(2)}) copy-start(bf16[3,128,128]{2,1,0:T(8,128)(2,1)} %param.27) | copy-start | bytes 294916
  64.7 1.7 copy-start.4
  66.4 0.9 copy-start.13
  116.7 0.9 copy-start.2
  116.7 0.9 copy-start.6
  116.8 0.9 copy-start.12
  118.8 5.6 %collective-permute-start.8 = (f32[1,3,2048]{2,1,0:T(4,128)S(1)}, f32[1,3,2048]{2,1,0:T(4,128)S(1)}, u32[]{:S(2)}, u32[]{:S(2)}) collective-permute-start(f32[1,3,2048]{2,1,0:T(4,128)S(1)} %fusion.14), channel_id=1, source_target_pairs={{0,4},{4,8},{8,12},{12,16},{16,20},{20,24},{24,28},{28,0},{1,5},{5... | collective-permute-start | bytes 73736 | tf_op jit(solution)/shard_map/ppermute | solution.py:43
  122.8 14.3 %copy-start.1 = (f32[8,4,2048]{2,1,0:T(4,128)}, f32[8,4,2048]{2,1,0:T(4,128)S(1)}, u32[]{:S(2)}) copy-start(f32[8,4,2048]{2,1,0:T(4,128)S(1)} %pad_maximum_fusion.2.true_ref) | copy-start | bytes 786436
  124.4 4.7 %collective-permute-start.9 = (f32[2,3,2048]{2,1,0:T(4,128)S(1)}, f32[2,3,2048]{2,1,0:T(4,128)S(1)}, u32[]{:S(2)}, u32[]{:S(2)}) collective-permute-start(f32[2,3,2048]{2,1,0:T(4,128)S(1)} %pad_maximum_fusion.7), channel_id=1, source_target_pairs={{0,8},{4,12},{8,16},{12,20},{16,24},{20,28},{24,0},{28,4},{1,9},{5... | collective-permute-start | bytes 147464 | tf_op jit(solution)/shard_map/ppermute | solution.py:43
  129.1 7.3 %collective-permute-start.10 = (f32[4,3,2048]{2,1,0:T(4,128)S(1)}, f32[4,3,2048]{2,1,0:T(4,128)S(1)}, u32[]{:S(2)}, u32[]{:S(2)}) collective-permute-start(f32[4,3,2048]{2,1,0:T(4,128)S(1)} %pad_maximum_fusion.4), channel_id=1, source_target_pairs={{0,16},{4,20},{8,24},{12,28},{16,0},{20,4},{24,8},{28,12},{1,17},{... | collective-permute-start | bytes 294920 | tf_op jit(solution)/shard_map/ppermute | solution.py:43

commit v6 on v5

--- a/solution.py
+++ b/solution.py
@@ -213,28 +213,39 @@
         "kti,kio->to", feat_parts, proj_parts, preferred_element_type=jnp.float32
     )
     token_proj = token_sum.astype(jnp.bfloat16)
-    padded_tok = extended(token_proj, (("atoms", 0),), HALO_TOK)
-    first_token = atom_rank * tok_rows - HALO_TOK
-    relative = atom_token - first_token
-    onehot = (
-        relative[:, None] == jnp.arange(tok_rows + 2 * HALO_TOK, dtype=jnp.int32)[None, :]
-    ).astype(jnp.bfloat16)
-    atom_base = atom_single.astype(jnp.float32) + jnp.dot(
-        onehot, padded_tok, preferred_element_type=jnp.float32
-    )
-    sigma_col = sigma[:, None, None]
-    noisy = true_coords[None] + sigma_col * noise
-    noise_total = sigma_col * sigma_col + sigma_data * sigma_data
-    scaled = noisy / jnp.sqrt(noise_total)
-    hidden = atom_base[None] + jnp.einsum(
-        "sda,dc->sac", scaled, coord_in, precision=lax.Precision.HIGHEST
-    )
     key_halo = (KWIN - QBLK) // 2
     reaches = [0]
     for _ in range(LAYERS - 1):
         reaches.insert(0, -(-(reaches[0] + key_halo) // QBLK) * QBLK)
     buffer_start = -(reaches[0] + key_halo)
-    hidden = extended(hidden, (("atoms", 1),), -buffer_start)
+    atom_halo = -buffer_start
+    per_token = atom_rows // tok_rows
+    tok_halo = -(-(-(-atom_halo // per_token) + HALO_TOK) // 16) * 16
+    samples = noise.shape[0]
+    atom_floats = jnp.concatenate(
+        [true_coords, noise.reshape(samples * 3, atom_rows), atom_token.astype(jnp.float32)[None]]
+    )
+    floats_ext = extended(atom_floats, (("atoms", 1),), atom_halo)
+    single_ext = extended(atom_single, (("atoms", 0),), atom_halo)
+    true_ext = floats_ext[:3]
+    noise_ext = floats_ext[3 : 3 + 3 * samples].reshape(samples, 3, -1)
+    token_ext = floats_ext[3 + 3 * samples].astype(jnp.int32)
+    padded_tok = extended(token_proj, (("atoms", 0),), tok_halo)
+    first_token = atom_rank * tok_rows - tok_halo
+    relative = token_ext - first_token
+    onehot = (
+        relative[:, None] == jnp.arange(tok_rows + 2 * tok_halo, dtype=jnp.int32)[None, :]
+    ).astype(jnp.bfloat16)
+    atom_base = single_ext.astype(jnp.float32) + jnp.dot(
+        onehot, padded_tok, preferred_element_type=jnp.float32
+    )
+    sigma_col = sigma[:, None, None]
+    noisy = true_coords[None] + sigma_col * noise
+    noise_total = sigma_col * sigma_col + sigma_data * sigma_data
+    scaled = (true_ext[None] + sigma_col * noise_ext) / jnp.sqrt(noise_total)
+    hidden = atom_base[None] + jnp.einsum(
+        "sda,dc->sac", scaled, coord_in, precision=lax.Precision.HIGHEST
+    )
     query_win = jnp.arange(Q_TILE, dtype=jnp.int32)[:, None] // QBLK * QBLK
     key_index = jnp.arange(K_SPAN, dtype=jnp.int32)[None, :]
     band = ((key_index >= query_win) & (key_index < query_win + KWIN)).astype(jnp.float32)

time: 181 us -> 188 us (1.039)
  the two profiles are of different devices: /device:TPU:26 before, /device:TPU:24 now
where the time goes in v6:
time: 188 us; the launch traced here: 185 us
  Pallas kernels  95.6 us (51%)
  starting transfers between devices  31.2 us (17%)
  matrix products  16.4 us (9%)
  waiting for transfers between devices  14.3 us (8%)
  local copies, waits for them, and re-layouts  12.2 us (6%)
  other arithmetic  11.6 us (6%)
  between operations  3.86 us (2%)
    pallas_call x3, Pallas kernels, window_attend(): pl.pallas_call(attend_kernel, grid=(atoms // Q_TILE,), in_specs=[pl.Block...  58.1 us
    pallas_call x1, Pallas kernels, lddt_sums(): pl.pallas_call(lddt_kernel, grid_spec=pltpu.PrefetchScalarGridSpec(num_sc...  37.5 us
    ppermute x10, waiting for transfers between devices, ring_parts(): parts = jnp.concatenate([parts, lax.ppermute(parts, axis, pairs)])  13.5 us
    ppermute x3, starting transfers between devices, extended(): after = lax.ppermute(first, axis, down)  12.4 us
    dot_general x12, matrix products, dense(): jnp.einsum('sac,cf->saf', left, right, preferred_element_type=jnp.float32)  11.8 us
    ppermute x10, starting transfers between devices, ring_parts(): parts = jnp.concatenate([parts, lax.ppermute(parts, axis, pairs)])  10.9 us
    ppermute x3, starting transfers between devices, extended(): before = lax.ppermute(last, axis, up)  7.93 us
  transfers between devices with their start and end apart: 16, of which 7 were waited for; matrix products, arithmetic and copies ran while one was open for 20% of the time, Pallas kernels for 31%

profile of v6, /device:TPU:24, one launch (start us, length us, event | category | flops | bytes accessed | tf_op | source)
XLA Modules:
  0.0 185.2 jit_solution(13184900030585810685)
XLA Ops:
  0.7 1.6 collective-permute-start.6
  4.7 3.4 %collective-permute-start.2 = (f32[7,176]{1,0:T(8,128)S(1)}, f32[7,176]{1,0:T(8,128)S(1)}, u32[]{:S(2)}, u32[]{:S(2)}) collective-permute-start(f32[7,176]{1,0:T(8,128)S(1)} %get-tuple-element.21), channel_id=1, source_target_pairs={{0,4},{4,8},{8,12},{12,16},{16,20},{20,24},{24,28},{1,5},{5,9},{9,... | collective-permute-start | bytes 14792 | tf_op jit(solution)/shard_map/ppermute | solution.py:31
  8.1 3.3 %collective-permute-start.3 = (f32[7,176]{1,0:T(8,128)S(1)}, f32[7,176]{1,0:T(8,128)S(1)}, u32[]{:S(2)}, u32[]{:S(2)}) collective-permute-start(f32[7,176]{1,0:T(8,128)S(1)} %get-tuple-element.20), channel_id=1, source_target_pairs={{4,0},{8,4},{12,8},{16,12},{20,16},{24,20},{28,24},{5,1},{9,5},{13... | collective-permute-start | bytes 14792 | tf_op jit(solution)/shard_map/ppermute | solution.py:32
  12.2 2.5 %collective-permute-start = (bf16[176,128]{1,0:T(8,128)(2,1)S(1)}, bf16[176,128]{1,0:T(8,128)(2,1)S(1)}, u32[]{:S(2)}, u32[]{:S(2)}) collective-permute-start(bf16[176,128]{1,0:T(8,128)(2,1)S(1)} %get-tuple-element.16), channel_id=1, source_target_pairs={{0,4},{4,8},{8,12},{12,16},{16,20},{20,24},{24,28},{1,5},{5,9},{9,... | collective-permute-start | bytes 135176 | tf_op jit(solution)/shard_map/ppermute | solution.py:31
  17.4 1.3 add_reduce_fusion
  24.6 4.2 %collective-permute-start.1 = (bf16[176,128]{1,0:T(8,128)(2,1)S(1)}, bf16[176,128]{1,0:T(8,128)(2,1)S(1)}, u32[]{:S(2)}, u32[]{:S(2)}) collective-permute-start(bf16[176,128]{1,0:T(8,128)(2,1)S(1)} %get-tuple-element.17), channel_id=1, source_target_pairs={{4,0},{8,4},{12,8},{16,12},{20,16},{24,20},{28,24},{5,1},{9,5},{13... | collective-permute-start | bytes 135176 | tf_op jit(solution)/shard_map/ppermute | solution.py:32
  30.5 1.6 collective-permute-start.5
  32.1 1.6 collective-permute-done.13
  33.8 1.9 %collective-permute-done.7 = bf16[2,192,128]{2,1,0:T(8,128)(2,1)S(1)} collective-permute-done((bf16[2,192,128]{2,1,0:T(8,128)(2,1)S(1)}, bf16[2,192,128]{2,1,0:T(8,128)(2,1)S(1)}, u32[]{:S(2)}, u32[]{:S(2)}) %collective-permute-start.7) | collective-permute-done | bytes 98336 | tf_op jit(solution)/shard_map/ppermute | solution.py:43
  35.7 2.1 %collective-permute-done.5 = bf16[2,256,192]{1,2,0:T(8,128)(2,1)S(1)} collective-permute-done((bf16[2,256,192]{1,2,0:T(8,128)(2,1)S(1)}, bf16[2,256,192]{1,2,0:T(8,128)(2,1)S(1)}, u32[]{:S(2)}, u32[]{:S(2)}) %collective-permute-start.5) | collective-permute-done | bytes 196640 | tf_op jit(solution)/shard_map/ppermute | solution.py:43
  38.2 2.1 %collective-permute-start.8 = (bf16[48,128]{1,0:T(8,128)(2,1)S(1)}, bf16[48,128]{1,0:T(8,128)(2,1)S(1)}, u32[]{:S(2)}, u32[]{:S(2)}) collective-permute-start(bf16[48,128]{1,0:T(8,128)(2,1)S(1)} %get-tuple-element.18), channel_id=1, source_target_pairs={{0,4},{4,8},{8,12},{12,16},{16,20},{20,24},{24,28},{1,5},{5,9},{9,... | collective-permute-start | bytes 36872 | tf_op jit(solution)/shard_map/ppermute | solution.py:31
  40.2 4.8 %collective-permute-start.9 = (bf16[48,128]{1,0:T(8,128)(2,1)S(1)}, bf16[48,128]{1,0:T(8,128)(2,1)S(1)}, u32[]{:S(2)}, u32[]{:S(2)}) collective-permute-start(bf16[48,128]{1,0:T(8,128)(2,1)S(1)} %get-tuple-element.19), channel_id=1, source_target_pairs={{4,0},{8,4},{12,8},{16,12},{20,16},{24,20},{28,24},{5,1},{9,5},{13... | collective-permute-start | bytes 36872 | tf_op jit(solution)/shard_map/ppermute | solution.py:32
  47.3 2.3 %multiply_reduce_fusion = (f32[2400]{0:T(1024)S(1)}, f32[2400,128]{1,0:T(8,128)S(1)}) fusion(f32[3,128]{1,0:T(4,128)S(1)} %copy-done, f32[7,2400]{1,0:T(8,128)S(1)} %concatenate.58, f32[]{:T(128)} %bitcast.9, f32[]{:T(128)} %bitcast.190, f32[2400,128]{1,0:T(8,128)S(1)} %fusion.7, bf16[176,128]{1,0:T(8,128)(2,1)S(1)} %collective-permute-done.1, ...), kind=kOutput, calls=%fused_computation.38 | convolution fusion | flops 14150400 | bytes 3150344 | tf_op jit(solution)/shard_map/sda,dc->sac/dot_general | solution.py:246
  50.4 1.1 fusion.16.kv_ref
  52.4 20.4 %shard_map.167 = bf16[2304,128]{1,0:T(8,128)(2,1)} custom-call(bf16[2304,128]{1,0:T(8,128)(2,1)} %slice_bitcast_fusion.q_ref, bf16[2432,256]{1,0:T(8,128)(2,1)} %fusion.16.kv_ref, f32[128,256]{1,0:T(8,128)} %fusion.68.band_ref, f32[18,256]{1,0:T(8,128)} %fusion.108.valid_ref), custom_call_target="tpu_custom_call" | custom-call | tf_op jit(solution)/shard_map/pallas_call | solution.py:95
  72.8 1.7 multiply_reduce_fusion.2
  75.4 0.9 multiply_reduce_fusion.1
  77.1 1.1 fusion.17.kv_ref
  79.0 19.3 %shard_map.168 = bf16[2176,128]{1,0:T(8,128)(2,1)} custom-call(bf16[2176,128]{1,0:T(8,128)(2,1)} %slice_bitcast_fusion.1.q_ref, bf16[2304,256]{1,0:T(8,128)(2,1)} %fusion.17.kv_ref, f32[128,256]{1,0:T(8,128)} %fusion.68.band_ref, f32[17,256]{1,0:T(8,128)} %fusion.110.valid_ref), custom_call_target="tpu_custom_call" | custom-call | tf_op jit(solution)/shard_map/pallas_call | solution.py:95
  98.4 1.6 multiply_reduce_fusion.4
  102.3 1.1 fusion.21.kv_ref
  104.2 18.3 %shard_map.169 = bf16[2048,128]{1,0:T(8,128)(2,1)} custom-call(bf16[2048,128]{1,0:T(8,128)(2,1)} %slice_bitcast_fusion.2.q_ref, bf16[2176,256]{1,0:T(8,128)(2,1)} %fusion.21.kv_ref, f32[128,256]{1,0:T(8,128)} %fusion.68.band_ref, f32[16,256]{1,0:T(8,128)} %fusion.116.valid_ref), custom_call_target="tpu_custom_call" | custom-call | tf_op jit(solution)/shard_map/pallas_call | solution.py:95
  122.5 1.6 multiply_reduce_fusion.6
  125.8 1.2 fusion.13
  126.9 1.0 collective-permute-start.10
  128.0 4.1 %collective-permute-done.10 = f32[1,3,2048]{2,1,0:T(4,128)S(1)} collective-permute-done((f32[1,3,2048]{2,1,0:T(4,128)S(1)}, f32[1,3,2048]{2,1,0:T(4,128)S(1)}, u32[]{:S(2)}, u32[]{:S(2)}) %collective-permute-start.10) | collective-permute-done | bytes 24608 | tf_op jit(solution)/shard_map/ppermute | solution.py:43
  132.0 3.9 %collective-permute-start.11 = (f32[2,3,2048]{2,1,0:T(4,128)S(1)}, f32[2,3,2048]{2,1,0:T(4,128)S(1)}, u32[]{:S(2)}, u32[]{:S(2)}) collective-permute-start(f32[2,3,2048]{2,1,0:T(4,128)S(1)} %pad_maximum_fusion.7), channel_id=1, source_target_pairs={{0,8},{4,12},{8,16},{12,20},{16,24},{20,28},{24,0},{28,4},{1,9},{5... | collective-permute-start | bytes 147464 | tf_op jit(solution)/shard_map/ppermute | solution.py:43
  138.1 1.5 collective-permute-start.12
  139.7 1.3 copy.25.own_ref
  141.0 3.0 %collective-permute-done.12 = f32[4,3,2048]{2,1,0:T(4,128)S(1)} collective-permute-done((f32[4,3,2048]{2,1,0:T(4,128)S(1)}, f32[4,3,2048]{2,1,0:T(4,128)S(1)}, u32[]{:S(2)}, u32[]{:S(2)}) %collective-permute-start.12) | collective-permute-done | bytes 98336 | tf_op jit(solution)/shard_map/ppermute | solution.py:43
  144.8 37.5 %shard_map.170 = f32[2048,128]{1,0:T(8,128)} custom-call(s32[208]{0:T(256)} %reshape.320.slots_ref, s32[16]{0:T(128)} %count_ref.1, f32[2048,8]{1,0:T(8,128)} %copy.25.own_ref, f32[8,3,2048]{2,1,0:T(4,128)} %pad_maximum_fusion.pred_ref, f32[8,4,2048]{2,1,0:T(4,128)} %copy-done.1), custom_call_target="tpu_custom_call" | custom-call | tf_op jit(solution)/shard_map/pallas_call | solution.py:166
  182.3 1.3 slice_multiply_fusion.3
  (97 shorter events, 26.7 us)
Async XLA Ops:
  0.6 46.7 %copy-start = (f32[3,128]{1,0:T(4,128)S(1)}, f32[3,128]{1,0:T(4,128)}, u32[]{:S(2)}) copy-start(f32[3,128]{1,0:T(4,128)} %param.25) | copy-start | bytes 4612
  0.6 29.8 %copy-start.8 = (bf16[256,192]{0,1:T(8,128)(2,1)S(1)}, bf16[256,192]{0,1:T(8,128)(2,1)}, u32[]{:S(2)}) copy-start(bf16[256,192]{0,1:T(8,128)(2,1)} %param.18) | copy-start | bytes 294916
  0.7 37.2 %copy-start.9 = (bf16[192,128]{1,0:T(8,128)(2,1)S(1)}, bf16[192,128]{1,0:T(8,128)(2,1)}, u32[]{:S(2)}) copy-start(bf16[192,128]{1,0:T(8,128)(2,1)} %param.19) | copy-start | bytes 147460
  0.7 29.8 %collective-permute-start.4 = (bf16[1,256,192]{1,2,0:T(8,128)(2,1)}, bf16[1,256,192]{1,2,0:T(8,128)(2,1)S(1)}, u32[]{:S(2)}, u32[]{:S(2)}) collective-permute-start(bf16[1,256,192]{1,2,0:T(8,128)(2,1)} %bitcast.195), channel_id=1, source_target_pairs={{0,1},{1,2},{2,3},{3,0},{4,5},{5,6},{6,7},{7,4},{8,9},{9,10},{10,1... | collective-permute-start | bytes 294920 | tf_op jit(solution)/shard_map/ppermute | solution.py:43
  0.7 28.3 %collective-permute-start.6 = (bf16[1,192,128]{2,1,0:T(8,128)(2,1)}, bf16[1,192,128]{2,1,0:T(8,128)(2,1)S(1)}, u32[]{:S(2)}, u32[]{:S(2)}) collective-permute-start(bf16[1,192,128]{2,1,0:T(8,128)(2,1)} %bitcast.198), channel_id=1, source_target_pairs={{0,1},{1,2},{2,3},{3,0},{4,5},{5,6},{6,7},{7,4},{8,9},{9,10},{10,1... | collective-permute-start | bytes 147464 | tf_op jit(solution)/shard_map/ppermute | solution.py:43
  4.7 19.9 %collective-permute-start.2 = (f32[7,176]{1,0:T(8,128)S(1)}, f32[7,176]{1,0:T(8,128)S(1)}, u32[]{:S(2)}, u32[]{:S(2)}) collective-permute-start(f32[7,176]{1,0:T(8,128)S(1)} %get-tuple-element.21), channel_id=1, source_target_pairs={{0,4},{4,8},{8,12},{12,16},{16,20},{20,24},{24,28},{1,5},{5,9},{9,... | collective-permute-start | bytes 14792 | tf_op jit(solution)/shard_map/ppermute | solution.py:31
  8.1 20.8 %collective-permute-start.3 = (f32[7,176]{1,0:T(8,128)S(1)}, f32[7,176]{1,0:T(8,128)S(1)}, u32[]{:S(2)}, u32[]{:S(2)}) collective-permute-start(f32[7,176]{1,0:T(8,128)S(1)} %get-tuple-element.20), channel_id=1, source_target_pairs={{4,0},{8,4},{12,8},{16,12},{20,16},{24,20},{28,24},{5,1},{9,5},{13... | collective-permute-start | bytes 14792 | tf_op jit(solution)/shard_map/ppermute | solution.py:32
  12.2 35.0 %collective-permute-start = (bf16[176,128]{1,0:T(8,128)(2,1)S(1)}, bf16[176,128]{1,0:T(8,128)(2,1)S(1)}, u32[]{:S(2)}, u32[]{:S(2)}) collective-permute-start(bf16[176,128]{1,0:T(8,128)(2,1)S(1)} %get-tuple-element.16), channel_id=1, source_target_pairs={{0,4},{4,8},{8,12},{12,16},{16,20},{20,24},{24,28},{1,5},{5,9},{9,... | collective-permute-start | bytes 135176 | tf_op jit(solution)/shard_map/ppermute | solution.py:31
  24.6 22.7 %collective-permute-start.1 = (bf16[176,128]{1,0:T(8,128)(2,1)S(1)}, bf16[176,128]{1,0:T(8,128)(2,1)S(1)}, u32[]{:S(2)}, u32[]{:S(2)}) collective-permute-start(bf16[176,128]{1,0:T(8,128)(2,1)S(1)} %get-tuple-element.17), channel_id=1, source_target_pairs={{4,0},{8,4},{12,8},{16,12},{20,16},{24,20},{28,24},{5,1},{9,5},{13... | collective-permute-start | bytes 135176 | tf_op jit(solution)/shard_map/ppermute | solution.py:32
  28.9 4.9 %collective-permute-start.13 = (f32[1,4,2048]{2,1,0:T(4,128)S(1)}, f32[1,4,2048]{2,1,0:T(4,128)S(1)}, u32[]{:S(2)}, u32[]{:S(2)}) collective-permute-start(f32[1,4,2048]{2,1,0:T(4,128)S(1)} %fusion.95), channel_id=1, source_target_pairs={{0,4},{4,8},{8,12},{12,16},{16,20},{20,24},{24,28},{28,0},{1,5},{5... | collective-permute-start | bytes 98312 | tf_op jit(solution)/shard_map/ppermute | solution.py:43
  29.9 5.8 %collective-permute-start.7 = (bf16[2,192,128]{2,1,0:T(8,128)(2,1)S(1)}, bf16[2,192,128]{2,1,0:T(8,128)(2,1)S(1)}, u32[]{:S(2)}, u32[]{:S(2)}) collective-permute-start(bf16[2,192,128]{2,1,0:T(8,128)(2,1)S(1)} %pad_maximum_fusion.5), channel_id=1, source_target_pairs={{0,2},{1,3},{2,0},{3,1},{4,6},{5,7},{6,4},{7,5},{8,10},{9,11},{10,... | collective-permute-start | bytes 294920 | tf_op jit(solution)/shard_map/ppermute | solution.py:43
  30.5 7.3 %collective-permute-start.5 = (bf16[2,256,192]{1,2,0:T(8,128)(2,1)S(1)}, bf16[2,256,192]{1,2,0:T(8,128)(2,1)S(1)}, u32[]{:S(2)}, u32[]{:S(2)}) collective-permute-start(bf16[2,256,192]{1,2,0:T(8,128)(2,1)S(1)} %pad_maximum_fusion.2), channel_id=1, source_target_pairs={{0,2},{1,3},{2,0},{3,1},{4,6},{5,7},{6,4},{7,5},{8,10},{9,11},{10,... | collective-permute-start | bytes 589832 | tf_op jit(solution)/shard_map/ppermute | solution.py:43
  33.7 11.3 %collective-permute-start.14 = (f32[2,4,2048]{2,1,0:T(4,128)S(1)}, f32[2,4,2048]{2,1,0:T(4,128)S(1)}, u32[]{:S(2)}, u32[]{:S(2)}) collective-permute-start(f32[2,4,2048]{2,1,0:T(4,128)S(1)} %pad_maximum_fusion.8), channel_id=1, source_target_pairs={{0,8},{4,12},{8,16},{12,20},{16,24},{20,28},{24,0},{28,4},{1,9},{5... | collective-permute-start | bytes 196616 | tf_op jit(solution)/shard_map/ppermute | solution.py:43
  38.1 9.2 %copy-start.3 = (bf16[2048,128]{1,0:T(8,128)(2,1)S(1)}, bf16[2048,128]{1,0:T(8,128)(2,1)}, u32[]{:S(2)}) copy-start(bf16[2048,128]{1,0:T(8,128)(2,1)} %param.20) | copy-start | bytes 1572868
  38.2 7.5 %collective-permute-start.8 = (bf16[48,128]{1,0:T(8,128)(2,1)S(1)}, bf16[48,128]{1,0:T(8,128)(2,1)S(1)}, u32[]{:S(2)}, u32[]{:S(2)}) collective-permute-start(bf16[48,128]{1,0:T(8,128)(2,1)S(1)} %get-tuple-element.18), channel_id=1, source_target_pairs={{0,4},{4,8},{8,12},{12,16},{16,20},{20,24},{24,28},{1,5},{5,9},{9,... | collective-permute-start | bytes 36872 | tf_op jit(solution)/shard_map/ppermute | solution.py:31
  40.2 6.2 %collective-permute-start.9 = (bf16[48,128]{1,0:T(8,128)(2,1)S(1)}, bf16[48,128]{1,0:T(8,128)(2,1)S(1)}, u32[]{:S(2)}, u32[]{:S(2)}) collective-permute-start(bf16[48,128]{1,0:T(8,128)(2,1)S(1)} %get-tuple-element.19), channel_id=1, source_target_pairs={{4,0},{8,4},{12,8},{16,12},{20,16},{24,20},{28,24},{5,1},{9,5},{13... | collective-permute-start | bytes 36872 | tf_op jit(solution)/shard_map/ppermute | solution.py:32
  45.1 82.8 %collective-permute-start.15 = (f32[4,4,2048]{2,1,0:T(4,128)S(1)}, f32[4,4,2048]{2,1,0:T(4,128)S(1)}, u32[]{:S(2)}, u32[]{:S(2)}) collective-permute-start(f32[4,4,2048]{2,1,0:T(4,128)S(1)} %pad_maximum_fusion.4), channel_id=1, source_target_pairs={{0,16},{4,20},{8,24},{12,28},{16,0},{20,4},{24,8},{28,12},{1,17},{... | collective-permute-start | bytes 393224 | tf_op jit(solution)/shard_map/ppermute | solution.py:43
  47.3 2.4 %copy-start.5 = (bf16[3,128,384]{2,1,0:T(8,128)(2,1)S(1)}, bf16[3,128,384]{2,1,0:T(8,128)(2,1)}, u32[]{:S(2)}) copy-start(bf16[3,128,384]{2,1,0:T(8,128)(2,1)} %param.26) | copy-start | bytes 884740
  52.4 20.4 %copy-start.7 = (bf16[3,128,128]{2,1,0:T(8,128)(2,1)S(1)}, bf16[3,128,128]{2,1,0:T(8,128)(2,1)}, u32[]{:S(2)}) copy-start(bf16[3,128,128]{2,1,0:T(8,128)(2,1)} %param.27) | copy-start | bytes 294916
  72.8 1.7 copy-start.4
  74.5 0.9 copy-start.11
  124.9 0.9 copy-start.2
  124.9 0.9 copy-start.6
  124.9 0.9 copy-start.10
  126.9 5.1 %collective-permute-start.10 = (f32[1,3,2048]{2,1,0:T(4,128)S(1)}, f32[1,3,2048]{2,1,0:T(4,128)S(1)}, u32[]{:S(2)}, u32[]{:S(2)}) collective-permute-start(f32[1,3,2048]{2,1,0:T(4,128)S(1)} %fusion.13), channel_id=1, source_target_pairs={{0,4},{4,8},{8,12},{12,16},{16,20},{20,24},{24,28},{28,0},{1,5},{5... | collective-permute-start | bytes 73736 | tf_op jit(solution)/shard_map/ppermute | solution.py:43
  127.9 16.8 %copy-start.1 = (f32[8,4,2048]{2,1,0:T(4,128)}, f32[8,4,2048]{2,1,0:T(4,128)S(1)}, u32[]{:S(2)}) copy-start(f32[8,4,2048]{2,1,0:T(4,128)S(1)} %pad_maximum_fusion.1.true_ref) | copy-start | bytes 786436
  132.0 6.0 %collective-permute-start.11 = (f32[2,3,2048]{2,1,0:T(4,128)S(1)}, f32[2,3,2048]{2,1,0:T(4,128)S(1)}, u32[]{:S(2)}, u32[]{:S(2)}) collective-permute-start(f32[2,3,2048]{2,1,0:T(4,128)S(1)} %pad_maximum_fusion.7), channel_id=1, source_target_pairs={{0,8},{4,12},{8,16},{12,20},{16,24},{20,28},{24,0},{28,4},{1,9},{5... | collective-permute-start | bytes 147464 | tf_op jit(solution)/shard_map/ppermute | solution.py:43
  138.1 5.9 %collective-permute-start.12 = (f32[4,3,2048]{2,1,0:T(4,128)S(1)}, f32[4,3,2048]{2,1,0:T(4,128)S(1)}, u32[]{:S(2)}, u32[]{:S(2)}) collective-permute-start(f32[4,3,2048]{2,1,0:T(4,128)S(1)} %pad_maximum_fusion.3), channel_id=1, source_target_pairs={{0,16},{4,20},{8,24},{12,28},{16,0},{20,4},{24,8},{28,12},{1,17},{... | collective-permute-start | bytes 294920 | tf_op jit(solution)/shard_map/ppermute | solution.py:43

commit v7 on v5

--- a/solution.py
+++ b/solution.py
@@ -108,7 +108,7 @@
 ROW_CHUNK = 64
 
 
-def lddt_kernel(slots_ref, count_ref, own_ref, pred_ref, true_ref, out_ref, cols_ref):
+def lddt_kernel(slots_ref, count_ref, own_ref, coord_ref, out_ref, cols_ref):
     block = pl.program_id(0)
     live = count_ref[block]
     blocks = count_ref.shape[0]
@@ -128,8 +128,9 @@
             slot = slots_ref[block * max_slots + slot_index]
             peer = slot // blocks
             start = pl.multiple_of((slot % blocks) * PAIR_BLK, PAIR_BLK)
-            part_pred = pred_ref[peer, :, pl.ds(start, PAIR_BLK)]
-            part_true = true_ref[peer, :, pl.ds(start, PAIR_BLK)]
+            part = coord_ref[peer, :, pl.ds(start, PAIR_BLK)]
+            part_pred = part[0:3]
+            part_true = part[3:6]
             gaps = [cols_ref[d, pl.ds(row, ROW_CHUNK), :] - part_pred[d : d + 1, :] for d in range(3)]
             true_gaps = [
                 cols_ref[3 + d, pl.ds(row, ROW_CHUNK), :] - part_true[d : d + 1, :] for d in range(3)
@@ -161,7 +162,7 @@
     lax.fori_loop(0, PAIR_BLK // ROW_CHUNK, row_body, 0)
 
 
-def lddt_sums(slots, counts, own_tab, pred_parts, true_parts):
+def lddt_sums(slots, counts, own_tab, coord_parts):
     blocks = counts.shape[0]
     out = pl.pallas_call(
         lddt_kernel,
@@ -170,14 +171,13 @@
             grid=(blocks,),
             in_specs=[
                 pl.BlockSpec((PAIR_BLK, own_tab.shape[1]), lambda b, *_: (b, 0)),
-                pl.BlockSpec(pred_parts.shape, lambda b, *_: (0, 0, 0)),
-                pl.BlockSpec(true_parts.shape, lambda b, *_: (0, 0, 0)),
+                pl.BlockSpec(coord_parts.shape, lambda b, *_: (0, 0, 0)),
             ],
             out_specs=pl.BlockSpec((PAIR_BLK, PAIR_BLK), lambda b, *_: (b, 0)),
             scratch_shapes=[pltpu.VMEM((6, PAIR_BLK, PAIR_BLK), jnp.float32)],
         ),
         out_shape=jax.ShapeDtypeStruct((blocks * PAIR_BLK, PAIR_BLK), jnp.float32),
-    )(slots, counts, own_tab, pred_parts, true_parts)
+    )(slots, counts, own_tab, coord_parts)
     return out[:, :3].T
 
 def dense(left, right):
@@ -281,15 +281,14 @@
     count_row = jnp.zeros((1, atom_rows), jnp.float32).at[0, 0].set(
         jnp.sum(pair_count.astype(jnp.float32) * (PAIR_BLK * PAIR_BLK) - PAIR_BLK)
     )
-    true_parts = ring_parts(jnp.concatenate([true_coords, count_row], axis=0), "atoms")
-    pred_parts = ring_parts(predicted[0], "atoms")
-    pair_total = jnp.sum(true_parts[:, 3, 0])
+    coord_parts = ring_parts(jnp.concatenate([predicted[0], true_coords, count_row], axis=0), "atoms")
+    pair_total = jnp.sum(coord_parts[:, 6, 0])
     own_tab = jnp.concatenate(
         [predicted[0], true_coords, jnp.zeros((2, atom_rows), jnp.float32)], axis=0
     ).T
     source = (atom_rank - pair_blocks // block_count) % atom_peers
     slots = (source * block_count + pair_blocks % block_count).reshape(-1)
-    pair_grad = 2.0 * lddt_sums(slots, pair_count, own_tab, pred_parts, true_parts)[None]
+    pair_grad = 2.0 * lddt_sums(slots, pair_count, own_tab, coord_parts)[None]
     lddt_grad = total_atoms * PAIR_BLK / pair_total * pair_grad.reshape(samples, 3, atom_rows)
     coord_grad = mse_part - lddt_grad / PAIR_BLK
     return (coord_grad, lddt_grad)

time: 181 us -> 178 us (0.983); the launches traced: 180 us -> 175 us
  waiting for transfers between devices: 12 us -> 16.3 us
  starting transfers between devices: 30.1 us -> 26.2 us
  Pallas kernels: 98.3 us -> 94.7 us
  other arithmetic: 9.63 us -> 6.82 us
    ppermute x10 -> x7, starting transfers between devices: 17.9 us -> 14 us  [ring_parts(): parts = jnp.concatenate([parts, lax.ppermute(parts, axis, pairs)])]
    ppermute x10 -> x7, waiting for transfers between devices: 12 us -> 15.7 us  [ring_parts(): parts = jnp.concatenate([parts, lax.ppermute(parts, axis, pairs)])]
    pallas_call x1, Pallas kernels: 40.3 us -> 36.6 us  [lddt_sums(): pl.pallas_call(lddt_kernel, grid_spec=pltpu.PrefetchScalarGridSpec(num_sc...]
  transfers between devices with their start and end apart: 14 -> 11, of which waited for: 5 -> 6; matrix products, arithmetic and copies ran while one was open for 18% -> 5% of each run, Pallas kernels for 32% -> 0%
where the time goes in v7:
time: 178 us; the launch traced here: 175 us
  Pallas kernels  94.7 us (53%)
  starting transfers between devices  26.2 us (15%)
  matrix products  17.6 us (10%)
  waiting for transfers between devices  16.3 us (9%)
  local copies, waits for them, and re-layouts  9.85 us (6%)
  other arithmetic  6.82 us (4%)
  between operations  3.83 us (2%)
    pallas_call x3, Pallas kernels, window_attend(): pl.pallas_call(attend_kernel, grid=(atoms // Q_TILE,), in_specs=[pl.Block...  58.1 us
    pallas_call x1, Pallas kernels, lddt_sums(): pl.pallas_call(lddt_kernel, grid_spec=pltpu.PrefetchScalarGridSpec(num_sc...  36.6 us
    ppermute x7, waiting for transfers between devices, ring_parts(): parts = jnp.concatenate([parts, lax.ppermute(parts, axis, pairs)])  15.7 us
    ppermute x7, starting transfers between devices, ring_parts(): parts = jnp.concatenate([parts, lax.ppermute(parts, axis, pairs)])  14 us
    dot_general x12, matrix products, dense(): jnp.einsum('sac,cf->saf', left, right, preferred_element_type=jnp.float32)  12.7 us
    ppermute x2, starting transfers between devices, extended(): after = lax.ppermute(first, axis, down)  9.54 us
  transfers between devices with their start and end apart: 11, of which 6 were waited for; matrix products, arithmetic and copies ran while one was open for 5% of the time, Pallas kernels for 0%

profile of v7, /device:TPU:26, one launch (start us, length us, event | category | flops | bytes accessed | tf_op | source)
XLA Modules:
  0.0 175.2 jit_solution(2872984935109909606)
XLA Ops:
  0.7 1.6 collective-permute-start.2
  5.2 2.6 %fusion.96 = f32[2048,128]{1,0:T(8,128)S(1)} fusion(f32[3,128]{1,0:T(4,128)S(1)} %copy-done, f32[]{:T(128)} %bitcast.8, f32[3,2048]{1,0:T(4,128)} %param.22, f32[1,3,2048]{2,0,1:T(1,128)} %param.23, f32[]{:T(128)} %bitcast.198), kind=kOutput, calls=%fused_computation.137 | convolution fusion | flops 9455616 | bytes 1099272 | tf_op jit(solution)/shard_map/sda,dc->sac/dot_general | solution.py:229
  9.1 1.6 collective-permute-start.1
  10.7 3.5 %collective-permute-done.3 = bf16[2,192,128]{2,1,0:T(8,128)(2,1)S(1)} collective-permute-done((bf16[2,192,128]{2,1,0:T(8,128)(2,1)S(1)}, bf16[2,192,128]{2,1,0:T(8,128)(2,1)S(1)}, u32[]{:S(2)}, u32[]{:S(2)}) %collective-permute-start.3) | collective-permute-done | bytes 98336 | tf_op jit(solution)/shard_map/ppermute | solution.py:43
  14.3 3.3 %collective-permute-done.1 = bf16[2,256,192]{1,2,0:T(8,128)(2,1)S(1)} collective-permute-done((bf16[2,256,192]{1,2,0:T(8,128)(2,1)S(1)}, bf16[2,256,192]{1,2,0:T(8,128)(2,1)S(1)}, u32[]{:S(2)}, u32[]{:S(2)}) %collective-permute-start.1) | collective-permute-done | bytes 196640 | tf_op jit(solution)/shard_map/ppermute | solution.py:43
  17.9 1.3 collective-permute-start.4
  19.2 4.5 %collective-permute-start.5 = (bf16[16,128]{1,0:T(8,128)(2,1)S(1)}, bf16[16,128]{1,0:T(8,128)(2,1)S(1)}, u32[]{:S(2)}, u32[]{:S(2)}) collective-permute-start(bf16[16,128]{1,0:T(8,128)(2,1)S(1)} %get-tuple-element.21), channel_id=1, source_target_pairs={{4,0},{8,4},{12,8},{16,12},{20,16},{24,20},{28,24},{5,1},{9,5},{13... | collective-permute-start | bytes 12296 | tf_op jit(solution)/shard_map/ppermute | solution.py:32
  25.9 1.3 collective-permute-start.6
  27.2 5.0 %collective-permute-start.7 = (f32[1,176,128]{2,1,0:T(8,128)S(1)}, f32[1,176,128]{2,1,0:T(8,128)S(1)}, u32[]{:S(2)}, u32[]{:S(2)}) collective-permute-start(f32[1,176,128]{2,1,0:T(8,128)S(1)} %get-tuple-element.19), channel_id=1, source_target_pairs={{4,0},{8,4},{12,8},{16,12},{20,16},{24,20},{28,24},{5,1},{9,5},{13... | collective-permute-start | bytes 270344 | tf_op jit(solution)/shard_map/ppermute | solution.py:32
  34.6 1.6 fusion.2
  36.2 1.1 fusion.17.kv_ref
  37.3 0.9 slice_bitcast_fusion.q_ref
  38.2 20.4 %shard_map.167 = bf16[2304,128]{1,0:T(8,128)(2,1)} custom-call(bf16[2304,128]{1,0:T(8,128)(2,1)} %slice_bitcast_fusion.q_ref, bf16[2432,256]{1,0:T(8,128)(2,1)} %fusion.17.kv_ref, f32[128,256]{1,0:T(8,128)} %fusion.72.band_ref, f32[18,256]{1,0:T(8,128)} %fusion.108.valid_ref), custom_call_target="tpu_custom_call" | custom-call | tf_op jit(solution)/shard_map/pallas_call | solution.py:95
  58.6 1.7 multiply_reduce_fusion.2
  61.2 0.9 multiply_reduce_fusion.1
  62.9 1.1 fusion.20.kv_ref
  64.0 0.9 slice_bitcast_fusion.1.q_ref
  64.9 19.3 %shard_map.168 = bf16[2176,128]{1,0:T(8,128)(2,1)} custom-call(bf16[2176,128]{1,0:T(8,128)(2,1)} %slice_bitcast_fusion.1.q_ref, bf16[2304,256]{1,0:T(8,128)(2,1)} %fusion.20.kv_ref, f32[128,256]{1,0:T(8,128)} %fusion.72.band_ref, f32[17,256]{1,0:T(8,128)} %fusion.110.valid_ref), custom_call_target="tpu_custom_call" | custom-call | tf_op jit(solution)/shard_map/pallas_call | solution.py:95
  84.2 1.6 multiply_reduce_fusion.4
  88.1 1.1 fusion.24.kv_ref
  90.0 18.3 %shard_map.169 = bf16[2048,128]{1,0:T(8,128)(2,1)} custom-call(bf16[2048,128]{1,0:T(8,128)(2,1)} %slice_bitcast_fusion.2.q_ref, bf16[2176,256]{1,0:T(8,128)(2,1)} %fusion.24.kv_ref, f32[128,256]{1,0:T(8,128)} %fusion.72.band_ref, f32[16,256]{1,0:T(8,128)} %fusion.115.valid_ref), custom_call_target="tpu_custom_call" | custom-call | tf_op jit(solution)/shard_map/pallas_call | solution.py:95
  108.3 1.6 multiply_reduce_fusion.6
  111.6 1.2 fusion.14
  112.8 4.5 %collective-permute-start.8 = (f32[1,7,2048]{2,1,0:T(8,128)S(1)}, f32[1,7,2048]{2,1,0:T(8,128)S(1)}, u32[]{:S(2)}, u32[]{:S(2)}) collective-permute-start(f32[1,7,2048]{2,1,0:T(8,128)S(1)} %fusion.84), channel_id=1, source_target_pairs={{0,4},{4,8},{8,12},{12,16},{16,20},{20,24},{24,28},{28,0},{1,5},{5... | collective-permute-start | bytes 172040 | tf_op jit(solution)/shard_map/ppermute | solution.py:43
  117.3 2.2 %collective-permute-done.8 = f32[1,7,2048]{2,1,0:T(8,128)S(1)} collective-permute-done((f32[1,7,2048]{2,1,0:T(8,128)S(1)}, f32[1,7,2048]{2,1,0:T(8,128)S(1)}, u32[]{:S(2)}, u32[]{:S(2)}) %collective-permute-start.8) | collective-permute-done | bytes 57376 | tf_op jit(solution)/shard_map/ppermute | solution.py:43
  119.5 2.1 %collective-permute-start.9 = (f32[2,7,2048]{2,1,0:T(8,128)S(1)}, f32[2,7,2048]{2,1,0:T(8,128)S(1)}, u32[]{:S(2)}, u32[]{:S(2)}) collective-permute-start(f32[2,7,2048]{2,1,0:T(8,128)S(1)} %pad_maximum_fusion.4), channel_id=1, source_target_pairs={{0,8},{4,12},{8,16},{12,20},{16,24},{20,28},{24,0},{28,4},{1,9},{5... | collective-permute-start | bytes 344072 | tf_op jit(solution)/shard_map/ppermute | solution.py:43
  122.5 3.7 %collective-permute-done.9 = f32[2,7,2048]{2,1,0:T(8,128)S(1)} collective-permute-done((f32[2,7,2048]{2,1,0:T(8,128)S(1)}, f32[2,7,2048]{2,1,0:T(8,128)S(1)}, u32[]{:S(2)}, u32[]{:S(2)}) %collective-permute-start.9) | collective-permute-done | bytes 114720 | tf_op jit(solution)/shard_map/ppermute | solution.py:43
  126.2 3.5 %collective-permute-start.10 = (f32[4,7,2048]{2,1,0:T(8,128)S(1)}, f32[4,7,2048]{2,1,0:T(8,128)S(1)}, u32[]{:S(2)}, u32[]{:S(2)}) collective-permute-start(f32[4,7,2048]{2,1,0:T(8,128)S(1)} %pad_maximum_fusion.2), channel_id=1, source_target_pairs={{0,16},{4,20},{8,24},{12,28},{16,0},{20,4},{24,8},{28,12},{1,17},{... | collective-permute-start | bytes 688136 | tf_op jit(solution)/shard_map/ppermute | solution.py:43
  129.8 1.3 copy.25.own_ref
  131.1 3.0 %collective-permute-done.10 = f32[4,7,2048]{2,1,0:T(8,128)S(1)} collective-permute-done((f32[4,7,2048]{2,1,0:T(8,128)S(1)}, f32[4,7,2048]{2,1,0:T(8,128)S(1)}, u32[]{:S(2)}, u32[]{:S(2)}) %collective-permute-start.10) | collective-permute-done | bytes 229408 | tf_op jit(solution)/shard_map/ppermute | solution.py:43
  135.0 36.6 %shard_map.170 = f32[2048,128]{1,0:T(8,128)} custom-call(s32[208]{0:T(256)} %reshape.383.slots_ref, s32[16]{0:T(128)} %count_ref.1, f32[2048,8]{1,0:T(8,128)} %copy.25.own_ref, f32[8,7,2048]{2,1,0:T(8,128)} %copy-done.1), custom_call_target="tpu_custom_call" | custom-call | tf_op jit(solution)/shard_map/pallas_call | solution.py:167
  172.3 1.3 slice_multiply_fusion.3
  (88 shorter events, 16.7 us)
Async XLA Ops:
  0.6 4.6 %copy-start = (f32[3,128]{1,0:T(4,128)S(1)}, f32[3,128]{1,0:T(4,128)}, u32[]{:S(2)}) copy-start(f32[3,128]{1,0:T(4,128)} %param.25) | copy-start | bytes 4612
  0.6 8.5 %copy-start.8 = (bf16[256,192]{0,1:T(8,128)(2,1)S(1)}, bf16[256,192]{0,1:T(8,128)(2,1)}, u32[]{:S(2)}) copy-start(bf16[256,192]{0,1:T(8,128)(2,1)} %param.18) | copy-start | bytes 294916
  0.7 7.9 %copy-start.9 = (bf16[192,128]{1,0:T(8,128)(2,1)S(1)}, bf16[192,128]{1,0:T(8,128)(2,1)}, u32[]{:S(2)}) copy-start(bf16[192,128]{1,0:T(8,128)(2,1)} %param.19) | copy-start | bytes 147460
  0.7 10.1 %copy-start.10 = (s32[2048]{0:T(1024)S(1)}, s32[2048]{0:T(1024)}, u32[]{:S(2)}) copy-start(s32[2048]{0:T(1024)} %param.21) | copy-start | bytes 24580
  0.7 8.4 %collective-permute-start = (bf16[1,256,192]{1,2,0:T(8,128)(2,1)}, bf16[1,256,192]{1,2,0:T(8,128)(2,1)S(1)}, u32[]{:S(2)}, u32[]{:S(2)}) collective-permute-start(bf16[1,256,192]{1,2,0:T(8,128)(2,1)} %bitcast.206), channel_id=1, source_target_pairs={{0,1},{1,2},{2,3},{3,0},{4,5},{5,6},{6,7},{7,4},{8,9},{9,10},{10,1... | collective-permute-start | bytes 294920 | tf_op jit(solution)/shard_map/ppermute | solution.py:43
  0.7 7.8 %collective-permute-start.2 = (bf16[1,192,128]{2,1,0:T(8,128)(2,1)}, bf16[1,192,128]{2,1,0:T(8,128)(2,1)S(1)}, u32[]{:S(2)}, u32[]{:S(2)}) collective-permute-start(bf16[1,192,128]{2,1,0:T(8,128)(2,1)} %bitcast.209), channel_id=1, source_target_pairs={{0,1},{1,2},{2,3},{3,0},{4,5},{5,6},{6,7},{7,4},{8,9},{9,10},{10,1... | collective-permute-start | bytes 147464 | tf_op jit(solution)/shard_map/ppermute | solution.py:43
  7.8 15.9 %copy-start.12 = (f32[3,2,128]{2,1,0:T(2,128)S(1)}, f32[3,2,128]{2,1,0:T(2,128)}, u32[]{:S(2)}) copy-start(f32[3,2,128]{2,1,0:T(2,128)} %param.30) | copy-start | bytes 9220
  7.8 17.2 %copy-start.3 = (bf16[2048,128]{1,0:T(8,128)(2,1)S(1)}, bf16[2048,128]{1,0:T(8,128)(2,1)}, u32[]{:S(2)}) copy-start(bf16[2048,128]{1,0:T(8,128)(2,1)} %param.20) | copy-start | bytes 1572868
  8.5 5.7 %collective-permute-start.3 = (bf16[2,192,128]{2,1,0:T(8,128)(2,1)S(1)}, bf16[2,192,128]{2,1,0:T(8,128)(2,1)S(1)}, u32[]{:S(2)}, u32[]{:S(2)}) collective-permute-start(bf16[2,192,128]{2,1,0:T(8,128)(2,1)S(1)} %pad_maximum_fusion.5), channel_id=1, source_target_pairs={{0,2},{1,3},{2,0},{3,1},{4,6},{5,7},{6,4},{7,5},{8,10},{9,11},{10,... | collective-permute-start | bytes 294920 | tf_op jit(solution)/shard_map/ppermute | solution.py:43
  9.1 8.4 %collective-permute-start.1 = (bf16[2,256,192]{1,2,0:T(8,128)(2,1)S(1)}, bf16[2,256,192]{1,2,0:T(8,128)(2,1)S(1)}, u32[]{:S(2)}, u32[]{:S(2)}) collective-permute-start(bf16[2,256,192]{1,2,0:T(8,128)(2,1)S(1)} %pad_maximum_fusion.3), channel_id=1, source_target_pairs={{0,2},{1,3},{2,0},{3,1},{4,6},{5,7},{6,4},{7,5},{8,10},{9,11},{10,... | collective-permute-start | bytes 589832 | tf_op jit(solution)/shard_map/ppermute | solution.py:43
  17.9 6.7 %collective-permute-start.4 = (bf16[16,128]{1,0:T(8,128)(2,1)S(1)}, bf16[16,128]{1,0:T(8,128)(2,1)S(1)}, u32[]{:S(2)}, u32[]{:S(2)}) collective-permute-start(bf16[16,128]{1,0:T(8,128)(2,1)S(1)} %get-tuple-element.20), channel_id=1, source_target_pairs={{0,4},{4,8},{8,12},{12,16},{16,20},{20,24},{24,28},{1,5},{5,9},{9,... | collective-permute-start | bytes 12296 | tf_op jit(solution)/shard_map/ppermute | solution.py:31
  19.2 5.9 %collective-permute-start.5 = (bf16[16,128]{1,0:T(8,128)(2,1)S(1)}, bf16[16,128]{1,0:T(8,128)(2,1)S(1)}, u32[]{:S(2)}, u32[]{:S(2)}) collective-permute-start(bf16[16,128]{1,0:T(8,128)(2,1)S(1)} %get-tuple-element.21), channel_id=1, source_target_pairs={{4,0},{8,4},{12,8},{16,12},{20,16},{24,20},{28,24},{5,1},{9,5},{13... | collective-permute-start | bytes 12296 | tf_op jit(solution)/shard_map/ppermute | solution.py:32
  24.6 7.6 %copy-start.14 = (s32[16]{0:T(128)S(1)}, s32[16]{0:T(128)}, u32[]{:S(2)}) copy-start(s32[16]{0:T(128)} %count_ref.1) | copy-start | bytes 196
  25.9 8.2 %collective-permute-start.6 = (f32[1,176,128]{2,1,0:T(8,128)S(1)}, f32[1,176,128]{2,1,0:T(8,128)S(1)}, u32[]{:S(2)}, u32[]{:S(2)}) collective-permute-start(f32[1,176,128]{2,1,0:T(8,128)S(1)} %get-tuple-element.18), channel_id=1, source_target_pairs={{0,4},{4,8},{8,12},{12,16},{16,20},{20,24},{24,28},{1,5},{5,9},{9,... | collective-permute-start | bytes 270344 | tf_op jit(solution)/shard_map/ppermute | solution.py:31
  27.2 6.9 %collective-permute-start.7 = (f32[1,176,128]{2,1,0:T(8,128)S(1)}, f32[1,176,128]{2,1,0:T(8,128)S(1)}, u32[]{:S(2)}, u32[]{:S(2)}) collective-permute-start(f32[1,176,128]{2,1,0:T(8,128)S(1)} %get-tuple-element.19), channel_id=1, source_target_pairs={{4,0},{8,4},{12,8},{16,12},{20,16},{24,20},{28,24},{5,1},{9,5},{13... | collective-permute-start | bytes 270344 | tf_op jit(solution)/shard_map/ppermute | solution.py:32
  38.2 20.4 %copy-start.7 = (bf16[3,128,128]{2,1,0:T(8,128)(2,1)S(1)}, bf16[3,128,128]{2,1,0:T(8,128)(2,1)}, u32[]{:S(2)}) copy-start(bf16[3,128,128]{2,1,0:T(8,128)(2,1)} %param.27) | copy-start | bytes 294916
  58.6 1.7 copy-start.4
  60.3 0.9 copy-start.15
  61.2 1.0 copy-start.5
  110.7 0.9 copy-start.2
  110.7 0.9 copy-start.6
  110.7 0.9 copy-start.13
  111.5 10.1 %copy-start.11 = (s32[16,13]{1,0:T(8,128)S(1)}, s32[16,13]{1,0:T(8,128)}, u32[]{:S(2)}) copy-start(s32[16,13]{1,0:T(8,128)} %param.32) | copy-start | bytes 2500
  112.8 6.8 %collective-permute-start.8 = (f32[1,7,2048]{2,1,0:T(8,128)S(1)}, f32[1,7,2048]{2,1,0:T(8,128)S(1)}, u32[]{:S(2)}, u32[]{:S(2)}) collective-permute-start(f32[1,7,2048]{2,1,0:T(8,128)S(1)} %fusion.84), channel_id=1, source_target_pairs={{0,4},{4,8},{8,12},{12,16},{16,20},{20,24},{24,28},{28,0},{1,5},{5... | collective-permute-start | bytes 172040 | tf_op jit(solution)/shard_map/ppermute | solution.py:43
  119.5 6.6 %collective-permute-start.9 = (f32[2,7,2048]{2,1,0:T(8,128)S(1)}, f32[2,7,2048]{2,1,0:T(8,128)S(1)}, u32[]{:S(2)}, u32[]{:S(2)}) collective-permute-start(f32[2,7,2048]{2,1,0:T(8,128)S(1)} %pad_maximum_fusion.4), channel_id=1, source_target_pairs={{0,8},{4,12},{8,16},{12,20},{16,24},{20,28},{24,0},{28,4},{1,9},{5... | collective-permute-start | bytes 344072 | tf_op jit(solution)/shard_map/ppermute | solution.py:43
  126.2 7.9 %collective-permute-start.10 = (f32[4,7,2048]{2,1,0:T(8,128)S(1)}, f32[4,7,2048]{2,1,0:T(8,128)S(1)}, u32[]{:S(2)}, u32[]{:S(2)}) collective-permute-start(f32[4,7,2048]{2,1,0:T(8,128)S(1)} %pad_maximum_fusion.2), channel_id=1, source_target_pairs={{0,16},{4,20},{8,24},{12,28},{16,0},{20,4},{24,8},{28,12},{1,17},{... | collective-permute-start | bytes 688136 | tf_op jit(solution)/shard_map/ppermute | solution.py:43
  134.2 0.8 copy-start.1

commit v8 on v7

--- a/solution.py
+++ b/solution.py
@@ -58,52 +58,55 @@
 K_SPAN = 256
 
 
-def attend_kernel(q_ref, kv_ref, band_ref, valid_ref, out_ref):
+def attend_kernel(q_ref, k_ref, v_ref, band_ref, valid_ref, out_ref):
     tile = pl.program_id(0)
-    head_dim = q_ref.shape[1] // HEADS
-    channels = q_ref.shape[1]
+    head_dim = q_ref.shape[2]
     scale = head_dim ** (-0.5)
     start = pl.multiple_of(tile * Q_TILE, Q_TILE)
-    keys_vals = kv_ref[pl.ds(start, K_SPAN), :]
     live = (band_ref[...] * valid_ref[pl.ds(tile, 1), :]) > 0.0
-    query_rows = q_ref[...]
-    heads = []
     for head in range(HEADS):
-        cols = slice(head * head_dim, (head + 1) * head_dim)
-        vcols = slice(channels + head * head_dim, channels + (head + 1) * head_dim)
+        keys = k_ref[head, pl.ds(start, K_SPAN), :]
         scores = lax.dot_general(
-            query_rows[:, cols], keys_vals[:, cols], (((1,), (1,)), ((), ())),
-            preferred_element_type=jnp.float32,
+            q_ref[head], keys, (((1,), (1,)), ((), ())), preferred_element_type=jnp.float32
         )
         scores = jnp.where(live, scores, -1e30)
         row_max = jnp.max(scores, axis=-1, keepdims=True)
         exp_scores = jnp.exp2((scores - row_max) * (scale * math.log2(math.e)))
         inverse = 1.0 / jnp.sum(exp_scores, axis=-1, keepdims=True)
         weights = (exp_scores * inverse).astype(jnp.bfloat16)
-        heads.append(
-            jnp.dot(weights, keys_vals[:, vcols], preferred_element_type=jnp.float32).astype(
-                jnp.bfloat16
-            )
-        )
-    out_ref[...] = jnp.concatenate(heads, axis=1)
+        values = v_ref[head, pl.ds(start, K_SPAN), :]
+        out_ref[head] = jnp.dot(weights, values, preferred_element_type=jnp.float32).astype(
+            jnp.bfloat16
+        )
+
+
+def head_major(block):
+    rows, channels = block.shape
+    return block.reshape(rows, HEADS, channels // HEADS).transpose(1, 0, 2)
 
 
 def window_attend(queries, padded_kv, band, valid_tab):
     atoms, channels = queries.shape
     extra = atoms + K_SPAN - Q_TILE - padded_kv.shape[0]
     padded_kv = jnp.pad(padded_kv, ((0, extra), (0, 0)))
-    return pl.pallas_call(
+    q_heads = head_major(queries)
+    k_heads = head_major(padded_kv[:, :channels])
+    v_heads = head_major(padded_kv[:, channels:])
+    head_dim = channels // HEADS
+    out = pl.pallas_call(
         attend_kernel,
         grid=(atoms // Q_TILE,),
         in_specs=[
-            pl.BlockSpec((Q_TILE, channels), lambda t: (t, 0)),
-            pl.BlockSpec(padded_kv.shape, lambda t: (0, 0)),
+            pl.BlockSpec((HEADS, Q_TILE, head_dim), lambda t: (0, t, 0)),
+            pl.BlockSpec(k_heads.shape, lambda t: (0, 0, 0)),
+            pl.BlockSpec(v_heads.shape, lambda t: (0, 0, 0)),
             pl.BlockSpec(band.shape, lambda t: (0, 0)),
             pl.BlockSpec(valid_tab.shape, lambda t: (0, 0)),
         ],
-        out_specs=pl.BlockSpec((Q_TILE, channels), lambda t: (t, 0)),
-        out_shape=jax.ShapeDtypeStruct((atoms, channels), jnp.bfloat16),
-    )(queries, padded_kv, band, valid_tab)
+        out_specs=pl.BlockSpec((HEADS, Q_TILE, head_dim), lambda t: (0, t, 0)),
+        out_shape=jax.ShapeDtypeStruct((HEADS, atoms, head_dim), jnp.bfloat16),
+    )(q_heads, k_heads, v_heads, band, valid_tab)
+    return out.transpose(1, 0, 2).reshape(atoms, channels)
 
 ROW_CHUNK = 64
 

time: 178 us -> 205 us (1.15)
  the two profiles are of different devices: /device:TPU:26 before, /device:TPU:18 now
where the time goes in v8:
time: 205 us; the launch traced here: 202 us
  Pallas kernels  91.7 us (45%)
  local copies, waits for them, and re-layouts  30.8 us (15%)
  waiting for transfers between devices  30.2 us (15%)
  matrix products  22.4 us (11%)
  starting transfers between devices  15.7 us (8%)
  other arithmetic  6.82 us (3%)
  between operations  3.97 us (2%)
    pallas_call x3, Pallas kernels, window_attend(): pl.pallas_call(attend_kernel, grid=(atoms // Q_TILE,), in_specs=[pl.Block...  56.8 us
    pallas_call x1, Pallas kernels, lddt_sums(): pl.pallas_call(lddt_kernel, grid_spec=pltpu.PrefetchScalarGridSpec(num_sc...  35 us
    ppermute x7, waiting for transfers between devices, ring_parts(): parts = jnp.concatenate([parts, lax.ppermute(parts, axis, pairs)])  24.9 us
    dot_general x12, matrix products, dense(): jnp.einsum('sac,cf->saf', left, right, preferred_element_type=jnp.float32)  17.6 us
    reshape x6, local copies, waits for them, and re-layouts, head_major(): return block.reshape(rows, HEADS, channels // HEADS).transpose(1, 0, 2)  11.7 us
    ppermute x2, starting transfers between devices, extended(): before = lax.ppermute(last, axis, up)  5.96 us
    transpose x3, local copies, waits for them, and re-layouts, window_attend(): return out.transpose(1, 0, 2).reshape(atoms, channels)  5.88 us
    ppermute x2, starting transfers between devices, extended(): after = lax.ppermute(first, axis, down)  5.73 us
  transfers between devices with their start and end apart: 11, of which 7 were waited for; matrix products, arithmetic and copies ran while one was open for 4% of the time, Pallas kernels for 0%

profile of v8, /device:TPU:18, one launch (start us, length us, event | category | flops | bytes accessed | tf_op | source)
XLA Modules:
  0.0 201.7 jit_solution(10842082795014507848)
XLA Ops:
  5.2 2.6 %fusion.96 = f32[2048,128]{1,0:T(8,128)S(1)} fusion(f32[3,128]{1,0:T(4,128)S(1)} %copy-done, f32[]{:T(128)} %bitcast.8, f32[3,2048]{1,0:T(4,128)} %param.22, f32[1,3,2048]{2,0,1:T(1,128)} %param.23, f32[]{:T(128)} %bitcast.216), kind=kOutput, calls=%fused_computation.134 | convolution fusion | flops 9455616 | bytes 1099272 | tf_op jit(solution)/shard_map/sda,dc->sac/dot_general | solution.py:232
  10.7 3.5 %collective-permute-done.3 = bf16[2,192,128]{2,1,0:T(8,128)(2,1)S(1)} collective-permute-done((bf16[2,192,128]{2,1,0:T(8,128)(2,1)S(1)}, bf16[2,192,128]{2,1,0:T(8,128)(2,1)S(1)}, u32[]{:S(2)}, u32[]{:S(2)}) %collective-permute-start.3) | collective-permute-done | bytes 98336 | tf_op jit(solution)/shard_map/ppermute | solution.py:43
  14.3 3.3 %collective-permute-done.1 = bf16[2,256,192]{1,2,0:T(8,128)(2,1)S(1)} collective-permute-done((bf16[2,256,192]{1,2,0:T(8,128)(2,1)S(1)}, bf16[2,256,192]{1,2,0:T(8,128)(2,1)S(1)}, u32[]{:S(2)}, u32[]{:S(2)}) %collective-permute-start.1) | collective-permute-done | bytes 196640 | tf_op jit(solution)/shard_map/ppermute | solution.py:43
  17.9 3.5 %collective-permute-start.4 = (bf16[16,128]{1,0:T(8,128)(2,1)S(1)}, bf16[16,128]{1,0:T(8,128)(2,1)S(1)}, u32[]{:S(2)}, u32[]{:S(2)}) collective-permute-start(bf16[16,128]{1,0:T(8,128)(2,1)S(1)} %get-tuple-element.28), channel_id=1, source_target_pairs={{0,4},{4,8},{8,12},{12,16},{16,20},{20,24},{24,28},{1,5},{5,9},{9,... | collective-permute-start | bytes 12296 | tf_op jit(solution)/shard_map/ppermute | solution.py:31
  21.4 2.4 %collective-permute-start.5 = (bf16[16,128]{1,0:T(8,128)(2,1)S(1)}, bf16[16,128]{1,0:T(8,128)(2,1)S(1)}, u32[]{:S(2)}, u32[]{:S(2)}) collective-permute-start(bf16[16,128]{1,0:T(8,128)(2,1)S(1)} %get-tuple-element.29), channel_id=1, source_target_pairs={{4,0},{8,4},{12,8},{16,12},{20,16},{24,20},{28,24},{5,1},{9,5},{13... | collective-permute-start | bytes 12296 | tf_op jit(solution)/shard_map/ppermute | solution.py:32
  24.5 3.2 %collective-permute-done.5 = bf16[16,128]{1,0:T(8,128)(2,1)S(1)} collective-permute-done((bf16[16,128]{1,0:T(8,128)(2,1)S(1)}, bf16[16,128]{1,0:T(8,128)(2,1)S(1)}, u32[]{:S(2)}, u32[]{:S(2)}) %collective-permute-start.5) | collective-permute-done | bytes 4128 | tf_op jit(solution)/shard_map/ppermute | solution.py:32
  28.6 2.5 %collective-permute-start.6 = (f32[1,176,128]{2,1,0:T(8,128)S(1)}, f32[1,176,128]{2,1,0:T(8,128)S(1)}, u32[]{:S(2)}, u32[]{:S(2)}) collective-permute-start(f32[1,176,128]{2,1,0:T(8,128)S(1)} %get-tuple-element.26), channel_id=1, source_target_pairs={{0,4},{4,8},{8,12},{12,16},{16,20},{20,24},{24,28},{1,5},{5,9},{9,... | collective-permute-start | bytes 270344 | tf_op jit(solution)/shard_map/ppermute | solution.py:31
  31.1 3.3 %collective-permute-start.7 = (f32[1,176,128]{2,1,0:T(8,128)S(1)}, f32[1,176,128]{2,1,0:T(8,128)S(1)}, u32[]{:S(2)}, u32[]{:S(2)}) collective-permute-start(f32[1,176,128]{2,1,0:T(8,128)S(1)} %get-tuple-element.27), channel_id=1, source_target_pairs={{4,0},{8,4},{12,8},{16,12},{20,16},{24,20},{28,24},{5,1},{9,5},{13... | collective-permute-start | bytes 270344 | tf_op jit(solution)/shard_map/ppermute | solution.py:32
  36.4 2.1 %collective-permute-done.7 = f32[1,176,128]{2,1,0:T(8,128)S(1)} collective-permute-done((f32[1,176,128]{2,1,0:T(8,128)S(1)}, f32[1,176,128]{2,1,0:T(8,128)S(1)}, u32[]{:S(2)}, u32[]{:S(2)}) %collective-permute-start.7) | collective-permute-done | bytes 90144 | tf_op jit(solution)/shard_map/ppermute | solution.py:32
  41.8 2.1 %copy.33 = bf16[2432,4,32]{2,0,1:T(8,128)(2,1)} copy(bf16[2432,4,32]{0,2,1:T(8,128)(2,1)S(1)} %bitcast.231) | data formatting | bytes 1245184 | tf_op jit(solution)/shard_map/reshape | solution.py:85
  44.2 2.0 copy.35
  46.5 1.9 copy.31
  48.3 19.9 %shard_map.167 = bf16[4,2304,32]{2,1,0:T(8,128)(2,1)} custom-call(bf16[4,2304,32]{2,1,0:T(8,128)(2,1)} %bitcast.223, bf16[4,2432,32]{2,1,0:T(8,128)(2,1)} %bitcast.219, bf16[4,2432,32]{2,1,0:T(8,128)(2,1)} %bitcast.220, f32[128,256]{1,0:T(8,128)} %fusion.72.band_ref, f32[18,256]{1,0:T(8,128)} %fusion.108.valid_ref), custom_call_target="tpu_custom_call" | custom-call | tf_op jit(solution)/shard_map/pallas_call | solution.py:96
  68.3 2.0 copy.36
  71.7 1.7 convolution_bitcast_fusion.1
  73.4 1.8 multiply_reduce_fusion.1
  77.3 1.9 copy.42
  79.4 1.9 copy.44
  81.6 1.8 copy.40
  83.4 18.9 %shard_map.168 = bf16[4,2176,32]{2,1,0:T(8,128)(2,1)} custom-call(bf16[4,2176,32]{2,1,0:T(8,128)(2,1)} %bitcast.227, bf16[4,2304,32]{2,1,0:T(8,128)(2,1)} %bitcast.221, bf16[4,2304,32]{2,1,0:T(8,128)(2,1)} %bitcast.222, f32[128,256]{1,0:T(8,128)} %fusion.72.band_ref, f32[17,256]{1,0:T(8,128)} %fusion.110.valid_ref), custom_call_target="tpu_custom_call" | custom-call | tf_op jit(solution)/shard_map/pallas_call | solution.py:96
  102.3 2.0 %copy.45 = bf16[2176,4,32]{0,2,1:T(8,128)(2,1)S(1)} copy(bf16[2176,4,32]{2,0,1:T(8,128)(2,1)} %bitcast.228) | data formatting | bytes 1114112 | tf_op jit(solution)/shard_map/transpose | solution.py:109
  105.0 1.7 convolution_bitcast_fusion
  106.7 1.7 multiply_reduce_fusion.3
  110.5 1.8 copy.51
  112.6 2.0 %copy.53 = bf16[2176,4,32]{2,0,1:T(8,128)(2,1)} copy(bf16[2176,4,32]{0,2,1:T(8,128)(2,1)S(1)} %bitcast.240) | data formatting | bytes 1114112 | tf_op jit(solution)/shard_map/reshape | solution.py:85
  114.9 1.8 copy.49
  116.7 17.9 %shard_map.169 = bf16[4,2048,32]{2,1,0:T(8,128)(2,1)} custom-call(bf16[4,2048,32]{2,1,0:T(8,128)(2,1)} %bitcast.229, bf16[4,2176,32]{2,1,0:T(8,128)(2,1)} %bitcast.225, bf16[4,2176,32]{2,1,0:T(8,128)(2,1)} %bitcast.226, f32[128,256]{1,0:T(8,128)} %fusion.72.band_ref, f32[16,256]{1,0:T(8,128)} %fusion.115.valid_ref), custom_call_target="tpu_custom_call" | custom-call | tf_op jit(solution)/shard_map/pallas_call | solution.py:96
  134.6 1.9 copy.54
  141.7 4.3 %collective-permute-done.8 = f32[1,7,2048]{2,1,0:T(8,128)S(1)} collective-permute-done((f32[1,7,2048]{2,1,0:T(8,128)S(1)}, f32[1,7,2048]{2,1,0:T(8,128)S(1)}, u32[]{:S(2)}, u32[]{:S(2)}) %collective-permute-start.8) | collective-permute-done | bytes 57376 | tf_op jit(solution)/shard_map/ppermute | solution.py:43
  146.9 8.0 %collective-permute-done.9 = f32[2,7,2048]{2,1,0:T(8,128)S(1)} collective-permute-done((f32[2,7,2048]{2,1,0:T(8,128)S(1)}, f32[2,7,2048]{2,1,0:T(8,128)S(1)}, u32[]{:S(2)}, u32[]{:S(2)}) %collective-permute-start.9) | collective-permute-done | bytes 114720 | tf_op jit(solution)/shard_map/ppermute | solution.py:43
  156.4 5.9 %collective-permute-done.10 = f32[4,7,2048]{2,1,0:T(8,128)S(1)} collective-permute-done((f32[4,7,2048]{2,1,0:T(8,128)S(1)}, f32[4,7,2048]{2,1,0:T(8,128)S(1)}, u32[]{:S(2)}, u32[]{:S(2)}) %collective-permute-start.10) | collective-permute-done | bytes 229408 | tf_op jit(solution)/shard_map/ppermute | solution.py:43
  163.1 35.0 %shard_map.170 = f32[2048,128]{1,0:T(8,128)} custom-call(s32[208]{0:T(256)} %reshape.416.slots_ref, s32[16]{0:T(128)} %count_ref.1, f32[2048,8]{1,0:T(8,128)} %copy.57.own_ref, f32[8,7,2048]{2,1,0:T(8,128)} %copy-done.3), custom_call_target="tpu_custom_call" | custom-call | tf_op jit(solution)/shard_map/pallas_call | solution.py:170
  (110 shorter events, 31.5 us)
Async XLA Ops:
  0.6 4.6 %copy-start = (f32[3,128]{1,0:T(4,128)S(1)}, f32[3,128]{1,0:T(4,128)}, u32[]{:S(2)}) copy-start(f32[3,128]{1,0:T(4,128)} %param.25) | copy-start | bytes 4612
  0.6 8.5 %copy-start.8 = (bf16[256,192]{0,1:T(8,128)(2,1)S(1)}, bf16[256,192]{0,1:T(8,128)(2,1)}, u32[]{:S(2)}) copy-start(bf16[256,192]{0,1:T(8,128)(2,1)} %param.18) | copy-start | bytes 294916
  0.7 7.8 %copy-start.9 = (bf16[192,128]{1,0:T(8,128)(2,1)S(1)}, bf16[192,128]{1,0:T(8,128)(2,1)}, u32[]{:S(2)}) copy-start(bf16[192,128]{1,0:T(8,128)(2,1)} %param.19) | copy-start | bytes 147460
  0.7 10.1 %copy-start.10 = (s32[2048]{0:T(1024)S(1)}, s32[2048]{0:T(1024)}, u32[]{:S(2)}) copy-start(s32[2048]{0:T(1024)} %param.21) | copy-start | bytes 24580
  0.7 8.4 %collective-permute-start = (bf16[1,256,192]{1,2,0:T(8,128)(2,1)}, bf16[1,256,192]{1,2,0:T(8,128)(2,1)S(1)}, u32[]{:S(2)}, u32[]{:S(2)}) collective-permute-start(bf16[1,256,192]{1,2,0:T(8,128)(2,1)} %bitcast.248), channel_id=1, source_target_pairs={{0,1},{1,2},{2,3},{3,0},{4,5},{5,6},{6,7},{7,4},{8,9},{9,10},{10,1... | collective-permute-start | bytes 294920 | tf_op jit(solution)/shard_map/ppermute | solution.py:43
  0.7 7.8 %collective-permute-start.2 = (bf16[1,192,128]{2,1,0:T(8,128)(2,1)}, bf16[1,192,128]{2,1,0:T(8,128)(2,1)S(1)}, u32[]{:S(2)}, u32[]{:S(2)}) collective-permute-start(bf16[1,192,128]{2,1,0:T(8,128)(2,1)} %bitcast.251), channel_id=1, source_target_pairs={{0,1},{1,2},{2,3},{3,0},{4,5},{5,6},{6,7},{7,4},{8,9},{9,10},{10,1... | collective-permute-start | bytes 147464 | tf_op jit(solution)/shard_map/ppermute | solution.py:43
  7.8 16.0 %copy-start.12 = (f32[3,2,128]{2,1,0:T(2,128)S(1)}, f32[3,2,128]{2,1,0:T(2,128)}, u32[]{:S(2)}) copy-start(f32[3,2,128]{2,1,0:T(2,128)} %param.30) | copy-start | bytes 9220
  7.8 19.9 %copy-start.5 = (bf16[2048,128]{1,0:T(8,128)(2,1)S(1)}, bf16[2048,128]{1,0:T(8,128)(2,1)}, u32[]{:S(2)}) copy-start(bf16[2048,128]{1,0:T(8,128)(2,1)} %param.20) | copy-start | bytes 1572868
  8.5 5.7 %collective-permute-start.3 = (bf16[2,192,128]{2,1,0:T(8,128)(2,1)S(1)}, bf16[2,192,128]{2,1,0:T(8,128)(2,1)S(1)}, u32[]{:S(2)}, u32[]{:S(2)}) collective-permute-start(bf16[2,192,128]{2,1,0:T(8,128)(2,1)S(1)} %pad_maximum_fusion.5), channel_id=1, source_target_pairs={{0,2},{1,3},{2,0},{3,1},{4,6},{5,7},{6,4},{7,5},{8,10},{9,11},{10,... | collective-permute-start | bytes 294920 | tf_op jit(solution)/shard_map/ppermute | solution.py:43
  9.1 8.4 %collective-permute-start.1 = (bf16[2,256,192]{1,2,0:T(8,128)(2,1)S(1)}, bf16[2,256,192]{1,2,0:T(8,128)(2,1)S(1)}, u32[]{:S(2)}, u32[]{:S(2)}) collective-permute-start(bf16[2,256,192]{1,2,0:T(8,128)(2,1)S(1)} %pad_maximum_fusion.3), channel_id=1, source_target_pairs={{0,2},{1,3},{2,0},{3,1},{4,6},{5,7},{6,4},{7,5},{8,10},{9,11},{10,... | collective-permute-start | bytes 589832 | tf_op jit(solution)/shard_map/ppermute | solution.py:43
  17.9 6.6 %collective-permute-start.4 = (bf16[16,128]{1,0:T(8,128)(2,1)S(1)}, bf16[16,128]{1,0:T(8,128)(2,1)S(1)}, u32[]{:S(2)}, u32[]{:S(2)}) collective-permute-start(bf16[16,128]{1,0:T(8,128)(2,1)S(1)} %get-tuple-element.28), channel_id=1, source_target_pairs={{0,4},{4,8},{8,12},{12,16},{16,20},{20,24},{24,28},{1,5},{5,9},{9,... | collective-permute-start | bytes 12296 | tf_op jit(solution)/shard_map/ppermute | solution.py:31
  21.4 6.4 %collective-permute-start.5 = (bf16[16,128]{1,0:T(8,128)(2,1)S(1)}, bf16[16,128]{1,0:T(8,128)(2,1)S(1)}, u32[]{:S(2)}, u32[]{:S(2)}) collective-permute-start(bf16[16,128]{1,0:T(8,128)(2,1)S(1)} %get-tuple-element.29), channel_id=1, source_target_pairs={{4,0},{8,4},{12,8},{16,12},{20,16},{24,20},{28,24},{5,1},{9,5},{13... | collective-permute-start | bytes 12296 | tf_op jit(solution)/shard_map/ppermute | solution.py:32
  24.5 9.9 %copy-start.14 = (s32[16]{0:T(128)S(1)}, s32[16]{0:T(128)}, u32[]{:S(2)}) copy-start(s32[16]{0:T(128)} %count_ref.1) | copy-start | bytes 196
  28.6 7.8 %collective-permute-start.6 = (f32[1,176,128]{2,1,0:T(8,128)S(1)}, f32[1,176,128]{2,1,0:T(8,128)S(1)}, u32[]{:S(2)}, u32[]{:S(2)}) collective-permute-start(f32[1,176,128]{2,1,0:T(8,128)S(1)} %get-tuple-element.26), channel_id=1, source_target_pairs={{0,4},{4,8},{8,12},{12,16},{16,20},{20,24},{24,28},{1,5},{5,9},{9,... | collective-permute-start | bytes 270344 | tf_op jit(solution)/shard_map/ppermute | solution.py:31
  31.1 7.3 %collective-permute-start.7 = (f32[1,176,128]{2,1,0:T(8,128)S(1)}, f32[1,176,128]{2,1,0:T(8,128)S(1)}, u32[]{:S(2)}, u32[]{:S(2)}) collective-permute-start(f32[1,176,128]{2,1,0:T(8,128)S(1)} %get-tuple-element.27), channel_id=1, source_target_pairs={{4,0},{8,4},{12,8},{16,12},{20,16},{24,20},{28,24},{5,1},{9,5},{13... | collective-permute-start | bytes 270344 | tf_op jit(solution)/shard_map/ppermute | solution.py:32
  44.2 2.0 copy-start.2
  102.3 2.1 %copy-start.7 = (bf16[3,128,128]{2,1,0:T(8,128)(2,1)S(1)}, bf16[3,128,128]{2,1,0:T(8,128)(2,1)}, u32[]{:S(2)}) copy-start(bf16[3,128,128]{2,1,0:T(8,128)(2,1)} %param.27) | copy-start | bytes 294916
  138.7 1.7 copy-start.4
  138.7 1.7 copy-start.6
  138.7 1.7 copy-start.13
  140.4 5.6 %copy-start.11 = (s32[16,13]{1,0:T(8,128)S(1)}, s32[16,13]{1,0:T(8,128)}, u32[]{:S(2)}) copy-start(s32[16,13]{1,0:T(8,128)} %param.32) | copy-start | bytes 2500
  141.7 4.3 %collective-permute-start.8 = (f32[1,7,2048]{2,1,0:T(8,128)S(1)}, f32[1,7,2048]{2,1,0:T(8,128)S(1)}, u32[]{:S(2)}, u32[]{:S(2)}) collective-permute-start(f32[1,7,2048]{2,1,0:T(8,128)S(1)} %fusion.84), channel_id=1, source_target_pairs={{0,4},{4,8},{8,12},{12,16},{16,20},{20,24},{24,28},{28,0},{1,5},{5... | collective-permute-start | bytes 172040 | tf_op jit(solution)/shard_map/ppermute | solution.py:43
  146.0 8.9 %collective-permute-start.9 = (f32[2,7,2048]{2,1,0:T(8,128)S(1)}, f32[2,7,2048]{2,1,0:T(8,128)S(1)}, u32[]{:S(2)}, u32[]{:S(2)}) collective-permute-start(f32[2,7,2048]{2,1,0:T(8,128)S(1)} %pad_maximum_fusion.4), channel_id=1, source_target_pairs={{0,8},{4,12},{8,16},{12,20},{16,24},{20,28},{24,0},{28,4},{1,9},{5... | collective-permute-start | bytes 344072 | tf_op jit(solution)/shard_map/ppermute | solution.py:43
  154.9 7.3 %collective-permute-start.10 = (f32[4,7,2048]{2,1,0:T(8,128)S(1)}, f32[4,7,2048]{2,1,0:T(8,128)S(1)}, u32[]{:S(2)}, u32[]{:S(2)}) collective-permute-start(f32[4,7,2048]{2,1,0:T(8,128)S(1)} %pad_maximum_fusion.2), channel_id=1, source_target_pairs={{0,16},{4,20},{8,24},{12,28},{16,0},{20,4},{24,8},{28,12},{1,17},{... | collective-permute-start | bytes 688136 | tf_op jit(solution)/shard_map/ppermute | solution.py:43
  162.3 0.8 copy-start.3
  198.7 2.9 %copy-start.1 = (f32[3,128]{1,0:T(4,128)S(1)}, f32[3,128]{1,0:T(4,128)}, u32[]{:S(2)}) copy-start(f32[3,128]{1,0:T(4,128)} %param.25) | copy-start | bytes 4612

commit v9 on v7

--- a/solution.py
+++ b/solution.py
@@ -34,11 +34,11 @@
     return value
 
 
-def ring_parts(value, axis):
+def ring_parts(value, axis, direct=False):
     peers = lax.axis_size(axis)
     parts = value[None]
     span = 1
-    while span < peers and peers % (2 * span) == 0:
+    while not direct and span < peers and peers % (2 * span) == 0:
         pairs = [(i, (i + span) % peers) for i in range(peers)]
         parts = jnp.concatenate([parts, lax.ppermute(parts, axis, pairs)])
         span *= 2
@@ -207,8 +207,8 @@
     atom_rows = atom_single.shape[0]
     total_atoms = atom_rows * lax.axis_size("atoms")
     samples = noise.shape[0]
-    feat_parts = ring_parts(token_feats, "samples")
-    proj_parts = ring_parts(proj_w, "samples")
+    feat_parts = ring_parts(token_feats, "samples", direct=True)
+    proj_parts = ring_parts(proj_w, "samples", direct=True)
     token_sum = jnp.einsum(
         "kti,kio->to", feat_parts, proj_parts, preferred_element_type=jnp.float32
     )

time: 178 us -> 176 us (0.989); the launches traced: 175 us -> 175 us
    ppermute x0 -> x6, starting transfers between devices: none -> 5 us  [ring_parts(): extra.append(lax.ppermute(value, axis, pairs)[None])]
    ppermute x7 -> x3, waiting for transfers between devices: 15.7 us -> 11.2 us  [ring_parts(): parts = jnp.concatenate([parts, lax.ppermute(parts, axis, pairs)])]
    ppermute x7 -> x3, starting transfers between devices: 14 us -> 10.3 us  [ring_parts(): parts = jnp.concatenate([parts, lax.ppermute(parts, axis, pairs)])]
  transfers between devices with their start and end apart: 11 -> 13, of which waited for: 6 -> 6; matrix products, arithmetic and copies ran while one was open for 5% -> 5% of each run, Pallas kernels for 0% -> 0%
where the time goes in v9:
time: 176 us; the launch traced here: 175 us
  Pallas kernels  95.3 us (54%)
  starting transfers between devices  27.4 us (16%)
  matrix products  17.6 us (10%)
  waiting for transfers between devices  14.6 us (8%)
  local copies, waits for them, and re-layouts  9.89 us (6%)
  other arithmetic  6.75 us (4%)
  between operations  3.78 us (2%)
    pallas_call x3, Pallas kernels, window_attend(): pl.pallas_call(attend_kernel, grid=(atoms // Q_TILE,), in_specs=[pl.Block...  58.1 us
    pallas_call x1, Pallas kernels, lddt_sums(): pl.pallas_call(lddt_kernel, grid_spec=pltpu.PrefetchScalarGridSpec(num_sc...  37.3 us
    dot_general x12, matrix products, dense(): jnp.einsum('sac,cf->saf', left, right, preferred_element_type=jnp.float32)  12.7 us
    ppermute x3, waiting for transfers between devices, ring_parts(): parts = jnp.concatenate([parts, lax.ppermute(parts, axis, pairs)])  11.2 us
    ppermute x3, starting transfers between devices, ring_parts(): parts = jnp.concatenate([parts, lax.ppermute(parts, axis, pairs)])  10.3 us
    ppermute x2, starting transfers between devices, extended(): after = lax.ppermute(first, axis, down)  9.54 us
    ppermute x6, starting transfers between devices, ring_parts(): extra.append(lax.ppermute(value, axis, pairs)[None])  5 us
  transfers between devices with their start and end apart: 13, of which 6 were waited for; matrix products, arithmetic and copies ran while one was open for 5% of the time, Pallas kernels for 0%

profile of v9, /device:TPU:26, one launch (start us, length us, event | category | flops | bytes accessed | tf_op | source)
XLA Modules:
  0.0 175.3 jit_solution(14261506233096481317)
XLA Ops:
  0.7 1.6 collective-permute-start.1
  2.3 1.4 collective-permute-start.2
  7.1 2.6 %fusion.100 = f32[2048,128]{1,0:T(8,128)S(1)} fusion(f32[3,128]{1,0:T(4,128)S(1)} %copy-done, f32[]{:T(128)} %bitcast.14, f32[3,2048]{1,0:T(4,128)} %param.22, f32[1,3,2048]{2,0,1:T(1,128)} %param.23, f32[]{:T(128)} %bitcast.204), kind=kOutput, calls=%fused_computation.139 | convolution fusion | flops 9455616 | bytes 1099272 | tf_op jit(solution)/shard_map/sda,dc->sac/dot_general | solution.py:229
  10.4 1.4 collective-permute-start.5
  11.8 1.7 collective-permute-done.5
  13.9 1.3 collective-permute-start.6
  15.2 4.5 %collective-permute-start.7 = (bf16[16,128]{1,0:T(8,128)(2,1)S(1)}, bf16[16,128]{1,0:T(8,128)(2,1)S(1)}, u32[]{:S(2)}, u32[]{:S(2)}) collective-permute-start(bf16[16,128]{1,0:T(8,128)(2,1)S(1)} %get-tuple-element.21), channel_id=1, source_target_pairs={{4,0},{8,4},{12,8},{16,12},{20,16},{24,20},{28,24},{5,1},{9,5},{13... | collective-permute-start | bytes 12296 | tf_op jit(solution)/shard_map/ppermute | solution.py:32
  22.0 1.3 collective-permute-start.8
  23.3 5.0 %collective-permute-start.9 = (f32[1,176,128]{2,1,0:T(8,128)S(1)}, f32[1,176,128]{2,1,0:T(8,128)S(1)}, u32[]{:S(2)}, u32[]{:S(2)}) collective-permute-start(f32[1,176,128]{2,1,0:T(8,128)S(1)} %get-tuple-element.19), channel_id=1, source_target_pairs={{4,0},{8,4},{12,8},{16,12},{20,16},{24,20},{28,24},{5,1},{9,5},{13... | collective-permute-start | bytes 270344 | tf_op jit(solution)/shard_map/ppermute | solution.py:32
  30.1 1.1 collective-permute-done.9
  31.6 1.6 fusion.2
  33.2 1.1 fusion.17.kv_ref
  34.4 0.9 slice_bitcast_fusion.q_ref
  35.3 20.4 %shard_map.167 = bf16[2304,128]{1,0:T(8,128)(2,1)} custom-call(bf16[2304,128]{1,0:T(8,128)(2,1)} %slice_bitcast_fusion.q_ref, bf16[2432,256]{1,0:T(8,128)(2,1)} %fusion.17.kv_ref, f32[128,256]{1,0:T(8,128)} %fusion.76.band_ref, f32[18,256]{1,0:T(8,128)} %fusion.112.valid_ref), custom_call_target="tpu_custom_call" | custom-call | tf_op jit(solution)/shard_map/pallas_call | solution.py:95
  55.7 1.7 multiply_reduce_fusion.2
  58.3 0.9 multiply_reduce_fusion.1
  60.0 1.1 fusion.20.kv_ref
  61.9 19.3 %shard_map.168 = bf16[2176,128]{1,0:T(8,128)(2,1)} custom-call(bf16[2176,128]{1,0:T(8,128)(2,1)} %slice_bitcast_fusion.1.q_ref, bf16[2304,256]{1,0:T(8,128)(2,1)} %fusion.20.kv_ref, f32[128,256]{1,0:T(8,128)} %fusion.76.band_ref, f32[17,256]{1,0:T(8,128)} %fusion.114.valid_ref), custom_call_target="tpu_custom_call" | custom-call | tf_op jit(solution)/shard_map/pallas_call | solution.py:95
  81.3 1.6 multiply_reduce_fusion.4
  85.2 1.1 fusion.24.kv_ref
  87.2 18.3 %shard_map.169 = bf16[2048,128]{1,0:T(8,128)(2,1)} custom-call(bf16[2048,128]{1,0:T(8,128)(2,1)} %slice_bitcast_fusion.2.q_ref, bf16[2176,256]{1,0:T(8,128)(2,1)} %fusion.24.kv_ref, f32[128,256]{1,0:T(8,128)} %fusion.76.band_ref, f32[16,256]{1,0:T(8,128)} %fusion.119.valid_ref), custom_call_target="tpu_custom_call" | custom-call | tf_op jit(solution)/shard_map/pallas_call | solution.py:95
  105.5 1.5 multiply_reduce_fusion.6
  108.7 1.2 fusion.14
  109.9 3.5 %collective-permute-start.10 = (f32[1,7,2048]{2,1,0:T(8,128)S(1)}, f32[1,7,2048]{2,1,0:T(8,128)S(1)}, u32[]{:S(2)}, u32[]{:S(2)}) collective-permute-start(f32[1,7,2048]{2,1,0:T(8,128)S(1)} %fusion.88), channel_id=1, source_target_pairs={{0,4},{4,8},{8,12},{12,16},{16,20},{20,24},{24,28},{28,0},{1,5},{5... | collective-permute-start | bytes 172040 | tf_op jit(solution)/shard_map/ppermute | solution.py:43
  113.4 1.9 %collective-permute-done.10 = f32[1,7,2048]{2,1,0:T(8,128)S(1)} collective-permute-done((f32[1,7,2048]{2,1,0:T(8,128)S(1)}, f32[1,7,2048]{2,1,0:T(8,128)S(1)}, u32[]{:S(2)}, u32[]{:S(2)}) %collective-permute-start.10) | collective-permute-done | bytes 57376 | tf_op jit(solution)/shard_map/ppermute | solution.py:43
  115.3 2.5 %collective-permute-start.11 = (f32[2,7,2048]{2,1,0:T(8,128)S(1)}, f32[2,7,2048]{2,1,0:T(8,128)S(1)}, u32[]{:S(2)}, u32[]{:S(2)}) collective-permute-start(f32[2,7,2048]{2,1,0:T(8,128)S(1)} %pad_maximum_fusion.3), channel_id=1, source_target_pairs={{0,8},{4,12},{8,16},{12,20},{16,24},{20,28},{24,0},{28,4},{1,9},{5... | collective-permute-start | bytes 344072 | tf_op jit(solution)/shard_map/ppermute | solution.py:43
  118.6 2.4 %collective-permute-done.11 = f32[2,7,2048]{2,1,0:T(8,128)S(1)} collective-permute-done((f32[2,7,2048]{2,1,0:T(8,128)S(1)}, f32[2,7,2048]{2,1,0:T(8,128)S(1)}, u32[]{:S(2)}, u32[]{:S(2)}) %collective-permute-start.11) | collective-permute-done | bytes 114720 | tf_op jit(solution)/shard_map/ppermute | solution.py:43
  121.0 4.4 %collective-permute-start.12 = (f32[4,7,2048]{2,1,0:T(8,128)S(1)}, f32[4,7,2048]{2,1,0:T(8,128)S(1)}, u32[]{:S(2)}, u32[]{:S(2)}) collective-permute-start(f32[4,7,2048]{2,1,0:T(8,128)S(1)} %pad_maximum_fusion.2), channel_id=1, source_target_pairs={{0,16},{4,20},{8,24},{12,28},{16,0},{20,4},{24,8},{28,12},{1,17},{... | collective-permute-start | bytes 688136 | tf_op jit(solution)/shard_map/ppermute | solution.py:43
  125.5 1.3 copy.25.own_ref
  126.8 6.8 %collective-permute-done.12 = f32[4,7,2048]{2,1,0:T(8,128)S(1)} collective-permute-done((f32[4,7,2048]{2,1,0:T(8,128)S(1)}, f32[4,7,2048]{2,1,0:T(8,128)S(1)}, u32[]{:S(2)}, u32[]{:S(2)}) %collective-permute-start.12) | collective-permute-done | bytes 229408 | tf_op jit(solution)/shard_map/ppermute | solution.py:43
  134.5 37.3 %shard_map.170 = f32[2048,128]{1,0:T(8,128)} custom-call(s32[208]{0:T(256)} %reshape.383.slots_ref, s32[16]{0:T(128)} %count_ref.1, f32[2048,8]{1,0:T(8,128)} %copy.25.own_ref, f32[8,7,2048]{2,1,0:T(8,128)} %copy-done.1), custom_call_target="tpu_custom_call" | custom-call | tf_op jit(solution)/shard_map/pallas_call | solution.py:167
  172.4 1.3 slice_multiply_fusion.3
  (90 shorter events, 17.5 us)
Async XLA Ops:
  0.6 6.5 %copy-start = (f32[3,128]{1,0:T(4,128)S(1)}, f32[3,128]{1,0:T(4,128)}, u32[]{:S(2)}) copy-start(f32[3,128]{1,0:T(4,128)} %param.25) | copy-start | bytes 4612
  0.6 13.0 %copy-start.14 = (bf16[256,192]{0,1:T(8,128)(2,1)S(1)}, bf16[256,192]{0,1:T(8,128)(2,1)}, u32[]{:S(2)}) copy-start(bf16[256,192]{0,1:T(8,128)(2,1)} %param.18) | copy-start | bytes 294916
  0.7 9.7 %copy-start.15 = (bf16[192,128]{1,0:T(8,128)(2,1)S(1)}, bf16[192,128]{1,0:T(8,128)(2,1)}, u32[]{:S(2)}) copy-start(bf16[192,128]{1,0:T(8,128)(2,1)} %param.19) | copy-start | bytes 147460
  0.7 11.2 %copy-start.8 = (s32[2048]{0:T(1024)S(1)}, s32[2048]{0:T(1024)}, u32[]{:S(2)}) copy-start(s32[2048]{0:T(1024)} %param.21) | copy-start | bytes 24580
  0.7 12.9 %collective-permute-start = (bf16[256,192]{0,1:T(8,128)(2,1)}, bf16[256,192]{0,1:T(8,128)(2,1)S(1)}, u32[]{:S(2)}, u32[]{:S(2)}) collective-permute-start(bf16[256,192]{0,1:T(8,128)(2,1)} %param.18), channel_id=1, source_target_pairs={{0,1},{1,2},{2,3},{3,0},{4,5},{5,6},{6,7},{7,4},{8,9},{9,10},{10,1... | collective-permute-start | bytes 294920 | tf_op jit(solution)/shard_map/ppermute | solution.py:49
  0.7 12.9 %collective-permute-start.1 = (bf16[256,192]{0,1:T(8,128)(2,1)}, bf16[256,192]{0,1:T(8,128)(2,1)S(1)}, u32[]{:S(2)}, u32[]{:S(2)}) collective-permute-start(bf16[256,192]{0,1:T(8,128)(2,1)} %param.18), channel_id=1, source_target_pairs={{0,2},{1,3},{2,0},{3,1},{4,6},{5,7},{6,4},{7,5},{8,10},{9,11},{10,... | collective-permute-start | bytes 294920 | tf_op jit(solution)/shard_map/ppermute | solution.py:49
  2.3 11.3 %collective-permute-start.2 = (bf16[256,192]{0,1:T(8,128)(2,1)}, bf16[256,192]{0,1:T(8,128)(2,1)S(1)}, u32[]{:S(2)}, u32[]{:S(2)}) collective-permute-start(bf16[256,192]{0,1:T(8,128)(2,1)} %param.18), channel_id=1, source_target_pairs={{0,3},{1,0},{2,1},{3,2},{4,7},{5,4},{6,5},{7,6},{8,11},{9,8},{10,9... | collective-permute-start | bytes 294920 | tf_op jit(solution)/shard_map/ppermute | solution.py:49
  3.7 6.7 %collective-permute-start.3 = (bf16[192,128]{1,0:T(8,128)(2,1)}, bf16[192,128]{1,0:T(8,128)(2,1)S(1)}, u32[]{:S(2)}, u32[]{:S(2)}) collective-permute-start(bf16[192,128]{1,0:T(8,128)(2,1)} %param.19), channel_id=1, source_target_pairs={{0,1},{1,2},{2,3},{3,0},{4,5},{5,6},{6,7},{7,4},{8,9},{9,10},{10,1... | collective-permute-start | bytes 147464 | tf_op jit(solution)/shard_map/ppermute | solution.py:49
  3.7 8.1 %collective-permute-start.4 = (bf16[192,128]{1,0:T(8,128)(2,1)}, bf16[192,128]{1,0:T(8,128)(2,1)S(1)}, u32[]{:S(2)}, u32[]{:S(2)}) collective-permute-start(bf16[192,128]{1,0:T(8,128)(2,1)} %param.19), channel_id=1, source_target_pairs={{0,2},{1,3},{2,0},{3,1},{4,6},{5,7},{6,4},{7,5},{8,10},{9,11},{10,... | collective-permute-start | bytes 147464 | tf_op jit(solution)/shard_map/ppermute | solution.py:49
  9.7 10.1 %copy-start.10 = (f32[3,2,128]{2,1,0:T(2,128)S(1)}, f32[3,2,128]{2,1,0:T(2,128)}, u32[]{:S(2)}) copy-start(f32[3,2,128]{2,1,0:T(2,128)} %param.30) | copy-start | bytes 9220
  9.7 11.4 %copy-start.3 = (bf16[2048,128]{1,0:T(8,128)(2,1)S(1)}, bf16[2048,128]{1,0:T(8,128)(2,1)}, u32[]{:S(2)}) copy-start(bf16[2048,128]{1,0:T(8,128)(2,1)} %param.20) | copy-start | bytes 1572868
  10.4 3.2 %collective-permute-start.5 = (bf16[192,128]{1,0:T(8,128)(2,1)S(1)}, bf16[192,128]{1,0:T(8,128)(2,1)S(1)}, u32[]{:S(2)}, u32[]{:S(2)}) collective-permute-start(bf16[192,128]{1,0:T(8,128)(2,1)S(1)} %copy-done.15), channel_id=1, source_target_pairs={{0,3},{1,0},{2,1},{3,2},{4,7},{5,4},{6,5},{7,6},{8,11},{9,8},{10,9... | collective-permute-start | bytes 147464 | tf_op jit(solution)/shard_map/ppermute | solution.py:49
  13.9 6.6 %collective-permute-start.6 = (bf16[16,128]{1,0:T(8,128)(2,1)S(1)}, bf16[16,128]{1,0:T(8,128)(2,1)S(1)}, u32[]{:S(2)}, u32[]{:S(2)}) collective-permute-start(bf16[16,128]{1,0:T(8,128)(2,1)S(1)} %get-tuple-element.20), channel_id=1, source_target_pairs={{0,4},{4,8},{8,12},{12,16},{16,20},{20,24},{24,28},{1,5},{5,9},{9,... | collective-permute-start | bytes 12296 | tf_op jit(solution)/shard_map/ppermute | solution.py:31
  15.2 5.9 %collective-permute-start.7 = (bf16[16,128]{1,0:T(8,128)(2,1)S(1)}, bf16[16,128]{1,0:T(8,128)(2,1)S(1)}, u32[]{:S(2)}, u32[]{:S(2)}) collective-permute-start(bf16[16,128]{1,0:T(8,128)(2,1)S(1)} %get-tuple-element.21), channel_id=1, source_target_pairs={{4,0},{8,4},{12,8},{16,12},{20,16},{24,20},{28,24},{5,1},{9,5},{13... | collective-permute-start | bytes 12296 | tf_op jit(solution)/shard_map/ppermute | solution.py:32
  20.6 7.7 %copy-start.12 = (s32[16]{0:T(128)S(1)}, s32[16]{0:T(128)}, u32[]{:S(2)}) copy-start(s32[16]{0:T(128)} %count_ref.1) | copy-start | bytes 196
  22.0 8.1 %collective-permute-start.8 = (f32[1,176,128]{2,1,0:T(8,128)S(1)}, f32[1,176,128]{2,1,0:T(8,128)S(1)}, u32[]{:S(2)}, u32[]{:S(2)}) collective-permute-start(f32[1,176,128]{2,1,0:T(8,128)S(1)} %get-tuple-element.18), channel_id=1, source_target_pairs={{0,4},{4,8},{8,12},{12,16},{16,20},{20,24},{24,28},{1,5},{5,9},{9,... | collective-permute-start | bytes 270344 | tf_op jit(solution)/shard_map/ppermute | solution.py:31
  23.3 8.0 %collective-permute-start.9 = (f32[1,176,128]{2,1,0:T(8,128)S(1)}, f32[1,176,128]{2,1,0:T(8,128)S(1)}, u32[]{:S(2)}, u32[]{:S(2)}) collective-permute-start(f32[1,176,128]{2,1,0:T(8,128)S(1)} %get-tuple-element.19), channel_id=1, source_target_pairs={{4,0},{8,4},{12,8},{16,12},{20,16},{24,20},{28,24},{5,1},{9,5},{13... | collective-permute-start | bytes 270344 | tf_op jit(solution)/shard_map/ppermute | solution.py:32
  35.3 20.4 %copy-start.7 = (bf16[3,128,128]{2,1,0:T(8,128)(2,1)S(1)}, bf16[3,128,128]{2,1,0:T(8,128)(2,1)}, u32[]{:S(2)}) copy-start(bf16[3,128,128]{2,1,0:T(8,128)(2,1)} %param.27) | copy-start | bytes 294916
  55.7 1.7 copy-start.4
  57.4 0.9 copy-start.13
  58.3 1.0 copy-start.5
  107.8 0.9 copy-start.2
  107.8 0.9 copy-start.6
  107.8 0.9 copy-start.11
  108.6 9.1 %copy-start.9 = (s32[16,13]{1,0:T(8,128)S(1)}, s32[16,13]{1,0:T(8,128)}, u32[]{:S(2)}) copy-start(s32[16,13]{1,0:T(8,128)} %param.32) | copy-start | bytes 2500
  109.9 5.4 %collective-permute-start.10 = (f32[1,7,2048]{2,1,0:T(8,128)S(1)}, f32[1,7,2048]{2,1,0:T(8,128)S(1)}, u32[]{:S(2)}, u32[]{:S(2)}) collective-permute-start(f32[1,7,2048]{2,1,0:T(8,128)S(1)} %fusion.88), channel_id=1, source_target_pairs={{0,4},{4,8},{8,12},{12,16},{16,20},{20,24},{24,28},{28,0},{1,5},{5... | collective-permute-start | bytes 172040 | tf_op jit(solution)/shard_map/ppermute | solution.py:43
  115.3 5.7 %collective-permute-start.11 = (f32[2,7,2048]{2,1,0:T(8,128)S(1)}, f32[2,7,2048]{2,1,0:T(8,128)S(1)}, u32[]{:S(2)}, u32[]{:S(2)}) collective-permute-start(f32[2,7,2048]{2,1,0:T(8,128)S(1)} %pad_maximum_fusion.3), channel_id=1, source_target_pairs={{0,8},{4,12},{8,16},{12,20},{16,24},{20,28},{24,0},{28,4},{1,9},{5... | collective-permute-start | bytes 344072 | tf_op jit(solution)/shard_map/ppermute | solution.py:43
  121.0 12.6 %collective-permute-start.12 = (f32[4,7,2048]{2,1,0:T(8,128)S(1)}, f32[4,7,2048]{2,1,0:T(8,128)S(1)}, u32[]{:S(2)}, u32[]{:S(2)}) collective-permute-start(f32[4,7,2048]{2,1,0:T(8,128)S(1)} %pad_maximum_fusion.2), channel_id=1, source_target_pairs={{0,16},{4,20},{8,24},{12,28},{16,0},{20,4},{24,8},{28,12},{1,17},{... | collective-permute-start | bytes 688136 | tf_op jit(solution)/shard_map/ppermute | solution.py:43
  133.7 0.8 copy-start.1

commit v10 on v7

--- a/solution.py
+++ b/solution.py
@@ -108,9 +108,10 @@
 ROW_CHUNK = 64
 
 
-def lddt_kernel(slots_ref, count_ref, own_ref, coord_ref, out_ref, cols_ref):
+def lddt_kernel(slots_ref, lo_ref, count_ref, own_ref, coord_ref, out_ref, cols_ref):
     block = pl.program_id(0)
     live = count_ref[block]
+    first = lo_ref[block]
     blocks = count_ref.shape[0]
     max_slots = slots_ref.shape[0] // blocks
     shape = (ROW_CHUNK, PAIR_BLK)
@@ -153,7 +154,7 @@
             return tuple(acc + coef * gap for acc, gap in zip(accs, gaps))
 
         zero = jnp.zeros(shape, jnp.float32)
-        accs = lax.fori_loop(0, live, slot_body, (zero, zero, zero))
+        accs = lax.fori_loop(first, live, slot_body, (zero, zero, zero))
         sums = [-0.25 * jnp.sum(acc, axis=1, keepdims=True) for acc in accs]
         tile = jnp.where(lane == 0, sums[0], jnp.where(lane == 1, sums[1], jnp.where(lane == 2, sums[2], 0.0)))
         out_ref[pl.ds(row, ROW_CHUNK), :] = tile
@@ -162,12 +163,12 @@
     lax.fori_loop(0, PAIR_BLK // ROW_CHUNK, row_body, 0)
 
 
-def lddt_sums(slots, counts, own_tab, coord_parts):
+def lddt_sums(slots, lows, counts, own_tab, coord_parts):
     blocks = counts.shape[0]
     out = pl.pallas_call(
         lddt_kernel,
         grid_spec=pltpu.PrefetchScalarGridSpec(
-            num_scalar_prefetch=2,
+            num_scalar_prefetch=3,
             grid=(blocks,),
             in_specs=[
                 pl.BlockSpec((PAIR_BLK, own_tab.shape[1]), lambda b, *_: (b, 0)),
@@ -177,7 +178,7 @@
             scratch_shapes=[pltpu.VMEM((6, PAIR_BLK, PAIR_BLK), jnp.float32)],
         ),
         out_shape=jax.ShapeDtypeStruct((blocks * PAIR_BLK, PAIR_BLK), jnp.float32),
-    )(slots, counts, own_tab, coord_parts)
+    )(slots, lows, counts, own_tab, coord_parts)
     return out[:, :3].T
 
 def dense(left, right):
@@ -287,8 +288,20 @@
         [predicted[0], true_coords, jnp.zeros((2, atom_rows), jnp.float32)], axis=0
     ).T
     source = (atom_rank - pair_blocks // block_count) % atom_peers
-    slots = (source * block_count + pair_blocks % block_count).reshape(-1)
-    pair_grad = 2.0 * lddt_sums(slots, pair_count, own_tab, coord_parts)[None]
+    slot_ids = jnp.arange(pair_blocks.shape[1], dtype=jnp.int32)[None, :]
+    live_slot = slot_ids < pair_count[:, None]
+    order = jnp.argsort(
+        jnp.where(live_slot, (source != 0).astype(jnp.int32), 2) * pair_blocks.shape[1] + slot_ids,
+        axis=1,
+    )
+    slots = jnp.take_along_axis(source * block_count + pair_blocks % block_count, order, axis=1)
+    slots = slots.reshape(-1)
+    local_count = jnp.sum((live_slot & (source == 0)).astype(jnp.int32), axis=1)
+    no_slots = jnp.zeros_like(pair_count)
+    own_coords = jnp.concatenate([predicted[0], true_coords, count_row], axis=0)[None]
+    near = lddt_sums(slots, no_slots, local_count, own_tab, own_coords)
+    far = lddt_sums(slots, local_count, pair_count, own_tab, coord_parts)
+    pair_grad = 2.0 * (near + far)[None]
     lddt_grad = total_atoms * PAIR_BLK / pair_total * pair_grad.reshape(samples, 3, atom_rows)
     coord_grad = mse_part - lddt_grad / PAIR_BLK
     return (coord_grad, lddt_grad)

time: 178 us -> 193 us (1.084)
  Pallas kernels: 94.7 us -> 108 us
  local copies, waits for them, and re-layouts: 9.85 us -> 16.2 us
  waiting for transfers between devices: 16.3 us -> 10.2 us
  other arithmetic: 6.82 us -> 10 us
    pallas_call x1 -> x2, Pallas kernels: 36.6 us -> 49.5 us  [lddt_sums(): pl.pallas_call(lddt_kernel, grid_spec=pltpu.PrefetchScalarGridSpec(num_sc...]
    ppermute x7, waiting for transfers between devices: 15.7 us -> 10.2 us  [ring_parts(): parts = jnp.concatenate([parts, lax.ppermute(parts, axis, pairs)])]
    gather x0 -> x3, local copies, waits for them, and re-layouts: none -> 2.94 us  [on_device(): jnp.take_along_axis(source * block_count + pair_blocks % block_count, ord...]
    unnamed x35 -> x36, local copies, waits for them, and re-layouts: 1.9 us -> 4.54 us
  transfers between devices with their start and end apart: 11 -> 11, of which waited for: 6 -> 3; matrix products, arithmetic and copies ran while one was open for 5% -> 9% of each run, Pallas kernels for 0% -> 9%
where the time goes in v10:
time: 193 us; the launch traced here: 191 us
  Pallas kernels  108 us (56%)
  starting transfers between devices  25.6 us (13%)
  matrix products  17.6 us (9%)
  local copies, waits for them, and re-layouts  16.2 us (8%)
  waiting for transfers between devices  10.2 us (5%)
  other arithmetic  10 us (5%)
  between operations  3.95 us (2%)
    pallas_call x3, Pallas kernels, window_attend(): pl.pallas_call(attend_kernel, grid=(atoms // Q_TILE,), in_specs=[pl.Block...  58.1 us
    pallas_call x2, Pallas kernels, lddt_sums(): pl.pallas_call(lddt_kernel, grid_spec=pltpu.PrefetchScalarGridSpec(num_sc...  49.5 us
    ppermute x7, starting transfers between devices, ring_parts(): parts = jnp.concatenate([parts, lax.ppermute(parts, axis, pairs)])  13.7 us
    dot_general x12, matrix products, dense(): jnp.einsum('sac,cf->saf', left, right, preferred_element_type=jnp.float32)  12.7 us
    ppermute x7, waiting for transfers between devices, ring_parts(): parts = jnp.concatenate([parts, lax.ppermute(parts, axis, pairs)])  10.2 us
    ppermute x2, starting transfers between devices, extended(): after = lax.ppermute(first, axis, down)  9.28 us
    unnamed x36, local copies, waits for them, and re-layouts  4.54 us
  transfers between devices with their start and end apart: 11, of which 3 were waited for; matrix products, arithmetic and copies ran while one was open for 9% of the time, Pallas kernels for 9%

profile of v10, /device:TPU:26, one launch (start us, length us, event | category | flops | bytes accessed | tf_op | source)
XLA Modules:
  0.0 191.1 jit_solution(4713988088977035852)
XLA Ops:
  0.7 1.6 collective-permute-start.2
  4.5 1.4 convert_reduce_fusion
  7.4 2.6 %fusion.96 = f32[2048,128]{1,0:T(8,128)S(1)} fusion(f32[3,128]{1,0:T(4,128)S(1)} %copy-done, f32[]{:T(128)} %bitcast.8, f32[3,2048]{1,0:T(4,128)} %param.22, f32[1,3,2048]{2,0,1:T(1,128)} %param.23, f32[]{:T(128)} %bitcast.205), kind=kOutput, calls=%fused_computation.137 | convolution fusion | flops 9455616 | bytes 1099272 | tf_op jit(solution)/shard_map/sda,dc->sac/dot_general | solution.py:230
  11.3 1.6 collective-permute-start.1
  12.9 3.5 %collective-permute-done.3 = bf16[2,192,128]{2,1,0:T(8,128)(2,1)S(1)} collective-permute-done((bf16[2,192,128]{2,1,0:T(8,128)(2,1)S(1)}, bf16[2,192,128]{2,1,0:T(8,128)(2,1)S(1)}, u32[]{:S(2)}, u32[]{:S(2)}) %collective-permute-start.3) | collective-permute-done | bytes 98336 | tf_op jit(solution)/shard_map/ppermute | solution.py:43
  16.5 3.3 %collective-permute-done.1 = bf16[2,256,192]{1,2,0:T(8,128)(2,1)S(1)} collective-permute-done((bf16[2,256,192]{1,2,0:T(8,128)(2,1)S(1)}, bf16[2,256,192]{1,2,0:T(8,128)(2,1)S(1)}, u32[]{:S(2)}, u32[]{:S(2)}) %collective-permute-start.1) | collective-permute-done | bytes 196640 | tf_op jit(solution)/shard_map/ppermute | solution.py:43
  20.1 1.3 collective-permute-start.4
  21.4 4.5 %collective-permute-start.5 = (bf16[16,128]{1,0:T(8,128)(2,1)S(1)}, bf16[16,128]{1,0:T(8,128)(2,1)S(1)}, u32[]{:S(2)}, u32[]{:S(2)}) collective-permute-start(bf16[16,128]{1,0:T(8,128)(2,1)S(1)} %get-tuple-element.27), channel_id=1, source_target_pairs={{4,0},{8,4},{12,8},{16,12},{20,16},{24,20},{28,24},{5,1},{9,5},{13... | collective-permute-start | bytes 12296 | tf_op jit(solution)/shard_map/ppermute | solution.py:32
  28.5 1.3 collective-permute-start.6
  29.8 4.7 %collective-permute-start.7 = (f32[1,176,128]{2,1,0:T(8,128)S(1)}, f32[1,176,128]{2,1,0:T(8,128)S(1)}, u32[]{:S(2)}, u32[]{:S(2)}) collective-permute-start(f32[1,176,128]{2,1,0:T(8,128)S(1)} %get-tuple-element.25), channel_id=1, source_target_pairs={{4,0},{8,4},{12,8},{16,12},{20,16},{24,20},{28,24},{5,1},{9,5},{13... | collective-permute-start | bytes 270344 | tf_op jit(solution)/shard_map/ppermute | solution.py:32
  37.0 1.6 fusion.2
  38.6 1.1 fusion.17.kv_ref
  40.6 20.4 %shard_map.167 = bf16[2304,128]{1,0:T(8,128)(2,1)} custom-call(bf16[2304,128]{1,0:T(8,128)(2,1)} %slice_bitcast_fusion.q_ref, bf16[2432,256]{1,0:T(8,128)(2,1)} %fusion.17.kv_ref, f32[128,256]{1,0:T(8,128)} %fusion.72.band_ref, f32[18,256]{1,0:T(8,128)} %fusion.108.valid_ref), custom_call_target="tpu_custom_call" | custom-call | tf_op jit(solution)/shard_map/pallas_call | solution.py:95
  61.1 1.6 multiply_reduce_fusion.2
  65.3 1.1 fusion.20.kv_ref
  67.3 19.3 %shard_map.168 = bf16[2176,128]{1,0:T(8,128)(2,1)} custom-call(bf16[2176,128]{1,0:T(8,128)(2,1)} %slice_bitcast_fusion.1.q_ref, bf16[2304,256]{1,0:T(8,128)(2,1)} %fusion.20.kv_ref, f32[128,256]{1,0:T(8,128)} %fusion.72.band_ref, f32[17,256]{1,0:T(8,128)} %fusion.110.valid_ref), custom_call_target="tpu_custom_call" | custom-call | tf_op jit(solution)/shard_map/pallas_call | solution.py:95
  86.6 1.6 multiply_reduce_fusion.4
  90.6 1.1 fusion.24.kv_ref
  92.5 18.3 %shard_map.169 = bf16[2048,128]{1,0:T(8,128)(2,1)} custom-call(bf16[2048,128]{1,0:T(8,128)(2,1)} %slice_bitcast_fusion.2.q_ref, bf16[2176,256]{1,0:T(8,128)(2,1)} %fusion.24.kv_ref, f32[128,256]{1,0:T(8,128)} %fusion.72.band_ref, f32[16,256]{1,0:T(8,128)} %fusion.115.valid_ref), custom_call_target="tpu_custom_call" | custom-call | tf_op jit(solution)/shard_map/pallas_call | solution.py:95
  110.8 1.6 multiply_reduce_fusion.6
  114.0 1.2 fusion.14
  115.2 4.3 %collective-permute-start.8 = (f32[1,7,2048]{2,1,0:T(8,128)S(1)}, f32[1,7,2048]{2,1,0:T(8,128)S(1)}, u32[]{:S(2)}, u32[]{:S(2)}) collective-permute-start(f32[1,7,2048]{2,1,0:T(8,128)S(1)} %fusion.84.coord_ref), channel_id=1, source_target_pairs={{0,4},{4,8},{8,12},{12,16},{16,20},{20,24},{24,28},{28,0},{1,5},{5... | collective-permute-start | bytes 172040 | tf_op jit(solution)/shard_map/ppermute | solution.py:43
  119.6 2.8 %gather_fusion = s32[208]{0:T(256)S(1)} fusion(s32[16,13]{1,0:T(8,128)S(1)} %get-tuple-element.29, s32[208]{0:T(256)S(1)} %reshape.397), kind=kCustom, calls=%fused_computation | custom fusion | bytes 3328 | tf_op jit(solution)/shard_map/jit(take_along_axis)/gather | solution.py:297
  122.5 1.6 collective-permute-start.9
  124.9 3.4 %collective-permute-done.9 = f32[2,7,2048]{2,1,0:T(8,128)S(1)} collective-permute-done((f32[2,7,2048]{2,1,0:T(8,128)S(1)}, f32[2,7,2048]{2,1,0:T(8,128)S(1)}, u32[]{:S(2)}, u32[]{:S(2)}) %collective-permute-start.9) | collective-permute-done | bytes 114720 | tf_op jit(solution)/shard_map/ppermute | solution.py:43
  128.3 3.9 %collective-permute-start.10 = (f32[4,7,2048]{2,1,0:T(8,128)S(1)}, f32[4,7,2048]{2,1,0:T(8,128)S(1)}, u32[]{:S(2)}, u32[]{:S(2)}) collective-permute-start(f32[4,7,2048]{2,1,0:T(8,128)S(1)} %pad_maximum_fusion.2), channel_id=1, source_target_pairs={{0,16},{4,20},{8,24},{12,28},{16,0},{20,4},{24,8},{28,12},{1,17},{... | collective-permute-start | bytes 688136 | tf_op jit(solution)/shard_map/ppermute | solution.py:43
  132.3 1.3 copy.42.own_ref
  134.2 16.8 %shard_map.170 = f32[2048,128]{1,0:T(8,128)} custom-call(s32[208]{0:T(256)} %select_n.56.slots_ref, s32[16]{0:T(128)} %broadcast_22_lo_ref.2.lo_ref, s32[16]{0:T(128)} %get-tuple-element.20.count_ref.lo_ref, f32[2048,8]{1,0:T(8,128)} %copy.42.own_ref, f32[1,7,2048]{2,1,0:T(8,128)} %copy-done.1), custom_call_target="tpu_custom_call" | custom-call | tf_op jit(solution)/shard_map/pallas_call | solution.py:168
  151.1 1.6 copy.54
  153.5 32.7 %shard_map.171 = f32[2048,128]{1,0:T(8,128)} custom-call(s32[208]{0:T(256)} %select_n.56.slots_ref, s32[16]{0:T(128)} %get-tuple-element.20.count_ref.lo_ref, s32[16]{0:T(128)} %count_ref.1, f32[2048,8]{1,0:T(8,128)} %copy.42.own_ref, f32[8,7,2048]{2,1,0:T(8,128)} %pad_maximum_fusion.1.coord_ref), custom_call_target="tpu_custom_call" | custom-call | tf_op jit(solution)/shard_map/pallas_call | solution.py:168
  186.2 1.4 slice_reduce_fusion
  187.5 1.6 copy.55
  (101 shorter events, 21.1 us)
Async XLA Ops:
  0.6 6.8 %copy-start = (f32[3,128]{1,0:T(4,128)S(1)}, f32[3,128]{1,0:T(4,128)}, u32[]{:S(2)}) copy-start(f32[3,128]{1,0:T(4,128)} %param.25) | copy-start | bytes 4612
  0.6 10.7 %copy-start.9 = (bf16[256,192]{0,1:T(8,128)(2,1)S(1)}, bf16[256,192]{0,1:T(8,128)(2,1)}, u32[]{:S(2)}) copy-start(bf16[256,192]{0,1:T(8,128)(2,1)} %param.18) | copy-start | bytes 294916
  0.7 10.1 %copy-start.10 = (bf16[192,128]{1,0:T(8,128)(2,1)S(1)}, bf16[192,128]{1,0:T(8,128)(2,1)}, u32[]{:S(2)}) copy-start(bf16[192,128]{1,0:T(8,128)(2,1)} %param.19) | copy-start | bytes 147460
  0.7 12.3 %copy-start.11 = (s32[2048]{0:T(1024)S(1)}, s32[2048]{0:T(1024)}, u32[]{:S(2)}) copy-start(s32[2048]{0:T(1024)} %param.21) | copy-start | bytes 24580
  0.7 10.6 %collective-permute-start = (bf16[1,256,192]{1,2,0:T(8,128)(2,1)}, bf16[1,256,192]{1,2,0:T(8,128)(2,1)S(1)}, u32[]{:S(2)}, u32[]{:S(2)}) collective-permute-start(bf16[1,256,192]{1,2,0:T(8,128)(2,1)} %bitcast.214), channel_id=1, source_target_pairs={{0,1},{1,2},{2,3},{3,0},{4,5},{5,6},{6,7},{7,4},{8,9},{9,10},{10,1... | collective-permute-start | bytes 294920 | tf_op jit(solution)/shard_map/ppermute | solution.py:43
  0.7 10.0 %collective-permute-start.2 = (bf16[1,192,128]{2,1,0:T(8,128)(2,1)}, bf16[1,192,128]{2,1,0:T(8,128)(2,1)S(1)}, u32[]{:S(2)}, u32[]{:S(2)}) collective-permute-start(bf16[1,192,128]{2,1,0:T(8,128)(2,1)} %bitcast.217), channel_id=1, source_target_pairs={{0,1},{1,2},{2,3},{3,0},{4,5},{5,6},{6,7},{7,4},{8,9},{9,10},{10,1... | collective-permute-start | bytes 147464 | tf_op jit(solution)/shard_map/ppermute | solution.py:43
  10.0 15.9 %copy-start.13 = (f32[3,2,128]{2,1,0:T(2,128)S(1)}, f32[3,2,128]{2,1,0:T(2,128)}, u32[]{:S(2)}) copy-start(f32[3,2,128]{2,1,0:T(2,128)} %param.30) | copy-start | bytes 9220
  10.0 17.7 %copy-start.4 = (bf16[2048,128]{1,0:T(8,128)(2,1)S(1)}, bf16[2048,128]{1,0:T(8,128)(2,1)}, u32[]{:S(2)}) copy-start(bf16[2048,128]{1,0:T(8,128)(2,1)} %param.20) | copy-start | bytes 1572868
  10.7 5.7 %collective-permute-start.3 = (bf16[2,192,128]{2,1,0:T(8,128)(2,1)S(1)}, bf16[2,192,128]{2,1,0:T(8,128)(2,1)S(1)}, u32[]{:S(2)}, u32[]{:S(2)}) collective-permute-start(bf16[2,192,128]{2,1,0:T(8,128)(2,1)S(1)} %pad_maximum_fusion.5), channel_id=1, source_target_pairs={{0,2},{1,3},{2,0},{3,1},{4,6},{5,7},{6,4},{7,5},{8,10},{9,11},{10,... | collective-permute-start | bytes 294920 | tf_op jit(solution)/shard_map/ppermute | solution.py:43
  11.3 8.4 %collective-permute-start.1 = (bf16[2,256,192]{1,2,0:T(8,128)(2,1)S(1)}, bf16[2,256,192]{1,2,0:T(8,128)(2,1)S(1)}, u32[]{:S(2)}, u32[]{:S(2)}) collective-permute-start(bf16[2,256,192]{1,2,0:T(8,128)(2,1)S(1)} %pad_maximum_fusion.3), channel_id=1, source_target_pairs={{0,2},{1,3},{2,0},{3,1},{4,6},{5,7},{6,4},{7,5},{8,10},{9,11},{10,... | collective-permute-start | bytes 589832 | tf_op jit(solution)/shard_map/ppermute | solution.py:43
  20.1 7.6 %collective-permute-start.4 = (bf16[16,128]{1,0:T(8,128)(2,1)S(1)}, bf16[16,128]{1,0:T(8,128)(2,1)S(1)}, u32[]{:S(2)}, u32[]{:S(2)}) collective-permute-start(bf16[16,128]{1,0:T(8,128)(2,1)S(1)} %get-tuple-element.26), channel_id=1, source_target_pairs={{0,4},{4,8},{8,12},{12,16},{16,20},{20,24},{24,28},{1,5},{5,9},{9,... | collective-permute-start | bytes 12296 | tf_op jit(solution)/shard_map/ppermute | solution.py:31
  21.4 6.3 %collective-permute-start.5 = (bf16[16,128]{1,0:T(8,128)(2,1)S(1)}, bf16[16,128]{1,0:T(8,128)(2,1)S(1)}, u32[]{:S(2)}, u32[]{:S(2)}) collective-permute-start(bf16[16,128]{1,0:T(8,128)(2,1)S(1)} %get-tuple-element.27), channel_id=1, source_target_pairs={{4,0},{8,4},{12,8},{16,12},{20,16},{24,20},{28,24},{5,1},{9,5},{13... | collective-permute-start | bytes 12296 | tf_op jit(solution)/shard_map/ppermute | solution.py:32
  27.7 6.9 %copy-start.12 = (s32[16]{0:T(128)S(1)}, s32[16]{0:T(128)}, u32[]{:S(2)}) copy-start(s32[16]{0:T(128)} %count_ref.1) | copy-start | bytes 196
  28.5 8.0 %collective-permute-start.6 = (f32[1,176,128]{2,1,0:T(8,128)S(1)}, f32[1,176,128]{2,1,0:T(8,128)S(1)}, u32[]{:S(2)}, u32[]{:S(2)}) collective-permute-start(f32[1,176,128]{2,1,0:T(8,128)S(1)} %get-tuple-element.24), channel_id=1, source_target_pairs={{0,4},{4,8},{8,12},{12,16},{16,20},{20,24},{24,28},{1,5},{5,9},{9,... | collective-permute-start | bytes 270344 | tf_op jit(solution)/shard_map/ppermute | solution.py:31
  29.8 6.8 %collective-permute-start.7 = (f32[1,176,128]{2,1,0:T(8,128)S(1)}, f32[1,176,128]{2,1,0:T(8,128)S(1)}, u32[]{:S(2)}, u32[]{:S(2)}) collective-permute-start(f32[1,176,128]{2,1,0:T(8,128)S(1)} %get-tuple-element.25), channel_id=1, source_target_pairs={{4,0},{8,4},{12,8},{16,12},{20,16},{24,20},{28,24},{5,1},{9,5},{13... | collective-permute-start | bytes 270344 | tf_op jit(solution)/shard_map/ppermute | solution.py:32
  40.6 20.4 %copy-start.8 = (bf16[3,128,128]{2,1,0:T(8,128)(2,1)S(1)}, bf16[3,128,128]{2,1,0:T(8,128)(2,1)}, u32[]{:S(2)}) copy-start(bf16[3,128,128]{2,1,0:T(8,128)(2,1)} %param.27) | copy-start | bytes 294916
  61.1 1.7 copy-start.5
  62.7 0.9 copy-start.15
  63.7 1.0 copy-start.6
  113.1 0.9 copy-start.3
  113.1 0.9 copy-start.7
  113.1 0.9 copy-start.14
  115.2 13.1 %copy-start.1 = (f32[1,7,2048]{2,1,0:T(8,128)}, f32[1,7,2048]{2,1,0:T(8,128)S(1)}, u32[]{:S(2)}) copy-start(f32[1,7,2048]{2,1,0:T(8,128)S(1)} %fusion.84.coord_ref) | copy-start | bytes 172036
  115.2 7.3 %collective-permute-start.8 = (f32[1,7,2048]{2,1,0:T(8,128)S(1)}, f32[1,7,2048]{2,1,0:T(8,128)S(1)}, u32[]{:S(2)}, u32[]{:S(2)}) collective-permute-start(f32[1,7,2048]{2,1,0:T(8,128)S(1)} %fusion.84.coord_ref), channel_id=1, source_target_pairs={{0,4},{4,8},{8,12},{12,16},{16,20},{20,24},{24,28},{28,0},{1,5},{5... | collective-permute-start | bytes 172040 | tf_op jit(solution)/shard_map/ppermute | solution.py:43
  122.5 5.8 %collective-permute-start.9 = (f32[2,7,2048]{2,1,0:T(8,128)S(1)}, f32[2,7,2048]{2,1,0:T(8,128)S(1)}, u32[]{:S(2)}, u32[]{:S(2)}) collective-permute-start(f32[2,7,2048]{2,1,0:T(8,128)S(1)} %pad_maximum_fusion.4), channel_id=1, source_target_pairs={{0,8},{4,12},{8,16},{12,20},{16,24},{20,28},{24,0},{28,4},{1,9},{5... | collective-permute-start | bytes 344072 | tf_op jit(solution)/shard_map/ppermute | solution.py:43
  128.3 24.3 %collective-permute-start.10 = (f32[4,7,2048]{2,1,0:T(8,128)S(1)}, f32[4,7,2048]{2,1,0:T(8,128)S(1)}, u32[]{:S(2)}, u32[]{:S(2)}) collective-permute-start(f32[4,7,2048]{2,1,0:T(8,128)S(1)} %pad_maximum_fusion.2), channel_id=1, source_target_pairs={{0,16},{4,20},{8,24},{12,28},{16,0},{20,4},{24,8},{28,12},{1,17},{... | collective-permute-start | bytes 688136 | tf_op jit(solution)/shard_map/ppermute | solution.py:43
  134.2 18.4 %copy-start.2 = (f32[1,7,2048]{2,1,0:T(8,128)S(1)}, f32[1,7,2048]{2,1,0:T(8,128)}, u32[]{:S(2)}) copy-start(f32[1,7,2048]{2,1,0:T(8,128)} %copy-done.1) | copy-start | bytes 172036

commit v11 on v7

--- a/solution.py
+++ b/solution.py
@@ -143,18 +143,15 @@
             gap_dist = square_pred * inv_pred - square_true * lax.rsqrt(square_true)
             square_err = gap_dist * gap_dist + 0.01
             inv_err = lax.rsqrt(square_err)
-            decay = jnp.exp(-(square_err * inv_err))
-            ys = [decay * math.exp(t) for t in thresholds]
-            dens = [(1.0 + y) * (1.0 + y) for y in ys]
-            low = dens[0] * dens[1]
-            high = dens[2] * dens[3]
-            numer = (ys[0] * dens[1] + ys[1] * dens[0]) * high + (ys[2] * dens[3] + ys[3] * dens[2]) * low
-            coef = (numer * gap_dist * (inv_err * inv_pred)) / (low * high)
+            half_err = 0.5 * (square_err * inv_err)
+            curve = [jnp.tanh(0.5 * t - half_err) for t in thresholds]
+            bend = curve[0] * curve[0] + curve[1] * curve[1] + curve[2] * curve[2] + curve[3] * curve[3]
+            coef = ((4.0 - bend) * gap_dist) * (inv_err * inv_pred)
             return tuple(acc + coef * gap for acc, gap in zip(accs, gaps))
 
         zero = jnp.zeros(shape, jnp.float32)
         accs = lax.fori_loop(0, live, slot_body, (zero, zero, zero))
-        sums = [-0.25 * jnp.sum(acc, axis=1, keepdims=True) for acc in accs]
+        sums = [-0.0625 * jnp.sum(acc, axis=1, keepdims=True) for acc in accs]
         tile = jnp.where(lane == 0, sums[0], jnp.where(lane == 1, sums[1], jnp.where(lane == 2, sums[2], 0.0)))
         out_ref[pl.ds(row, ROW_CHUNK), :] = tile
         return carry

time: 178 us -> 176 us (0.989); the launches traced: 175 us -> 177 us
  no operation moved by 1% of the time
where the time goes in v11:
time: 176 us; the launch traced here: 177 us
  Pallas kernels  96.1 us (55%)
  starting transfers between devices  26.2 us (15%)
  matrix products  17.6 us (10%)
  waiting for transfers between devices  16.3 us (9%)
  local copies, waits for them, and re-layouts  9.85 us (6%)
  other arithmetic  6.82 us (4%)
  between operations  3.83 us (2%)
    pallas_call x3, Pallas kernels, window_attend(): pl.pallas_call(attend_kernel, grid=(atoms // Q_TILE,), in_specs=[pl.Block...  58.1 us
    pallas_call x1, Pallas kernels, lddt_sums(): pl.pallas_call(lddt_kernel, grid_spec=pltpu.PrefetchScalarGridSpec(num_sc...  38 us
    ppermute x7, waiting for transfers between devices, ring_parts(): parts = jnp.concatenate([parts, lax.ppermute(parts, axis, pairs)])  15.7 us
    ppermute x7, starting transfers between devices, ring_parts(): parts = jnp.concatenate([parts, lax.ppermute(parts, axis, pairs)])  14 us
    dot_general x12, matrix products, dense(): jnp.einsum('sac,cf->saf', left, right, preferred_element_type=jnp.float32)  12.7 us
    ppermute x2, starting transfers between devices, extended(): after = lax.ppermute(first, axis, down)  9.54 us
  transfers between devices with their start and end apart: 11, of which 6 were waited for; matrix products, arithmetic and copies ran while one was open for 5% of the time, Pallas kernels for 0%

profile of v11, /device:TPU:26, one launch (start us, length us, event | category | flops | bytes accessed | tf_op | source)
XLA Modules:
  0.0 176.6 jit_solution(17308444041533347388)
XLA Ops:
  0.7 1.6 collective-permute-start.2
  5.2 2.6 %fusion.96 = f32[2048,128]{1,0:T(8,128)S(1)} fusion(f32[3,128]{1,0:T(4,128)S(1)} %copy-done, f32[]{:T(128)} %bitcast.8, f32[3,2048]{1,0:T(4,128)} %param.22, f32[1,3,2048]{2,0,1:T(1,128)} %param.23, f32[]{:T(128)} %bitcast.198), kind=kOutput, calls=%fused_computation.137 | convolution fusion | flops 9455616 | bytes 1099272 | tf_op jit(solution)/shard_map/sda,dc->sac/dot_general | solution.py:226
  9.1 1.6 collective-permute-start.1
  10.7 3.5 %collective-permute-done.3 = bf16[2,192,128]{2,1,0:T(8,128)(2,1)S(1)} collective-permute-done((bf16[2,192,128]{2,1,0:T(8,128)(2,1)S(1)}, bf16[2,192,128]{2,1,0:T(8,128)(2,1)S(1)}, u32[]{:S(2)}, u32[]{:S(2)}) %collective-permute-start.3) | collective-permute-done | bytes 98336 | tf_op jit(solution)/shard_map/ppermute | solution.py:43
  14.3 3.3 %collective-permute-done.1 = bf16[2,256,192]{1,2,0:T(8,128)(2,1)S(1)} collective-permute-done((bf16[2,256,192]{1,2,0:T(8,128)(2,1)S(1)}, bf16[2,256,192]{1,2,0:T(8,128)(2,1)S(1)}, u32[]{:S(2)}, u32[]{:S(2)}) %collective-permute-start.1) | collective-permute-done | bytes 196640 | tf_op jit(solution)/shard_map/ppermute | solution.py:43
  17.9 1.3 collective-permute-start.4
  19.2 4.5 %collective-permute-start.5 = (bf16[16,128]{1,0:T(8,128)(2,1)S(1)}, bf16[16,128]{1,0:T(8,128)(2,1)S(1)}, u32[]{:S(2)}, u32[]{:S(2)}) collective-permute-start(bf16[16,128]{1,0:T(8,128)(2,1)S(1)} %get-tuple-element.21), channel_id=1, source_target_pairs={{4,0},{8,4},{12,8},{16,12},{20,16},{24,20},{28,24},{5,1},{9,5},{13... | collective-permute-start | bytes 12296 | tf_op jit(solution)/shard_map/ppermute | solution.py:32
  25.9 1.3 collective-permute-start.6
  27.2 5.0 %collective-permute-start.7 = (f32[1,176,128]{2,1,0:T(8,128)S(1)}, f32[1,176,128]{2,1,0:T(8,128)S(1)}, u32[]{:S(2)}, u32[]{:S(2)}) collective-permute-start(f32[1,176,128]{2,1,0:T(8,128)S(1)} %get-tuple-element.19), channel_id=1, source_target_pairs={{4,0},{8,4},{12,8},{16,12},{20,16},{24,20},{28,24},{5,1},{9,5},{13... | collective-permute-start | bytes 270344 | tf_op jit(solution)/shard_map/ppermute | solution.py:32
  34.6 1.6 fusion.2
  36.2 1.1 fusion.17.kv_ref
  37.3 0.9 slice_bitcast_fusion.q_ref
  38.2 20.4 %shard_map.167 = bf16[2304,128]{1,0:T(8,128)(2,1)} custom-call(bf16[2304,128]{1,0:T(8,128)(2,1)} %slice_bitcast_fusion.q_ref, bf16[2432,256]{1,0:T(8,128)(2,1)} %fusion.17.kv_ref, f32[128,256]{1,0:T(8,128)} %fusion.72.band_ref, f32[18,256]{1,0:T(8,128)} %fusion.108.valid_ref), custom_call_target="tpu_custom_call" | custom-call | tf_op jit(solution)/shard_map/pallas_call | solution.py:95
  58.6 1.7 multiply_reduce_fusion.2
  61.2 0.9 multiply_reduce_fusion.1
  62.9 1.1 fusion.20.kv_ref
  64.0 0.9 slice_bitcast_fusion.1.q_ref
  64.9 19.3 %shard_map.168 = bf16[2176,128]{1,0:T(8,128)(2,1)} custom-call(bf16[2176,128]{1,0:T(8,128)(2,1)} %slice_bitcast_fusion.1.q_ref, bf16[2304,256]{1,0:T(8,128)(2,1)} %fusion.20.kv_ref, f32[128,256]{1,0:T(8,128)} %fusion.72.band_ref, f32[17,256]{1,0:T(8,128)} %fusion.110.valid_ref), custom_call_target="tpu_custom_call" | custom-call | tf_op jit(solution)/shard_map/pallas_call | solution.py:95
  84.2 1.6 multiply_reduce_fusion.4
  88.1 1.1 fusion.24.kv_ref
  90.0 18.3 %shard_map.169 = bf16[2048,128]{1,0:T(8,128)(2,1)} custom-call(bf16[2048,128]{1,0:T(8,128)(2,1)} %slice_bitcast_fusion.2.q_ref, bf16[2176,256]{1,0:T(8,128)(2,1)} %fusion.24.kv_ref, f32[128,256]{1,0:T(8,128)} %fusion.72.band_ref, f32[16,256]{1,0:T(8,128)} %fusion.115.valid_ref), custom_call_target="tpu_custom_call" | custom-call | tf_op jit(solution)/shard_map/pallas_call | solution.py:95
  108.3 1.6 multiply_reduce_fusion.6
  111.6 1.2 fusion.14
  112.8 4.5 %collective-permute-start.8 = (f32[1,7,2048]{2,1,0:T(8,128)S(1)}, f32[1,7,2048]{2,1,0:T(8,128)S(1)}, u32[]{:S(2)}, u32[]{:S(2)}) collective-permute-start(f32[1,7,2048]{2,1,0:T(8,128)S(1)} %fusion.84), channel_id=1, source_target_pairs={{0,4},{4,8},{8,12},{12,16},{16,20},{20,24},{24,28},{28,0},{1,5},{5... | collective-permute-start | bytes 172040 | tf_op jit(solution)/shard_map/ppermute | solution.py:43
  117.3 2.2 %collective-permute-done.8 = f32[1,7,2048]{2,1,0:T(8,128)S(1)} collective-permute-done((f32[1,7,2048]{2,1,0:T(8,128)S(1)}, f32[1,7,2048]{2,1,0:T(8,128)S(1)}, u32[]{:S(2)}, u32[]{:S(2)}) %collective-permute-start.8) | collective-permute-done | bytes 57376 | tf_op jit(solution)/shard_map/ppermute | solution.py:43
  119.5 2.1 %collective-permute-start.9 = (f32[2,7,2048]{2,1,0:T(8,128)S(1)}, f32[2,7,2048]{2,1,0:T(8,128)S(1)}, u32[]{:S(2)}, u32[]{:S(2)}) collective-permute-start(f32[2,7,2048]{2,1,0:T(8,128)S(1)} %pad_maximum_fusion.4), channel_id=1, source_target_pairs={{0,8},{4,12},{8,16},{12,20},{16,24},{20,28},{24,0},{28,4},{1,9},{5... | collective-permute-start | bytes 344072 | tf_op jit(solution)/shard_map/ppermute | solution.py:43
  122.5 3.7 %collective-permute-done.9 = f32[2,7,2048]{2,1,0:T(8,128)S(1)} collective-permute-done((f32[2,7,2048]{2,1,0:T(8,128)S(1)}, f32[2,7,2048]{2,1,0:T(8,128)S(1)}, u32[]{:S(2)}, u32[]{:S(2)}) %collective-permute-start.9) | collective-permute-done | bytes 114720 | tf_op jit(solution)/shard_map/ppermute | solution.py:43
  126.2 3.5 %collective-permute-start.10 = (f32[4,7,2048]{2,1,0:T(8,128)S(1)}, f32[4,7,2048]{2,1,0:T(8,128)S(1)}, u32[]{:S(2)}, u32[]{:S(2)}) collective-permute-start(f32[4,7,2048]{2,1,0:T(8,128)S(1)} %pad_maximum_fusion.2), channel_id=1, source_target_pairs={{0,16},{4,20},{8,24},{12,28},{16,0},{20,4},{24,8},{28,12},{1,17},{... | collective-permute-start | bytes 688136 | tf_op jit(solution)/shard_map/ppermute | solution.py:43
  129.8 1.3 copy.25.own_ref
  131.1 3.0 %collective-permute-done.10 = f32[4,7,2048]{2,1,0:T(8,128)S(1)} collective-permute-done((f32[4,7,2048]{2,1,0:T(8,128)S(1)}, f32[4,7,2048]{2,1,0:T(8,128)S(1)}, u32[]{:S(2)}, u32[]{:S(2)}) %collective-permute-start.10) | collective-permute-done | bytes 229408 | tf_op jit(solution)/shard_map/ppermute | solution.py:43
  135.0 38.0 %shard_map.170 = f32[2048,128]{1,0:T(8,128)} custom-call(s32[208]{0:T(256)} %reshape.383.slots_ref, s32[16]{0:T(128)} %count_ref.1, f32[2048,8]{1,0:T(8,128)} %copy.25.own_ref, f32[8,7,2048]{2,1,0:T(8,128)} %copy-done.1), custom_call_target="tpu_custom_call" | custom-call | tf_op jit(solution)/shard_map/pallas_call | solution.py:164
  173.7 1.3 slice_multiply_fusion.3
  (88 shorter events, 16.7 us)
Async XLA Ops:
  0.6 4.6 %copy-start = (f32[3,128]{1,0:T(4,128)S(1)}, f32[3,128]{1,0:T(4,128)}, u32[]{:S(2)}) copy-start(f32[3,128]{1,0:T(4,128)} %param.25) | copy-start | bytes 4612
  0.6 8.5 %copy-start.8 = (bf16[256,192]{0,1:T(8,128)(2,1)S(1)}, bf16[256,192]{0,1:T(8,128)(2,1)}, u32[]{:S(2)}) copy-start(bf16[256,192]{0,1:T(8,128)(2,1)} %param.18) | copy-start | bytes 294916
  0.7 7.9 %copy-start.9 = (bf16[192,128]{1,0:T(8,128)(2,1)S(1)}, bf16[192,128]{1,0:T(8,128)(2,1)}, u32[]{:S(2)}) copy-start(bf16[192,128]{1,0:T(8,128)(2,1)} %param.19) | copy-start | bytes 147460
  0.7 10.1 %copy-start.10 = (s32[2048]{0:T(1024)S(1)}, s32[2048]{0:T(1024)}, u32[]{:S(2)}) copy-start(s32[2048]{0:T(1024)} %param.21) | copy-start | bytes 24580
  0.7 8.4 %collective-permute-start = (bf16[1,256,192]{1,2,0:T(8,128)(2,1)}, bf16[1,256,192]{1,2,0:T(8,128)(2,1)S(1)}, u32[]{:S(2)}, u32[]{:S(2)}) collective-permute-start(bf16[1,256,192]{1,2,0:T(8,128)(2,1)} %bitcast.206), channel_id=1, source_target_pairs={{0,1},{1,2},{2,3},{3,0},{4,5},{5,6},{6,7},{7,4},{8,9},{9,10},{10,1... | collective-permute-start | bytes 294920 | tf_op jit(solution)/shard_map/ppermute | solution.py:43
  0.7 7.8 %collective-permute-start.2 = (bf16[1,192,128]{2,1,0:T(8,128)(2,1)}, bf16[1,192,128]{2,1,0:T(8,128)(2,1)S(1)}, u32[]{:S(2)}, u32[]{:S(2)}) collective-permute-start(bf16[1,192,128]{2,1,0:T(8,128)(2,1)} %bitcast.209), channel_id=1, source_target_pairs={{0,1},{1,2},{2,3},{3,0},{4,5},{5,6},{6,7},{7,4},{8,9},{9,10},{10,1... | collective-permute-start | bytes 147464 | tf_op jit(solution)/shard_map/ppermute | solution.py:43
  7.8 15.9 %copy-start.12 = (f32[3,2,128]{2,1,0:T(2,128)S(1)}, f32[3,2,128]{2,1,0:T(2,128)}, u32[]{:S(2)}) copy-start(f32[3,2,128]{2,1,0:T(2,128)} %param.30) | copy-start | bytes 9220
  7.8 17.2 %copy-start.3 = (bf16[2048,128]{1,0:T(8,128)(2,1)S(1)}, bf16[2048,128]{1,0:T(8,128)(2,1)}, u32[]{:S(2)}) copy-start(bf16[2048,128]{1,0:T(8,128)(2,1)} %param.20) | copy-start | bytes 1572868
  8.5 5.7 %collective-permute-start.3 = (bf16[2,192,128]{2,1,0:T(8,128)(2,1)S(1)}, bf16[2,192,128]{2,1,0:T(8,128)(2,1)S(1)}, u32[]{:S(2)}, u32[]{:S(2)}) collective-permute-start(bf16[2,192,128]{2,1,0:T(8,128)(2,1)S(1)} %pad_maximum_fusion.5), channel_id=1, source_target_pairs={{0,2},{1,3},{2,0},{3,1},{4,6},{5,7},{6,4},{7,5},{8,10},{9,11},{10,... | collective-permute-start | bytes 294920 | tf_op jit(solution)/shard_map/ppermute | solution.py:43
  9.1 8.4 %collective-permute-start.1 = (bf16[2,256,192]{1,2,0:T(8,128)(2,1)S(1)}, bf16[2,256,192]{1,2,0:T(8,128)(2,1)S(1)}, u32[]{:S(2)}, u32[]{:S(2)}) collective-permute-start(bf16[2,256,192]{1,2,0:T(8,128)(2,1)S(1)} %pad_maximum_fusion.3), channel_id=1, source_target_pairs={{0,2},{1,3},{2,0},{3,1},{4,6},{5,7},{6,4},{7,5},{8,10},{9,11},{10,... | collective-permute-start | bytes 589832 | tf_op jit(solution)/shard_map/ppermute | solution.py:43
  17.9 6.7 %collective-permute-start.4 = (bf16[16,128]{1,0:T(8,128)(2,1)S(1)}, bf16[16,128]{1,0:T(8,128)(2,1)S(1)}, u32[]{:S(2)}, u32[]{:S(2)}) collective-permute-start(bf16[16,128]{1,0:T(8,128)(2,1)S(1)} %get-tuple-element.20), channel_id=1, source_target_pairs={{0,4},{4,8},{8,12},{12,16},{16,20},{20,24},{24,28},{1,5},{5,9},{9,... | collective-permute-start | bytes 12296 | tf_op jit(solution)/shard_map/ppermute | solution.py:31
  19.2 5.9 %collective-permute-start.5 = (bf16[16,128]{1,0:T(8,128)(2,1)S(1)}, bf16[16,128]{1,0:T(8,128)(2,1)S(1)}, u32[]{:S(2)}, u32[]{:S(2)}) collective-permute-start(bf16[16,128]{1,0:T(8,128)(2,1)S(1)} %get-tuple-element.21), channel_id=1, source_target_pairs={{4,0},{8,4},{12,8},{16,12},{20,16},{24,20},{28,24},{5,1},{9,5},{13... | collective-permute-start | bytes 12296 | tf_op jit(solution)/shard_map/ppermute | solution.py:32
  24.6 7.6 %copy-start.14 = (s32[16]{0:T(128)S(1)}, s32[16]{0:T(128)}, u32[]{:S(2)}) copy-start(s32[16]{0:T(128)} %count_ref.1) | copy-start | bytes 196
  25.9 8.2 %collective-permute-start.6 = (f32[1,176,128]{2,1,0:T(8,128)S(1)}, f32[1,176,128]{2,1,0:T(8,128)S(1)}, u32[]{:S(2)}, u32[]{:S(2)}) collective-permute-start(f32[1,176,128]{2,1,0:T(8,128)S(1)} %get-tuple-element.18), channel_id=1, source_target_pairs={{0,4},{4,8},{8,12},{12,16},{16,20},{20,24},{24,28},{1,5},{5,9},{9,... | collective-permute-start | bytes 270344 | tf_op jit(solution)/shard_map/ppermute | solution.py:31
  27.2 6.9 %collective-permute-start.7 = (f32[1,176,128]{2,1,0:T(8,128)S(1)}, f32[1,176,128]{2,1,0:T(8,128)S(1)}, u32[]{:S(2)}, u32[]{:S(2)}) collective-permute-start(f32[1,176,128]{2,1,0:T(8,128)S(1)} %get-tuple-element.19), channel_id=1, source_target_pairs={{4,0},{8,4},{12,8},{16,12},{20,16},{24,20},{28,24},{5,1},{9,5},{13... | collective-permute-start | bytes 270344 | tf_op jit(solution)/shard_map/ppermute | solution.py:32
  38.2 20.4 %copy-start.7 = (bf16[3,128,128]{2,1,0:T(8,128)(2,1)S(1)}, bf16[3,128,128]{2,1,0:T(8,128)(2,1)}, u32[]{:S(2)}) copy-start(bf16[3,128,128]{2,1,0:T(8,128)(2,1)} %param.27) | copy-start | bytes 294916
  58.6 1.7 copy-start.4
  60.3 0.9 copy-start.15
  61.2 1.0 copy-start.5
  110.7 0.9 copy-start.2
  110.7 0.9 copy-start.6
  110.7 0.9 copy-start.13
  111.5 10.1 %copy-start.11 = (s32[16,13]{1,0:T(8,128)S(1)}, s32[16,13]{1,0:T(8,128)}, u32[]{:S(2)}) copy-start(s32[16,13]{1,0:T(8,128)} %param.32) | copy-start | bytes 2500
  112.8 6.8 %collective-permute-start.8 = (f32[1,7,2048]{2,1,0:T(8,128)S(1)}, f32[1,7,2048]{2,1,0:T(8,128)S(1)}, u32[]{:S(2)}, u32[]{:S(2)}) collective-permute-start(f32[1,7,2048]{2,1,0:T(8,128)S(1)} %fusion.84), channel_id=1, source_target_pairs={{0,4},{4,8},{8,12},{12,16},{16,20},{20,24},{24,28},{28,0},{1,5},{5... | collective-permute-start | bytes 172040 | tf_op jit(solution)/shard_map/ppermute | solution.py:43
  119.5 6.6 %collective-permute-start.9 = (f32[2,7,2048]{2,1,0:T(8,128)S(1)}, f32[2,7,2048]{2,1,0:T(8,128)S(1)}, u32[]{:S(2)}, u32[]{:S(2)}) collective-permute-start(f32[2,7,2048]{2,1,0:T(8,128)S(1)} %pad_maximum_fusion.4), channel_id=1, source_target_pairs={{0,8},{4,12},{8,16},{12,20},{16,24},{20,28},{24,0},{28,4},{1,9},{5... | collective-permute-start | bytes 344072 | tf_op jit(solution)/shard_map/ppermute | solution.py:43
  126.2 7.9 %collective-permute-start.10 = (f32[4,7,2048]{2,1,0:T(8,128)S(1)}, f32[4,7,2048]{2,1,0:T(8,128)S(1)}, u32[]{:S(2)}, u32[]{:S(2)}) collective-permute-start(f32[4,7,2048]{2,1,0:T(8,128)S(1)} %pad_maximum_fusion.2), channel_id=1, source_target_pairs={{0,16},{4,20},{8,24},{12,28},{16,0},{20,4},{24,8},{28,12},{1,17},{... | collective-permute-start | bytes 688136 | tf_op jit(solution)/shard_map/ppermute | solution.py:43
  134.2 0.8 copy-start.1

commit v12 on v11

--- a/solution.py
+++ b/solution.py
@@ -105,7 +105,7 @@
         out_shape=jax.ShapeDtypeStruct((atoms, channels), jnp.bfloat16),
     )(queries, padded_kv, band, valid_tab)
 
-ROW_CHUNK = 64
+ROW_CHUNK = 128
 
 
 def lddt_kernel(slots_ref, count_ref, own_ref, coord_ref, out_ref, cols_ref):

time: 176 us -> 171 us (0.972)
  Pallas kernels: 96.1 us -> 90.1 us
    pallas_call x1, Pallas kernels: 38 us -> 32 us  [lddt_sums(): pl.pallas_call(lddt_kernel, grid_spec=pltpu.PrefetchScalarGridSpec(num_sc...]
where the time goes in v12:
time: 171 us
  Pallas kernels  90.1 us (53%)
  starting transfers between devices  26.2 us (15%)
  matrix products  17.6 us (10%)
  waiting for transfers between devices  16.3 us (10%)
  local copies, waits for them, and re-layouts  9.85 us (6%)
  other arithmetic  6.82 us (4%)
  between operations  3.83 us (2%)
    pallas_call x3, Pallas kernels, window_attend(): pl.pallas_call(attend_kernel, grid=(atoms // Q_TILE,), in_specs=[pl.Block...  58.1 us
    pallas_call x1, Pallas kernels, lddt_sums(): pl.pallas_call(lddt_kernel, grid_spec=pltpu.PrefetchScalarGridSpec(num_sc...  32 us
    ppermute x7, waiting for transfers between devices, ring_parts(): parts = jnp.concatenate([parts, lax.ppermute(parts, axis, pairs)])  15.7 us
    ppermute x7, starting transfers between devices, ring_parts(): parts = jnp.concatenate([parts, lax.ppermute(parts, axis, pairs)])  14 us
    dot_general x12, matrix products, dense(): jnp.einsum('sac,cf->saf', left, right, preferred_element_type=jnp.float32)  12.7 us
    ppermute x2, starting transfers between devices, extended(): after = lax.ppermute(first, axis, down)  9.54 us
  transfers between devices with their start and end apart: 11, of which 6 were waited for; matrix products, arithmetic and copies ran while one was open for 5% of the time, Pallas kernels for 0%

profile of v12, /device:TPU:26, one launch (start us, length us, event | category | flops | bytes accessed | tf_op | source)
XLA Modules:
  0.0 170.6 jit_solution(9872805427378600197)
XLA Ops:
  0.7 1.6 collective-permute-start.2
  5.2 2.6 %fusion.96 = f32[2048,128]{1,0:T(8,128)S(1)} fusion(f32[3,128]{1,0:T(4,128)S(1)} %copy-done, f32[]{:T(128)} %bitcast.8, f32[3,2048]{1,0:T(4,128)} %param.22, f32[1,3,2048]{2,0,1:T(1,128)} %param.23, f32[]{:T(128)} %bitcast.198), kind=kOutput, calls=%fused_computation.137 | convolution fusion | flops 9455616 | bytes 1099272 | tf_op jit(solution)/shard_map/sda,dc->sac/dot_general | solution.py:226
  9.1 1.6 collective-permute-start.1
  10.7 3.5 %collective-permute-done.3 = bf16[2,192,128]{2,1,0:T(8,128)(2,1)S(1)} collective-permute-done((bf16[2,192,128]{2,1,0:T(8,128)(2,1)S(1)}, bf16[2,192,128]{2,1,0:T(8,128)(2,1)S(1)}, u32[]{:S(2)}, u32[]{:S(2)}) %collective-permute-start.3) | collective-permute-done | bytes 98336 | tf_op jit(solution)/shard_map/ppermute | solution.py:43
  14.3 3.3 %collective-permute-done.1 = bf16[2,256,192]{1,2,0:T(8,128)(2,1)S(1)} collective-permute-done((bf16[2,256,192]{1,2,0:T(8,128)(2,1)S(1)}, bf16[2,256,192]{1,2,0:T(8,128)(2,1)S(1)}, u32[]{:S(2)}, u32[]{:S(2)}) %collective-permute-start.1) | collective-permute-done | bytes 196640 | tf_op jit(solution)/shard_map/ppermute | solution.py:43
  17.9 1.3 collective-permute-start.4
  19.2 4.5 %collective-permute-start.5 = (bf16[16,128]{1,0:T(8,128)(2,1)S(1)}, bf16[16,128]{1,0:T(8,128)(2,1)S(1)}, u32[]{:S(2)}, u32[]{:S(2)}) collective-permute-start(bf16[16,128]{1,0:T(8,128)(2,1)S(1)} %get-tuple-element.21), channel_id=1, source_target_pairs={{4,0},{8,4},{12,8},{16,12},{20,16},{24,20},{28,24},{5,1},{9,5},{13... | collective-permute-start | bytes 12296 | tf_op jit(solution)/shard_map/ppermute | solution.py:32
  25.9 1.3 collective-permute-start.6
  27.2 5.0 %collective-permute-start.7 = (f32[1,176,128]{2,1,0:T(8,128)S(1)}, f32[1,176,128]{2,1,0:T(8,128)S(1)}, u32[]{:S(2)}, u32[]{:S(2)}) collective-permute-start(f32[1,176,128]{2,1,0:T(8,128)S(1)} %get-tuple-element.19), channel_id=1, source_target_pairs={{4,0},{8,4},{12,8},{16,12},{20,16},{24,20},{28,24},{5,1},{9,5},{13... | collective-permute-start | bytes 270344 | tf_op jit(solution)/shard_map/ppermute | solution.py:32
  34.6 1.6 fusion.2
  36.2 1.1 fusion.17.kv_ref
  37.3 0.9 slice_bitcast_fusion.q_ref
  38.2 20.4 %shard_map.167 = bf16[2304,128]{1,0:T(8,128)(2,1)} custom-call(bf16[2304,128]{1,0:T(8,128)(2,1)} %slice_bitcast_fusion.q_ref, bf16[2432,256]{1,0:T(8,128)(2,1)} %fusion.17.kv_ref, f32[128,256]{1,0:T(8,128)} %fusion.72.band_ref, f32[18,256]{1,0:T(8,128)} %fusion.108.valid_ref), custom_call_target="tpu_custom_call" | custom-call | tf_op jit(solution)/shard_map/pallas_call | solution.py:95
  58.6 1.7 multiply_reduce_fusion.2
  61.2 0.9 multiply_reduce_fusion.1
  62.9 1.1 fusion.20.kv_ref
  64.0 0.9 slice_bitcast_fusion.1.q_ref
  64.9 19.3 %shard_map.168 = bf16[2176,128]{1,0:T(8,128)(2,1)} custom-call(bf16[2176,128]{1,0:T(8,128)(2,1)} %slice_bitcast_fusion.1.q_ref, bf16[2304,256]{1,0:T(8,128)(2,1)} %fusion.20.kv_ref, f32[128,256]{1,0:T(8,128)} %fusion.72.band_ref, f32[17,256]{1,0:T(8,128)} %fusion.110.valid_ref), custom_call_target="tpu_custom_call" | custom-call | tf_op jit(solution)/shard_map/pallas_call | solution.py:95
  84.2 1.6 multiply_reduce_fusion.4
  88.1 1.1 fusion.24.kv_ref
  90.0 18.3 %shard_map.169 = bf16[2048,128]{1,0:T(8,128)(2,1)} custom-call(bf16[2048,128]{1,0:T(8,128)(2,1)} %slice_bitcast_fusion.2.q_ref, bf16[2176,256]{1,0:T(8,128)(2,1)} %fusion.24.kv_ref, f32[128,256]{1,0:T(8,128)} %fusion.72.band_ref, f32[16,256]{1,0:T(8,128)} %fusion.115.valid_ref), custom_call_target="tpu_custom_call" | custom-call | tf_op jit(solution)/shard_map/pallas_call | solution.py:95
  108.3 1.6 multiply_reduce_fusion.6
  111.6 1.2 fusion.14
  112.8 4.5 %collective-permute-start.8 = (f32[1,7,2048]{2,1,0:T(8,128)S(1)}, f32[1,7,2048]{2,1,0:T(8,128)S(1)}, u32[]{:S(2)}, u32[]{:S(2)}) collective-permute-start(f32[1,7,2048]{2,1,0:T(8,128)S(1)} %fusion.84), channel_id=1, source_target_pairs={{0,4},{4,8},{8,12},{12,16},{16,20},{20,24},{24,28},{28,0},{1,5},{5... | collective-permute-start | bytes 172040 | tf_op jit(solution)/shard_map/ppermute | solution.py:43
  117.3 2.2 %collective-permute-done.8 = f32[1,7,2048]{2,1,0:T(8,128)S(1)} collective-permute-done((f32[1,7,2048]{2,1,0:T(8,128)S(1)}, f32[1,7,2048]{2,1,0:T(8,128)S(1)}, u32[]{:S(2)}, u32[]{:S(2)}) %collective-permute-start.8) | collective-permute-done | bytes 57376 | tf_op jit(solution)/shard_map/ppermute | solution.py:43
  119.5 2.1 %collective-permute-start.9 = (f32[2,7,2048]{2,1,0:T(8,128)S(1)}, f32[2,7,2048]{2,1,0:T(8,128)S(1)}, u32[]{:S(2)}, u32[]{:S(2)}) collective-permute-start(f32[2,7,2048]{2,1,0:T(8,128)S(1)} %pad_maximum_fusion.4), channel_id=1, source_target_pairs={{0,8},{4,12},{8,16},{12,20},{16,24},{20,28},{24,0},{28,4},{1,9},{5... | collective-permute-start | bytes 344072 | tf_op jit(solution)/shard_map/ppermute | solution.py:43
  122.5 3.7 %collective-permute-done.9 = f32[2,7,2048]{2,1,0:T(8,128)S(1)} collective-permute-done((f32[2,7,2048]{2,1,0:T(8,128)S(1)}, f32[2,7,2048]{2,1,0:T(8,128)S(1)}, u32[]{:S(2)}, u32[]{:S(2)}) %collective-permute-start.9) | collective-permute-done | bytes 114720 | tf_op jit(solution)/shard_map/ppermute | solution.py:43
  126.2 3.5 %collective-permute-start.10 = (f32[4,7,2048]{2,1,0:T(8,128)S(1)}, f32[4,7,2048]{2,1,0:T(8,128)S(1)}, u32[]{:S(2)}, u32[]{:S(2)}) collective-permute-start(f32[4,7,2048]{2,1,0:T(8,128)S(1)} %pad_maximum_fusion.2), channel_id=1, source_target_pairs={{0,16},{4,20},{8,24},{12,28},{16,0},{20,4},{24,8},{28,12},{1,17},{... | collective-permute-start | bytes 688136 | tf_op jit(solution)/shard_map/ppermute | solution.py:43
  129.8 1.3 copy.25.own_ref
  131.1 3.0 %collective-permute-done.10 = f32[4,7,2048]{2,1,0:T(8,128)S(1)} collective-permute-done((f32[4,7,2048]{2,1,0:T(8,128)S(1)}, f32[4,7,2048]{2,1,0:T(8,128)S(1)}, u32[]{:S(2)}, u32[]{:S(2)}) %collective-permute-start.10) | collective-permute-done | bytes 229408 | tf_op jit(solution)/shard_map/ppermute | solution.py:43
  135.0 32.0 %shard_map.170 = f32[2048,128]{1,0:T(8,128)} custom-call(s32[208]{0:T(256)} %reshape.383.slots_ref, s32[16]{0:T(128)} %count_ref.1, f32[2048,8]{1,0:T(8,128)} %copy.25.own_ref, f32[8,7,2048]{2,1,0:T(8,128)} %copy-done.1), custom_call_target="tpu_custom_call" | custom-call | tf_op jit(solution)/shard_map/pallas_call | solution.py:164
  167.7 1.3 slice_multiply_fusion.3
  (88 shorter events, 16.7 us)
Async XLA Ops:
  0.6 4.6 %copy-start = (f32[3,128]{1,0:T(4,128)S(1)}, f32[3,128]{1,0:T(4,128)}, u32[]{:S(2)}) copy-start(f32[3,128]{1,0:T(4,128)} %param.25) | copy-start | bytes 4612
  0.6 8.5 %copy-start.8 = (bf16[256,192]{0,1:T(8,128)(2,1)S(1)}, bf16[256,192]{0,1:T(8,128)(2,1)}, u32[]{:S(2)}) copy-start(bf16[256,192]{0,1:T(8,128)(2,1)} %param.18) | copy-start | bytes 294916
  0.7 7.9 %copy-start.9 = (bf16[192,128]{1,0:T(8,128)(2,1)S(1)}, bf16[192,128]{1,0:T(8,128)(2,1)}, u32[]{:S(2)}) copy-start(bf16[192,128]{1,0:T(8,128)(2,1)} %param.19) | copy-start | bytes 147460
  0.7 10.1 %copy-start.10 = (s32[2048]{0:T(1024)S(1)}, s32[2048]{0:T(1024)}, u32[]{:S(2)}) copy-start(s32[2048]{0:T(1024)} %param.21) | copy-start | bytes 24580
  0.7 8.4 %collective-permute-start = (bf16[1,256,192]{1,2,0:T(8,128)(2,1)}, bf16[1,256,192]{1,2,0:T(8,128)(2,1)S(1)}, u32[]{:S(2)}, u32[]{:S(2)}) collective-permute-start(bf16[1,256,192]{1,2,0:T(8,128)(2,1)} %bitcast.206), channel_id=1, source_target_pairs={{0,1},{1,2},{2,3},{3,0},{4,5},{5,6},{6,7},{7,4},{8,9},{9,10},{10,1... | collective-permute-start | bytes 294920 | tf_op jit(solution)/shard_map/ppermute | solution.py:43
  0.7 7.8 %collective-permute-start.2 = (bf16[1,192,128]{2,1,0:T(8,128)(2,1)}, bf16[1,192,128]{2,1,0:T(8,128)(2,1)S(1)}, u32[]{:S(2)}, u32[]{:S(2)}) collective-permute-start(bf16[1,192,128]{2,1,0:T(8,128)(2,1)} %bitcast.209), channel_id=1, source_target_pairs={{0,1},{1,2},{2,3},{3,0},{4,5},{5,6},{6,7},{7,4},{8,9},{9,10},{10,1... | collective-permute-start | bytes 147464 | tf_op jit(solution)/shard_map/ppermute | solution.py:43
  7.8 15.9 %copy-start.12 = (f32[3,2,128]{2,1,0:T(2,128)S(1)}, f32[3,2,128]{2,1,0:T(2,128)}, u32[]{:S(2)}) copy-start(f32[3,2,128]{2,1,0:T(2,128)} %param.30) | copy-start | bytes 9220
  7.8 17.2 %copy-start.3 = (bf16[2048,128]{1,0:T(8,128)(2,1)S(1)}, bf16[2048,128]{1,0:T(8,128)(2,1)}, u32[]{:S(2)}) copy-start(bf16[2048,128]{1,0:T(8,128)(2,1)} %param.20) | copy-start | bytes 1572868
  8.5 5.7 %collective-permute-start.3 = (bf16[2,192,128]{2,1,0:T(8,128)(2,1)S(1)}, bf16[2,192,128]{2,1,0:T(8,128)(2,1)S(1)}, u32[]{:S(2)}, u32[]{:S(2)}) collective-permute-start(bf16[2,192,128]{2,1,0:T(8,128)(2,1)S(1)} %pad_maximum_fusion.5), channel_id=1, source_target_pairs={{0,2},{1,3},{2,0},{3,1},{4,6},{5,7},{6,4},{7,5},{8,10},{9,11},{10,... | collective-permute-start | bytes 294920 | tf_op jit(solution)/shard_map/ppermute | solution.py:43
  9.1 8.4 %collective-permute-start.1 = (bf16[2,256,192]{1,2,0:T(8,128)(2,1)S(1)}, bf16[2,256,192]{1,2,0:T(8,128)(2,1)S(1)}, u32[]{:S(2)}, u32[]{:S(2)}) collective-permute-start(bf16[2,256,192]{1,2,0:T(8,128)(2,1)S(1)} %pad_maximum_fusion.3), channel_id=1, source_target_pairs={{0,2},{1,3},{2,0},{3,1},{4,6},{5,7},{6,4},{7,5},{8,10},{9,11},{10,... | collective-permute-start | bytes 589832 | tf_op jit(solution)/shard_map/ppermute | solution.py:43
  17.9 6.7 %collective-permute-start.4 = (bf16[16,128]{1,0:T(8,128)(2,1)S(1)}, bf16[16,128]{1,0:T(8,128)(2,1)S(1)}, u32[]{:S(2)}, u32[]{:S(2)}) collective-permute-start(bf16[16,128]{1,0:T(8,128)(2,1)S(1)} %get-tuple-element.20), channel_id=1, source_target_pairs={{0,4},{4,8},{8,12},{12,16},{16,20},{20,24},{24,28},{1,5},{5,9},{9,... | collective-permute-start | bytes 12296 | tf_op jit(solution)/shard_map/ppermute | solution.py:31
  19.2 5.9 %collective-permute-start.5 = (bf16[16,128]{1,0:T(8,128)(2,1)S(1)}, bf16[16,128]{1,0:T(8,128)(2,1)S(1)}, u32[]{:S(2)}, u32[]{:S(2)}) collective-permute-start(bf16[16,128]{1,0:T(8,128)(2,1)S(1)} %get-tuple-element.21), channel_id=1, source_target_pairs={{4,0},{8,4},{12,8},{16,12},{20,16},{24,20},{28,24},{5,1},{9,5},{13... | collective-permute-start | bytes 12296 | tf_op jit(solution)/shard_map/ppermute | solution.py:32
  24.6 7.6 %copy-start.14 = (s32[16]{0:T(128)S(1)}, s32[16]{0:T(128)}, u32[]{:S(2)}) copy-start(s32[16]{0:T(128)} %count_ref.1) | copy-start | bytes 196
  25.9 8.2 %collective-permute-start.6 = (f32[1,176,128]{2,1,0:T(8,128)S(1)}, f32[1,176,128]{2,1,0:T(8,128)S(1)}, u32[]{:S(2)}, u32[]{:S(2)}) collective-permute-start(f32[1,176,128]{2,1,0:T(8,128)S(1)} %get-tuple-element.18), channel_id=1, source_target_pairs={{0,4},{4,8},{8,12},{12,16},{16,20},{20,24},{24,28},{1,5},{5,9},{9,... | collective-permute-start | bytes 270344 | tf_op jit(solution)/shard_map/ppermute | solution.py:31
  27.2 6.9 %collective-permute-start.7 = (f32[1,176,128]{2,1,0:T(8,128)S(1)}, f32[1,176,128]{2,1,0:T(8,128)S(1)}, u32[]{:S(2)}, u32[]{:S(2)}) collective-permute-start(f32[1,176,128]{2,1,0:T(8,128)S(1)} %get-tuple-element.19), channel_id=1, source_target_pairs={{4,0},{8,4},{12,8},{16,12},{20,16},{24,20},{28,24},{5,1},{9,5},{13... | collective-permute-start | bytes 270344 | tf_op jit(solution)/shard_map/ppermute | solution.py:32
  38.2 20.4 %copy-start.7 = (bf16[3,128,128]{2,1,0:T(8,128)(2,1)S(1)}, bf16[3,128,128]{2,1,0:T(8,128)(2,1)}, u32[]{:S(2)}) copy-start(bf16[3,128,128]{2,1,0:T(8,128)(2,1)} %param.27) | copy-start | bytes 294916
  58.6 1.7 copy-start.4
  60.3 0.9 copy-start.15
  61.2 1.0 copy-start.5
  110.7 0.9 copy-start.2
  110.7 0.9 copy-start.6
  110.7 0.9 copy-start.13
  111.5 10.1 %copy-start.11 = (s32[16,13]{1,0:T(8,128)S(1)}, s32[16,13]{1,0:T(8,128)}, u32[]{:S(2)}) copy-start(s32[16,13]{1,0:T(8,128)} %param.32) | copy-start | bytes 2500
  112.8 6.8 %collective-permute-start.8 = (f32[1,7,2048]{2,1,0:T(8,128)S(1)}, f32[1,7,2048]{2,1,0:T(8,128)S(1)}, u32[]{:S(2)}, u32[]{:S(2)}) collective-permute-start(f32[1,7,2048]{2,1,0:T(8,128)S(1)} %fusion.84), channel_id=1, source_target_pairs={{0,4},{4,8},{8,12},{12,16},{16,20},{20,24},{24,28},{28,0},{1,5},{5... | collective-permute-start | bytes 172040 | tf_op jit(solution)/shard_map/ppermute | solution.py:43
  119.5 6.6 %collective-permute-start.9 = (f32[2,7,2048]{2,1,0:T(8,128)S(1)}, f32[2,7,2048]{2,1,0:T(8,128)S(1)}, u32[]{:S(2)}, u32[]{:S(2)}) collective-permute-start(f32[2,7,2048]{2,1,0:T(8,128)S(1)} %pad_maximum_fusion.4), channel_id=1, source_target_pairs={{0,8},{4,12},{8,16},{12,20},{16,24},{20,28},{24,0},{28,4},{1,9},{5... | collective-permute-start | bytes 344072 | tf_op jit(solution)/shard_map/ppermute | solution.py:43
  126.2 7.9 %collective-permute-start.10 = (f32[4,7,2048]{2,1,0:T(8,128)S(1)}, f32[4,7,2048]{2,1,0:T(8,128)S(1)}, u32[]{:S(2)}, u32[]{:S(2)}) collective-permute-start(f32[4,7,2048]{2,1,0:T(8,128)S(1)} %pad_maximum_fusion.2), channel_id=1, source_target_pairs={{0,16},{4,20},{8,24},{12,28},{16,0},{20,4},{24,8},{28,12},{1,17},{... | collective-permute-start | bytes 688136 | tf_op jit(solution)/shard_map/ppermute | solution.py:43
  134.2 0.8 copy-start.1

commit v13 on v12

--- a/solution.py
+++ b/solution.py
@@ -106,10 +106,16 @@
     )(queries, padded_kv, band, valid_tab)
 
 ROW_CHUNK = 128
+BLOCK_STEP = 2
 
 
 def lddt_kernel(slots_ref, count_ref, own_ref, coord_ref, out_ref, cols_ref):
-    block = pl.program_id(0)
+    for sub in range(BLOCK_STEP):
+        lddt_block(pl.program_id(0) * BLOCK_STEP + sub, sub * PAIR_BLK, slots_ref, count_ref,
+                   own_ref, coord_ref, out_ref, cols_ref)
+
+
+def lddt_block(block, base, slots_ref, count_ref, own_ref, coord_ref, out_ref, cols_ref):
     live = count_ref[block]
     blocks = count_ref.shape[0]
     max_slots = slots_ref.shape[0] // blocks
@@ -117,7 +123,7 @@
     lane = lax.broadcasted_iota(jnp.int32, shape, 1)
     for chunk in range(PAIR_BLK // ROW_CHUNK):
         rows = slice(chunk * ROW_CHUNK, (chunk + 1) * ROW_CHUNK)
-        own = own_ref[rows, :]
+        own = own_ref[base + chunk * ROW_CHUNK : base + (chunk + 1) * ROW_CHUNK, :]
         for d in range(6):
             cols_ref[d, rows, :] = jnp.broadcast_to(own[:, d : d + 1], shape)
 
@@ -153,7 +159,7 @@
         accs = lax.fori_loop(0, live, slot_body, (zero, zero, zero))
         sums = [-0.0625 * jnp.sum(acc, axis=1, keepdims=True) for acc in accs]
         tile = jnp.where(lane == 0, sums[0], jnp.where(lane == 1, sums[1], jnp.where(lane == 2, sums[2], 0.0)))
-        out_ref[pl.ds(row, ROW_CHUNK), :] = tile
+        out_ref[pl.ds(base + row, ROW_CHUNK), :] = tile
         return carry
 
     lax.fori_loop(0, PAIR_BLK // ROW_CHUNK, row_body, 0)
@@ -165,12 +171,12 @@
         lddt_kernel,
         grid_spec=pltpu.PrefetchScalarGridSpec(
             num_scalar_prefetch=2,
-            grid=(blocks,),
+            grid=(blocks // BLOCK_STEP,),
             in_specs=[
-                pl.BlockSpec((PAIR_BLK, own_tab.shape[1]), lambda b, *_: (b, 0)),
+                pl.BlockSpec((BLOCK_STEP * PAIR_BLK, own_tab.shape[1]), lambda b, *_: (b, 0)),
                 pl.BlockSpec(coord_parts.shape, lambda b, *_: (0, 0, 0)),
             ],
-            out_specs=pl.BlockSpec((PAIR_BLK, PAIR_BLK), lambda b, *_: (b, 0)),
+            out_specs=pl.BlockSpec((BLOCK_STEP * PAIR_BLK, PAIR_BLK), lambda b, *_: (b, 0)),
             scratch_shapes=[pltpu.VMEM((6, PAIR_BLK, PAIR_BLK), jnp.float32)],
         ),
         out_shape=jax.ShapeDtypeStruct((blocks * PAIR_BLK, PAIR_BLK), jnp.float32),

time: 171 us -> 171 us (level)
  the two profiles are of different devices: /device:TPU:26 before, /device:TPU:16 now
where the time goes in v13:
time: 171 us; the launch traced here: 170 us
  Pallas kernels  84.3 us (49%)
  waiting for transfers between devices  27.6 us (16%)
  starting transfers between devices  19.7 us (12%)
  matrix products  17.6 us (10%)
  local copies, waits for them, and re-layouts  9.85 us (6%)
  other arithmetic  6.82 us (4%)
  between operations  3.83 us (2%)
    pallas_call x3, Pallas kernels, window_attend(): pl.pallas_call(attend_kernel, grid=(atoms // Q_TILE,), in_specs=[pl.Block...  58.1 us
    pallas_call x1, Pallas kernels, lddt_sums(): pl.pallas_call(lddt_kernel, grid_spec=pltpu.PrefetchScalarGridSpec(num_sc...  26.3 us
    ppermute x7, waiting for transfers between devices, ring_parts(): parts = jnp.concatenate([parts, lax.ppermute(parts, axis, pairs)])  24.3 us
    dot_general x12, matrix products, dense(): jnp.einsum('sac,cf->saf', left, right, preferred_element_type=jnp.float32)  12.7 us
    ppermute x2, starting transfers between devices, extended(): before = lax.ppermute(last, axis, up)  7.75 us
    ppermute x7, starting transfers between devices, ring_parts(): parts = jnp.concatenate([parts, lax.ppermute(parts, axis, pairs)])  6.06 us
    ppermute x2, starting transfers between devices, extended(): after = lax.ppermute(first, axis, down)  5.91 us
  transfers between devices with their start and end apart: 11, of which 7 were waited for; matrix products, arithmetic and copies ran while one was open for 5% of the time, Pallas kernels for 0%

profile of v13, /device:TPU:16, one launch (start us, length us, event | category | flops | bytes accessed | tf_op | source)
XLA Modules:
  0.0 169.7 jit_solution(10207718545064701870)
XLA Ops:
  0.7 1.6 collective-permute-start.2
  5.2 2.6 %fusion.96 = f32[2048,128]{1,0:T(8,128)S(1)} fusion(f32[3,128]{1,0:T(4,128)S(1)} %copy-done, f32[]{:T(128)} %bitcast.8, f32[3,2048]{1,0:T(4,128)} %param.22, f32[1,3,2048]{2,0,1:T(1,128)} %param.23, f32[]{:T(128)} %bitcast.198), kind=kOutput, calls=%fused_computation.137 | convolution fusion | flops 9455616 | bytes 1099272 | tf_op jit(solution)/shard_map/sda,dc->sac/dot_general | solution.py:232
  9.1 1.6 collective-permute-start.1
  10.7 3.5 %collective-permute-done.3 = bf16[2,192,128]{2,1,0:T(8,128)(2,1)S(1)} collective-permute-done((bf16[2,192,128]{2,1,0:T(8,128)(2,1)S(1)}, bf16[2,192,128]{2,1,0:T(8,128)(2,1)S(1)}, u32[]{:S(2)}, u32[]{:S(2)}) %collective-permute-start.3) | collective-permute-done | bytes 98336 | tf_op jit(solution)/shard_map/ppermute | solution.py:43
  14.3 3.3 %collective-permute-done.1 = bf16[2,256,192]{1,2,0:T(8,128)(2,1)S(1)} collective-permute-done((bf16[2,256,192]{1,2,0:T(8,128)(2,1)S(1)}, bf16[2,256,192]{1,2,0:T(8,128)(2,1)S(1)}, u32[]{:S(2)}, u32[]{:S(2)}) %collective-permute-start.1) | collective-permute-done | bytes 196640 | tf_op jit(solution)/shard_map/ppermute | solution.py:43
  17.9 3.4 %collective-permute-start.4 = (bf16[16,128]{1,0:T(8,128)(2,1)S(1)}, bf16[16,128]{1,0:T(8,128)(2,1)S(1)}, u32[]{:S(2)}, u32[]{:S(2)}) collective-permute-start(bf16[16,128]{1,0:T(8,128)(2,1)S(1)} %get-tuple-element.20), channel_id=1, source_target_pairs={{0,4},{4,8},{8,12},{12,16},{16,20},{20,24},{24,28},{1,5},{5,9},{9,... | collective-permute-start | bytes 12296 | tf_op jit(solution)/shard_map/ppermute | solution.py:31
  21.3 3.3 %collective-permute-start.5 = (bf16[16,128]{1,0:T(8,128)(2,1)S(1)}, bf16[16,128]{1,0:T(8,128)(2,1)S(1)}, u32[]{:S(2)}, u32[]{:S(2)}) collective-permute-start(bf16[16,128]{1,0:T(8,128)(2,1)S(1)} %get-tuple-element.21), channel_id=1, source_target_pairs={{4,0},{8,4},{12,8},{16,12},{20,16},{24,20},{28,24},{5,1},{9,5},{13... | collective-permute-start | bytes 12296 | tf_op jit(solution)/shard_map/ppermute | solution.py:32
  25.5 1.3 collective-permute-done.5
  27.7 4.4 %collective-permute-start.6 = (f32[1,176,128]{2,1,0:T(8,128)S(1)}, f32[1,176,128]{2,1,0:T(8,128)S(1)}, u32[]{:S(2)}, u32[]{:S(2)}) collective-permute-start(f32[1,176,128]{2,1,0:T(8,128)S(1)} %get-tuple-element.18), channel_id=1, source_target_pairs={{0,4},{4,8},{8,12},{12,16},{16,20},{20,24},{24,28},{1,5},{5,9},{9,... | collective-permute-start | bytes 270344 | tf_op jit(solution)/shard_map/ppermute | solution.py:31
  32.0 2.6 %collective-permute-start.7 = (f32[1,176,128]{2,1,0:T(8,128)S(1)}, f32[1,176,128]{2,1,0:T(8,128)S(1)}, u32[]{:S(2)}, u32[]{:S(2)}) collective-permute-start(f32[1,176,128]{2,1,0:T(8,128)S(1)} %get-tuple-element.19), channel_id=1, source_target_pairs={{4,0},{8,4},{12,8},{16,12},{20,16},{24,20},{28,24},{5,1},{9,5},{13... | collective-permute-start | bytes 270344 | tf_op jit(solution)/shard_map/ppermute | solution.py:32
  36.5 2.0 %collective-permute-done.7 = f32[1,176,128]{2,1,0:T(8,128)S(1)} collective-permute-done((f32[1,176,128]{2,1,0:T(8,128)S(1)}, f32[1,176,128]{2,1,0:T(8,128)S(1)}, u32[]{:S(2)}, u32[]{:S(2)}) %collective-permute-start.7) | collective-permute-done | bytes 90144 | tf_op jit(solution)/shard_map/ppermute | solution.py:32
  38.9 1.6 fusion.2
  40.5 1.1 fusion.17.kv_ref
  41.6 0.9 slice_bitcast_fusion.q_ref
  42.5 20.4 %shard_map.167 = bf16[2304,128]{1,0:T(8,128)(2,1)} custom-call(bf16[2304,128]{1,0:T(8,128)(2,1)} %slice_bitcast_fusion.q_ref, bf16[2432,256]{1,0:T(8,128)(2,1)} %fusion.17.kv_ref, f32[128,256]{1,0:T(8,128)} %fusion.72.band_ref, f32[18,256]{1,0:T(8,128)} %fusion.108.valid_ref), custom_call_target="tpu_custom_call" | custom-call | tf_op jit(solution)/shard_map/pallas_call | solution.py:95
  62.9 1.7 multiply_reduce_fusion.2
  65.5 0.9 multiply_reduce_fusion.1
  67.2 1.1 fusion.20.kv_ref
  68.3 0.9 slice_bitcast_fusion.1.q_ref
  69.2 19.3 %shard_map.168 = bf16[2176,128]{1,0:T(8,128)(2,1)} custom-call(bf16[2176,128]{1,0:T(8,128)(2,1)} %slice_bitcast_fusion.1.q_ref, bf16[2304,256]{1,0:T(8,128)(2,1)} %fusion.20.kv_ref, f32[128,256]{1,0:T(8,128)} %fusion.72.band_ref, f32[17,256]{1,0:T(8,128)} %fusion.110.valid_ref), custom_call_target="tpu_custom_call" | custom-call | tf_op jit(solution)/shard_map/pallas_call | solution.py:95
  88.5 1.6 multiply_reduce_fusion.4
  92.4 1.1 fusion.24.kv_ref
  94.3 18.3 %shard_map.169 = bf16[2048,128]{1,0:T(8,128)(2,1)} custom-call(bf16[2048,128]{1,0:T(8,128)(2,1)} %slice_bitcast_fusion.2.q_ref, bf16[2176,256]{1,0:T(8,128)(2,1)} %fusion.24.kv_ref, f32[128,256]{1,0:T(8,128)} %fusion.72.band_ref, f32[16,256]{1,0:T(8,128)} %fusion.115.valid_ref), custom_call_target="tpu_custom_call" | custom-call | tf_op jit(solution)/shard_map/pallas_call | solution.py:95
  112.6 1.6 multiply_reduce_fusion.6
  115.9 1.2 fusion.14
  117.1 1.5 collective-permute-start.8
  118.6 3.7 %collective-permute-done.8 = f32[1,7,2048]{2,1,0:T(8,128)S(1)} collective-permute-done((f32[1,7,2048]{2,1,0:T(8,128)S(1)}, f32[1,7,2048]{2,1,0:T(8,128)S(1)}, u32[]{:S(2)}, u32[]{:S(2)}) %collective-permute-start.8) | collective-permute-done | bytes 57376 | tf_op jit(solution)/shard_map/ppermute | solution.py:43
  123.5 8.1 %collective-permute-done.9 = f32[2,7,2048]{2,1,0:T(8,128)S(1)} collective-permute-done((f32[2,7,2048]{2,1,0:T(8,128)S(1)}, f32[2,7,2048]{2,1,0:T(8,128)S(1)}, u32[]{:S(2)}, u32[]{:S(2)}) %collective-permute-start.9) | collective-permute-done | bytes 114720 | tf_op jit(solution)/shard_map/ppermute | solution.py:43
  132.0 1.3 copy.25.own_ref
  133.3 5.6 %collective-permute-done.10 = f32[4,7,2048]{2,1,0:T(8,128)S(1)} collective-permute-done((f32[4,7,2048]{2,1,0:T(8,128)S(1)}, f32[4,7,2048]{2,1,0:T(8,128)S(1)}, u32[]{:S(2)}, u32[]{:S(2)}) %collective-permute-start.10) | collective-permute-done | bytes 229408 | tf_op jit(solution)/shard_map/ppermute | solution.py:43
  139.8 26.3 %shard_map.170 = f32[2048,128]{1,0:T(8,128)} custom-call(s32[208]{0:T(256)} %reshape.383.slots_ref, s32[16]{0:T(128)} %count_ref.1, f32[2048,8]{1,0:T(8,128)} %copy.25.own_ref, f32[8,7,2048]{2,1,0:T(8,128)} %copy-done.1), custom_call_target="tpu_custom_call" | custom-call | tf_op jit(solution)/shard_map/pallas_call | solution.py:170
  166.8 1.3 slice_multiply_fusion.3
  (88 shorter events, 16.9 us)
Async XLA Ops:
  0.6 4.6 %copy-start = (f32[3,128]{1,0:T(4,128)S(1)}, f32[3,128]{1,0:T(4,128)}, u32[]{:S(2)}) copy-start(f32[3,128]{1,0:T(4,128)} %param.25) | copy-start | bytes 4612
  0.6 8.5 %copy-start.8 = (bf16[256,192]{0,1:T(8,128)(2,1)S(1)}, bf16[256,192]{0,1:T(8,128)(2,1)}, u32[]{:S(2)}) copy-start(bf16[256,192]{0,1:T(8,128)(2,1)} %param.18) | copy-start | bytes 294916
  0.7 7.9 %copy-start.9 = (bf16[192,128]{1,0:T(8,128)(2,1)S(1)}, bf16[192,128]{1,0:T(8,128)(2,1)}, u32[]{:S(2)}) copy-start(bf16[192,128]{1,0:T(8,128)(2,1)} %param.19) | copy-start | bytes 147460
  0.7 10.1 %copy-start.10 = (s32[2048]{0:T(1024)S(1)}, s32[2048]{0:T(1024)}, u32[]{:S(2)}) copy-start(s32[2048]{0:T(1024)} %param.21) | copy-start | bytes 24580
  0.7 8.4 %collective-permute-start = (bf16[1,256,192]{1,2,0:T(8,128)(2,1)}, bf16[1,256,192]{1,2,0:T(8,128)(2,1)S(1)}, u32[]{:S(2)}, u32[]{:S(2)}) collective-permute-start(bf16[1,256,192]{1,2,0:T(8,128)(2,1)} %bitcast.206), channel_id=1, source_target_pairs={{0,1},{1,2},{2,3},{3,0},{4,5},{5,6},{6,7},{7,4},{8,9},{9,10},{10,1... | collective-permute-start | bytes 294920 | tf_op jit(solution)/shard_map/ppermute | solution.py:43
  0.7 7.8 %collective-permute-start.2 = (bf16[1,192,128]{2,1,0:T(8,128)(2,1)}, bf16[1,192,128]{2,1,0:T(8,128)(2,1)S(1)}, u32[]{:S(2)}, u32[]{:S(2)}) collective-permute-start(bf16[1,192,128]{2,1,0:T(8,128)(2,1)} %bitcast.209), channel_id=1, source_target_pairs={{0,1},{1,2},{2,3},{3,0},{4,5},{5,6},{6,7},{7,4},{8,9},{9,10},{10,1... | collective-permute-start | bytes 147464 | tf_op jit(solution)/shard_map/ppermute | solution.py:43
  7.8 16.8 %copy-start.12 = (f32[3,2,128]{2,1,0:T(2,128)S(1)}, f32[3,2,128]{2,1,0:T(2,128)}, u32[]{:S(2)}) copy-start(f32[3,2,128]{2,1,0:T(2,128)} %param.30) | copy-start | bytes 9220
  7.8 19.0 %copy-start.3 = (bf16[2048,128]{1,0:T(8,128)(2,1)S(1)}, bf16[2048,128]{1,0:T(8,128)(2,1)}, u32[]{:S(2)}) copy-start(bf16[2048,128]{1,0:T(8,128)(2,1)} %param.20) | copy-start | bytes 1572868
  8.5 5.7 %collective-permute-start.3 = (bf16[2,192,128]{2,1,0:T(8,128)(2,1)S(1)}, bf16[2,192,128]{2,1,0:T(8,128)(2,1)S(1)}, u32[]{:S(2)}, u32[]{:S(2)}) collective-permute-start(bf16[2,192,128]{2,1,0:T(8,128)(2,1)S(1)} %pad_maximum_fusion.5), channel_id=1, source_target_pairs={{0,2},{1,3},{2,0},{3,1},{4,6},{5,7},{6,4},{7,5},{8,10},{9,11},{10,... | collective-permute-start | bytes 294920 | tf_op jit(solution)/shard_map/ppermute | solution.py:43
  9.1 8.4 %collective-permute-start.1 = (bf16[2,256,192]{1,2,0:T(8,128)(2,1)S(1)}, bf16[2,256,192]{1,2,0:T(8,128)(2,1)S(1)}, u32[]{:S(2)}, u32[]{:S(2)}) collective-permute-start(bf16[2,256,192]{1,2,0:T(8,128)(2,1)S(1)} %pad_maximum_fusion.3), channel_id=1, source_target_pairs={{0,2},{1,3},{2,0},{3,1},{4,6},{5,7},{6,4},{7,5},{8,10},{9,11},{10,... | collective-permute-start | bytes 589832 | tf_op jit(solution)/shard_map/ppermute | solution.py:43
  17.9 7.6 %collective-permute-start.4 = (bf16[16,128]{1,0:T(8,128)(2,1)S(1)}, bf16[16,128]{1,0:T(8,128)(2,1)S(1)}, u32[]{:S(2)}, u32[]{:S(2)}) collective-permute-start(bf16[16,128]{1,0:T(8,128)(2,1)S(1)} %get-tuple-element.20), channel_id=1, source_target_pairs={{0,4},{4,8},{8,12},{12,16},{16,20},{20,24},{24,28},{1,5},{5,9},{9,... | collective-permute-start | bytes 12296 | tf_op jit(solution)/shard_map/ppermute | solution.py:31
  21.3 5.5 %collective-permute-start.5 = (bf16[16,128]{1,0:T(8,128)(2,1)S(1)}, bf16[16,128]{1,0:T(8,128)(2,1)S(1)}, u32[]{:S(2)}, u32[]{:S(2)}) collective-permute-start(bf16[16,128]{1,0:T(8,128)(2,1)S(1)} %get-tuple-element.21), channel_id=1, source_target_pairs={{4,0},{8,4},{12,8},{16,12},{20,16},{24,20},{28,24},{5,1},{9,5},{13... | collective-permute-start | bytes 12296 | tf_op jit(solution)/shard_map/ppermute | solution.py:32
  25.5 9.1 %copy-start.14 = (s32[16]{0:T(128)S(1)}, s32[16]{0:T(128)}, u32[]{:S(2)}) copy-start(s32[16]{0:T(128)} %count_ref.1) | copy-start | bytes 196
  27.7 8.8 %collective-permute-start.6 = (f32[1,176,128]{2,1,0:T(8,128)S(1)}, f32[1,176,128]{2,1,0:T(8,128)S(1)}, u32[]{:S(2)}, u32[]{:S(2)}) collective-permute-start(f32[1,176,128]{2,1,0:T(8,128)S(1)} %get-tuple-element.18), channel_id=1, source_target_pairs={{0,4},{4,8},{8,12},{12,16},{16,20},{20,24},{24,28},{1,5},{5,9},{9,... | collective-permute-start | bytes 270344 | tf_op jit(solution)/shard_map/ppermute | solution.py:31
  32.0 6.4 %collective-permute-start.7 = (f32[1,176,128]{2,1,0:T(8,128)S(1)}, f32[1,176,128]{2,1,0:T(8,128)S(1)}, u32[]{:S(2)}, u32[]{:S(2)}) collective-permute-start(f32[1,176,128]{2,1,0:T(8,128)S(1)} %get-tuple-element.19), channel_id=1, source_target_pairs={{4,0},{8,4},{12,8},{16,12},{20,16},{24,20},{28,24},{5,1},{9,5},{13... | collective-permute-start | bytes 270344 | tf_op jit(solution)/shard_map/ppermute | solution.py:32
  42.5 20.4 %copy-start.7 = (bf16[3,128,128]{2,1,0:T(8,128)(2,1)S(1)}, bf16[3,128,128]{2,1,0:T(8,128)(2,1)}, u32[]{:S(2)}) copy-start(bf16[3,128,128]{2,1,0:T(8,128)(2,1)} %param.27) | copy-start | bytes 294916
  62.9 1.7 copy-start.4
  64.6 0.9 copy-start.15
  65.5 1.0 copy-start.5
  115.0 0.9 copy-start.2
  115.0 0.9 copy-start.6
  115.0 0.9 copy-start.13
  115.8 6.9 %copy-start.11 = (s32[16,13]{1,0:T(8,128)S(1)}, s32[16,13]{1,0:T(8,128)}, u32[]{:S(2)}) copy-start(s32[16,13]{1,0:T(8,128)} %param.32) | copy-start | bytes 2500
  117.1 5.3 %collective-permute-start.8 = (f32[1,7,2048]{2,1,0:T(8,128)S(1)}, f32[1,7,2048]{2,1,0:T(8,128)S(1)}, u32[]{:S(2)}, u32[]{:S(2)}) collective-permute-start(f32[1,7,2048]{2,1,0:T(8,128)S(1)} %fusion.84), channel_id=1, source_target_pairs={{0,4},{4,8},{8,12},{12,16},{16,20},{20,24},{24,28},{28,0},{1,5},{5... | collective-permute-start | bytes 172040 | tf_op jit(solution)/shard_map/ppermute | solution.py:43
  122.4 9.2 %collective-permute-start.9 = (f32[2,7,2048]{2,1,0:T(8,128)S(1)}, f32[2,7,2048]{2,1,0:T(8,128)S(1)}, u32[]{:S(2)}, u32[]{:S(2)}) collective-permute-start(f32[2,7,2048]{2,1,0:T(8,128)S(1)} %pad_maximum_fusion.4), channel_id=1, source_target_pairs={{0,8},{4,12},{8,16},{12,20},{16,24},{20,28},{24,0},{28,4},{1,9},{5... | collective-permute-start | bytes 344072 | tf_op jit(solution)/shard_map/ppermute | solution.py:43
  131.6 7.3 %collective-permute-start.10 = (f32[4,7,2048]{2,1,0:T(8,128)S(1)}, f32[4,7,2048]{2,1,0:T(8,128)S(1)}, u32[]{:S(2)}, u32[]{:S(2)}) collective-permute-start(f32[4,7,2048]{2,1,0:T(8,128)S(1)} %pad_maximum_fusion.2), channel_id=1, source_target_pairs={{0,16},{4,20},{8,24},{12,28},{16,0},{20,4},{24,8},{28,12},{1,17},{... | collective-permute-start | bytes 688136 | tf_op jit(solution)/shard_map/ppermute | solution.py:43
  139.0 0.8 copy-start.1

commit v14 on v12

--- a/solution.py
+++ b/solution.py
@@ -108,7 +108,7 @@
 ROW_CHUNK = 128
 
 
-def lddt_kernel(slots_ref, count_ref, own_ref, coord_ref, out_ref, cols_ref):
+def lddt_kernel(slots_ref, count_ref, own_ref, coord_ref, out_ref, cols_ref, acc_ref):
     block = pl.program_id(0)
     live = count_ref[block]
     blocks = count_ref.shape[0]
@@ -147,11 +147,17 @@
             curve = [jnp.tanh(0.5 * t - half_err) for t in thresholds]
             bend = curve[0] * curve[0] + curve[1] * curve[1] + curve[2] * curve[2] + curve[3] * curve[3]
             coef = ((4.0 - bend) * gap_dist) * (inv_err * inv_pred)
-            return tuple(acc + coef * gap for acc, gap in zip(accs, gaps))
-
-        zero = jnp.zeros(shape, jnp.float32)
-        accs = lax.fori_loop(0, live, slot_body, (zero, zero, zero))
-        sums = [-0.0625 * jnp.sum(acc, axis=1, keepdims=True) for acc in accs]
+            for d in range(3):
+                acc_ref[d, pl.ds(row, ROW_CHUNK), :] += coef * gaps[d]
+            return accs
+
+        for d in range(3):
+            acc_ref[d, pl.ds(row, ROW_CHUNK), :] = jnp.zeros(shape, jnp.float32)
+        lax.fori_loop(0, live, slot_body, 0)
+        sums = [
+            -0.0625 * jnp.sum(acc_ref[d, pl.ds(row, ROW_CHUNK), :], axis=1, keepdims=True)
+            for d in range(3)
+        ]
         tile = jnp.where(lane == 0, sums[0], jnp.where(lane == 1, sums[1], jnp.where(lane == 2, sums[2], 0.0)))
         out_ref[pl.ds(row, ROW_CHUNK), :] = tile
         return carry
@@ -171,7 +177,10 @@
                 pl.BlockSpec(coord_parts.shape, lambda b, *_: (0, 0, 0)),
             ],
             out_specs=pl.BlockSpec((PAIR_BLK, PAIR_BLK), lambda b, *_: (b, 0)),
-            scratch_shapes=[pltpu.VMEM((6, PAIR_BLK, PAIR_BLK), jnp.float32)],
+            scratch_shapes=[
+                pltpu.VMEM((6, PAIR_BLK, PAIR_BLK), jnp.float32),
+                pltpu.VMEM((3, PAIR_BLK, PAIR_BLK), jnp.float32),
+            ],
         ),
         out_shape=jax.ShapeDtypeStruct((blocks * PAIR_BLK, PAIR_BLK), jnp.float32),
     )(slots, counts, own_tab, coord_parts)

time: 171 us -> 169 us (0.988); the launches traced: 171 us -> 166 us
  Pallas kernels: 90.1 us -> 85.4 us
    pallas_call x1, Pallas kernels: 32 us -> 27.3 us  [lddt_sums(): pl.pallas_call(lddt_kernel, grid_spec=pltpu.PrefetchScalarGridSpec(num_sc...]
where the time goes in v14:
time: 169 us; the launch traced here: 166 us
  Pallas kernels  85.4 us (51%)
  starting transfers between devices  26.2 us (16%)
  matrix products  17.6 us (10%)
  waiting for transfers between devices  16.3 us (10%)
  local copies, waits for them, and re-layouts  9.85 us (6%)
  other arithmetic  6.82 us (4%)
  between operations  3.83 us (2%)
    pallas_call x3, Pallas kernels, window_attend(): pl.pallas_call(attend_kernel, grid=(atoms // Q_TILE,), in_specs=[pl.Block...  58.1 us
    pallas_call x1, Pallas kernels, lddt_sums(): pl.pallas_call(lddt_kernel, grid_spec=pltpu.PrefetchScalarGridSpec(num_sc...  27.3 us
    ppermute x7, waiting for transfers between devices, ring_parts(): parts = jnp.concatenate([parts, lax.ppermute(parts, axis, pairs)])  15.7 us
    ppermute x7, starting transfers between devices, ring_parts(): parts = jnp.concatenate([parts, lax.ppermute(parts, axis, pairs)])  14 us
    dot_general x12, matrix products, dense(): jnp.einsum('sac,cf->saf', left, right, preferred_element_type=jnp.float32)  12.7 us
    ppermute x2, starting transfers between devices, extended(): after = lax.ppermute(first, axis, down)  9.54 us
  transfers between devices with their start and end apart: 11, of which 6 were waited for; matrix products, arithmetic and copies ran while one was open for 5% of the time, Pallas kernels for 0%

profile of v14, /device:TPU:26, one launch (start us, length us, event | category | flops | bytes accessed | tf_op | source)
XLA Modules:
  0.0 165.9 jit_solution(13740778084766752836)
XLA Ops:
  0.7 1.6 collective-permute-start.2
  5.2 2.6 %fusion.96 = f32[2048,128]{1,0:T(8,128)S(1)} fusion(f32[3,128]{1,0:T(4,128)S(1)} %copy-done, f32[]{:T(128)} %bitcast.8, f32[3,2048]{1,0:T(4,128)} %param.22, f32[1,3,2048]{2,0,1:T(1,128)} %param.23, f32[]{:T(128)} %bitcast.198), kind=kOutput, calls=%fused_computation.137 | convolution fusion | flops 9455616 | bytes 1099272 | tf_op jit(solution)/shard_map/sda,dc->sac/dot_general | solution.py:235
  9.1 1.6 collective-permute-start.1
  10.7 3.5 %collective-permute-done.3 = bf16[2,192,128]{2,1,0:T(8,128)(2,1)S(1)} collective-permute-done((bf16[2,192,128]{2,1,0:T(8,128)(2,1)S(1)}, bf16[2,192,128]{2,1,0:T(8,128)(2,1)S(1)}, u32[]{:S(2)}, u32[]{:S(2)}) %collective-permute-start.3) | collective-permute-done | bytes 98336 | tf_op jit(solution)/shard_map/ppermute | solution.py:43
  14.3 3.3 %collective-permute-done.1 = bf16[2,256,192]{1,2,0:T(8,128)(2,1)S(1)} collective-permute-done((bf16[2,256,192]{1,2,0:T(8,128)(2,1)S(1)}, bf16[2,256,192]{1,2,0:T(8,128)(2,1)S(1)}, u32[]{:S(2)}, u32[]{:S(2)}) %collective-permute-start.1) | collective-permute-done | bytes 196640 | tf_op jit(solution)/shard_map/ppermute | solution.py:43
  17.9 1.3 collective-permute-start.4
  19.2 4.5 %collective-permute-start.5 = (bf16[16,128]{1,0:T(8,128)(2,1)S(1)}, bf16[16,128]{1,0:T(8,128)(2,1)S(1)}, u32[]{:S(2)}, u32[]{:S(2)}) collective-permute-start(bf16[16,128]{1,0:T(8,128)(2,1)S(1)} %get-tuple-element.21), channel_id=1, source_target_pairs={{4,0},{8,4},{12,8},{16,12},{20,16},{24,20},{28,24},{5,1},{9,5},{13... | collective-permute-start | bytes 12296 | tf_op jit(solution)/shard_map/ppermute | solution.py:32
  25.9 1.3 collective-permute-start.6
  27.2 5.0 %collective-permute-start.7 = (f32[1,176,128]{2,1,0:T(8,128)S(1)}, f32[1,176,128]{2,1,0:T(8,128)S(1)}, u32[]{:S(2)}, u32[]{:S(2)}) collective-permute-start(f32[1,176,128]{2,1,0:T(8,128)S(1)} %get-tuple-element.19), channel_id=1, source_target_pairs={{4,0},{8,4},{12,8},{16,12},{20,16},{24,20},{28,24},{5,1},{9,5},{13... | collective-permute-start | bytes 270344 | tf_op jit(solution)/shard_map/ppermute | solution.py:32
  34.6 1.6 fusion.2
  36.2 1.1 fusion.17.kv_ref
  38.2 20.4 %shard_map.167 = bf16[2304,128]{1,0:T(8,128)(2,1)} custom-call(bf16[2304,128]{1,0:T(8,128)(2,1)} %slice_bitcast_fusion.q_ref, bf16[2432,256]{1,0:T(8,128)(2,1)} %fusion.17.kv_ref, f32[128,256]{1,0:T(8,128)} %fusion.72.band_ref, f32[18,256]{1,0:T(8,128)} %fusion.108.valid_ref), custom_call_target="tpu_custom_call" | custom-call | tf_op jit(solution)/shard_map/pallas_call | solution.py:95
  58.6 1.7 multiply_reduce_fusion.2
  61.2 0.9 multiply_reduce_fusion.1
  62.9 1.1 fusion.20.kv_ref
  64.0 0.9 slice_bitcast_fusion.1.q_ref
  64.9 19.3 %shard_map.168 = bf16[2176,128]{1,0:T(8,128)(2,1)} custom-call(bf16[2176,128]{1,0:T(8,128)(2,1)} %slice_bitcast_fusion.1.q_ref, bf16[2304,256]{1,0:T(8,128)(2,1)} %fusion.20.kv_ref, f32[128,256]{1,0:T(8,128)} %fusion.72.band_ref, f32[17,256]{1,0:T(8,128)} %fusion.110.valid_ref), custom_call_target="tpu_custom_call" | custom-call | tf_op jit(solution)/shard_map/pallas_call | solution.py:95
  84.2 1.6 multiply_reduce_fusion.4
  86.6 0.9 multiply_reduce_fusion.3
  88.1 1.1 fusion.24.kv_ref
  90.0 18.3 %shard_map.169 = bf16[2048,128]{1,0:T(8,128)(2,1)} custom-call(bf16[2048,128]{1,0:T(8,128)(2,1)} %slice_bitcast_fusion.2.q_ref, bf16[2176,256]{1,0:T(8,128)(2,1)} %fusion.24.kv_ref, f32[128,256]{1,0:T(8,128)} %fusion.72.band_ref, f32[16,256]{1,0:T(8,128)} %fusion.115.valid_ref), custom_call_target="tpu_custom_call" | custom-call | tf_op jit(solution)/shard_map/pallas_call | solution.py:95
  108.3 1.6 multiply_reduce_fusion.6
  111.6 1.2 fusion.14
  112.8 4.5 %collective-permute-start.8 = (f32[1,7,2048]{2,1,0:T(8,128)S(1)}, f32[1,7,2048]{2,1,0:T(8,128)S(1)}, u32[]{:S(2)}, u32[]{:S(2)}) collective-permute-start(f32[1,7,2048]{2,1,0:T(8,128)S(1)} %fusion.84), channel_id=1, source_target_pairs={{0,4},{4,8},{8,12},{12,16},{16,20},{20,24},{24,28},{28,0},{1,5},{5... | collective-permute-start | bytes 172040 | tf_op jit(solution)/shard_map/ppermute | solution.py:43
  117.3 2.2 %collective-permute-done.8 = f32[1,7,2048]{2,1,0:T(8,128)S(1)} collective-permute-done((f32[1,7,2048]{2,1,0:T(8,128)S(1)}, f32[1,7,2048]{2,1,0:T(8,128)S(1)}, u32[]{:S(2)}, u32[]{:S(2)}) %collective-permute-start.8) | collective-permute-done | bytes 57376 | tf_op jit(solution)/shard_map/ppermute | solution.py:43
  119.5 2.1 %collective-permute-start.9 = (f32[2,7,2048]{2,1,0:T(8,128)S(1)}, f32[2,7,2048]{2,1,0:T(8,128)S(1)}, u32[]{:S(2)}, u32[]{:S(2)}) collective-permute-start(f32[2,7,2048]{2,1,0:T(8,128)S(1)} %pad_maximum_fusion.4), channel_id=1, source_target_pairs={{0,8},{4,12},{8,16},{12,20},{16,24},{20,28},{24,0},{28,4},{1,9},{5... | collective-permute-start | bytes 344072 | tf_op jit(solution)/shard_map/ppermute | solution.py:43
  122.5 3.7 %collective-permute-done.9 = f32[2,7,2048]{2,1,0:T(8,128)S(1)} collective-permute-done((f32[2,7,2048]{2,1,0:T(8,128)S(1)}, f32[2,7,2048]{2,1,0:T(8,128)S(1)}, u32[]{:S(2)}, u32[]{:S(2)}) %collective-permute-start.9) | collective-permute-done | bytes 114720 | tf_op jit(solution)/shard_map/ppermute | solution.py:43
  126.2 3.5 %collective-permute-start.10 = (f32[4,7,2048]{2,1,0:T(8,128)S(1)}, f32[4,7,2048]{2,1,0:T(8,128)S(1)}, u32[]{:S(2)}, u32[]{:S(2)}) collective-permute-start(f32[4,7,2048]{2,1,0:T(8,128)S(1)} %pad_maximum_fusion.2), channel_id=1, source_target_pairs={{0,16},{4,20},{8,24},{12,28},{16,0},{20,4},{24,8},{28,12},{1,17},{... | collective-permute-start | bytes 688136 | tf_op jit(solution)/shard_map/ppermute | solution.py:43
  129.8 1.3 copy.25.own_ref
  131.1 3.0 %collective-permute-done.10 = f32[4,7,2048]{2,1,0:T(8,128)S(1)} collective-permute-done((f32[4,7,2048]{2,1,0:T(8,128)S(1)}, f32[4,7,2048]{2,1,0:T(8,128)S(1)}, u32[]{:S(2)}, u32[]{:S(2)}) %collective-permute-start.10) | collective-permute-done | bytes 229408 | tf_op jit(solution)/shard_map/ppermute | solution.py:43
  135.0 27.3 %shard_map.170 = f32[2048,128]{1,0:T(8,128)} custom-call(s32[208]{0:T(256)} %reshape.383.slots_ref, s32[16]{0:T(128)} %count_ref.1, f32[2048,8]{1,0:T(8,128)} %copy.25.own_ref, f32[8,7,2048]{2,1,0:T(8,128)} %copy-done.1), custom_call_target="tpu_custom_call" | custom-call | tf_op jit(solution)/shard_map/pallas_call | solution.py:170
  163.0 1.3 slice_multiply_fusion.3
  (88 shorter events, 16.7 us)
Async XLA Ops:
  0.6 4.6 %copy-start = (f32[3,128]{1,0:T(4,128)S(1)}, f32[3,128]{1,0:T(4,128)}, u32[]{:S(2)}) copy-start(f32[3,128]{1,0:T(4,128)} %param.25) | copy-start | bytes 4612
  0.6 8.5 %copy-start.8 = (bf16[256,192]{0,1:T(8,128)(2,1)S(1)}, bf16[256,192]{0,1:T(8,128)(2,1)}, u32[]{:S(2)}) copy-start(bf16[256,192]{0,1:T(8,128)(2,1)} %param.18) | copy-start | bytes 294916
  0.7 7.9 %copy-start.9 = (bf16[192,128]{1,0:T(8,128)(2,1)S(1)}, bf16[192,128]{1,0:T(8,128)(2,1)}, u32[]{:S(2)}) copy-start(bf16[192,128]{1,0:T(8,128)(2,1)} %param.19) | copy-start | bytes 147460
  0.7 10.1 %copy-start.10 = (s32[2048]{0:T(1024)S(1)}, s32[2048]{0:T(1024)}, u32[]{:S(2)}) copy-start(s32[2048]{0:T(1024)} %param.21) | copy-start | bytes 24580
  0.7 8.4 %collective-permute-start = (bf16[1,256,192]{1,2,0:T(8,128)(2,1)}, bf16[1,256,192]{1,2,0:T(8,128)(2,1)S(1)}, u32[]{:S(2)}, u32[]{:S(2)}) collective-permute-start(bf16[1,256,192]{1,2,0:T(8,128)(2,1)} %bitcast.206), channel_id=1, source_target_pairs={{0,1},{1,2},{2,3},{3,0},{4,5},{5,6},{6,7},{7,4},{8,9},{9,10},{10,1... | collective-permute-start | bytes 294920 | tf_op jit(solution)/shard_map/ppermute | solution.py:43
  0.7 7.8 %collective-permute-start.2 = (bf16[1,192,128]{2,1,0:T(8,128)(2,1)}, bf16[1,192,128]{2,1,0:T(8,128)(2,1)S(1)}, u32[]{:S(2)}, u32[]{:S(2)}) collective-permute-start(bf16[1,192,128]{2,1,0:T(8,128)(2,1)} %bitcast.209), channel_id=1, source_target_pairs={{0,1},{1,2},{2,3},{3,0},{4,5},{5,6},{6,7},{7,4},{8,9},{9,10},{10,1... | collective-permute-start | bytes 147464 | tf_op jit(solution)/shard_map/ppermute | solution.py:43
  7.8 15.9 %copy-start.12 = (f32[3,2,128]{2,1,0:T(2,128)S(1)}, f32[3,2,128]{2,1,0:T(2,128)}, u32[]{:S(2)}) copy-start(f32[3,2,128]{2,1,0:T(2,128)} %param.30) | copy-start | bytes 9220
  7.8 17.2 %copy-start.3 = (bf16[2048,128]{1,0:T(8,128)(2,1)S(1)}, bf16[2048,128]{1,0:T(8,128)(2,1)}, u32[]{:S(2)}) copy-start(bf16[2048,128]{1,0:T(8,128)(2,1)} %param.20) | copy-start | bytes 1572868
  8.5 5.7 %collective-permute-start.3 = (bf16[2,192,128]{2,1,0:T(8,128)(2,1)S(1)}, bf16[2,192,128]{2,1,0:T(8,128)(2,1)S(1)}, u32[]{:S(2)}, u32[]{:S(2)}) collective-permute-start(bf16[2,192,128]{2,1,0:T(8,128)(2,1)S(1)} %pad_maximum_fusion.5), channel_id=1, source_target_pairs={{0,2},{1,3},{2,0},{3,1},{4,6},{5,7},{6,4},{7,5},{8,10},{9,11},{10,... | collective-permute-start | bytes 294920 | tf_op jit(solution)/shard_map/ppermute | solution.py:43
  9.1 8.4 %collective-permute-start.1 = (bf16[2,256,192]{1,2,0:T(8,128)(2,1)S(1)}, bf16[2,256,192]{1,2,0:T(8,128)(2,1)S(1)}, u32[]{:S(2)}, u32[]{:S(2)}) collective-permute-start(bf16[2,256,192]{1,2,0:T(8,128)(2,1)S(1)} %pad_maximum_fusion.3), channel_id=1, source_target_pairs={{0,2},{1,3},{2,0},{3,1},{4,6},{5,7},{6,4},{7,5},{8,10},{9,11},{10,... | collective-permute-start | bytes 589832 | tf_op jit(solution)/shard_map/ppermute | solution.py:43
  17.9 6.7 %collective-permute-start.4 = (bf16[16,128]{1,0:T(8,128)(2,1)S(1)}, bf16[16,128]{1,0:T(8,128)(2,1)S(1)}, u32[]{:S(2)}, u32[]{:S(2)}) collective-permute-start(bf16[16,128]{1,0:T(8,128)(2,1)S(1)} %get-tuple-element.20), channel_id=1, source_target_pairs={{0,4},{4,8},{8,12},{12,16},{16,20},{20,24},{24,28},{1,5},{5,9},{9,... | collective-permute-start | bytes 12296 | tf_op jit(solution)/shard_map/ppermute | solution.py:31
  19.2 5.9 %collective-permute-start.5 = (bf16[16,128]{1,0:T(8,128)(2,1)S(1)}, bf16[16,128]{1,0:T(8,128)(2,1)S(1)}, u32[]{:S(2)}, u32[]{:S(2)}) collective-permute-start(bf16[16,128]{1,0:T(8,128)(2,1)S(1)} %get-tuple-element.21), channel_id=1, source_target_pairs={{4,0},{8,4},{12,8},{16,12},{20,16},{24,20},{28,24},{5,1},{9,5},{13... | collective-permute-start | bytes 12296 | tf_op jit(solution)/shard_map/ppermute | solution.py:32
  24.6 7.6 %copy-start.14 = (s32[16]{0:T(128)S(1)}, s32[16]{0:T(128)}, u32[]{:S(2)}) copy-start(s32[16]{0:T(128)} %count_ref.1) | copy-start | bytes 196
  25.9 8.2 %collective-permute-start.6 = (f32[1,176,128]{2,1,0:T(8,128)S(1)}, f32[1,176,128]{2,1,0:T(8,128)S(1)}, u32[]{:S(2)}, u32[]{:S(2)}) collective-permute-start(f32[1,176,128]{2,1,0:T(8,128)S(1)} %get-tuple-element.18), channel_id=1, source_target_pairs={{0,4},{4,8},{8,12},{12,16},{16,20},{20,24},{24,28},{1,5},{5,9},{9,... | collective-permute-start | bytes 270344 | tf_op jit(solution)/shard_map/ppermute | solution.py:31
  27.2 6.9 %collective-permute-start.7 = (f32[1,176,128]{2,1,0:T(8,128)S(1)}, f32[1,176,128]{2,1,0:T(8,128)S(1)}, u32[]{:S(2)}, u32[]{:S(2)}) collective-permute-start(f32[1,176,128]{2,1,0:T(8,128)S(1)} %get-tuple-element.19), channel_id=1, source_target_pairs={{4,0},{8,4},{12,8},{16,12},{20,16},{24,20},{28,24},{5,1},{9,5},{13... | collective-permute-start | bytes 270344 | tf_op jit(solution)/shard_map/ppermute | solution.py:32
  38.2 20.4 %copy-start.7 = (bf16[3,128,128]{2,1,0:T(8,128)(2,1)S(1)}, bf16[3,128,128]{2,1,0:T(8,128)(2,1)}, u32[]{:S(2)}) copy-start(bf16[3,128,128]{2,1,0:T(8,128)(2,1)} %param.27) | copy-start | bytes 294916
  58.6 1.7 %copy-start.4 = (bf16[3,128,512]{2,1,0:T(8,128)(2,1)S(1)}, bf16[3,128,512]{2,1,0:T(8,128)(2,1)}, u32[]{:S(2)}) copy-start(bf16[3,128,512]{2,1,0:T(8,128)(2,1)} %param.28) | copy-start | bytes 1179652
  60.3 0.9 copy-start.15
  61.2 1.0 copy-start.5
  110.7 0.9 copy-start.2
  110.7 0.9 copy-start.6
  110.7 0.9 copy-start.13
  111.5 10.1 %copy-start.11 = (s32[16,13]{1,0:T(8,128)S(1)}, s32[16,13]{1,0:T(8,128)}, u32[]{:S(2)}) copy-start(s32[16,13]{1,0:T(8,128)} %param.32) | copy-start | bytes 2500
  112.8 6.8 %collective-permute-start.8 = (f32[1,7,2048]{2,1,0:T(8,128)S(1)}, f32[1,7,2048]{2,1,0:T(8,128)S(1)}, u32[]{:S(2)}, u32[]{:S(2)}) collective-permute-start(f32[1,7,2048]{2,1,0:T(8,128)S(1)} %fusion.84), channel_id=1, source_target_pairs={{0,4},{4,8},{8,12},{12,16},{16,20},{20,24},{24,28},{28,0},{1,5},{5... | collective-permute-start | bytes 172040 | tf_op jit(solution)/shard_map/ppermute | solution.py:43
  119.5 6.6 %collective-permute-start.9 = (f32[2,7,2048]{2,1,0:T(8,128)S(1)}, f32[2,7,2048]{2,1,0:T(8,128)S(1)}, u32[]{:S(2)}, u32[]{:S(2)}) collective-permute-start(f32[2,7,2048]{2,1,0:T(8,128)S(1)} %pad_maximum_fusion.4), channel_id=1, source_target_pairs={{0,8},{4,12},{8,16},{12,20},{16,24},{20,28},{24,0},{28,4},{1,9},{5... | collective-permute-start | bytes 344072 | tf_op jit(solution)/shard_map/ppermute | solution.py:43
  126.2 7.9 %collective-permute-start.10 = (f32[4,7,2048]{2,1,0:T(8,128)S(1)}, f32[4,7,2048]{2,1,0:T(8,128)S(1)}, u32[]{:S(2)}, u32[]{:S(2)}) collective-permute-start(f32[4,7,2048]{2,1,0:T(8,128)S(1)} %pad_maximum_fusion.2), channel_id=1, source_target_pairs={{0,16},{4,20},{8,24},{12,28},{16,0},{20,4},{24,8},{28,12},{1,17},{... | collective-permute-start | bytes 688136 | tf_op jit(solution)/shard_map/ppermute | solution.py:43
  134.2 0.8 copy-start.1

commit v15 on v14

--- a/solution.py
+++ b/solution.py
@@ -34,11 +34,11 @@
     return value
 
 
-def ring_parts(value, axis):
+def ring_parts(value, axis, direct=False):
     peers = lax.axis_size(axis)
     parts = value[None]
     span = 1
-    while span < peers and peers % (2 * span) == 0:
+    while not direct and span < peers and peers % (2 * span) == 0:
         pairs = [(i, (i + span) % peers) for i in range(peers)]
         parts = jnp.concatenate([parts, lax.ppermute(parts, axis, pairs)])
         span *= 2
@@ -287,7 +287,9 @@
     count_row = jnp.zeros((1, atom_rows), jnp.float32).at[0, 0].set(
         jnp.sum(pair_count.astype(jnp.float32) * (PAIR_BLK * PAIR_BLK) - PAIR_BLK)
     )
-    coord_parts = ring_parts(jnp.concatenate([predicted[0], true_coords, count_row], axis=0), "atoms")
+    coord_parts = ring_parts(
+        jnp.concatenate([predicted[0], true_coords, count_row], axis=0), "atoms", direct=atom_peers <= 8
+    )
     pair_total = jnp.sum(coord_parts[:, 6, 0])
     own_tab = jnp.concatenate(
         [predicted[0], true_coords, jnp.zeros((2, atom_rows), jnp.float32)], axis=0

time: 169 us -> 167 us (0.988); the launches traced: 166 us -> 168 us
  waiting for transfers between devices: 16.3 us -> 13.3 us
  Pallas kernels: 85.4 us -> 88.3 us
  starting transfers between devices: 26.2 us -> 28.4 us
    ppermute x0 -> x7, starting transfers between devices: none -> 12.5 us  [ring_parts(): extra.append(lax.ppermute(value, axis, pairs)[None])]
    ppermute x7 -> x4, starting transfers between devices: 14 us -> 3.86 us  [ring_parts(): parts = jnp.concatenate([parts, lax.ppermute(parts, axis, pairs)])]
    ppermute x7 -> x4, waiting for transfers between devices: 15.7 us -> 6.83 us  [ring_parts(): parts = jnp.concatenate([parts, lax.ppermute(parts, axis, pairs)])]
    ppermute x0 -> x7, waiting for transfers between devices: none -> 6.43 us  [ring_parts(): extra.append(lax.ppermute(value, axis, pairs)[None])]
    pallas_call x1, Pallas kernels: 27.3 us -> 30.3 us  [lddt_sums(): pl.pallas_call(lddt_kernel, grid_spec=pltpu.PrefetchScalarGridSpec(num_sc...]
  transfers between devices with their start and end apart: 11 -> 15, of which waited for: 6 -> 5; matrix products, arithmetic and copies ran while one was open for 5% -> 5% of each run, Pallas kernels for 0% -> 0%
where the time goes in v15:
time: 167 us; the launch traced here: 168 us
  Pallas kernels  88.3 us (53%)
  starting transfers between devices  28.4 us (17%)
  matrix products  17.6 us (11%)
  waiting for transfers between devices  13.3 us (8%)
  local copies, waits for them, and re-layouts  9.87 us (6%)
  other arithmetic  6.74 us (4%)
  between operations  3.85 us (2%)
    pallas_call x3, Pallas kernels, window_attend(): pl.pallas_call(attend_kernel, grid=(atoms // Q_TILE,), in_specs=[pl.Block...  58 us
    pallas_call x1, Pallas kernels, lddt_sums(): pl.pallas_call(lddt_kernel, grid_spec=pltpu.PrefetchScalarGridSpec(num_sc...  30.3 us
    dot_general x12, matrix products, dense(): jnp.einsum('sac,cf->saf', left, right, preferred_element_type=jnp.float32)  12.7 us
    ppermute x7, starting transfers between devices, ring_parts(): extra.append(lax.ppermute(value, axis, pairs)[None])  12.5 us
    ppermute x2, starting transfers between devices, extended(): after = lax.ppermute(first, axis, down)  9.41 us
    ppermute x4, waiting for transfers between devices, ring_parts(): parts = jnp.concatenate([parts, lax.ppermute(parts, axis, pairs)])  6.83 us
    ppermute x7, waiting for transfers between devices, ring_parts(): extra.append(lax.ppermute(value, axis, pairs)[None])  6.43 us
    ppermute x4, starting transfers between devices, ring_parts(): parts = jnp.concatenate([parts, lax.ppermute(parts, axis, pairs)])  3.86 us
  transfers between devices with their start and end apart: 15, of which 5 were waited for; matrix products, arithmetic and copies ran while one was open for 5% of the time, Pallas kernels for 0%

profile of v15, /device:TPU:26, one launch (start us, length us, event | category | flops | bytes accessed | tf_op | source)
XLA Modules:
  0.0 168.0 jit_solution(11976417024967597084)
XLA Ops:
  0.8 1.6 collective-permute-start.2
  5.9 2.6 %fusion.95 = f32[2048,128]{1,0:T(8,128)S(1)} fusion(f32[3,128]{1,0:T(4,128)S(1)} %copy-done, f32[]{:T(128)} %bitcast.8, f32[3,2048]{1,0:T(4,128)} %param.22, f32[1,3,2048]{2,0,1:T(1,128)} %param.23, f32[]{:T(128)} %bitcast.212), kind=kOutput, calls=%fused_computation.141 | convolution fusion | flops 9455616 | bytes 1099272 | tf_op jit(solution)/shard_map/sda,dc->sac/dot_general | solution.py:235
  9.2 1.6 collective-permute-start.1
  10.8 3.5 %collective-permute-done.3 = bf16[2,192,128]{2,1,0:T(8,128)(2,1)S(1)} collective-permute-done((bf16[2,192,128]{2,1,0:T(8,128)(2,1)S(1)}, bf16[2,192,128]{2,1,0:T(8,128)(2,1)S(1)}, u32[]{:S(2)}, u32[]{:S(2)}) %collective-permute-start.3) | collective-permute-done | bytes 98336 | tf_op jit(solution)/shard_map/ppermute | solution.py:43
  14.4 3.3 %collective-permute-done.1 = bf16[2,256,192]{1,2,0:T(8,128)(2,1)S(1)} collective-permute-done((bf16[2,256,192]{1,2,0:T(8,128)(2,1)S(1)}, bf16[2,256,192]{1,2,0:T(8,128)(2,1)S(1)}, u32[]{:S(2)}, u32[]{:S(2)}) %collective-permute-start.1) | collective-permute-done | bytes 196640 | tf_op jit(solution)/shard_map/ppermute | solution.py:43
  18.0 1.3 collective-permute-start.4
  19.3 4.5 %collective-permute-start.5 = (bf16[16,128]{1,0:T(8,128)(2,1)S(1)}, bf16[16,128]{1,0:T(8,128)(2,1)S(1)}, u32[]{:S(2)}, u32[]{:S(2)}) collective-permute-start(bf16[16,128]{1,0:T(8,128)(2,1)S(1)} %get-tuple-element.23), channel_id=1, source_target_pairs={{4,0},{8,4},{12,8},{16,12},{20,16},{24,20},{28,24},{5,1},{9,5},{13... | collective-permute-start | bytes 12296 | tf_op jit(solution)/shard_map/ppermute | solution.py:32
  26.1 1.3 collective-permute-start.6
  27.4 4.9 %collective-permute-start.7 = (f32[1,176,128]{2,1,0:T(8,128)S(1)}, f32[1,176,128]{2,1,0:T(8,128)S(1)}, u32[]{:S(2)}, u32[]{:S(2)}) collective-permute-start(f32[1,176,128]{2,1,0:T(8,128)S(1)} %get-tuple-element.21), channel_id=1, source_target_pairs={{4,0},{8,4},{12,8},{16,12},{20,16},{24,20},{28,24},{5,1},{9,5},{13... | collective-permute-start | bytes 270344 | tf_op jit(solution)/shard_map/ppermute | solution.py:32
  34.7 1.6 fusion.2
  36.3 1.1 fusion.17.kv_ref
  37.5 0.9 slice_bitcast_fusion.q_ref
  38.3 20.4 %shard_map.167 = bf16[2304,128]{1,0:T(8,128)(2,1)} custom-call(bf16[2304,128]{1,0:T(8,128)(2,1)} %slice_bitcast_fusion.q_ref, bf16[2432,256]{1,0:T(8,128)(2,1)} %fusion.17.kv_ref, f32[128,256]{1,0:T(8,128)} %fusion.72.band_ref, f32[18,256]{1,0:T(8,128)} %fusion.107.valid_ref), custom_call_target="tpu_custom_call" | custom-call | tf_op jit(solution)/shard_map/pallas_call | solution.py:95
  58.8 1.7 multiply_reduce_fusion.2
  61.4 0.9 multiply_reduce_fusion.1
  63.0 1.1 fusion.20.kv_ref
  65.0 19.3 %shard_map.168 = bf16[2176,128]{1,0:T(8,128)(2,1)} custom-call(bf16[2176,128]{1,0:T(8,128)(2,1)} %slice_bitcast_fusion.1.q_ref, bf16[2304,256]{1,0:T(8,128)(2,1)} %fusion.20.kv_ref, f32[128,256]{1,0:T(8,128)} %fusion.72.band_ref, f32[17,256]{1,0:T(8,128)} %fusion.109.valid_ref), custom_call_target="tpu_custom_call" | custom-call | tf_op jit(solution)/shard_map/pallas_call | solution.py:95
  84.3 1.6 multiply_reduce_fusion.4
  88.3 1.1 fusion.24.kv_ref
  90.2 18.3 %shard_map.169 = bf16[2048,128]{1,0:T(8,128)(2,1)} custom-call(bf16[2048,128]{1,0:T(8,128)(2,1)} %slice_bitcast_fusion.2.q_ref, bf16[2176,256]{1,0:T(8,128)(2,1)} %fusion.24.kv_ref, f32[128,256]{1,0:T(8,128)} %fusion.72.band_ref, f32[16,256]{1,0:T(8,128)} %fusion.114.valid_ref), custom_call_target="tpu_custom_call" | custom-call | tf_op jit(solution)/shard_map/pallas_call | solution.py:95
  108.5 1.5 multiply_reduce_fusion.6
  111.7 1.2 fusion.14
  112.9 4.5 %collective-permute-start.8 = (f32[7,2048]{1,0:T(8,128)S(1)}, f32[7,2048]{1,0:T(8,128)S(1)}, u32[]{:S(2)}, u32[]{:S(2)}) collective-permute-start(f32[7,2048]{1,0:T(8,128)S(1)} %get-tuple-element.17), channel_id=1, source_target_pairs={{0,4},{4,8},{8,12},{12,16},{16,20},{20,24},{24,28},{28,0},{1,5},{5... | collective-permute-start | bytes 172040 | tf_op jit(solution)/shard_map/ppermute | solution.py:49
  117.4 1.6 collective-permute-start.9
  118.9 1.6 collective-permute-start.10
  120.5 1.2 collective-permute-start.11
  122.1 1.3 copy.25.own_ref
  123.5 2.8 %collective-permute-start.13 = (f32[7,2048]{1,0:T(8,128)S(1)}, f32[7,2048]{1,0:T(8,128)S(1)}, u32[]{:S(2)}, u32[]{:S(2)}) collective-permute-start(f32[7,2048]{1,0:T(8,128)S(1)} %get-tuple-element.17), channel_id=1, source_target_pairs={{0,24},{4,28},{8,0},{12,4},{16,8},{20,12},{24,16},{28,20},{1,25},{... | collective-permute-start | bytes 172040 | tf_op jit(solution)/shard_map/ppermute | solution.py:49
  127.0 2.7 %collective-permute-done.12 = f32[7,2048]{1,0:T(8,128)S(1)} collective-permute-done((f32[7,2048]{1,0:T(8,128)S(1)}, f32[7,2048]{1,0:T(8,128)S(1)}, u32[]{:S(2)}, u32[]{:S(2)}) %collective-permute-start.12) | collective-permute-done | bytes 57376 | tf_op jit(solution)/shard_map/ppermute | solution.py:49
  129.7 3.6 %collective-permute-done.14 = f32[7,2048]{1,0:T(8,128)S(1)} collective-permute-done((f32[7,2048]{1,0:T(8,128)S(1)}, f32[7,2048]{1,0:T(8,128)S(1)}, u32[]{:S(2)}, u32[]{:S(2)}) %collective-permute-start.14) | collective-permute-done | bytes 57376 | tf_op jit(solution)/shard_map/ppermute | solution.py:49
  134.1 30.3 %shard_map.170 = f32[2048,128]{1,0:T(8,128)} custom-call(s32[208]{0:T(256)} %reshape.383.slots_ref, s32[16]{0:T(128)} %count_ref.1, f32[2048,8]{1,0:T(8,128)} %copy.25.own_ref, f32[8,7,2048]{2,1,0:T(8,128)} %copy-done.2), custom_call_target="tpu_custom_call" | custom-call | tf_op jit(solution)/shard_map/pallas_call | solution.py:170
  165.1 1.3 slice_multiply_fusion.3
  (100 shorter events, 17.9 us)
Async XLA Ops:
  0.6 5.3 %copy-start = (f32[3,128]{1,0:T(4,128)S(1)}, f32[3,128]{1,0:T(4,128)}, u32[]{:S(2)}) copy-start(f32[3,128]{1,0:T(4,128)} %param.25) | copy-start | bytes 4612
  0.6 8.5 %copy-start.8 = (bf16[256,192]{0,1:T(8,128)(2,1)S(1)}, bf16[256,192]{0,1:T(8,128)(2,1)}, u32[]{:S(2)}) copy-start(bf16[256,192]{0,1:T(8,128)(2,1)} %param.18) | copy-start | bytes 294916
  0.7 7.9 %copy-start.9 = (bf16[192,128]{1,0:T(8,128)(2,1)S(1)}, bf16[192,128]{1,0:T(8,128)(2,1)}, u32[]{:S(2)}) copy-start(bf16[192,128]{1,0:T(8,128)(2,1)} %param.19) | copy-start | bytes 147460
  0.7 7.8 %copy-start.10 = (s32[16,13]{1,0:T(8,128)S(1)}, s32[16,13]{1,0:T(8,128)}, u32[]{:S(2)}) copy-start(s32[16,13]{1,0:T(8,128)} %param.32) | copy-start | bytes 2500
  0.7 10.1 %copy-start.11 = (s32[2048]{0:T(1024)S(1)}, s32[2048]{0:T(1024)}, u32[]{:S(2)}) copy-start(s32[2048]{0:T(1024)} %param.21) | copy-start | bytes 24580
  0.7 8.5 %collective-permute-start = (bf16[1,256,192]{1,2,0:T(8,128)(2,1)}, bf16[1,256,192]{1,2,0:T(8,128)(2,1)S(1)}, u32[]{:S(2)}, u32[]{:S(2)}) collective-permute-start(bf16[1,256,192]{1,2,0:T(8,128)(2,1)} %bitcast.220), channel_id=1, source_target_pairs={{0,1},{1,2},{2,3},{3,0},{4,5},{5,6},{6,7},{7,4},{8,9},{9,10},{10,1... | collective-permute-start | bytes 294920 | tf_op jit(solution)/shard_map/ppermute | solution.py:43
  0.8 7.8 %collective-permute-start.2 = (bf16[1,192,128]{2,1,0:T(8,128)(2,1)}, bf16[1,192,128]{2,1,0:T(8,128)(2,1)S(1)}, u32[]{:S(2)}, u32[]{:S(2)}) collective-permute-start(bf16[1,192,128]{2,1,0:T(8,128)(2,1)} %bitcast.223), channel_id=1, source_target_pairs={{0,1},{1,2},{2,3},{3,0},{4,5},{5,6},{6,7},{7,4},{8,9},{9,10},{10,1... | collective-permute-start | bytes 147464 | tf_op jit(solution)/shard_map/ppermute | solution.py:43
  8.5 15.3 %copy-start.12 = (f32[3,2,128]{2,1,0:T(2,128)S(1)}, f32[3,2,128]{2,1,0:T(2,128)}, u32[]{:S(2)}) copy-start(f32[3,2,128]{2,1,0:T(2,128)} %param.30) | copy-start | bytes 9220
  8.5 16.7 %copy-start.3 = (bf16[2048,128]{1,0:T(8,128)(2,1)S(1)}, bf16[2048,128]{1,0:T(8,128)(2,1)}, u32[]{:S(2)}) copy-start(bf16[2048,128]{1,0:T(8,128)(2,1)} %param.20) | copy-start | bytes 1572868
  8.6 5.7 %collective-permute-start.3 = (bf16[2,192,128]{2,1,0:T(8,128)(2,1)S(1)}, bf16[2,192,128]{2,1,0:T(8,128)(2,1)S(1)}, u32[]{:S(2)}, u32[]{:S(2)}) collective-permute-start(bf16[2,192,128]{2,1,0:T(8,128)(2,1)S(1)} %pad_maximum_fusion.2), channel_id=1, source_target_pairs={{0,2},{1,3},{2,0},{3,1},{4,6},{5,7},{6,4},{7,5},{8,10},{9,11},{10,... | collective-permute-start | bytes 294920 | tf_op jit(solution)/shard_map/ppermute | solution.py:43
  9.2 8.4 %collective-permute-start.1 = (bf16[2,256,192]{1,2,0:T(8,128)(2,1)S(1)}, bf16[2,256,192]{1,2,0:T(8,128)(2,1)S(1)}, u32[]{:S(2)}, u32[]{:S(2)}) collective-permute-start(bf16[2,256,192]{1,2,0:T(8,128)(2,1)S(1)} %pad_maximum_fusion.1), channel_id=1, source_target_pairs={{0,2},{1,3},{2,0},{3,1},{4,6},{5,7},{6,4},{7,5},{8,10},{9,11},{10,... | collective-permute-start | bytes 589832 | tf_op jit(solution)/shard_map/ppermute | solution.py:43
  18.0 7.3 %collective-permute-start.4 = (bf16[16,128]{1,0:T(8,128)(2,1)S(1)}, bf16[16,128]{1,0:T(8,128)(2,1)S(1)}, u32[]{:S(2)}, u32[]{:S(2)}) collective-permute-start(bf16[16,128]{1,0:T(8,128)(2,1)S(1)} %get-tuple-element.22), channel_id=1, source_target_pairs={{0,4},{4,8},{8,12},{12,16},{16,20},{20,24},{24,28},{1,5},{5,9},{9,... | collective-permute-start | bytes 12296 | tf_op jit(solution)/shard_map/ppermute | solution.py:31
  19.3 6.0 %collective-permute-start.5 = (bf16[16,128]{1,0:T(8,128)(2,1)S(1)}, bf16[16,128]{1,0:T(8,128)(2,1)S(1)}, u32[]{:S(2)}, u32[]{:S(2)}) collective-permute-start(bf16[16,128]{1,0:T(8,128)(2,1)S(1)} %get-tuple-element.23), channel_id=1, source_target_pairs={{4,0},{8,4},{12,8},{16,12},{20,16},{24,20},{28,24},{5,1},{9,5},{13... | collective-permute-start | bytes 12296 | tf_op jit(solution)/shard_map/ppermute | solution.py:32
  25.2 7.0 %copy-start.14 = (s32[16]{0:T(128)S(1)}, s32[16]{0:T(128)}, u32[]{:S(2)}) copy-start(s32[16]{0:T(128)} %count_ref.1) | copy-start | bytes 196
  26.1 8.2 %collective-permute-start.6 = (f32[1,176,128]{2,1,0:T(8,128)S(1)}, f32[1,176,128]{2,1,0:T(8,128)S(1)}, u32[]{:S(2)}, u32[]{:S(2)}) collective-permute-start(f32[1,176,128]{2,1,0:T(8,128)S(1)} %get-tuple-element.20), channel_id=1, source_target_pairs={{0,4},{4,8},{8,12},{12,16},{16,20},{20,24},{24,28},{1,5},{5,9},{9,... | collective-permute-start | bytes 270344 | tf_op jit(solution)/shard_map/ppermute | solution.py:31
  27.4 6.9 %collective-permute-start.7 = (f32[1,176,128]{2,1,0:T(8,128)S(1)}, f32[1,176,128]{2,1,0:T(8,128)S(1)}, u32[]{:S(2)}, u32[]{:S(2)}) collective-permute-start(f32[1,176,128]{2,1,0:T(8,128)S(1)} %get-tuple-element.21), channel_id=1, source_target_pairs={{4,0},{8,4},{12,8},{16,12},{20,16},{24,20},{28,24},{5,1},{9,5},{13... | collective-permute-start | bytes 270344 | tf_op jit(solution)/shard_map/ppermute | solution.py:32
  38.3 20.4 %copy-start.7 = (bf16[3,128,128]{2,1,0:T(8,128)(2,1)S(1)}, bf16[3,128,128]{2,1,0:T(8,128)(2,1)}, u32[]{:S(2)}) copy-start(bf16[3,128,128]{2,1,0:T(8,128)(2,1)} %param.27) | copy-start | bytes 294916
  58.8 1.7 copy-start.4
  60.5 0.9 copy-start.15
  61.4 1.0 copy-start.5
  110.8 0.9 copy-start.1
  110.8 0.9 copy-start.6
  110.8 0.9 copy-start.13
  112.9 10.6 %collective-permute-start.8 = (f32[7,2048]{1,0:T(8,128)S(1)}, f32[7,2048]{1,0:T(8,128)S(1)}, u32[]{:S(2)}, u32[]{:S(2)}) collective-permute-start(f32[7,2048]{1,0:T(8,128)S(1)} %get-tuple-element.17), channel_id=1, source_target_pairs={{0,4},{4,8},{8,12},{12,16},{16,20},{20,24},{24,28},{28,0},{1,5},{5... | collective-permute-start | bytes 172040 | tf_op jit(solution)/shard_map/ppermute | solution.py:49
  117.4 8.9 %collective-permute-start.9 = (f32[7,2048]{1,0:T(8,128)S(1)}, f32[7,2048]{1,0:T(8,128)S(1)}, u32[]{:S(2)}, u32[]{:S(2)}) collective-permute-start(f32[7,2048]{1,0:T(8,128)S(1)} %get-tuple-element.17), channel_id=1, source_target_pairs={{0,8},{4,12},{8,16},{12,20},{16,24},{20,28},{24,0},{28,4},{1,9},{5... | collective-permute-start | bytes 172040 | tf_op jit(solution)/shard_map/ppermute | solution.py:49
  118.9 7.9 %collective-permute-start.10 = (f32[7,2048]{1,0:T(8,128)S(1)}, f32[7,2048]{1,0:T(8,128)S(1)}, u32[]{:S(2)}, u32[]{:S(2)}) collective-permute-start(f32[7,2048]{1,0:T(8,128)S(1)} %get-tuple-element.17), channel_id=1, source_target_pairs={{0,12},{4,16},{8,20},{12,24},{16,28},{20,0},{24,4},{28,8},{1,13},{... | collective-permute-start | bytes 172040 | tf_op jit(solution)/shard_map/ppermute | solution.py:49
  120.5 6.4 %collective-permute-start.11 = (f32[7,2048]{1,0:T(8,128)S(1)}, f32[7,2048]{1,0:T(8,128)S(1)}, u32[]{:S(2)}, u32[]{:S(2)}) collective-permute-start(f32[7,2048]{1,0:T(8,128)S(1)} %get-tuple-element.17), channel_id=1, source_target_pairs={{0,16},{4,20},{8,24},{12,28},{16,0},{20,4},{24,8},{28,12},{1,17},{... | collective-permute-start | bytes 172040 | tf_op jit(solution)/shard_map/ppermute | solution.py:49
  121.8 7.9 %collective-permute-start.12 = (f32[7,2048]{1,0:T(8,128)S(1)}, f32[7,2048]{1,0:T(8,128)S(1)}, u32[]{:S(2)}, u32[]{:S(2)}) collective-permute-start(f32[7,2048]{1,0:T(8,128)S(1)} %get-tuple-element.17), channel_id=1, source_target_pairs={{0,20},{4,24},{8,28},{12,0},{16,4},{20,8},{24,12},{28,16},{1,21},{... | collective-permute-start | bytes 172040 | tf_op jit(solution)/shard_map/ppermute | solution.py:49
  123.5 6.2 %collective-permute-start.13 = (f32[7,2048]{1,0:T(8,128)S(1)}, f32[7,2048]{1,0:T(8,128)S(1)}, u32[]{:S(2)}, u32[]{:S(2)}) collective-permute-start(f32[7,2048]{1,0:T(8,128)S(1)} %get-tuple-element.17), channel_id=1, source_target_pairs={{0,24},{4,28},{8,0},{12,4},{16,8},{20,12},{24,16},{28,20},{1,25},{... | collective-permute-start | bytes 172040 | tf_op jit(solution)/shard_map/ppermute | solution.py:49
  126.3 7.0 %collective-permute-start.14 = (f32[7,2048]{1,0:T(8,128)S(1)}, f32[7,2048]{1,0:T(8,128)S(1)}, u32[]{:S(2)}, u32[]{:S(2)}) collective-permute-start(f32[7,2048]{1,0:T(8,128)S(1)} %get-tuple-element.17), channel_id=1, source_target_pairs={{0,28},{4,0},{8,4},{12,8},{16,12},{20,16},{24,20},{28,24},{1,29},{... | collective-permute-start | bytes 172040 | tf_op jit(solution)/shard_map/ppermute | solution.py:49
  133.3 0.8 copy-start.2

commit v16 on v15

--- a/solution.py
+++ b/solution.py
@@ -159,7 +159,7 @@
             for d in range(3)
         ]
         tile = jnp.where(lane == 0, sums[0], jnp.where(lane == 1, sums[1], jnp.where(lane == 2, sums[2], 0.0)))
-        out_ref[pl.ds(row, ROW_CHUNK), :] = tile
+        out_ref[pl.ds(row, ROW_CHUNK), :] = tile[:, : out_ref.shape[1]]
         return carry
 
     lax.fori_loop(0, PAIR_BLK // ROW_CHUNK, row_body, 0)
@@ -176,13 +176,13 @@
                 pl.BlockSpec((PAIR_BLK, own_tab.shape[1]), lambda b, *_: (b, 0)),
                 pl.BlockSpec(coord_parts.shape, lambda b, *_: (0, 0, 0)),
             ],
-            out_specs=pl.BlockSpec((PAIR_BLK, PAIR_BLK), lambda b, *_: (b, 0)),
+            out_specs=pl.BlockSpec((PAIR_BLK, 8), lambda b, *_: (b, 0)),
             scratch_shapes=[
                 pltpu.VMEM((6, PAIR_BLK, PAIR_BLK), jnp.float32),
                 pltpu.VMEM((3, PAIR_BLK, PAIR_BLK), jnp.float32),
             ],
         ),
-        out_shape=jax.ShapeDtypeStruct((blocks * PAIR_BLK, PAIR_BLK), jnp.float32),
+        out_shape=jax.ShapeDtypeStruct((blocks * PAIR_BLK, 8), jnp.float32),
     )(slots, counts, own_tab, coord_parts)
     return out[:, :3].T
 

time: 167 us -> 167 us (level)
  no operation moved by 1% of the time
where the time goes in v16:
time: 167 us
  Pallas kernels  86.9 us (52%)
  starting transfers between devices  28.4 us (17%)
  matrix products  17.6 us (11%)
  waiting for transfers between devices  13.3 us (8%)
  local copies, waits for them, and re-layouts  9.87 us (6%)
  other arithmetic  6.74 us (4%)
  between operations  3.85 us (2%)
    pallas_call x3, Pallas kernels, window_attend(): pl.pallas_call(attend_kernel, grid=(atoms // Q_TILE,), in_specs=[pl.Block...  58 us
    pallas_call x1, Pallas kernels, lddt_sums(): pl.pallas_call(lddt_kernel, grid_spec=pltpu.PrefetchScalarGridSpec(num_sc...  28.9 us
    dot_general x12, matrix products, dense(): jnp.einsum('sac,cf->saf', left, right, preferred_element_type=jnp.float32)  12.7 us
    ppermute x7, starting transfers between devices, ring_parts(): extra.append(lax.ppermute(value, axis, pairs)[None])  12.5 us
    ppermute x2, starting transfers between devices, extended(): after = lax.ppermute(first, axis, down)  9.41 us
    ppermute x4, waiting for transfers between devices, ring_parts(): parts = jnp.concatenate([parts, lax.ppermute(parts, axis, pairs)])  6.83 us
    ppermute x7, waiting for transfers between devices, ring_parts(): extra.append(lax.ppermute(value, axis, pairs)[None])  6.43 us
    ppermute x4, starting transfers between devices, ring_parts(): parts = jnp.concatenate([parts, lax.ppermute(parts, axis, pairs)])  3.86 us
  transfers between devices with their start and end apart: 15, of which 5 were waited for; matrix products, arithmetic and copies ran while one was open for 5% of the time, Pallas kernels for 0%

profile of v16, /device:TPU:26, one launch (start us, length us, event | category | flops | bytes accessed | tf_op | source)
XLA Modules:
  0.0 166.6 jit_solution(16602992431647180708)
XLA Ops:
  0.8 1.6 collective-permute-start.2
  5.9 2.6 %fusion.95 = f32[2048,128]{1,0:T(8,128)S(1)} fusion(f32[3,128]{1,0:T(4,128)S(1)} %copy-done, f32[]{:T(128)} %bitcast.8, f32[3,2048]{1,0:T(4,128)} %param.22, f32[1,3,2048]{2,0,1:T(1,128)} %param.23, f32[]{:T(128)} %bitcast.212), kind=kOutput, calls=%fused_computation.141 | convolution fusion | flops 9455616 | bytes 1099272 | tf_op jit(solution)/shard_map/sda,dc->sac/dot_general | solution.py:235
  9.2 1.6 collective-permute-start.1
  10.8 3.5 %collective-permute-done.3 = bf16[2,192,128]{2,1,0:T(8,128)(2,1)S(1)} collective-permute-done((bf16[2,192,128]{2,1,0:T(8,128)(2,1)S(1)}, bf16[2,192,128]{2,1,0:T(8,128)(2,1)S(1)}, u32[]{:S(2)}, u32[]{:S(2)}) %collective-permute-start.3) | collective-permute-done | bytes 98336 | tf_op jit(solution)/shard_map/ppermute | solution.py:43
  14.4 3.3 %collective-permute-done.1 = bf16[2,256,192]{1,2,0:T(8,128)(2,1)S(1)} collective-permute-done((bf16[2,256,192]{1,2,0:T(8,128)(2,1)S(1)}, bf16[2,256,192]{1,2,0:T(8,128)(2,1)S(1)}, u32[]{:S(2)}, u32[]{:S(2)}) %collective-permute-start.1) | collective-permute-done | bytes 196640 | tf_op jit(solution)/shard_map/ppermute | solution.py:43
  18.0 1.3 collective-permute-start.4
  19.3 4.5 %collective-permute-start.5 = (bf16[16,128]{1,0:T(8,128)(2,1)S(1)}, bf16[16,128]{1,0:T(8,128)(2,1)S(1)}, u32[]{:S(2)}, u32[]{:S(2)}) collective-permute-start(bf16[16,128]{1,0:T(8,128)(2,1)S(1)} %get-tuple-element.23), channel_id=1, source_target_pairs={{4,0},{8,4},{12,8},{16,12},{20,16},{24,20},{28,24},{5,1},{9,5},{13... | collective-permute-start | bytes 12296 | tf_op jit(solution)/shard_map/ppermute | solution.py:32
  26.1 1.3 collective-permute-start.6
  27.4 4.9 %collective-permute-start.7 = (f32[1,176,128]{2,1,0:T(8,128)S(1)}, f32[1,176,128]{2,1,0:T(8,128)S(1)}, u32[]{:S(2)}, u32[]{:S(2)}) collective-permute-start(f32[1,176,128]{2,1,0:T(8,128)S(1)} %get-tuple-element.21), channel_id=1, source_target_pairs={{4,0},{8,4},{12,8},{16,12},{20,16},{24,20},{28,24},{5,1},{9,5},{13... | collective-permute-start | bytes 270344 | tf_op jit(solution)/shard_map/ppermute | solution.py:32
  34.7 1.6 fusion.2
  36.3 1.1 fusion.17.kv_ref
  37.5 0.9 slice_bitcast_fusion.q_ref
  38.3 20.4 %shard_map.167 = bf16[2304,128]{1,0:T(8,128)(2,1)} custom-call(bf16[2304,128]{1,0:T(8,128)(2,1)} %slice_bitcast_fusion.q_ref, bf16[2432,256]{1,0:T(8,128)(2,1)} %fusion.17.kv_ref, f32[128,256]{1,0:T(8,128)} %fusion.72.band_ref, f32[18,256]{1,0:T(8,128)} %fusion.107.valid_ref), custom_call_target="tpu_custom_call" | custom-call | tf_op jit(solution)/shard_map/pallas_call | solution.py:95
  58.8 1.7 multiply_reduce_fusion.2
  61.4 0.9 multiply_reduce_fusion.1
  63.0 1.1 fusion.20.kv_ref
  65.0 19.3 %shard_map.168 = bf16[2176,128]{1,0:T(8,128)(2,1)} custom-call(bf16[2176,128]{1,0:T(8,128)(2,1)} %slice_bitcast_fusion.1.q_ref, bf16[2304,256]{1,0:T(8,128)(2,1)} %fusion.20.kv_ref, f32[128,256]{1,0:T(8,128)} %fusion.72.band_ref, f32[17,256]{1,0:T(8,128)} %fusion.109.valid_ref), custom_call_target="tpu_custom_call" | custom-call | tf_op jit(solution)/shard_map/pallas_call | solution.py:95
  84.3 1.6 multiply_reduce_fusion.4
  88.3 1.1 fusion.24.kv_ref
  90.2 18.3 %shard_map.169 = bf16[2048,128]{1,0:T(8,128)(2,1)} custom-call(bf16[2048,128]{1,0:T(8,128)(2,1)} %slice_bitcast_fusion.2.q_ref, bf16[2176,256]{1,0:T(8,128)(2,1)} %fusion.24.kv_ref, f32[128,256]{1,0:T(8,128)} %fusion.72.band_ref, f32[16,256]{1,0:T(8,128)} %fusion.114.valid_ref), custom_call_target="tpu_custom_call" | custom-call | tf_op jit(solution)/shard_map/pallas_call | solution.py:95
  108.5 1.5 multiply_reduce_fusion.6
  111.7 1.2 fusion.14
  112.9 4.5 %collective-permute-start.8 = (f32[7,2048]{1,0:T(8,128)S(1)}, f32[7,2048]{1,0:T(8,128)S(1)}, u32[]{:S(2)}, u32[]{:S(2)}) collective-permute-start(f32[7,2048]{1,0:T(8,128)S(1)} %get-tuple-element.17), channel_id=1, source_target_pairs={{0,4},{4,8},{8,12},{12,16},{16,20},{20,24},{24,28},{28,0},{1,5},{5... | collective-permute-start | bytes 172040 | tf_op jit(solution)/shard_map/ppermute | solution.py:49
  117.4 1.6 collective-permute-start.9
  118.9 1.6 collective-permute-start.10
  120.5 1.2 collective-permute-start.11
  122.1 1.3 copy.25.own_ref
  123.5 2.8 %collective-permute-start.13 = (f32[7,2048]{1,0:T(8,128)S(1)}, f32[7,2048]{1,0:T(8,128)S(1)}, u32[]{:S(2)}, u32[]{:S(2)}) collective-permute-start(f32[7,2048]{1,0:T(8,128)S(1)} %get-tuple-element.17), channel_id=1, source_target_pairs={{0,24},{4,28},{8,0},{12,4},{16,8},{20,12},{24,16},{28,20},{1,25},{... | collective-permute-start | bytes 172040 | tf_op jit(solution)/shard_map/ppermute | solution.py:49
  127.0 2.7 %collective-permute-done.12 = f32[7,2048]{1,0:T(8,128)S(1)} collective-permute-done((f32[7,2048]{1,0:T(8,128)S(1)}, f32[7,2048]{1,0:T(8,128)S(1)}, u32[]{:S(2)}, u32[]{:S(2)}) %collective-permute-start.12) | collective-permute-done | bytes 57376 | tf_op jit(solution)/shard_map/ppermute | solution.py:49
  129.7 3.6 %collective-permute-done.14 = f32[7,2048]{1,0:T(8,128)S(1)} collective-permute-done((f32[7,2048]{1,0:T(8,128)S(1)}, f32[7,2048]{1,0:T(8,128)S(1)}, u32[]{:S(2)}, u32[]{:S(2)}) %collective-permute-start.14) | collective-permute-done | bytes 57376 | tf_op jit(solution)/shard_map/ppermute | solution.py:49
  134.1 28.9 %shard_map.170 = f32[2048,8]{1,0:T(8,128)} custom-call(s32[208]{0:T(256)} %reshape.383.slots_ref, s32[16]{0:T(128)} %count_ref.1, f32[2048,8]{1,0:T(8,128)} %copy.25.own_ref, f32[8,7,2048]{2,1,0:T(8,128)} %copy-done.2), custom_call_target="tpu_custom_call" | custom-call | tf_op jit(solution)/shard_map/pallas_call | solution.py:170
  163.7 1.3 slice_multiply_fusion.3
  (100 shorter events, 17.9 us)
Async XLA Ops:
  0.6 5.3 %copy-start = (f32[3,128]{1,0:T(4,128)S(1)}, f32[3,128]{1,0:T(4,128)}, u32[]{:S(2)}) copy-start(f32[3,128]{1,0:T(4,128)} %param.25) | copy-start | bytes 4612
  0.6 8.5 %copy-start.8 = (bf16[256,192]{0,1:T(8,128)(2,1)S(1)}, bf16[256,192]{0,1:T(8,128)(2,1)}, u32[]{:S(2)}) copy-start(bf16[256,192]{0,1:T(8,128)(2,1)} %param.18) | copy-start | bytes 294916
  0.7 7.9 %copy-start.9 = (bf16[192,128]{1,0:T(8,128)(2,1)S(1)}, bf16[192,128]{1,0:T(8,128)(2,1)}, u32[]{:S(2)}) copy-start(bf16[192,128]{1,0:T(8,128)(2,1)} %param.19) | copy-start | bytes 147460
  0.7 7.8 %copy-start.10 = (s32[16,13]{1,0:T(8,128)S(1)}, s32[16,13]{1,0:T(8,128)}, u32[]{:S(2)}) copy-start(s32[16,13]{1,0:T(8,128)} %param.32) | copy-start | bytes 2500
  0.7 10.1 %copy-start.11 = (s32[2048]{0:T(1024)S(1)}, s32[2048]{0:T(1024)}, u32[]{:S(2)}) copy-start(s32[2048]{0:T(1024)} %param.21) | copy-start | bytes 24580
  0.7 8.5 %collective-permute-start = (bf16[1,256,192]{1,2,0:T(8,128)(2,1)}, bf16[1,256,192]{1,2,0:T(8,128)(2,1)S(1)}, u32[]{:S(2)}, u32[]{:S(2)}) collective-permute-start(bf16[1,256,192]{1,2,0:T(8,128)(2,1)} %bitcast.220), channel_id=1, source_target_pairs={{0,1},{1,2},{2,3},{3,0},{4,5},{5,6},{6,7},{7,4},{8,9},{9,10},{10,1... | collective-permute-start | bytes 294920 | tf_op jit(solution)/shard_map/ppermute | solution.py:43
  0.8 7.8 %collective-permute-start.2 = (bf16[1,192,128]{2,1,0:T(8,128)(2,1)}, bf16[1,192,128]{2,1,0:T(8,128)(2,1)S(1)}, u32[]{:S(2)}, u32[]{:S(2)}) collective-permute-start(bf16[1,192,128]{2,1,0:T(8,128)(2,1)} %bitcast.223), channel_id=1, source_target_pairs={{0,1},{1,2},{2,3},{3,0},{4,5},{5,6},{6,7},{7,4},{8,9},{9,10},{10,1... | collective-permute-start | bytes 147464 | tf_op jit(solution)/shard_map/ppermute | solution.py:43
  8.5 15.3 %copy-start.12 = (f32[3,2,128]{2,1,0:T(2,128)S(1)}, f32[3,2,128]{2,1,0:T(2,128)}, u32[]{:S(2)}) copy-start(f32[3,2,128]{2,1,0:T(2,128)} %param.30) | copy-start | bytes 9220
  8.5 16.7 %copy-start.3 = (bf16[2048,128]{1,0:T(8,128)(2,1)S(1)}, bf16[2048,128]{1,0:T(8,128)(2,1)}, u32[]{:S(2)}) copy-start(bf16[2048,128]{1,0:T(8,128)(2,1)} %param.20) | copy-start | bytes 1572868
  8.6 5.7 %collective-permute-start.3 = (bf16[2,192,128]{2,1,0:T(8,128)(2,1)S(1)}, bf16[2,192,128]{2,1,0:T(8,128)(2,1)S(1)}, u32[]{:S(2)}, u32[]{:S(2)}) collective-permute-start(bf16[2,192,128]{2,1,0:T(8,128)(2,1)S(1)} %pad_maximum_fusion.2), channel_id=1, source_target_pairs={{0,2},{1,3},{2,0},{3,1},{4,6},{5,7},{6,4},{7,5},{8,10},{9,11},{10,... | collective-permute-start | bytes 294920 | tf_op jit(solution)/shard_map/ppermute | solution.py:43
  9.2 8.4 %collective-permute-start.1 = (bf16[2,256,192]{1,2,0:T(8,128)(2,1)S(1)}, bf16[2,256,192]{1,2,0:T(8,128)(2,1)S(1)}, u32[]{:S(2)}, u32[]{:S(2)}) collective-permute-start(bf16[2,256,192]{1,2,0:T(8,128)(2,1)S(1)} %pad_maximum_fusion.1), channel_id=1, source_target_pairs={{0,2},{1,3},{2,0},{3,1},{4,6},{5,7},{6,4},{7,5},{8,10},{9,11},{10,... | collective-permute-start | bytes 589832 | tf_op jit(solution)/shard_map/ppermute | solution.py:43
  18.0 7.3 %collective-permute-start.4 = (bf16[16,128]{1,0:T(8,128)(2,1)S(1)}, bf16[16,128]{1,0:T(8,128)(2,1)S(1)}, u32[]{:S(2)}, u32[]{:S(2)}) collective-permute-start(bf16[16,128]{1,0:T(8,128)(2,1)S(1)} %get-tuple-element.22), channel_id=1, source_target_pairs={{0,4},{4,8},{8,12},{12,16},{16,20},{20,24},{24,28},{1,5},{5,9},{9,... | collective-permute-start | bytes 12296 | tf_op jit(solution)/shard_map/ppermute | solution.py:31
  19.3 6.0 %collective-permute-start.5 = (bf16[16,128]{1,0:T(8,128)(2,1)S(1)}, bf16[16,128]{1,0:T(8,128)(2,1)S(1)}, u32[]{:S(2)}, u32[]{:S(2)}) collective-permute-start(bf16[16,128]{1,0:T(8,128)(2,1)S(1)} %get-tuple-element.23), channel_id=1, source_target_pairs={{4,0},{8,4},{12,8},{16,12},{20,16},{24,20},{28,24},{5,1},{9,5},{13... | collective-permute-start | bytes 12296 | tf_op jit(solution)/shard_map/ppermute | solution.py:32
  25.2 7.0 %copy-start.14 = (s32[16]{0:T(128)S(1)}, s32[16]{0:T(128)}, u32[]{:S(2)}) copy-start(s32[16]{0:T(128)} %count_ref.1) | copy-start | bytes 196
  26.1 8.2 %collective-permute-start.6 = (f32[1,176,128]{2,1,0:T(8,128)S(1)}, f32[1,176,128]{2,1,0:T(8,128)S(1)}, u32[]{:S(2)}, u32[]{:S(2)}) collective-permute-start(f32[1,176,128]{2,1,0:T(8,128)S(1)} %get-tuple-element.20), channel_id=1, source_target_pairs={{0,4},{4,8},{8,12},{12,16},{16,20},{20,24},{24,28},{1,5},{5,9},{9,... | collective-permute-start | bytes 270344 | tf_op jit(solution)/shard_map/ppermute | solution.py:31
  27.4 6.9 %collective-permute-start.7 = (f32[1,176,128]{2,1,0:T(8,128)S(1)}, f32[1,176,128]{2,1,0:T(8,128)S(1)}, u32[]{:S(2)}, u32[]{:S(2)}) collective-permute-start(f32[1,176,128]{2,1,0:T(8,128)S(1)} %get-tuple-element.21), channel_id=1, source_target_pairs={{4,0},{8,4},{12,8},{16,12},{20,16},{24,20},{28,24},{5,1},{9,5},{13... | collective-permute-start | bytes 270344 | tf_op jit(solution)/shard_map/ppermute | solution.py:32
  38.3 20.4 %copy-start.7 = (bf16[3,128,128]{2,1,0:T(8,128)(2,1)S(1)}, bf16[3,128,128]{2,1,0:T(8,128)(2,1)}, u32[]{:S(2)}) copy-start(bf16[3,128,128]{2,1,0:T(8,128)(2,1)} %param.27) | copy-start | bytes 294916
  58.8 1.7 %copy-start.4 = (bf16[3,128,512]{2,1,0:T(8,128)(2,1)S(1)}, bf16[3,128,512]{2,1,0:T(8,128)(2,1)}, u32[]{:S(2)}) copy-start(bf16[3,128,512]{2,1,0:T(8,128)(2,1)} %param.28) | copy-start | bytes 1179652
  60.5 0.9 copy-start.15
  61.4 1.0 copy-start.5
  110.8 0.9 copy-start.1
  110.8 0.9 copy-start.6
  110.8 0.9 copy-start.13
  112.9 10.6 %collective-permute-start.8 = (f32[7,2048]{1,0:T(8,128)S(1)}, f32[7,2048]{1,0:T(8,128)S(1)}, u32[]{:S(2)}, u32[]{:S(2)}) collective-permute-start(f32[7,2048]{1,0:T(8,128)S(1)} %get-tuple-element.17), channel_id=1, source_target_pairs={{0,4},{4,8},{8,12},{12,16},{16,20},{20,24},{24,28},{28,0},{1,5},{5... | collective-permute-start | bytes 172040 | tf_op jit(solution)/shard_map/ppermute | solution.py:49
  117.4 8.9 %collective-permute-start.9 = (f32[7,2048]{1,0:T(8,128)S(1)}, f32[7,2048]{1,0:T(8,128)S(1)}, u32[]{:S(2)}, u32[]{:S(2)}) collective-permute-start(f32[7,2048]{1,0:T(8,128)S(1)} %get-tuple-element.17), channel_id=1, source_target_pairs={{0,8},{4,12},{8,16},{12,20},{16,24},{20,28},{24,0},{28,4},{1,9},{5... | collective-permute-start | bytes 172040 | tf_op jit(solution)/shard_map/ppermute | solution.py:49
  118.9 7.9 %collective-permute-start.10 = (f32[7,2048]{1,0:T(8,128)S(1)}, f32[7,2048]{1,0:T(8,128)S(1)}, u32[]{:S(2)}, u32[]{:S(2)}) collective-permute-start(f32[7,2048]{1,0:T(8,128)S(1)} %get-tuple-element.17), channel_id=1, source_target_pairs={{0,12},{4,16},{8,20},{12,24},{16,28},{20,0},{24,4},{28,8},{1,13},{... | collective-permute-start | bytes 172040 | tf_op jit(solution)/shard_map/ppermute | solution.py:49
  120.5 6.4 %collective-permute-start.11 = (f32[7,2048]{1,0:T(8,128)S(1)}, f32[7,2048]{1,0:T(8,128)S(1)}, u32[]{:S(2)}, u32[]{:S(2)}) collective-permute-start(f32[7,2048]{1,0:T(8,128)S(1)} %get-tuple-element.17), channel_id=1, source_target_pairs={{0,16},{4,20},{8,24},{12,28},{16,0},{20,4},{24,8},{28,12},{1,17},{... | collective-permute-start | bytes 172040 | tf_op jit(solution)/shard_map/ppermute | solution.py:49
  121.8 7.9 %collective-permute-start.12 = (f32[7,2048]{1,0:T(8,128)S(1)}, f32[7,2048]{1,0:T(8,128)S(1)}, u32[]{:S(2)}, u32[]{:S(2)}) collective-permute-start(f32[7,2048]{1,0:T(8,128)S(1)} %get-tuple-element.17), channel_id=1, source_target_pairs={{0,20},{4,24},{8,28},{12,0},{16,4},{20,8},{24,12},{28,16},{1,21},{... | collective-permute-start | bytes 172040 | tf_op jit(solution)/shard_map/ppermute | solution.py:49
  123.5 6.2 %collective-permute-start.13 = (f32[7,2048]{1,0:T(8,128)S(1)}, f32[7,2048]{1,0:T(8,128)S(1)}, u32[]{:S(2)}, u32[]{:S(2)}) collective-permute-start(f32[7,2048]{1,0:T(8,128)S(1)} %get-tuple-element.17), channel_id=1, source_target_pairs={{0,24},{4,28},{8,0},{12,4},{16,8},{20,12},{24,16},{28,20},{1,25},{... | collective-permute-start | bytes 172040 | tf_op jit(solution)/shard_map/ppermute | solution.py:49
  126.3 7.0 %collective-permute-start.14 = (f32[7,2048]{1,0:T(8,128)S(1)}, f32[7,2048]{1,0:T(8,128)S(1)}, u32[]{:S(2)}, u32[]{:S(2)}) collective-permute-start(f32[7,2048]{1,0:T(8,128)S(1)} %get-tuple-element.17), channel_id=1, source_target_pairs={{0,28},{4,0},{8,4},{12,8},{16,12},{20,16},{24,20},{28,24},{1,29},{... | collective-permute-start | bytes 172040 | tf_op jit(solution)/shard_map/ppermute | solution.py:49
  133.3 0.8 copy-start.2

commit v17 on v16

--- a/solution.py
+++ b/solution.py
@@ -1,3 +1,4 @@
+import functools
 import math
 
 import jax
@@ -58,15 +59,16 @@
 K_SPAN = 256
 
 
-def attend_kernel(q_ref, kv_ref, band_ref, valid_ref, out_ref):
+def attend_kernel(qkv_ref, band_ref, valid_ref, out_ref, *, kv_off):
     tile = pl.program_id(0)
-    head_dim = q_ref.shape[1] // HEADS
-    channels = q_ref.shape[1]
+    channels = out_ref.shape[1]
+    head_dim = channels // HEADS
     scale = head_dim ** (-0.5)
     start = pl.multiple_of(tile * Q_TILE, Q_TILE)
-    keys_vals = kv_ref[pl.ds(start, K_SPAN), :]
+    block = qkv_ref[pl.ds(start + kv_off, K_SPAN), :]
+    keys_vals = block[:, channels:]
+    query_rows = qkv_ref[pl.ds(start + kv_off + (KWIN - QBLK) // 2, Q_TILE), :][:, :channels]
     live = (band_ref[...] * valid_ref[pl.ds(tile, 1), :]) > 0.0
-    query_rows = q_ref[...]
     heads = []
     for head in range(HEADS):
         cols = slice(head * head_dim, (head + 1) * head_dim)
@@ -88,22 +90,19 @@
     out_ref[...] = jnp.concatenate(heads, axis=1)
 
 
-def window_attend(queries, padded_kv, band, valid_tab):
-    atoms, channels = queries.shape
-    extra = atoms + K_SPAN - Q_TILE - padded_kv.shape[0]
-    padded_kv = jnp.pad(padded_kv, ((0, extra), (0, 0)))
+def window_attend(qkv, kv_off, tiles, band, valid_tab):
+    channels = qkv.shape[1] // 3
     return pl.pallas_call(
-        attend_kernel,
-        grid=(atoms // Q_TILE,),
+        functools.partial(attend_kernel, kv_off=kv_off),
+        grid=(tiles,),
         in_specs=[
-            pl.BlockSpec((Q_TILE, channels), lambda t: (t, 0)),
-            pl.BlockSpec(padded_kv.shape, lambda t: (0, 0)),
+            pl.BlockSpec(qkv.shape, lambda t: (0, 0)),
             pl.BlockSpec(band.shape, lambda t: (0, 0)),
             pl.BlockSpec(valid_tab.shape, lambda t: (0, 0)),
         ],
         out_specs=pl.BlockSpec((Q_TILE, channels), lambda t: (t, 0)),
-        out_shape=jax.ShapeDtypeStruct((atoms, channels), jnp.bfloat16),
-    )(queries, padded_kv, band, valid_tab)
+        out_shape=jax.ShapeDtypeStruct((tiles * Q_TILE, channels), jnp.bfloat16),
+    )(qkv, band, valid_tab)
 
 ROW_CHUNK = 128
 
@@ -259,10 +258,8 @@
         qkv_all = dense(normed, w_qkv[layer_index]).astype(jnp.bfloat16)
         span_rows = kv_off + tiles * Q_TILE + K_SPAN - Q_TILE
         qkv_all = jnp.pad(qkv_all, ((0, 0), (0, max(0, span_rows - qkv_all.shape[1])), (0, 0)))
-        queries = qkv_all[:, q_off : q_off + tiles * Q_TILE, :channels]
-        key_vals = qkv_all[:, kv_off:span_rows, channels:]
         attended = jnp.stack(
-            [window_attend(queries[s], key_vals[s], band, valid_tab) for s in range(samples)]
+            [window_attend(qkv_all[s], kv_off, tiles, band, valid_tab) for s in range(samples)]
         )
         hidden = jnp.pad(hidden, ((0, 0), (0, max(0, span_rows - hidden.shape[1])), (0, 0)))
         hidden = hidden[:, q_off : q_off + tiles * Q_TILE] + dense(attended, w_o[layer_index])

time: 167 us -> 164 us (0.982)
    pallas_call x1, Pallas kernels: 28.9 us -> 27 us  [lddt_sums(): pl.pallas_call(lddt_kernel, grid_spec=pltpu.PrefetchScalarGridSpec(num_sc...]
    squeeze x6 -> x3, local copies, waits for them, and re-layouts: 5.91 us -> 4.27 us  [on_device(): qkv_all[s]]
where the time goes in v17:
time: 164 us
  Pallas kernels  85.5 us (52%)
  starting transfers between devices  28.4 us (17%)
  matrix products  17.6 us (11%)
  waiting for transfers between devices  13.3 us (8%)
  local copies, waits for them, and re-layouts  8.23 us (5%)
  other arithmetic  6.73 us (4%)
  between operations  3.86 us (2%)
    pallas_call x3, Pallas kernels, window_attend(): pl.pallas_call(functools.partial(attend_kernel, kv_off=kv_off), grid=(til...  58.4 us
    pallas_call x1, Pallas kernels, lddt_sums(): pl.pallas_call(lddt_kernel, grid_spec=pltpu.PrefetchScalarGridSpec(num_sc...  27 us
    dot_general x12, matrix products, dense(): jnp.einsum('sac,cf->saf', left, right, preferred_element_type=jnp.float32)  12.7 us
    ppermute x7, starting transfers between devices, ring_parts(): extra.append(lax.ppermute(value, axis, pairs)[None])  12.5 us
    ppermute x2, starting transfers between devices, extended(): after = lax.ppermute(first, axis, down)  9.4 us
    ppermute x4, waiting for transfers between devices, ring_parts(): parts = jnp.concatenate([parts, lax.ppermute(parts, axis, pairs)])  6.83 us
    ppermute x7, waiting for transfers between devices, ring_parts(): extra.append(lax.ppermute(value, axis, pairs)[None])  6.44 us
    squeeze x3, local copies, waits for them, and re-layouts, on_device(): qkv_all[s]  4.27 us
  transfers between devices with their start and end apart: 15, of which 5 were waited for; matrix products, arithmetic and copies ran while one was open for 5% of the time, Pallas kernels for 0%

profile of v17, /device:TPU:26, one launch (start us, length us, event | category | flops | bytes accessed | tf_op | source)
XLA Modules:
  0.0 163.5 jit_solution(17510311107402754954)
XLA Ops:
  0.8 1.6 collective-permute-start.2
  5.9 2.6 %fusion.92 = f32[2048,128]{1,0:T(8,128)S(1)} fusion(f32[3,128]{1,0:T(4,128)S(1)} %copy-done, f32[]{:T(128)} %bitcast.8, f32[3,2048]{1,0:T(4,128)} %param.22, f32[1,3,2048]{2,0,1:T(1,128)} %param.23, f32[]{:T(128)} %bitcast.206), kind=kOutput, calls=%fused_computation.135 | convolution fusion | flops 9455616 | bytes 1099272 | tf_op jit(solution)/shard_map/sda,dc->sac/dot_general | solution.py:234
  9.2 1.6 collective-permute-start.1
  10.8 3.5 %collective-permute-done.3 = bf16[2,192,128]{2,1,0:T(8,128)(2,1)S(1)} collective-permute-done((bf16[2,192,128]{2,1,0:T(8,128)(2,1)S(1)}, bf16[2,192,128]{2,1,0:T(8,128)(2,1)S(1)}, u32[]{:S(2)}, u32[]{:S(2)}) %collective-permute-start.3) | collective-permute-done | bytes 98336 | tf_op jit(solution)/shard_map/ppermute | solution.py:44
  14.3 3.3 %collective-permute-done.1 = bf16[2,256,192]{1,2,0:T(8,128)(2,1)S(1)} collective-permute-done((bf16[2,256,192]{1,2,0:T(8,128)(2,1)S(1)}, bf16[2,256,192]{1,2,0:T(8,128)(2,1)S(1)}, u32[]{:S(2)}, u32[]{:S(2)}) %collective-permute-start.1) | collective-permute-done | bytes 196640 | tf_op jit(solution)/shard_map/ppermute | solution.py:44
  18.0 1.3 collective-permute-start.4
  19.3 4.5 %collective-permute-start.5 = (bf16[16,128]{1,0:T(8,128)(2,1)S(1)}, bf16[16,128]{1,0:T(8,128)(2,1)S(1)}, u32[]{:S(2)}, u32[]{:S(2)}) collective-permute-start(bf16[16,128]{1,0:T(8,128)(2,1)S(1)} %get-tuple-element.23), channel_id=1, source_target_pairs={{4,0},{8,4},{12,8},{16,12},{20,16},{24,20},{28,24},{5,1},{9,5},{13... | collective-permute-start | bytes 12296 | tf_op jit(solution)/shard_map/ppermute | solution.py:33
  26.1 1.3 collective-permute-start.6
  27.4 4.9 %collective-permute-start.7 = (f32[1,176,128]{2,1,0:T(8,128)S(1)}, f32[1,176,128]{2,1,0:T(8,128)S(1)}, u32[]{:S(2)}, u32[]{:S(2)}) collective-permute-start(f32[1,176,128]{2,1,0:T(8,128)S(1)} %get-tuple-element.21), channel_id=1, source_target_pairs={{4,0},{8,4},{12,8},{16,12},{20,16},{24,20},{28,24},{5,1},{9,5},{13... | collective-permute-start | bytes 270344 | tf_op jit(solution)/shard_map/ppermute | solution.py:33
  34.7 1.6 fusion.2
  36.3 1.5 pad_bitcast_fusion.qkv_ref
  37.8 20.6 %shard_map.167 = bf16[2304,128]{1,0:T(8,128)(2,1)} custom-call(bf16[2432,384]{1,0:T(8,128)(2,1)} %pad_bitcast_fusion.qkv_ref, f32[128,256]{1,0:T(8,128)} %fusion.69.band_ref, f32[18,256]{1,0:T(8,128)} %fusion.104.valid_ref), custom_call_target="tpu_custom_call" | custom-call | tf_op jit(solution)/shard_map/pallas_call | solution.py:95
  58.3 1.7 %multiply_reduce_fusion.2 = (f32[2304]{0:T(1024)S(1)}, f32[1,2304,128]{2,1,0:T(8,128)S(1)}) fusion(bf16[2304,128]{1,0:T(8,128)(2,1)} %shard_map.167, bf16[3,128,128]{2,1,0:T(8,128)(2,1)S(1)} %copy-done.7, f32[1,2400,128]{2,1,0:T(8,128)S(1)} %get-tuple-element.19), kind=kOutput, calls=%fused_computation.47 | convolution fusion | flops 76379904 | bytes 2991104 | tf_op jit(solution)/shard_map/sac,cf->saf/dot_general | solution.py:189
  61.0 0.9 multiply_reduce_fusion.1
  62.6 1.4 pad_bitcast_fusion.1.qkv_ref
  64.0 19.5 %shard_map.168 = bf16[2176,128]{1,0:T(8,128)(2,1)} custom-call(bf16[2320,384]{1,0:T(8,128)(2,1)} %pad_bitcast_fusion.1.qkv_ref, f32[128,256]{1,0:T(8,128)} %fusion.69.band_ref, f32[17,256]{1,0:T(8,128)} %fusion.106.valid_ref), custom_call_target="tpu_custom_call" | custom-call | tf_op jit(solution)/shard_map/pallas_call | solution.py:95
  83.5 1.6 multiply_reduce_fusion.4
  85.9 0.9 multiply_reduce_fusion.3
  87.4 1.4 pad_bitcast_fusion.2.qkv_ref
  88.8 18.4 %shard_map.169 = bf16[2048,128]{1,0:T(8,128)(2,1)} custom-call(bf16[2192,384]{1,0:T(8,128)(2,1)} %pad_bitcast_fusion.2.qkv_ref, f32[128,256]{1,0:T(8,128)} %fusion.69.band_ref, f32[16,256]{1,0:T(8,128)} %fusion.111.valid_ref), custom_call_target="tpu_custom_call" | custom-call | tf_op jit(solution)/shard_map/pallas_call | solution.py:95
  107.2 1.5 multiply_reduce_fusion.6
  110.5 1.2 fusion.14
  111.6 4.5 %collective-permute-start.8 = (f32[7,2048]{1,0:T(8,128)S(1)}, f32[7,2048]{1,0:T(8,128)S(1)}, u32[]{:S(2)}, u32[]{:S(2)}) collective-permute-start(f32[7,2048]{1,0:T(8,128)S(1)} %get-tuple-element.17), channel_id=1, source_target_pairs={{0,4},{4,8},{8,12},{12,16},{16,20},{20,24},{24,28},{28,0},{1,5},{5... | collective-permute-start | bytes 172040 | tf_op jit(solution)/shard_map/ppermute | solution.py:50
  116.1 1.6 collective-permute-start.9
  117.7 1.6 collective-permute-start.10
  119.3 1.2 collective-permute-start.11
  120.9 1.3 copy.25.own_ref
  122.2 2.8 %collective-permute-start.13 = (f32[7,2048]{1,0:T(8,128)S(1)}, f32[7,2048]{1,0:T(8,128)S(1)}, u32[]{:S(2)}, u32[]{:S(2)}) collective-permute-start(f32[7,2048]{1,0:T(8,128)S(1)} %get-tuple-element.17), channel_id=1, source_target_pairs={{0,24},{4,28},{8,0},{12,4},{16,8},{20,12},{24,16},{28,20},{1,25},{... | collective-permute-start | bytes 172040 | tf_op jit(solution)/shard_map/ppermute | solution.py:50
  125.7 2.7 %collective-permute-done.12 = f32[7,2048]{1,0:T(8,128)S(1)} collective-permute-done((f32[7,2048]{1,0:T(8,128)S(1)}, f32[7,2048]{1,0:T(8,128)S(1)}, u32[]{:S(2)}, u32[]{:S(2)}) %collective-permute-start.12) | collective-permute-done | bytes 57376 | tf_op jit(solution)/shard_map/ppermute | solution.py:50
  128.5 3.6 %collective-permute-done.14 = f32[7,2048]{1,0:T(8,128)S(1)} collective-permute-done((f32[7,2048]{1,0:T(8,128)S(1)}, f32[7,2048]{1,0:T(8,128)S(1)}, u32[]{:S(2)}, u32[]{:S(2)}) %collective-permute-start.14) | collective-permute-done | bytes 57376 | tf_op jit(solution)/shard_map/ppermute | solution.py:50
  132.9 27.0 %shard_map.170 = f32[2048,8]{1,0:T(8,128)} custom-call(s32[208]{0:T(256)} %reshape.383.slots_ref, s32[16]{0:T(128)} %count_ref.1, f32[2048,8]{1,0:T(8,128)} %copy.25.own_ref, f32[8,7,2048]{2,1,0:T(8,128)} %copy-done.2), custom_call_target="tpu_custom_call" | custom-call | tf_op jit(solution)/shard_map/pallas_call | solution.py:169
  160.6 1.3 slice_multiply_fusion.3
  (97 shorter events, 15.3 us)
Async XLA Ops:
  0.6 5.3 %copy-start = (f32[3,128]{1,0:T(4,128)S(1)}, f32[3,128]{1,0:T(4,128)}, u32[]{:S(2)}) copy-start(f32[3,128]{1,0:T(4,128)} %param.25) | copy-start | bytes 4612
  0.6 8.5 %copy-start.8 = (bf16[256,192]{0,1:T(8,128)(2,1)S(1)}, bf16[256,192]{0,1:T(8,128)(2,1)}, u32[]{:S(2)}) copy-start(bf16[256,192]{0,1:T(8,128)(2,1)} %param.18) | copy-start | bytes 294916
  0.7 7.9 %copy-start.9 = (bf16[192,128]{1,0:T(8,128)(2,1)S(1)}, bf16[192,128]{1,0:T(8,128)(2,1)}, u32[]{:S(2)}) copy-start(bf16[192,128]{1,0:T(8,128)(2,1)} %param.19) | copy-start | bytes 147460
  0.7 7.8 %copy-start.10 = (s32[16,13]{1,0:T(8,128)S(1)}, s32[16,13]{1,0:T(8,128)}, u32[]{:S(2)}) copy-start(s32[16,13]{1,0:T(8,128)} %param.32) | copy-start | bytes 2500
  0.7 10.1 %copy-start.11 = (s32[2048]{0:T(1024)S(1)}, s32[2048]{0:T(1024)}, u32[]{:S(2)}) copy-start(s32[2048]{0:T(1024)} %param.21) | copy-start | bytes 24580
  0.7 8.5 %collective-permute-start = (bf16[1,256,192]{1,2,0:T(8,128)(2,1)}, bf16[1,256,192]{1,2,0:T(8,128)(2,1)S(1)}, u32[]{:S(2)}, u32[]{:S(2)}) collective-permute-start(bf16[1,256,192]{1,2,0:T(8,128)(2,1)} %bitcast.214), channel_id=1, source_target_pairs={{0,1},{1,2},{2,3},{3,0},{4,5},{5,6},{6,7},{7,4},{8,9},{9,10},{10,1... | collective-permute-start | bytes 294920 | tf_op jit(solution)/shard_map/ppermute | solution.py:44
  0.8 7.8 %collective-permute-start.2 = (bf16[1,192,128]{2,1,0:T(8,128)(2,1)}, bf16[1,192,128]{2,1,0:T(8,128)(2,1)S(1)}, u32[]{:S(2)}, u32[]{:S(2)}) collective-permute-start(bf16[1,192,128]{2,1,0:T(8,128)(2,1)} %bitcast.217), channel_id=1, source_target_pairs={{0,1},{1,2},{2,3},{3,0},{4,5},{5,6},{6,7},{7,4},{8,9},{9,10},{10,1... | collective-permute-start | bytes 147464 | tf_op jit(solution)/shard_map/ppermute | solution.py:44
  8.5 15.3 %copy-start.12 = (f32[3,2,128]{2,1,0:T(2,128)S(1)}, f32[3,2,128]{2,1,0:T(2,128)}, u32[]{:S(2)}) copy-start(f32[3,2,128]{2,1,0:T(2,128)} %param.30) | copy-start | bytes 9220
  8.5 16.8 %copy-start.3 = (bf16[2048,128]{1,0:T(8,128)(2,1)S(1)}, bf16[2048,128]{1,0:T(8,128)(2,1)}, u32[]{:S(2)}) copy-start(bf16[2048,128]{1,0:T(8,128)(2,1)} %param.20) | copy-start | bytes 1572868
  8.6 5.7 %collective-permute-start.3 = (bf16[2,192,128]{2,1,0:T(8,128)(2,1)S(1)}, bf16[2,192,128]{2,1,0:T(8,128)(2,1)S(1)}, u32[]{:S(2)}, u32[]{:S(2)}) collective-permute-start(bf16[2,192,128]{2,1,0:T(8,128)(2,1)S(1)} %pad_maximum_fusion.2), channel_id=1, source_target_pairs={{0,2},{1,3},{2,0},{3,1},{4,6},{5,7},{6,4},{7,5},{8,10},{9,11},{10,... | collective-permute-start | bytes 294920 | tf_op jit(solution)/shard_map/ppermute | solution.py:44
  9.2 8.4 %collective-permute-start.1 = (bf16[2,256,192]{1,2,0:T(8,128)(2,1)S(1)}, bf16[2,256,192]{1,2,0:T(8,128)(2,1)S(1)}, u32[]{:S(2)}, u32[]{:S(2)}) collective-permute-start(bf16[2,256,192]{1,2,0:T(8,128)(2,1)S(1)} %pad_maximum_fusion.1), channel_id=1, source_target_pairs={{0,2},{1,3},{2,0},{3,1},{4,6},{5,7},{6,4},{7,5},{8,10},{9,11},{10,... | collective-permute-start | bytes 589832 | tf_op jit(solution)/shard_map/ppermute | solution.py:44
  18.0 7.3 %collective-permute-start.4 = (bf16[16,128]{1,0:T(8,128)(2,1)S(1)}, bf16[16,128]{1,0:T(8,128)(2,1)S(1)}, u32[]{:S(2)}, u32[]{:S(2)}) collective-permute-start(bf16[16,128]{1,0:T(8,128)(2,1)S(1)} %get-tuple-element.22), channel_id=1, source_target_pairs={{0,4},{4,8},{8,12},{12,16},{16,20},{20,24},{24,28},{1,5},{5,9},{9,... | collective-permute-start | bytes 12296 | tf_op jit(solution)/shard_map/ppermute | solution.py:32
  19.3 6.0 %collective-permute-start.5 = (bf16[16,128]{1,0:T(8,128)(2,1)S(1)}, bf16[16,128]{1,0:T(8,128)(2,1)S(1)}, u32[]{:S(2)}, u32[]{:S(2)}) collective-permute-start(bf16[16,128]{1,0:T(8,128)(2,1)S(1)} %get-tuple-element.23), channel_id=1, source_target_pairs={{4,0},{8,4},{12,8},{16,12},{20,16},{24,20},{28,24},{5,1},{9,5},{13... | collective-permute-start | bytes 12296 | tf_op jit(solution)/shard_map/ppermute | solution.py:33
  25.2 7.0 %copy-start.14 = (s32[16]{0:T(128)S(1)}, s32[16]{0:T(128)}, u32[]{:S(2)}) copy-start(s32[16]{0:T(128)} %count_ref.1) | copy-start | bytes 196
  26.1 8.2 %collective-permute-start.6 = (f32[1,176,128]{2,1,0:T(8,128)S(1)}, f32[1,176,128]{2,1,0:T(8,128)S(1)}, u32[]{:S(2)}, u32[]{:S(2)}) collective-permute-start(f32[1,176,128]{2,1,0:T(8,128)S(1)} %get-tuple-element.20), channel_id=1, source_target_pairs={{0,4},{4,8},{8,12},{12,16},{16,20},{20,24},{24,28},{1,5},{5,9},{9,... | collective-permute-start | bytes 270344 | tf_op jit(solution)/shard_map/ppermute | solution.py:32
  27.4 6.9 %collective-permute-start.7 = (f32[1,176,128]{2,1,0:T(8,128)S(1)}, f32[1,176,128]{2,1,0:T(8,128)S(1)}, u32[]{:S(2)}, u32[]{:S(2)}) collective-permute-start(f32[1,176,128]{2,1,0:T(8,128)S(1)} %get-tuple-element.21), channel_id=1, source_target_pairs={{4,0},{8,4},{12,8},{16,12},{20,16},{24,20},{28,24},{5,1},{9,5},{13... | collective-permute-start | bytes 270344 | tf_op jit(solution)/shard_map/ppermute | solution.py:33
  37.8 20.6 %copy-start.7 = (bf16[3,128,128]{2,1,0:T(8,128)(2,1)S(1)}, bf16[3,128,128]{2,1,0:T(8,128)(2,1)}, u32[]{:S(2)}) copy-start(bf16[3,128,128]{2,1,0:T(8,128)(2,1)} %param.27) | copy-start | bytes 294916
  58.3 1.7 %copy-start.4 = (bf16[3,128,512]{2,1,0:T(8,128)(2,1)S(1)}, bf16[3,128,512]{2,1,0:T(8,128)(2,1)}, u32[]{:S(2)}) copy-start(bf16[3,128,512]{2,1,0:T(8,128)(2,1)} %param.28) | copy-start | bytes 1179652
  60.0 0.9 copy-start.15
  61.0 1.0 copy-start.5
  109.6 0.9 copy-start.1
  109.6 0.9 copy-start.6
  109.6 0.9 copy-start.13
  111.6 10.6 %collective-permute-start.8 = (f32[7,2048]{1,0:T(8,128)S(1)}, f32[7,2048]{1,0:T(8,128)S(1)}, u32[]{:S(2)}, u32[]{:S(2)}) collective-permute-start(f32[7,2048]{1,0:T(8,128)S(1)} %get-tuple-element.17), channel_id=1, source_target_pairs={{0,4},{4,8},{8,12},{12,16},{16,20},{20,24},{24,28},{28,0},{1,5},{5... | collective-permute-start | bytes 172040 | tf_op jit(solution)/shard_map/ppermute | solution.py:50
  116.1 8.9 %collective-permute-start.9 = (f32[7,2048]{1,0:T(8,128)S(1)}, f32[7,2048]{1,0:T(8,128)S(1)}, u32[]{:S(2)}, u32[]{:S(2)}) collective-permute-start(f32[7,2048]{1,0:T(8,128)S(1)} %get-tuple-element.17), channel_id=1, source_target_pairs={{0,8},{4,12},{8,16},{12,20},{16,24},{20,28},{24,0},{28,4},{1,9},{5... | collective-permute-start | bytes 172040 | tf_op jit(solution)/shard_map/ppermute | solution.py:50
  117.7 7.9 %collective-permute-start.10 = (f32[7,2048]{1,0:T(8,128)S(1)}, f32[7,2048]{1,0:T(8,128)S(1)}, u32[]{:S(2)}, u32[]{:S(2)}) collective-permute-start(f32[7,2048]{1,0:T(8,128)S(1)} %get-tuple-element.17), channel_id=1, source_target_pairs={{0,12},{4,16},{8,20},{12,24},{16,28},{20,0},{24,4},{28,8},{1,13},{... | collective-permute-start | bytes 172040 | tf_op jit(solution)/shard_map/ppermute | solution.py:50
  119.3 6.4 %collective-permute-start.11 = (f32[7,2048]{1,0:T(8,128)S(1)}, f32[7,2048]{1,0:T(8,128)S(1)}, u32[]{:S(2)}, u32[]{:S(2)}) collective-permute-start(f32[7,2048]{1,0:T(8,128)S(1)} %get-tuple-element.17), channel_id=1, source_target_pairs={{0,16},{4,20},{8,24},{12,28},{16,0},{20,4},{24,8},{28,12},{1,17},{... | collective-permute-start | bytes 172040 | tf_op jit(solution)/shard_map/ppermute | solution.py:50
  120.5 7.9 %collective-permute-start.12 = (f32[7,2048]{1,0:T(8,128)S(1)}, f32[7,2048]{1,0:T(8,128)S(1)}, u32[]{:S(2)}, u32[]{:S(2)}) collective-permute-start(f32[7,2048]{1,0:T(8,128)S(1)} %get-tuple-element.17), channel_id=1, source_target_pairs={{0,20},{4,24},{8,28},{12,0},{16,4},{20,8},{24,12},{28,16},{1,21},{... | collective-permute-start | bytes 172040 | tf_op jit(solution)/shard_map/ppermute | solution.py:50
  122.2 6.2 %collective-permute-start.13 = (f32[7,2048]{1,0:T(8,128)S(1)}, f32[7,2048]{1,0:T(8,128)S(1)}, u32[]{:S(2)}, u32[]{:S(2)}) collective-permute-start(f32[7,2048]{1,0:T(8,128)S(1)} %get-tuple-element.17), channel_id=1, source_target_pairs={{0,24},{4,28},{8,0},{12,4},{16,8},{20,12},{24,16},{28,20},{1,25},{... | collective-permute-start | bytes 172040 | tf_op jit(solution)/shard_map/ppermute | solution.py:50
  125.1 7.0 %collective-permute-start.14 = (f32[7,2048]{1,0:T(8,128)S(1)}, f32[7,2048]{1,0:T(8,128)S(1)}, u32[]{:S(2)}, u32[]{:S(2)}) collective-permute-start(f32[7,2048]{1,0:T(8,128)S(1)} %get-tuple-element.17), channel_id=1, source_target_pairs={{0,28},{4,0},{8,4},{12,8},{16,12},{20,16},{24,20},{28,24},{1,29},{... | collective-permute-start | bytes 172040 | tf_op jit(solution)/shard_map/ppermute | solution.py:50
  132.1 0.8 copy-start.2
